TPU v7x, 32 devices: a whole 2x2x4 slice. The times are simulated.
32 devices in a mesh: blk: 4 (over y, x), patch: 8 (over z, core).
Axes of the slice: x: 2, y: 2, z: 4, core: 2. Of those that a mesh axis runs over, the one named last changes fastest.
Arguments:
- patches: bfloat16 [64, 256, 256], P(('blk', 'patch')), may hold values from -6 to 6
- owner_of_patch: int32 [64], P('blk'), may hold values from 0 to 7, as said below
- group_of_patch: int32 [64], P('blk'), may hold values from 0 to 31
- defocus: float32 [32], replicated, may hold values from 10 to 60
- templ_re: bfloat16 [16, 256, 256], P('blk'), may hold values from -6 to 6
- templ_im: bfloat16 [16, 256, 256], P('blk'), may hold values from -6 to 6
- orientation: int32 [16], replicated, may hold values from 0 to 15, each once
Outputs:
- top_map: float32 [128, 256, 256], P(('blk', 'patch'))
- mean_map: float32 [128, 256, 256], P(('blk', 'patch'))
- var_map: float32 [128, 256, 256], P(('blk', 'patch'))
- peak_table: float32 [128, 16], P(('blk', 'patch'))
Inputs may be any that keep to these rules, and one draw needn't show every extreme that they name: `owner_of_patch`: within each block of 16 consecutive entries, the 2 entries of one device name no owner more than 2 times and no owner is named more than 4 times; both bounds are reached in every block.
All inputs are finite; a program needn't handle non-finite values.
Results may differ from a plain program's by a relative error of at most 0.015.
Values may be sent and summed in bfloat16 or wider, within the bound.
No kernel may reach another device: no remote copies, remote signals or barrier semaphores. Data moves between devices by JAX's collectives and lax.ppermute only.
A program may use at most 256 MiB of HBM per device.

v0:
```python
import math

import jax
import jax.numpy as jnp
from jax import lax
from jax.sharding import PartitionSpec as P

SLOT = 2
CAP = 4
TILE_T = 4


AMPLITUDE = 0.07


def dft_tables(extent):
    indices = jnp.arange(extent, dtype=jnp.int32)
    turn_count = indices[:, None] * indices[None, :] % extent
    angles = turn_count.astype(jnp.float32) * (2.0 * math.pi / extent)
    return (jnp.cos(angles).astype(jnp.bfloat16), jnp.sin(angles).astype(jnp.bfloat16))


def ctf_filter(defocus_values, extent):
    indices = jnp.arange(extent, dtype=jnp.int32)
    signed = (
        jnp.where(indices < extent // 2, indices, indices - extent).astype(jnp.float32) / extent
    )
    radius = signed[:, None] * signed[:, None] + signed[None, :] * signed[None, :]
    phases = math.pi * defocus_values[:, None, None] * radius[None, :, :] - AMPLITUDE
    return -jnp.sin(phases)


def routing(row_owner, my_index):
    sources, number = row_owner.shape
    owner_ids = jnp.arange(sources, dtype=jnp.int32)
    owner_hits = (row_owner[:, :, None] == owner_ids[None, None, :]).astype(jnp.int32)
    earlier = jnp.cumsum(owner_hits, axis=1) - owner_hits
    rank_in = jnp.sum(earlier * owner_hits, axis=2)
    counts = jnp.sum(owner_hits, axis=1)
    slot_key = row_owner * SLOT + rank_in
    targets = jnp.arange(sources * SLOT, dtype=jnp.int32)
    matches = slot_key[:, :, None] == targets[None, None, :]
    local_idx = jnp.sum(
        jnp.where(matches, jnp.arange(number, dtype=jnp.int32)[None, :, None], 0), axis=1
    )
    send_table = jnp.where(jnp.any(matches, axis=1), local_idx, number)
    arrived = lax.dynamic_slice_in_dim(counts, my_index, 1, 1)[:, 0]
    offsets = jnp.cumsum(arrived) - arrived
    within = jnp.arange(SLOT, dtype=jnp.int32)
    usable = within[None, :] < arrived[:, None]
    position = jnp.where(usable, offsets[:, None] + within[None, :], -1).reshape(-1)
    slot_ids = jnp.arange(CAP, dtype=jnp.int32)
    picked = position[None, :] == slot_ids[:, None]
    received_row = jnp.sum(jnp.where(picked, targets[None, :], 0), axis=1)
    take_table = jnp.where(jnp.any(picked, axis=1), received_row, sources * SLOT)
    my_columns = lax.dynamic_slice_in_dim(send_table, my_index * SLOT, SLOT, 1)
    row_of = jnp.where(
        my_columns < number, owner_ids[:, None] * number + my_columns, sources * number
    ).reshape(-1)
    row_of = jnp.concatenate([row_of, jnp.full((1,), sources * number, jnp.int32)])
    slot_row = jnp.take(row_of, take_table)
    my_send = lax.dynamic_slice_in_dim(send_table, my_index, 1, 0)[0]
    return (my_send, take_table, slot_row)


def make_spectra(images, focus_values, cosine, sine):
    count, extent = (images.shape[0], images.shape[-1])
    flat_images = images.reshape(count * extent, extent)
    half_re = jnp.dot(flat_images, cosine, preferred_element_type=jnp.float32).astype(jnp.bfloat16)
    half_im = jnp.dot(flat_images, -sine, preferred_element_type=jnp.float32).astype(jnp.bfloat16)
    half_stack = jnp.concatenate(
        [half_re.reshape(count, extent, extent), half_im.reshape(count, extent, extent)], axis=1
    )
    left_real = jnp.concatenate([cosine, sine], axis=1)
    left_imag = jnp.concatenate([-sine, cosine], axis=1)
    real = jnp.einsum("xk,nky->nxy", left_real, half_stack, preferred_element_type=jnp.float32)
    imag = jnp.einsum("xk,nky->nxy", left_imag, half_stack, preferred_element_type=jnp.float32)
    scale = ctf_filter(focus_values, extent) / extent
    return ((real * scale).astype(jnp.bfloat16), (imag * scale).astype(jnp.bfloat16))


def correlate_all(spec_re, spec_im, templ_re, templ_im, orientation, cosine, sine):
    count, extent = (spec_re.shape[0], spec_re.shape[-1])
    orient_total = orientation.shape[0]
    forward_re = jnp.concatenate([cosine, -sine], axis=0)
    forward_im = jnp.concatenate([sine, cosine], axis=0)
    inverse_left = jnp.concatenate([cosine, -sine], axis=1)
    spec_rw = spec_re.astype(jnp.float32)[None]
    spec_iw = spec_im.astype(jnp.float32)[None]
    map_shape = (count, extent, extent)
    initial = (
        jnp.full(map_shape, -1e30, jnp.float32),
        jnp.zeros(map_shape, jnp.float32),
        jnp.zeros(map_shape, jnp.float32),
        jnp.zeros((count, orient_total), jnp.float32),
    )
    orient_ids = jnp.arange(orient_total, dtype=jnp.int32)

    def one_group(carry, item):
        group_re, group_im, which_ones = item
        top_now, totals, squares, peak_rows = carry
        tiles = group_re.shape[0]
        templ_rw = group_re.astype(jnp.float32)[:, None]
        templ_iw = group_im.astype(jnp.float32)[:, None]
        prod_re = (spec_rw * templ_rw + spec_iw * templ_iw).astype(jnp.bfloat16)
        prod_im = (spec_iw * templ_rw - spec_rw * templ_iw).astype(jnp.bfloat16)
        batch = tiles * count
        prod_cat = jnp.concatenate([prod_re, prod_im], axis=-1).reshape(batch * extent, 2 * extent)
        q_re = jnp.dot(prod_cat, forward_re, preferred_element_type=jnp.float32).astype(
            jnp.bfloat16
        )
        q_im = jnp.dot(prod_cat, forward_im, preferred_element_type=jnp.float32).astype(
            jnp.bfloat16
        )
        q_stack = jnp.concatenate(
            [q_re.reshape(batch, extent, extent), q_im.reshape(batch, extent, extent)], axis=1
        )
        corr = (
            jnp.einsum("xk,nky->nxy", inverse_left, q_stack, preferred_element_type=jnp.float32)
            / extent
        )
        corr = corr.reshape(tiles, count, extent, extent)
        peak_now = jnp.max(corr, axis=(2, 3))
        one_hot = (orientation[which_ones][:, None] == orient_ids[None, :]).astype(jnp.float32)
        peak_add = jnp.sum(peak_now[:, :, None] * one_hot[:, None, :], axis=0)
        updated = (
            jnp.maximum(top_now, jnp.max(corr, axis=0)),
            totals + jnp.sum(corr, axis=0),
            squares + jnp.sum(corr * corr, axis=0),
            peak_rows + peak_add,
        )
        return (updated, None)

    carry = initial
    piece = (
        lax.all_gather(templ_re, "blk", axis=0, tiled=True),
        lax.all_gather(templ_im, "blk", axis=0, tiled=True),
    )
    pieces = piece[0].shape[0]
    blocks = pieces // TILE_T
    which_ones = jnp.arange(pieces, dtype=jnp.int32).reshape(blocks, TILE_T)
    grouped_re = piece[0].reshape(blocks, TILE_T, extent, extent)
    grouped_im = piece[1].reshape(blocks, TILE_T, extent, extent)
    carry, unused = lax.scan(one_group, carry, (grouped_re, grouped_im, which_ones))
    top_map, totals, squares, peak_rows = carry
    mean_map = totals / orient_total
    var_map = squares / orient_total - mean_map * mean_map
    return (top_map, mean_map, var_map, peak_rows)


def body(patches, owner_of_patch, group_of_patch, defocus, templ_re, templ_im, orientation):
    sources = lax.axis_size("patch")
    my_index = lax.axis_index("patch")
    number, extent = (patches.shape[0], patches.shape[1])
    cosine, sine = dft_tables(extent)
    row_owner = owner_of_patch.reshape(sources, number)
    my_send, take_table, slot_row = routing(row_owner, my_index)
    padded = jnp.concatenate([patches, jnp.zeros((1, extent, extent), jnp.bfloat16)], axis=0)
    outgoing = jnp.take(padded, my_send, axis=0).reshape(sources, SLOT, extent, extent)
    incoming = lax.all_to_all(outgoing, "patch", split_axis=0, concat_axis=0, tiled=True)
    flattened = jnp.concatenate(
        [
            incoming.reshape(sources * SLOT, extent, extent),
            jnp.zeros((1, extent, extent), jnp.bfloat16),
        ],
        axis=0,
    )
    my_slots = jnp.take(flattened, take_table, axis=0)
    groups = jnp.take(jnp.concatenate([group_of_patch, jnp.zeros((1,), jnp.int32)]), slot_row)
    focus_values = jnp.take(defocus, groups)
    spec_re, spec_im = make_spectra(my_slots, focus_values, cosine, sine)
    return correlate_all(spec_re, spec_im, templ_re, templ_im, orientation, cosine, sine)


def solution(mesh):
    placed = (
        P(("blk", "patch"), None, None),
        P("blk"),
        P("blk"),
        P(),
        P("blk", None, None),
        P("blk", None, None),
        P(),
    )
    return jax.shard_map(
        body,
        mesh=mesh,
        in_specs=placed,
        out_specs=(
            P(("blk", "patch"), None, None),
            P(("blk", "patch"), None, None),
            P(("blk", "patch"), None, None),
            P(("blk", "patch"), None),
        ),
        check_vma=False,
    )
```

profile of v0, /device:TPU:0, one launch (start us, length us, event | category | flops | bytes accessed | tf_op | source)
XLA Modules:
  0.0 213.4 jit_solution(6633334334820609648)
XLA Ops:
  11.4 1.6 broadcast_select_fusion
  13.1 6.5 %all-to-all-start = ((bf16[8,2,256,256]{3,2,1,0:T(8,128)(2,1)}), bf16[8,2,256,256]{3,2,1,0:T(8,128)(2,1)S(1)}, u32[]{:S(2)}, u32[]{:S(2)}) async-start(bf16[8,2,256,256]{3,2,1,0:T(8,128)(2,1)} %broadcast_select_fusion), calls=%async_computation | async-start | bytes 4194304 | tf_op jit(solution)/shard_map/all_to_all | solution.py:160
  27.3 41.3 %all-to-all-done = bf16[8,2,256,256]{3,2,1,0:T(8,128)(2,1)S(1)} async-done(((bf16[8,2,256,256]{3,2,1,0:T(8,128)(2,1)}), bf16[8,2,256,256]{3,2,1,0:T(8,128)(2,1)S(1)}, u32[]{:S(2)}, u32[]{:S(2)}) %all-to-all-start) | async-done | bytes 2097184 | tf_op jit(solution)/shard_map/all_to_all | solution.py:160
  68.6 1.7 concatenate.38
  70.2 2.4 %gather_fusion.2 = bf16[4,256,256]{2,1,0:T(8,128)(2,1)S(1)} fusion(bf16[17,256,256]{2,1,0:T(8,128)(2,1)} %concatenate.38, s32[1024]{0:T(1024)S(1)} %pad_clamp_fusion.4), kind=kCustom, calls=%fused_computation.4 | custom fusion | bytes 1048592 | tf_op jit(solution)/shard_map/jit(_take)/gather | solution.py:168
  72.9 1.2 convolution_convert_fusion.3
  74.3 1.2 convolution_convert_fusion.2
  75.8 4.6 %fusion.22 = f32[1,4,256,256]{2,3,1,0:T(8,128)S(1)} fusion(bf16[4,256,256]{1,2,0:T(8,128)(2,1)S(1)} %copy.61, bf16[4,256,256]{1,2,0:T(8,128)(2,1)S(1)} %copy.60, f32[256,256]{0,1:T(8,128)} %broadcast_add_fusion, f32[4]{0:T(128)S(1)} %fusion.48, bf16[256,256]{1,0:T(8,128)(2,1)S(1)} %cosine_convert_fusion, bf16[256,256]{1,0:T(8,128)(2,1)S(1)} %fusion.35), kind=kOutput, calls=%fused_computation.48 | convolution fusion | flops 272891904 | bytes 2621456 | tf_op jit(solution)/shard_map/xk,nky->nxy/dot_general | solution.py:77
  80.4 1.3 copy.64
  81.7 4.8 %fusion.20 = f32[1,4,256,256]{2,3,1,0:T(8,128)S(1)} fusion(bf16[4,256,256]{1,2,0:T(8,128)(2,1)S(1)} %copy.61, bf16[4,256,256]{1,2,0:T(8,128)(2,1)S(1)} %copy.60, f32[256,256]{0,1:T(8,128)} %broadcast_add_fusion, f32[4]{0:T(128)S(1)} %fusion.48, bf16[256,256]{1,0:T(8,128)(2,1)S(1)} %cosine_convert_fusion, bf16[256,256]{1,0:T(8,128)(2,1)S(1)} %sine_convert_fusion), kind=kOutput, calls=%fused_computation.46 | convolution fusion | flops 272891904 | bytes 2621456 | tf_op jit(solution)/shard_map/xk,nky->nxy/dot_general | solution.py:76
  86.4 1.4 copy.63
  87.8 112.8 %while.17 = (s32[]{:T(128)}, f32[4,256,256]{1,2,0:T(8,128)}, f32[4,256,256]{1,2,0:T(8,128)}, f32[4,256,256]{1,2,0:T(8,128)}, f32[4,16]{1,0:T(4,128)S(1)}, /*inde...) while((s32[]{:T(128)}, f32[4,256,256]{1,2,0:T(8,128)}, ...), condition=%wide.region_14.16_spmd.clone, body=%wide.region_8.15_spmd.clone.sunk | while | flops 3264480768 | bytes 87824640 | solution.py:144
  87.8 1.3 bitcast_convert_fusion.4
  90.3 2.7 %add_convert_fusion.2 = (bf16[4,4,256,256]{3,2,1,0:T(8,128)(2,1)S(1)}, bf16[4,4,256,256]{3,2,1,0:T(8,128)(2,1)S(1)}) fusion(f32[4,256,256]{2,1,0:T(8,128)S(1)} %bitcast_convert_fusion.4, f32[4,256,256]{2,1,0:T(8,128)} %bitcast.105, f32[4,256,256]{2,1,0:T(8,128)S(1)} %bitcast_convert_fusion.5, f32[4,256,256]{2,1,0:T(8,128)} %bitcast.106), kind=kLoop, calls=%fused_computation.16.clone.1 | loop fusion | flops 8388608 | bytes 8388608 | tf_op jit(solution)/shard_map/while/body/eval_jaxpr/convert_element_type | solution.py:105
  93.0 2.6 %convolution_convert_fusion.7 = bf16[4096,256]{1,0:T(8,128)(2,1)} fusion(bf16[512,256]{1,0:T(8,128)(2,1)S(1)} %get-tuple-element.409, bf16[4096,256]{1,0:T(8,128)(2,1)S(1)} %bitcast.117, bf16[4096,256]{1,0:T(8,128)(2,1)S(1)} %bitcast.115), kind=kOutput, calls=%fused_computation.8.clone.1 | convolution fusion | flops 1083179008 | bytes 6553600 | tf_op jit(solution)/shard_map/while/body/eval_jaxpr/dot_general | solution.py:109
  95.6 2.8 %copy.71 = bf16[16,256,256]{1,2,0:T(8,128)(2,1)S(1)} copy(bf16[16,256,256]{2,1,0:T(8,128)(2,1)} %bitcast.114) | data formatting | bytes 4194304 | tf_op jit(solution)/shard_map/while/body/eval_jaxpr/reshape | solution.py:116
  98.5 4.8 %convolution_convert_fusion.6 = bf16[4096,256]{1,0:T(8,128)(2,1)} fusion(bf16[512,256]{1,0:T(8,128)(2,1)S(1)} %get-tuple-element.410, bf16[4096,256]{1,0:T(8,128)(2,1)} %bitcast.118, bf16[4096,256]{1,0:T(8,128)(2,1)} %bitcast.116), kind=kOutput, calls=%fused_computation.7.clone.1 | convolution fusion | flops 1083179008 | bytes 6553600 | tf_op jit(solution)/shard_map/while/body/eval_jaxpr/dot_general | solution.py:112
  103.3 4.0 %copy.70 = bf16[16,256,256]{1,2,0:T(8,128)(2,1)} copy(bf16[16,256,256]{2,1,0:T(8,128)(2,1)} %bitcast.113) | data formatting | bytes 4194304 | tf_op jit(solution)/shard_map/while/body/eval_jaxpr/reshape | solution.py:116
  107.3 3.0 %fusion.71 = (f32[16]{0:T(128)S(1)}, f32[16,256,256]{2,1,0:T(8,128)S(1)}) fusion(bf16[256,512]{1,0:T(8,128)(2,1)S(1)} %get-tuple-element.411, bf16[16,256,256]{1,2,0:T(8,128)(2,1)} %copy.70, bf16[16,256,256]{1,2,0:T(8,128)(2,1)S(1)} %copy.71), kind=kOutput, calls=%fused_computation.134.clone.1 | convolution fusion | flops 1084227584 | bytes 8650816 | tf_op jit(solution)/shard_map/while/body/eval_jaxpr/xk,nky->nxy/dot_general | solution.py:119
  111.0 1.5 select_add_fusion.5
  114.8 1.3 bitcast_convert_fusion.4
  117.3 2.7 %add_convert_fusion.2 = (bf16[4,4,256,256]{3,2,1,0:T(8,128)(2,1)S(1)}, bf16[4,4,256,256]{3,2,1,0:T(8,128)(2,1)S(1)}) fusion(f32[4,256,256]{2,1,0:T(8,128)S(1)} %bitcast_convert_fusion.4, f32[4,256,256]{2,1,0:T(8,128)} %bitcast.105, f32[4,256,256]{2,1,0:T(8,128)S(1)} %bitcast_convert_fusion.5, f32[4,256,256]{2,1,0:T(8,128)} %bitcast.106), kind=kLoop, calls=%fused_computation.16.clone.1 | loop fusion | flops 8388608 | bytes 8388608 | tf_op jit(solution)/shard_map/while/body/eval_jaxpr/convert_element_type | solution.py:105
  120.0 2.6 %convolution_convert_fusion.7 = bf16[4096,256]{1,0:T(8,128)(2,1)} fusion(bf16[512,256]{1,0:T(8,128)(2,1)S(1)} %get-tuple-element.409, bf16[4096,256]{1,0:T(8,128)(2,1)S(1)} %bitcast.117, bf16[4096,256]{1,0:T(8,128)(2,1)S(1)} %bitcast.115), kind=kOutput, calls=%fused_computation.8.clone.1 | convolution fusion | flops 1083179008 | bytes 6553600 | tf_op jit(solution)/shard_map/while/body/eval_jaxpr/dot_general | solution.py:109
  122.6 2.8 %copy.71 = bf16[16,256,256]{1,2,0:T(8,128)(2,1)S(1)} copy(bf16[16,256,256]{2,1,0:T(8,128)(2,1)} %bitcast.114) | data formatting | bytes 4194304 | tf_op jit(solution)/shard_map/while/body/eval_jaxpr/reshape | solution.py:116
  125.5 4.8 %convolution_convert_fusion.6 = bf16[4096,256]{1,0:T(8,128)(2,1)} fusion(bf16[512,256]{1,0:T(8,128)(2,1)S(1)} %get-tuple-element.410, bf16[4096,256]{1,0:T(8,128)(2,1)} %bitcast.118, bf16[4096,256]{1,0:T(8,128)(2,1)} %bitcast.116), kind=kOutput, calls=%fused_computation.7.clone.1 | convolution fusion | flops 1083179008 | bytes 6553600 | tf_op jit(solution)/shard_map/while/body/eval_jaxpr/dot_general | solution.py:112
  130.3 4.0 %copy.70 = bf16[16,256,256]{1,2,0:T(8,128)(2,1)} copy(bf16[16,256,256]{2,1,0:T(8,128)(2,1)} %bitcast.113) | data formatting | bytes 4194304 | tf_op jit(solution)/shard_map/while/body/eval_jaxpr/reshape | solution.py:116
  134.3 3.0 %fusion.71 = (f32[16]{0:T(128)S(1)}, f32[16,256,256]{2,1,0:T(8,128)S(1)}) fusion(bf16[256,512]{1,0:T(8,128)(2,1)S(1)} %get-tuple-element.411, bf16[16,256,256]{1,2,0:T(8,128)(2,1)} %copy.70, bf16[16,256,256]{1,2,0:T(8,128)(2,1)S(1)} %copy.71), kind=kOutput, calls=%fused_computation.134.clone.1 | convolution fusion | flops 1084227584 | bytes 8650816 | tf_op jit(solution)/shard_map/while/body/eval_jaxpr/xk,nky->nxy/dot_general | solution.py:119
  138.0 3.2 %select_add_fusion.5 = (f32[4,256,256]{1,2,0:T(8,128)}, f32[4,256,256]{1,2,0:T(8,128)}) fusion(f32[4,256,256]{1,2,0:T(8,128)S(1)} %get-tuple-element.363, f32[4,256,256]{1,2,0:T(8,128)} %get-tuple-element.387, pred[]{:T(512)S(6)} %compare.6, f32[4,256,256]{1,2,0:T(8,128)S(1)} %get-tuple-element.364, f32[4,256,256]{1,2,0:T(8,128)} %get-tuple-element.386), kind=kLoop, calls=%fused_computation.18.clone.1 | loop fusion | flops 1048576 | bytes 6291457 | tf_op jit(solution)/shard_map/while/body/eval_jaxpr/add | solution.py:129
  143.4 1.3 bitcast_convert_fusion.4
  145.9 2.7 %add_convert_fusion.2 = (bf16[4,4,256,256]{3,2,1,0:T(8,128)(2,1)S(1)}, bf16[4,4,256,256]{3,2,1,0:T(8,128)(2,1)S(1)}) fusion(f32[4,256,256]{2,1,0:T(8,128)S(1)} %bitcast_convert_fusion.4, f32[4,256,256]{2,1,0:T(8,128)} %bitcast.105, f32[4,256,256]{2,1,0:T(8,128)S(1)} %bitcast_convert_fusion.5, f32[4,256,256]{2,1,0:T(8,128)} %bitcast.106), kind=kLoop, calls=%fused_computation.16.clone.1 | loop fusion | flops 8388608 | bytes 8388608 | tf_op jit(solution)/shard_map/while/body/eval_jaxpr/convert_element_type | solution.py:105
  148.6 2.6 %convolution_convert_fusion.7 = bf16[4096,256]{1,0:T(8,128)(2,1)} fusion(bf16[512,256]{1,0:T(8,128)(2,1)S(1)} %get-tuple-element.409, bf16[4096,256]{1,0:T(8,128)(2,1)S(1)} %bitcast.117, bf16[4096,256]{1,0:T(8,128)(2,1)S(1)} %bitcast.115), kind=kOutput, calls=%fused_computation.8.clone.1 | convolution fusion | flops 1083179008 | bytes 6553600 | tf_op jit(solution)/shard_map/while/body/eval_jaxpr/dot_general | solution.py:109
  151.3 2.8 %copy.71 = bf16[16,256,256]{1,2,0:T(8,128)(2,1)S(1)} copy(bf16[16,256,256]{2,1,0:T(8,128)(2,1)} %bitcast.114) | data formatting | bytes 4194304 | tf_op jit(solution)/shard_map/while/body/eval_jaxpr/reshape | solution.py:116
  154.1 4.8 %convolution_convert_fusion.6 = bf16[4096,256]{1,0:T(8,128)(2,1)} fusion(bf16[512,256]{1,0:T(8,128)(2,1)S(1)} %get-tuple-element.410, bf16[4096,256]{1,0:T(8,128)(2,1)} %bitcast.118, bf16[4096,256]{1,0:T(8,128)(2,1)} %bitcast.116), kind=kOutput, calls=%fused_computation.7.clone.1 | convolution fusion | flops 1083179008 | bytes 6553600 | tf_op jit(solution)/shard_map/while/body/eval_jaxpr/dot_general | solution.py:112
  158.9 4.0 %copy.70 = bf16[16,256,256]{1,2,0:T(8,128)(2,1)} copy(bf16[16,256,256]{2,1,0:T(8,128)(2,1)} %bitcast.113) | data formatting | bytes 4194304 | tf_op jit(solution)/shard_map/while/body/eval_jaxpr/reshape | solution.py:116
  162.9 3.0 %fusion.71 = (f32[16]{0:T(128)S(1)}, f32[16,256,256]{2,1,0:T(8,128)S(1)}) fusion(bf16[256,512]{1,0:T(8,128)(2,1)S(1)} %get-tuple-element.411, bf16[16,256,256]{1,2,0:T(8,128)(2,1)} %copy.70, bf16[16,256,256]{1,2,0:T(8,128)(2,1)S(1)} %copy.71), kind=kOutput, calls=%fused_computation.134.clone.1 | convolution fusion | flops 1084227584 | bytes 8650816 | tf_op jit(solution)/shard_map/while/body/eval_jaxpr/xk,nky->nxy/dot_general | solution.py:119
  166.6 3.2 %select_add_fusion.5 = (f32[4,256,256]{1,2,0:T(8,128)}, f32[4,256,256]{1,2,0:T(8,128)}) fusion(f32[4,256,256]{1,2,0:T(8,128)S(1)} %get-tuple-element.363, f32[4,256,256]{1,2,0:T(8,128)} %get-tuple-element.387, pred[]{:T(512)S(6)} %compare.6, f32[4,256,256]{1,2,0:T(8,128)S(1)} %get-tuple-element.364, f32[4,256,256]{1,2,0:T(8,128)} %get-tuple-element.386), kind=kLoop, calls=%fused_computation.18.clone.1 | loop fusion | flops 1048576 | bytes 6291457 | tf_op jit(solution)/shard_map/while/body/eval_jaxpr/add | solution.py:129
  172.1 1.3 bitcast_convert_fusion.4
  174.5 2.7 %add_convert_fusion.2 = (bf16[4,4,256,256]{3,2,1,0:T(8,128)(2,1)S(1)}, bf16[4,4,256,256]{3,2,1,0:T(8,128)(2,1)S(1)}) fusion(f32[4,256,256]{2,1,0:T(8,128)S(1)} %bitcast_convert_fusion.4, f32[4,256,256]{2,1,0:T(8,128)} %bitcast.105, f32[4,256,256]{2,1,0:T(8,128)S(1)} %bitcast_convert_fusion.5, f32[4,256,256]{2,1,0:T(8,128)} %bitcast.106), kind=kLoop, calls=%fused_computation.16.clone.1 | loop fusion | flops 8388608 | bytes 8388608 | tf_op jit(solution)/shard_map/while/body/eval_jaxpr/convert_element_type | solution.py:105
  177.3 2.6 %convolution_convert_fusion.7 = bf16[4096,256]{1,0:T(8,128)(2,1)} fusion(bf16[512,256]{1,0:T(8,128)(2,1)S(1)} %get-tuple-element.409, bf16[4096,256]{1,0:T(8,128)(2,1)S(1)} %bitcast.117, bf16[4096,256]{1,0:T(8,128)(2,1)S(1)} %bitcast.115), kind=kOutput, calls=%fused_computation.8.clone.1 | convolution fusion | flops 1083179008 | bytes 6553600 | tf_op jit(solution)/shard_map/while/body/eval_jaxpr/dot_general | solution.py:109
  179.9 2.8 %copy.71 = bf16[16,256,256]{1,2,0:T(8,128)(2,1)S(1)} copy(bf16[16,256,256]{2,1,0:T(8,128)(2,1)} %bitcast.114) | data formatting | bytes 4194304 | tf_op jit(solution)/shard_map/while/body/eval_jaxpr/reshape | solution.py:116
  182.7 4.8 %convolution_convert_fusion.6 = bf16[4096,256]{1,0:T(8,128)(2,1)} fusion(bf16[512,256]{1,0:T(8,128)(2,1)S(1)} %get-tuple-element.410, bf16[4096,256]{1,0:T(8,128)(2,1)} %bitcast.118, bf16[4096,256]{1,0:T(8,128)(2,1)} %bitcast.116), kind=kOutput, calls=%fused_computation.7.clone.1 | convolution fusion | flops 1083179008 | bytes 6553600 | tf_op jit(solution)/shard_map/while/body/eval_jaxpr/dot_general | solution.py:112
  187.6 4.0 %copy.70 = bf16[16,256,256]{1,2,0:T(8,128)(2,1)} copy(bf16[16,256,256]{2,1,0:T(8,128)(2,1)} %bitcast.113) | data formatting | bytes 4194304 | tf_op jit(solution)/shard_map/while/body/eval_jaxpr/reshape | solution.py:116
  191.5 3.0 %fusion.71 = (f32[16]{0:T(128)S(1)}, f32[16,256,256]{2,1,0:T(8,128)S(1)}) fusion(bf16[256,512]{1,0:T(8,128)(2,1)S(1)} %get-tuple-element.411, bf16[16,256,256]{1,2,0:T(8,128)(2,1)} %copy.70, bf16[16,256,256]{1,2,0:T(8,128)(2,1)S(1)} %copy.71), kind=kOutput, calls=%fused_computation.134.clone.1 | convolution fusion | flops 1084227584 | bytes 8650816 | tf_op jit(solution)/shard_map/while/body/eval_jaxpr/xk,nky->nxy/dot_general | solution.py:119
  195.2 3.2 %select_add_fusion.5 = (f32[4,256,256]{1,2,0:T(8,128)}, f32[4,256,256]{1,2,0:T(8,128)}) fusion(f32[4,256,256]{1,2,0:T(8,128)S(1)} %get-tuple-element.363, f32[4,256,256]{1,2,0:T(8,128)} %get-tuple-element.387, pred[]{:T(512)S(6)} %compare.6, f32[4,256,256]{1,2,0:T(8,128)S(1)} %get-tuple-element.364, f32[4,256,256]{1,2,0:T(8,128)} %get-tuple-element.386), kind=kLoop, calls=%fused_computation.18.clone.1 | loop fusion | flops 1048576 | bytes 6291457 | tf_op jit(solution)/shard_map/while/body/eval_jaxpr/add | solution.py:129
  200.7 1.7 copy.65
  202.4 1.3 copy.66
  203.7 1.3 copy.67
  205.0 1.5 multiply_subtract_fusion
  (184 shorter events, 28.9 us)
Async XLA Ops:
  7.2 15.6 %copy-start = (f32[32]{0:T(128)S(1)}, f32[32]{0:T(128)}, u32[]{:S(2)}) copy-start(f32[32]{0:T(128)} %param.14) | copy-start | bytes 388
  7.2 80.6 %all-gather.3.cloned.1.call-start = ((), (), s32[]{:S(2)}) async-start(), calls=%async_computation.1 | async-start | bytes 2621440 | tf_op jit(solution)/shard_map/all_gather | solution.py:136
  13.0 8.3 %copy-start.14 = (s32[16]{0:T(128)S(1)}, s32[16]{0:T(128)}, u32[]{:S(2)}) copy-start(s32[16]{0:T(128)} %param.13) | copy-start | bytes 196
  13.1 55.5 %all-to-all-start = ((bf16[8,2,256,256]{3,2,1,0:T(8,128)(2,1)}), bf16[8,2,256,256]{3,2,1,0:T(8,128)(2,1)S(1)}, u32[]{:S(2)}, u32[]{:S(2)}) async-start(bf16[8,2,256,256]{3,2,1,0:T(8,128)(2,1)} %broadcast_select_fusion), calls=%async_computation | async-start | bytes 4194304 | tf_op jit(solution)/shard_map/all_to_all | solution.py:160
  19.5 68.3 %all-gather.5.cloned.1.call-start = ((), (), s32[]{:S(2)}) async-start(), calls=%async_computation.2 | async-start | bytes 2621440 | tf_op jit(solution)/shard_map/all_gather | solution.py:137
  81.7 6.1 %copy-start.1 = (s32[16]{0:T(128)S(1)}, s32[16]{0:T(128)}, u32[]{:S(2)}) copy-start(s32[16]{0:T(128)} %param.17) | copy-start | bytes 196
  87.8 5.2 %copy-start.9 = (bf16[512,256]{1,0:T(8,128)(2,1)}, bf16[512,256]{1,0:T(8,128)(2,1)S(1)}, u32[]{:S(2)}) copy-start(bf16[512,256]{1,0:T(8,128)(2,1)S(1)} %get-tuple-element.409) | copy-start | bytes 786436 | tf_op jit(solution)/shard_map/while
  87.8 19.5 %copy-start.11 = (bf16[256,512]{1,0:T(8,128)(2,1)}, bf16[256,512]{1,0:T(8,128)(2,1)S(1)}, u32[]{:S(2)}) copy-start(bf16[256,512]{1,0:T(8,128)(2,1)S(1)} %get-tuple-element.411) | copy-start | bytes 786436 | tf_op jit(solution)/shard_map/while
  93.0 2.6 %copy-start.2 = (bf16[4,4,256,256]{3,2,1,0:T(8,128)(2,1)}, bf16[4,4,256,256]{3,2,1,0:T(8,128)(2,1)S(1)}, u32[]{:S(2)}) copy-start(bf16[4,4,256,256]{3,2,1,0:T(8,128)(2,1)S(1)} %get-tuple-element.360) | copy-start | bytes 6291460 | tf_op jit(solution)/shard_map/while
  93.0 2.6 %copy-start.3 = (bf16[4,4,256,256]{3,2,1,0:T(8,128)(2,1)}, bf16[4,4,256,256]{3,2,1,0:T(8,128)(2,1)S(1)}, u32[]{:S(2)}) copy-start(bf16[4,4,256,256]{3,2,1,0:T(8,128)(2,1)S(1)} %get-tuple-element.359) | copy-start | bytes 6291460 | tf_op jit(solution)/shard_map/while
  111.0 1.6 copy-start.5
  112.5 2.2 %copy-start.10 = (bf16[512,256]{1,0:T(8,128)(2,1)S(1)}, bf16[512,256]{1,0:T(8,128)(2,1)}, u32[]{:S(2)}) copy-start(bf16[512,256]{1,0:T(8,128)(2,1)} %copy-done.9) | copy-start | bytes 786436 | tf_op jit(solution)/shard_map/while
  112.5 2.2 %copy-start.12 = (bf16[256,512]{1,0:T(8,128)(2,1)S(1)}, bf16[256,512]{1,0:T(8,128)(2,1)}, u32[]{:S(2)}) copy-start(bf16[256,512]{1,0:T(8,128)(2,1)} %copy-done.11) | copy-start | bytes 786436 | tf_op jit(solution)/shard_map/while
  112.9 1.0 copy-start.6
  114.8 5.2 %copy-start.9 = (bf16[512,256]{1,0:T(8,128)(2,1)}, bf16[512,256]{1,0:T(8,128)(2,1)S(1)}, u32[]{:S(2)}) copy-start(bf16[512,256]{1,0:T(8,128)(2,1)S(1)} %get-tuple-element.409) | copy-start | bytes 786436 | tf_op jit(solution)/shard_map/while
  114.8 19.5 %copy-start.11 = (bf16[256,512]{1,0:T(8,128)(2,1)}, bf16[256,512]{1,0:T(8,128)(2,1)S(1)}, u32[]{:S(2)}) copy-start(bf16[256,512]{1,0:T(8,128)(2,1)S(1)} %get-tuple-element.411) | copy-start | bytes 786436 | tf_op jit(solution)/shard_map/while
  120.0 2.6 %copy-start.2 = (bf16[4,4,256,256]{3,2,1,0:T(8,128)(2,1)}, bf16[4,4,256,256]{3,2,1,0:T(8,128)(2,1)S(1)}, u32[]{:S(2)}) copy-start(bf16[4,4,256,256]{3,2,1,0:T(8,128)(2,1)S(1)} %get-tuple-element.360) | copy-start | bytes 6291460 | tf_op jit(solution)/shard_map/while
  120.0 2.6 %copy-start.3 = (bf16[4,4,256,256]{3,2,1,0:T(8,128)(2,1)}, bf16[4,4,256,256]{3,2,1,0:T(8,128)(2,1)S(1)}, u32[]{:S(2)}) copy-start(bf16[4,4,256,256]{3,2,1,0:T(8,128)(2,1)S(1)} %get-tuple-element.359) | copy-start | bytes 6291460 | tf_op jit(solution)/shard_map/while
  138.0 3.2 %copy-start.5 = (f32[4,256,256]{1,2,0:T(8,128)S(1)}, f32[4,256,256]{1,2,0:T(8,128)}, u32[]{:S(2)}) copy-start(f32[4,256,256]{1,2,0:T(8,128)} %get-tuple-element.385) | copy-start | bytes 3145732 | tf_op jit(solution)/shard_map/while
  141.2 2.2 %copy-start.10 = (bf16[512,256]{1,0:T(8,128)(2,1)S(1)}, bf16[512,256]{1,0:T(8,128)(2,1)}, u32[]{:S(2)}) copy-start(bf16[512,256]{1,0:T(8,128)(2,1)} %copy-done.9) | copy-start | bytes 786436 | tf_op jit(solution)/shard_map/while
  141.2 2.2 %copy-start.12 = (bf16[256,512]{1,0:T(8,128)(2,1)S(1)}, bf16[256,512]{1,0:T(8,128)(2,1)}, u32[]{:S(2)}) copy-start(bf16[256,512]{1,0:T(8,128)(2,1)} %copy-done.11) | copy-start | bytes 786436 | tf_op jit(solution)/shard_map/while
  141.5 1.0 copy-start.6
  143.4 5.2 %copy-start.9 = (bf16[512,256]{1,0:T(8,128)(2,1)}, bf16[512,256]{1,0:T(8,128)(2,1)S(1)}, u32[]{:S(2)}) copy-start(bf16[512,256]{1,0:T(8,128)(2,1)S(1)} %get-tuple-element.409) | copy-start | bytes 786436 | tf_op jit(solution)/shard_map/while
  143.4 19.5 %copy-start.11 = (bf16[256,512]{1,0:T(8,128)(2,1)}, bf16[256,512]{1,0:T(8,128)(2,1)S(1)}, u32[]{:S(2)}) copy-start(bf16[256,512]{1,0:T(8,128)(2,1)S(1)} %get-tuple-element.411) | copy-start | bytes 786436 | tf_op jit(solution)/shard_map/while
  148.6 2.6 %copy-start.2 = (bf16[4,4,256,256]{3,2,1,0:T(8,128)(2,1)}, bf16[4,4,256,256]{3,2,1,0:T(8,128)(2,1)S(1)}, u32[]{:S(2)}) copy-start(bf16[4,4,256,256]{3,2,1,0:T(8,128)(2,1)S(1)} %get-tuple-element.360) | copy-start | bytes 6291460 | tf_op jit(solution)/shard_map/while
  148.6 2.6 %copy-start.3 = (bf16[4,4,256,256]{3,2,1,0:T(8,128)(2,1)}, bf16[4,4,256,256]{3,2,1,0:T(8,128)(2,1)S(1)}, u32[]{:S(2)}) copy-start(bf16[4,4,256,256]{3,2,1,0:T(8,128)(2,1)S(1)} %get-tuple-element.359) | copy-start | bytes 6291460 | tf_op jit(solution)/shard_map/while
  166.6 3.2 %copy-start.5 = (f32[4,256,256]{1,2,0:T(8,128)S(1)}, f32[4,256,256]{1,2,0:T(8,128)}, u32[]{:S(2)}) copy-start(f32[4,256,256]{1,2,0:T(8,128)} %get-tuple-element.385) | copy-start | bytes 3145732 | tf_op jit(solution)/shard_map/while
  169.8 2.2 %copy-start.10 = (bf16[512,256]{1,0:T(8,128)(2,1)S(1)}, bf16[512,256]{1,0:T(8,128)(2,1)}, u32[]{:S(2)}) copy-start(bf16[512,256]{1,0:T(8,128)(2,1)} %copy-done.9) | copy-start | bytes 786436 | tf_op jit(solution)/shard_map/while
  169.8 2.2 %copy-start.12 = (bf16[256,512]{1,0:T(8,128)(2,1)S(1)}, bf16[256,512]{1,0:T(8,128)(2,1)}, u32[]{:S(2)}) copy-start(bf16[256,512]{1,0:T(8,128)(2,1)} %copy-done.11) | copy-start | bytes 786436 | tf_op jit(solution)/shard_map/while
  170.1 1.0 copy-start.6
  172.0 5.2 %copy-start.9 = (bf16[512,256]{1,0:T(8,128)(2,1)}, bf16[512,256]{1,0:T(8,128)(2,1)S(1)}, u32[]{:S(2)}) copy-start(bf16[512,256]{1,0:T(8,128)(2,1)S(1)} %get-tuple-element.409) | copy-start | bytes 786436 | tf_op jit(solution)/shard_map/while
  172.0 19.5 %copy-start.11 = (bf16[256,512]{1,0:T(8,128)(2,1)}, bf16[256,512]{1,0:T(8,128)(2,1)S(1)}, u32[]{:S(2)}) copy-start(bf16[256,512]{1,0:T(8,128)(2,1)S(1)} %get-tuple-element.411) | copy-start | bytes 786436 | tf_op jit(solution)/shard_map/while
  177.2 2.6 %copy-start.2 = (bf16[4,4,256,256]{3,2,1,0:T(8,128)(2,1)}, bf16[4,4,256,256]{3,2,1,0:T(8,128)(2,1)S(1)}, u32[]{:S(2)}) copy-start(bf16[4,4,256,256]{3,2,1,0:T(8,128)(2,1)S(1)} %get-tuple-element.360) | copy-start | bytes 6291460 | tf_op jit(solution)/shard_map/while
  177.2 2.6 %copy-start.3 = (bf16[4,4,256,256]{3,2,1,0:T(8,128)(2,1)}, bf16[4,4,256,256]{3,2,1,0:T(8,128)(2,1)S(1)}, u32[]{:S(2)}) copy-start(bf16[4,4,256,256]{3,2,1,0:T(8,128)(2,1)S(1)} %get-tuple-element.359) | copy-start | bytes 6291460 | tf_op jit(solution)/shard_map/while
  195.2 3.2 %copy-start.5 = (f32[4,256,256]{1,2,0:T(8,128)S(1)}, f32[4,256,256]{1,2,0:T(8,128)}, u32[]{:S(2)}) copy-start(f32[4,256,256]{1,2,0:T(8,128)} %get-tuple-element.385) | copy-start | bytes 3145732 | tf_op jit(solution)/shard_map/while
  198.4 2.2 %copy-start.10 = (bf16[512,256]{1,0:T(8,128)(2,1)S(1)}, bf16[512,256]{1,0:T(8,128)(2,1)}, u32[]{:S(2)}) copy-start(bf16[512,256]{1,0:T(8,128)(2,1)} %copy-done.9) | copy-start | bytes 786436 | tf_op jit(solution)/shard_map/while
  198.4 2.2 %copy-start.12 = (bf16[256,512]{1,0:T(8,128)(2,1)S(1)}, bf16[256,512]{1,0:T(8,128)(2,1)}, u32[]{:S(2)}) copy-start(bf16[256,512]{1,0:T(8,128)(2,1)} %copy-done.11) | copy-start | bytes 786436 | tf_op jit(solution)/shard_map/while
  198.7 1.0 copy-start.6
  200.6 4.4 %copy-start.13 = (f32[4,16]{1,0:T(4,128)}, f32[4,16]{1,0:T(4,128)S(1)}, u32[]{:S(2)}) copy-start(f32[4,16]{1,0:T(4,128)S(1)} %get-tuple-element.217) | copy-start | bytes 772
  200.7 1.7 copy-start.4
  200.7 3.0 %copy-start.7 = (f32[4,256,256]{1,2,0:T(8,128)S(1)}, f32[4,256,256]{1,2,0:T(8,128)}, u32[]{:S(2)}) copy-start(f32[4,256,256]{1,2,0:T(8,128)} %get-tuple-element.214) | copy-start | bytes 3145732
  203.7 1.3 copy-start.8
Sparse Core Ops, SparseCore 0:
  9.9 38.0 all-gather.2
  49.7 35.2 all-gather.4
where the time goes:
time: 215 us; the launch traced here: 213 us
  matrix products  53.4 us (25%)
  local copies, waits for them, and re-layouts  51 us (24%)
  other arithmetic  44.9 us (21%)
  waiting for transfers between devices  42.7 us (20%)
  between operations  14.3 us (7%)
  starting transfers between devices  6.53 us (3%)
    all_to_all x1, waiting for transfers between devices, body(): lax.all_to_all(outgoing, 'patch', split_axis=0, concat_axis=0, tiled=True)  41.3 us
    dot_general x4, matrix products, one_group(): jnp.dot(prod_cat, forward_im, preferred_element_type=jnp.float32)  19.3 us
    reshape x4, local copies, waits for them, and re-layouts, one_group(): q_im.reshape(batch, extent, extent)  15.8 us
    dot_general x4, matrix products, one_group(): jnp.einsum('xk,nky->nxy', inverse_left, q_stack, preferred_element_type=j...  11.9 us
    reshape x4, local copies, waits for them, and re-layouts, one_group(): q_re.reshape(batch, extent, extent)  11.4 us
    add x4, other arithmetic, one_group(): squares + jnp.sum(corr * corr, axis=0)  11 us
    convert_element_type x4, other arithmetic, one_group(): prod_re = (spec_rw * templ_rw + spec_iw * templ_iw).astype(jnp.bfloat16)  10.8 us
    dot_general x4, matrix products, one_group(): jnp.dot(prod_cat, forward_re, preferred_element_type=jnp.float32)  10.4 us
  transfers between devices with their start and end apart: 3, of which 1 were waited for; matrix products, arithmetic and copies ran while one was open for 15% of the time, Pallas kernels for 0%

commit v1 on v0

--- a/solution.py
+++ b/solution.py
@@ -1,8 +1,11 @@
+import functools
 import math
 
 import jax
 import jax.numpy as jnp
 from jax import lax
+from jax.experimental import pallas as pl
+from jax.experimental.pallas import tpu as pltpu
 from jax.sharding import PartitionSpec as P
 
 SLOT = 2
@@ -79,70 +82,103 @@
     return ((real * scale).astype(jnp.bfloat16), (imag * scale).astype(jnp.bfloat16))
 
 
+def corr_kernel(first, *refs):
+    if first:
+        (sr_ref, si_ref, tr_ref, ti_ref, c_ref, s_ref, top_ref, sum_ref, sq_ref, peak_ref) = refs
+    else:
+        (sr_ref, si_ref, tr_ref, ti_ref, c_ref, s_ref, top_in, sum_in, sq_in,
+         top_ref, sum_ref, sq_ref, peak_ref) = refs
+    t = pl.program_id(1)
+    extent = sr_ref.shape[-1]
+    sr = sr_ref[0].astype(jnp.float32)
+    si = si_ref[0].astype(jnp.float32)
+    tr = tr_ref[0].astype(jnp.float32)
+    ti = ti_ref[0].astype(jnp.float32)
+    pre = (sr * tr + si * ti).astype(jnp.bfloat16)
+    pim = (si * tr - sr * ti).astype(jnp.bfloat16)
+    cos_t = c_ref[...]
+    sin_t = s_ref[...]
+
+    def mm(a, b):
+        return jnp.dot(a, b, preferred_element_type=jnp.float32)
+
+    q_re = (mm(pre, cos_t) - mm(pim, sin_t)).astype(jnp.bfloat16)
+    q_im = (mm(pre, sin_t) + mm(pim, cos_t)).astype(jnp.bfloat16)
+    corr = (mm(cos_t, q_re) - mm(sin_t, q_im)) / extent
+    peak_ref[...] = jnp.full(peak_ref.shape, jnp.max(corr), jnp.float32)
+
+    if first:
+        @pl.when(t == 0)
+        def _():
+            top_ref[0] = corr
+            sum_ref[0] = corr
+            sq_ref[0] = corr * corr
+    else:
+        @pl.when(t == 0)
+        def _():
+            top_ref[0] = jnp.maximum(top_in[0], corr)
+            sum_ref[0] = sum_in[0] + corr
+            sq_ref[0] = sq_in[0] + corr * corr
+
+    @pl.when(t > 0)
+    def _():
+        top_ref[0] = jnp.maximum(top_ref[0], corr)
+        sum_ref[0] = sum_ref[0] + corr
+        sq_ref[0] = sq_ref[0] + corr * corr
+
+
+def correlate_chunk(spec_re, spec_im, templ_re, templ_im, cosine, sine, stats):
+    count, extent = (spec_re.shape[0], spec_re.shape[-1])
+    tiles = templ_re.shape[0]
+    first = stats is None
+    plane = pl.BlockSpec((1, extent, extent), lambda s, t: (s, 0, 0))
+    templ_spec = pl.BlockSpec((1, extent, extent), lambda s, t: (t, 0, 0))
+    table = pl.BlockSpec((extent, extent), lambda s, t: (0, 0))
+    in_specs = [plane, plane, templ_spec, templ_spec, table, table]
+    operands = [spec_re, spec_im, templ_re, templ_im, cosine, sine]
+    aliases = {}
+    if not first:
+        in_specs += [plane, plane, plane]
+        operands += list(stats)
+        aliases = {6: 0, 7: 1, 8: 2}
+    map_shape = jax.ShapeDtypeStruct((count, extent, extent), jnp.float32)
+    flops = tiles * count * 12 * extent * extent * extent
+    outs = pl.pallas_call(
+        functools.partial(corr_kernel, first),
+        grid=(count, tiles),
+        in_specs=in_specs,
+        out_specs=[plane, plane, plane, pl.BlockSpec((1, 1, 8, 128), lambda s, t: (s, t, 0, 0))],
+        out_shape=[map_shape, map_shape, map_shape,
+                   jax.ShapeDtypeStruct((count, tiles, 8, 128), jnp.float32)],
+        input_output_aliases=aliases,
+        compiler_params=pltpu.CompilerParams(dimension_semantics=("parallel", "arbitrary")),
+        cost_estimate=pl.CostEstimate(
+            flops=flops, transcendentals=0,
+            bytes_accessed=tiles * count * 4 * extent * extent * 2 + count * 6 * extent * extent * 4),
+    )(*operands)
+    return outs[:3], outs[3][:, :, 0, 0]
+
+
 def correlate_all(spec_re, spec_im, templ_re, templ_im, orientation, cosine, sine):
-    count, extent = (spec_re.shape[0], spec_re.shape[-1])
+    blocks = lax.axis_size("blk")
+    me = lax.axis_index("blk")
+    tiles = templ_re.shape[0]
+    stats, peak = correlate_chunk(spec_re, spec_im, templ_re, templ_im, cosine, sine, None)
+    peaks = [(me, peak)]
+    for k in range(1, blocks):
+        pairs = [(b, b ^ k) for b in range(blocks)]
+        got_re = lax.ppermute(templ_re, "blk", pairs)
+        got_im = lax.ppermute(templ_im, "blk", pairs)
+        stats, peak = correlate_chunk(spec_re, spec_im, got_re, got_im, cosine, sine, stats)
+        peaks.append((me ^ k, peak))
+    top_map, totals, squares = stats
     orient_total = orientation.shape[0]
-    forward_re = jnp.concatenate([cosine, -sine], axis=0)
-    forward_im = jnp.concatenate([sine, cosine], axis=0)
-    inverse_left = jnp.concatenate([cosine, -sine], axis=1)
-    spec_rw = spec_re.astype(jnp.float32)[None]
-    spec_iw = spec_im.astype(jnp.float32)[None]
-    map_shape = (count, extent, extent)
-    initial = (
-        jnp.full(map_shape, -1e30, jnp.float32),
-        jnp.zeros(map_shape, jnp.float32),
-        jnp.zeros(map_shape, jnp.float32),
-        jnp.zeros((count, orient_total), jnp.float32),
-    )
-    orient_ids = jnp.arange(orient_total, dtype=jnp.int32)
-
-    def one_group(carry, item):
-        group_re, group_im, which_ones = item
-        top_now, totals, squares, peak_rows = carry
-        tiles = group_re.shape[0]
-        templ_rw = group_re.astype(jnp.float32)[:, None]
-        templ_iw = group_im.astype(jnp.float32)[:, None]
-        prod_re = (spec_rw * templ_rw + spec_iw * templ_iw).astype(jnp.bfloat16)
-        prod_im = (spec_iw * templ_rw - spec_rw * templ_iw).astype(jnp.bfloat16)
-        batch = tiles * count
-        prod_cat = jnp.concatenate([prod_re, prod_im], axis=-1).reshape(batch * extent, 2 * extent)
-        q_re = jnp.dot(prod_cat, forward_re, preferred_element_type=jnp.float32).astype(
-            jnp.bfloat16
-        )
-        q_im = jnp.dot(prod_cat, forward_im, preferred_element_type=jnp.float32).astype(
-            jnp.bfloat16
-        )
-        q_stack = jnp.concatenate(
-            [q_re.reshape(batch, extent, extent), q_im.reshape(batch, extent, extent)], axis=1
-        )
-        corr = (
-            jnp.einsum("xk,nky->nxy", inverse_left, q_stack, preferred_element_type=jnp.float32)
-            / extent
-        )
-        corr = corr.reshape(tiles, count, extent, extent)
-        peak_now = jnp.max(corr, axis=(2, 3))
-        one_hot = (orientation[which_ones][:, None] == orient_ids[None, :]).astype(jnp.float32)
-        peak_add = jnp.sum(peak_now[:, :, None] * one_hot[:, None, :], axis=0)
-        updated = (
-            jnp.maximum(top_now, jnp.max(corr, axis=0)),
-            totals + jnp.sum(corr, axis=0),
-            squares + jnp.sum(corr * corr, axis=0),
-            peak_rows + peak_add,
-        )
-        return (updated, None)
-
-    carry = initial
-    piece = (
-        lax.all_gather(templ_re, "blk", axis=0, tiled=True),
-        lax.all_gather(templ_im, "blk", axis=0, tiled=True),
-    )
-    pieces = piece[0].shape[0]
-    blocks = pieces // TILE_T
-    which_ones = jnp.arange(pieces, dtype=jnp.int32).reshape(blocks, TILE_T)
-    grouped_re = piece[0].reshape(blocks, TILE_T, extent, extent)
-    grouped_im = piece[1].reshape(blocks, TILE_T, extent, extent)
-    carry, unused = lax.scan(one_group, carry, (grouped_re, grouped_im, which_ones))
-    top_map, totals, squares, peak_rows = carry
+    count = spec_re.shape[0]
+    peak_rows = jnp.zeros((count, orient_total), jnp.float32)
+    within = jnp.arange(tiles, dtype=jnp.int32)
+    for source, peak in peaks:
+        columns = jnp.take(orientation, source * tiles + within)
+        peak_rows = peak_rows.at[:, columns].set(peak)
     mean_map = totals / orient_total
     var_map = squares / orient_total - mean_map * mean_map
     return (top_map, mean_map, var_map, peak_rows)

time: 215 us -> 168 us (0.78)
  Pallas kernels: 0 us -> 69.8 us
  matrix products: 53.4 us -> 11.7 us
  other arithmetic: 44.9 us -> 8.32 us
  local copies, waits for them, and re-layouts: 51 us -> 20.5 us
  between operations: 14.3 us -> 0.94 us
  starting transfers between devices: 6.53 us -> 13.4 us
    pallas_call x0 -> x4, Pallas kernels: none -> 69.8 us  [correlate_chunk(): pl.pallas_call(functools.partial(corr_kernel, first), grid=(count, tiles)...]
    dot_general x12 -> x0, matrix products: 41.6 us -> none  [the longest x4 19.3 us: one_group(): jnp.dot(prod_cat, forward_im, preferred_element_type=jnp.float32)]
    reshape x8 -> x0, local copies, waits for them, and re-layouts: 27.2 us -> none  [the longest x4 15.8 us: one_group(): q_im.reshape(batch, extent, extent)]
    convert_element_type x17 -> x0, other arithmetic: 21.9 us -> none  [the longest x4 10.8 us: one_group(): prod_re = (spec_rw * templ_rw + spec_iw * templ_iw).astype(jnp.bfloat16)]
    add x8 -> x0, other arithmetic: 11.1 us -> none  [the longest x4 11 us: one_group(): squares + jnp.sum(corr * corr, axis=0)]
    ppermute x0 -> x6, starting transfers between devices: none -> 8.55 us  [the longest x3 7.42 us: correlate_all(): got_re = lax.ppermute(templ_re, 'blk', pairs)]
    while x66 -> x0, local copies, waits for them, and re-layouts: 6.99 us -> none
    slice x0 -> x4, local copies, waits for them, and re-layouts: none -> 3.83 us  [correlate_chunk(): return (outs[:3], outs[3][:, :, 0, 0])]
  transfers between devices with their start and end apart: 3 -> 7, of which waited for: 1 -> 1; matrix products, arithmetic and copies ran while one was open for 15% -> 19% of each run, Pallas kernels for 0% -> 32%
where the time goes in v1:
time: 168 us; the launch traced here: 166 us
  Pallas kernels  69.8 us (42%)
  waiting for transfers between devices  41 us (24%)
  local copies, waits for them, and re-layouts  20.5 us (12%)
  starting transfers between devices  13.4 us (8%)
  matrix products  11.7 us (7%)
  other arithmetic  8.32 us (5%)
    pallas_call x4, Pallas kernels, correlate_chunk(): pl.pallas_call(functools.partial(corr_kernel, first), grid=(count, tiles)...  69.8 us
    all_to_all x1, waiting for transfers between devices, body(): lax.all_to_all(outgoing, 'patch', split_axis=0, concat_axis=0, tiled=True)  41 us
    ppermute x3, starting transfers between devices, correlate_all(): got_re = lax.ppermute(templ_re, 'blk', pairs)  7.42 us
    all_to_all x1, starting transfers between devices, body(): lax.all_to_all(outgoing, 'patch', split_axis=0, concat_axis=0, tiled=True)  4.88 us
    dot_general x1, matrix products, make_spectra(): jnp.einsum('xk,nky->nxy', left_imag, half_stack, preferred_element_type=j...  4.61 us
    dot_general x1, matrix products, make_spectra(): jnp.einsum('xk,nky->nxy', left_real, half_stack, preferred_element_type=j...  4.58 us
    slice x4, local copies, waits for them, and re-layouts, correlate_chunk(): return (outs[:3], outs[3][:, :, 0, 0])  3.83 us
  transfers between devices with their start and end apart: 7, of which 1 were waited for; matrix products, arithmetic and copies ran while one was open for 19% of the time, Pallas kernels for 32%

profile of v1, /device:TPU:0, one launch (start us, length us, event | category | flops | bytes accessed | tf_op | source)
XLA Modules:
  0.0 165.6 jit_solution(17023190880340786397)
XLA Ops:
  0.6 3.0 %collective-permute-start.4 = (bf16[4,256,256]{2,1,0:T(8,128)(2,1)}, bf16[4,256,256]{2,1,0:T(8,128)(2,1)}, u32[]{:S(2)}, u32[]{:S(2)}) collective-permute-start(bf16[4,256,256]{2,1,0:T(8,128)(2,1)} %refs_2_.1), channel_id=1, source_target_pairs={{0,8},{8,0},{16,24},{24,16},{1,9},{9,1},{17,25},{25,17},{2,10},{10... | collective-permute-start | bytes 1572872 | tf_op jit(solution)/shard_map/ppermute | solution.py:170
  3.6 1.5 collective-permute-start.2
  5.2 0.5 collective-permute-start.5
  5.8 2.9 %collective-permute-start = (bf16[4,256,256]{2,1,0:T(8,128)(2,1)}, bf16[4,256,256]{2,1,0:T(8,128)(2,1)S(1)}, u32[]{:S(2)}, u32[]{:S(2)}) collective-permute-start(bf16[4,256,256]{2,1,0:T(8,128)(2,1)} %refs_2_.1), channel_id=1, source_target_pairs={{0,24},{8,16},{16,8},{24,0},{1,25},{9,17},{17,9},{25,1},{2,26},{10... | collective-permute-start | bytes 1572872 | tf_op jit(solution)/shard_map/ppermute | solution.py:170
  8.7 0.7 eq.22
  9.5 0.2 fusion.40
  10.0 0.2 dynamic-slice_reduce_fusion
  10.5 1.0 concatenate.21
  11.5 0.7 gather_fusion
  12.1 1.6 broadcast_select_fusion
  13.8 4.9 %all-to-all-start = ((bf16[8,2,256,256]{3,2,1,0:T(8,128)(2,1)}), bf16[8,2,256,256]{3,2,1,0:T(8,128)(2,1)S(1)}, u32[]{:S(2)}, u32[]{:S(2)}) async-start(bf16[8,2,256,256]{3,2,1,0:T(8,128)(2,1)} %broadcast_select_fusion), calls=%async_computation | async-start | bytes 4194304 | tf_op jit(solution)/shard_map/all_to_all | solution.py:196
  18.8 0.2 fusion.39
  19.7 0.6 gather_fusion.5
  20.4 0.6 gather_fusion.6
  21.0 0.6 gather_fusion.7
  21.7 0.6 gather_fusion.8
  22.4 0.6 gather_fusion.3
  23.1 0.6 gather_fusion.4
  23.7 0.6 gather_fusion.2
  24.4 1.0 fusion.15
  25.4 1.1 sine_convert_fusion
  26.7 41.0 %all-to-all-done = bf16[8,2,256,256]{3,2,1,0:T(8,128)(2,1)S(1)} async-done(((bf16[8,2,256,256]{3,2,1,0:T(8,128)(2,1)}), bf16[8,2,256,256]{3,2,1,0:T(8,128)(2,1)S(1)}, u32[]{:S(2)}, u32[]{:S(2)}) %all-to-all-start) | async-done | bytes 2097184 | tf_op jit(solution)/shard_map/all_to_all | solution.py:196
  67.7 1.6 concatenate.22
  69.3 2.2 %gather_fusion.1 = bf16[4,256,256]{2,1,0:T(8,128)(2,1)S(1)} fusion(bf16[17,256,256]{2,1,0:T(8,128)(2,1)} %concatenate.22, s32[1024]{0:T(1024)S(1)} %pad_clamp_fusion.7), kind=kCustom, calls=%fused_computation.7 | custom fusion | bytes 1048592 | tf_op jit(solution)/shard_map/jit(_take)/gather | solution.py:204
  71.6 0.2 bitcast_select_fusion
  71.8 1.2 convolution_convert_fusion.1
  73.0 1.2 convolution_convert_fusion
  74.3 0.2 copy.64
  74.5 0.2 copy.65
  74.7 4.6 %fusion.2.refs_1_ = bf16[4,256,256]{2,1,0:T(8,128)(2,1)} fusion(bf16[4,256,256]{1,2,0:T(8,128)(2,1)S(1)} %copy.65, bf16[4,256,256]{1,2,0:T(8,128)(2,1)S(1)} %copy.64, f32[256,256]{1,0:T(8,128)S(1)} %broadcast_add_fusion, f32[4]{0:T(128)S(1)} %fusion.30, bf16[256,256]{1,0:T(8,128)(2,1)S(1)} %get-tuple-element.67.refs_4_, bf16[256,256]{1,0:T(8,128)(2,1)S(1)} %fusion.15), kind=kOutput, calls=%fused_computation.20 | convolution fusion | flops 272629760 | bytes 2097168 | tf_op jit(solution)/shard_map/xk,nky->nxy/dot_general | solution.py:80
  79.3 4.6 %fusion.3.refs_0_ = bf16[4,256,256]{2,1,0:T(8,128)(2,1)} fusion(bf16[4,256,256]{1,2,0:T(8,128)(2,1)S(1)} %copy.65, bf16[4,256,256]{1,2,0:T(8,128)(2,1)S(1)} %copy.64, f32[256,256]{1,0:T(8,128)S(1)} %broadcast_add_fusion, f32[4]{0:T(128)S(1)} %fusion.30, bf16[256,256]{1,0:T(8,128)(2,1)S(1)} %get-tuple-element.66.refs_5_, ...), kind=kOutput, calls=%fused_computation.21 | convolution fusion | flops 272629760 | bytes 2097168 | tf_op jit(solution)/shard_map/xk,nky->nxy/dot_general | solution.py:79
  83.9 17.0 %shard_map.102 = (f32[4,256,256]{2,1,0:T(8,128)}, f32[4,256,256]{2,1,0:T(8,128)}, f32[4,256,256]{2,1,0:T(8,128)}, f32[4,4,8,128]{3,2,1,0:T(8,128)}) custom-call(bf16[4,256,256]{2,1,0:T(8,128)(2,1)} %fusion.3.refs_0_, bf16[4,256,256]{2,1,0:T(8,128)(2,1)} %fusion.2.refs_1_, bf16[4,256,256]{2,1,0:T(8,128)(2,1)} %refs_2_.1, bf16[4,256,256]{2,1,0:T(8,128)(2,1)} %refs_3_.1, ...), custom_call_target="tpu_custom_call" | custom-call | flops 3221225472 | bytes 14680064 | tf_op jit(solution)/shard_map/pallas_call | solution.py:146
  100.9 0.5 collective-permute-start.1
  101.5 17.6 %shard_map.103 = (f32[4,256,256]{2,1,0:T(8,128)}, f32[4,256,256]{2,1,0:T(8,128)}, f32[4,256,256]{2,1,0:T(8,128)}, f32[4,4,8,128]{3,2,1,0:T(8,128)}) custom-call(bf16[4,256,256]{2,1,0:T(8,128)(2,1)} %fusion.3.refs_0_, bf16[4,256,256]{2,1,0:T(8,128)(2,1)} %fusion.2.refs_1_, ...), custom_call_target="tpu_custom_call", output_to_operand_aliasing={{0}: (6, {}), {1}: (7, {}), {2}: (8, {})} | custom-call | flops 3221225472 | bytes 14680064 | tf_op jit(solution)/shard_map/pallas_call | solution.py:146
  119.0 1.0 slice_reduce_fusion.2
  120.1 1.0 slice_reduce_fusion.3
  121.2 17.6 %shard_map.104 = (f32[4,256,256]{2,1,0:T(8,128)}, f32[4,256,256]{2,1,0:T(8,128)}, f32[4,256,256]{2,1,0:T(8,128)}, f32[4,4,8,128]{3,2,1,0:T(8,128)}) custom-call(bf16[4,256,256]{2,1,0:T(8,128)(2,1)} %fusion.3.refs_0_, bf16[4,256,256]{2,1,0:T(8,128)(2,1)} %fusion.2.refs_1_, ...), custom_call_target="tpu_custom_call", output_to_operand_aliasing={{0}: (6, {}), {1}: (7, {}), {2}: (8, {})} | custom-call | flops 3221225472 | bytes 14680064 | tf_op jit(solution)/shard_map/pallas_call | solution.py:146
  138.7 1.0 slice_reduce_fusion.1
  139.8 0.8 copy-done.6
  140.6 0.2 copy-done.7
  140.8 17.6 %shard_map.105 = (f32[4,256,256]{2,1,0:T(8,128)}, f32[4,256,256]{2,1,0:T(8,128)}, f32[4,256,256]{2,1,0:T(8,128)}, f32[4,4,8,128]{3,2,1,0:T(8,128)}) custom-call(bf16[4,256,256]{2,1,0:T(8,128)(2,1)} %fusion.3.refs_0_, bf16[4,256,256]{2,1,0:T(8,128)(2,1)} %fusion.2.refs_1_, ...), custom_call_target="tpu_custom_call", output_to_operand_aliasing={{0}: (6, {}), {1}: (7, {}), {2}: (8, {})} | custom-call | flops 3221225472 | bytes 14680064 | tf_op jit(solution)/shard_map/pallas_call | solution.py:146
  158.4 1.0 slice_reduce_fusion
  159.5 0.6 scatter_custom_fusion
  160.1 0.6 scatter_fusion
  160.7 0.6 scatter_fusion.1
  161.3 0.6 scatter_fusion.2
  161.9 0.7 copy.73
  162.6 3.1 %multiply_subtract_fusion = (f32[4,256,256]{2,1,0:T(8,128)}, f32[4,256,256]{2,1,0:T(8,128)}) fusion(f32[4,256,256]{2,1,0:T(8,128)} %get-tuple-element.33, f32[4,256,256]{2,1,0:T(8,128)} %get-tuple-element.32), kind=kLoop, calls=%fused_computation.25 | loop fusion | flops 1048576 | bytes 4194304 | tf_op jit(solution)/shard_map/sub | solution.py:183
  (73 shorter events, 2.3 us)
Async XLA Ops:
  0.6 19.1 %copy-start = (s32[16]{0:T(128)S(1)}, s32[16]{0:T(128)}, u32[]{:S(2)}) copy-start(s32[16]{0:T(128)} %param.17) | copy-start | bytes 196
  0.6 100.3 %collective-permute-start.4 = (bf16[4,256,256]{2,1,0:T(8,128)(2,1)}, bf16[4,256,256]{2,1,0:T(8,128)(2,1)}, u32[]{:S(2)}, u32[]{:S(2)}) collective-permute-start(bf16[4,256,256]{2,1,0:T(8,128)(2,1)} %refs_2_.1), channel_id=1, source_target_pairs={{0,8},{8,0},{16,24},{24,16},{1,9},{9,1},{17,25},{25,17},{2,10},{10... | collective-permute-start | bytes 1572872 | tf_op jit(solution)/shard_map/ppermute | solution.py:170
  3.6 117.5 %collective-permute-start.2 = (bf16[4,256,256]{2,1,0:T(8,128)(2,1)}, bf16[4,256,256]{2,1,0:T(8,128)(2,1)}, u32[]{:S(2)}, u32[]{:S(2)}) collective-permute-start(bf16[4,256,256]{2,1,0:T(8,128)(2,1)} %refs_2_.1), channel_id=1, source_target_pairs={{0,16},{8,24},{16,0},{24,8},{1,17},{9,25},{17,1},{25,9},{2,18},{10... | collective-permute-start | bytes 1572872 | tf_op jit(solution)/shard_map/ppermute | solution.py:170
  5.2 96.3 %collective-permute-start.5 = (bf16[4,256,256]{2,1,0:T(8,128)(2,1)}, bf16[4,256,256]{2,1,0:T(8,128)(2,1)}, u32[]{:S(2)}, u32[]{:S(2)}) collective-permute-start(bf16[4,256,256]{2,1,0:T(8,128)(2,1)} %refs_3_.1), channel_id=1, source_target_pairs={{0,8},{8,0},{16,24},{24,16},{1,9},{9,1},{17,25},{25,17},{2,10},{10... | collective-permute-start | bytes 1572872 | tf_op jit(solution)/shard_map/ppermute | solution.py:171
  5.7 115.5 %collective-permute-start.3 = (bf16[4,256,256]{2,1,0:T(8,128)(2,1)}, bf16[4,256,256]{2,1,0:T(8,128)(2,1)}, u32[]{:S(2)}, u32[]{:S(2)}) collective-permute-start(bf16[4,256,256]{2,1,0:T(8,128)(2,1)} %refs_3_.1), channel_id=1, source_target_pairs={{0,16},{8,24},{16,0},{24,8},{1,17},{9,25},{17,1},{25,9},{2,18},{10... | collective-permute-start | bytes 1572872 | tf_op jit(solution)/shard_map/ppermute | solution.py:171
  5.8 134.0 %collective-permute-start = (bf16[4,256,256]{2,1,0:T(8,128)(2,1)}, bf16[4,256,256]{2,1,0:T(8,128)(2,1)S(1)}, u32[]{:S(2)}, u32[]{:S(2)}) collective-permute-start(bf16[4,256,256]{2,1,0:T(8,128)(2,1)} %refs_2_.1), channel_id=1, source_target_pairs={{0,24},{8,16},{16,8},{24,0},{1,25},{9,17},{17,9},{25,1},{2,26},{10... | collective-permute-start | bytes 1572872 | tf_op jit(solution)/shard_map/ppermute | solution.py:170
  13.8 53.9 %all-to-all-start = ((bf16[8,2,256,256]{3,2,1,0:T(8,128)(2,1)}), bf16[8,2,256,256]{3,2,1,0:T(8,128)(2,1)S(1)}, u32[]{:S(2)}, u32[]{:S(2)}) async-start(bf16[8,2,256,256]{3,2,1,0:T(8,128)(2,1)} %broadcast_select_fusion), calls=%async_computation | async-start | bytes 4194304 | tf_op jit(solution)/shard_map/all_to_all | solution.py:196
  18.6 3.7 %copy-start.4 = (s32[16]{0:T(128)S(1)}, s32[16]{0:T(128)}, u32[]{:S(2)}) copy-start(s32[16]{0:T(128)} %param.13) | copy-start | bytes 196
  18.6 5.1 %copy-start.1 = (f32[32]{0:T(128)S(1)}, f32[32]{0:T(128)}, u32[]{:S(2)}) copy-start(f32[32]{0:T(128)} %param.14) | copy-start | bytes 388
  26.5 52.8 %copy-start.2 = (bf16[256,256]{1,0:T(8,128)(2,1)}, bf16[256,256]{1,0:T(8,128)(2,1)S(1)}, u32[]{:S(2)}) copy-start(bf16[256,256]{1,0:T(8,128)(2,1)S(1)} %get-tuple-element.66.refs_5_) | copy-start | bytes 393220
  26.5 52.8 %copy-start.3 = (bf16[256,256]{1,0:T(8,128)(2,1)}, bf16[256,256]{1,0:T(8,128)(2,1)S(1)}, u32[]{:S(2)}) copy-start(bf16[256,256]{1,0:T(8,128)(2,1)S(1)} %get-tuple-element.67.refs_4_) | copy-start | bytes 393220
  83.9 17.1 %copy-start.5 = (bf16[4,256,256]{2,1,0:T(8,128)(2,1)S(1)}, bf16[4,256,256]{2,1,0:T(8,128)(2,1)}, u32[]{:S(2)}) copy-start(bf16[4,256,256]{2,1,0:T(8,128)(2,1)} %refs_3_.1) | copy-start | bytes 1572868
  100.9 38.9 %collective-permute-start.1 = (bf16[4,256,256]{2,1,0:T(8,128)(2,1)S(1)}, bf16[4,256,256]{2,1,0:T(8,128)(2,1)S(1)}, u32[]{:S(2)}, u32[]{:S(2)}) collective-permute-start(bf16[4,256,256]{2,1,0:T(8,128)(2,1)S(1)} %copy-done.5), channel_id=1, source_target_pairs={{0,24},{8,16},{16,8},{24,0},{1,25},{9,17},{17,9},{25,1},{2,26},{10... | collective-permute-start | bytes 1572872 | tf_op jit(solution)/shard_map/ppermute | solution.py:171
  139.8 0.8 copy-start.6
  139.8 1.0 copy-start.7

commit v2 on v1

--- a/solution.py
+++ b/solution.py
@@ -33,37 +33,61 @@
     return -jnp.sin(phases)
 
 
-def routing(row_owner, my_index):
+def xor_pairs(count, shift):
+    return [(d, d ^ shift) for d in range(count)]
+
+
+def route_patches(patches, row_owner, my_index):
     sources, number = row_owner.shape
-    owner_ids = jnp.arange(sources, dtype=jnp.int32)
-    owner_hits = (row_owner[:, :, None] == owner_ids[None, None, :]).astype(jnp.int32)
-    earlier = jnp.cumsum(owner_hits, axis=1) - owner_hits
-    rank_in = jnp.sum(earlier * owner_hits, axis=2)
-    counts = jnp.sum(owner_hits, axis=1)
-    slot_key = row_owner * SLOT + rank_in
-    targets = jnp.arange(sources * SLOT, dtype=jnp.int32)
-    matches = slot_key[:, :, None] == targets[None, None, :]
-    local_idx = jnp.sum(
-        jnp.where(matches, jnp.arange(number, dtype=jnp.int32)[None, :, None], 0), axis=1
-    )
-    send_table = jnp.where(jnp.any(matches, axis=1), local_idx, number)
-    arrived = lax.dynamic_slice_in_dim(counts, my_index, 1, 1)[:, 0]
-    offsets = jnp.cumsum(arrived) - arrived
-    within = jnp.arange(SLOT, dtype=jnp.int32)
-    usable = within[None, :] < arrived[:, None]
-    position = jnp.where(usable, offsets[:, None] + within[None, :], -1).reshape(-1)
+    extent = patches.shape[-1]
+    chips = sources // 2
+    devs = jnp.arange(sources, dtype=jnp.int32)
+    chip_of = devs // 2
+    owner_chip = row_owner // 2
+    masks = [row_owner == (devs ^ 1)[:, None]]
+    for m in range(1, chips):
+        masks.append(owner_chip == (chip_of ^ m)[:, None])
+    match = jnp.stack(masks, axis=1)
+    first = jnp.where(match[..., 0], 0, jnp.where(match[..., 1], 1, number))
+    second = jnp.where(match[..., 0] & match[..., 1], 1, number)
+    send_sel = jnp.stack([first, second], axis=-1)
+    send_pid = jnp.where(send_sel < number, devs[:, None, None] * number + send_sel, -1)
+    padded = jnp.concatenate([patches, jnp.zeros((1, extent, extent), patches.dtype)], axis=0)
+    my_sel = lax.dynamic_index_in_dim(send_sel, my_index, 0, keepdims=False)
+    outgoing = jnp.take(padded, my_sel.reshape(-1), axis=0).reshape(chips, 2, extent, extent)
+    partner = my_index ^ 1
+    my_chip = my_index // 2
+    direct = lax.ppermute(outgoing[0], "patch", xor_pairs(sources, 1))
+    received = []
+    for m in range(1, chips):
+        received.append(lax.ppermute(outgoing[m], "patch", xor_pairs(sources, 2 * m)))
+    received = jnp.concatenate(received, axis=0)
+    forwarded = lax.ppermute(received, "patch", xor_pairs(sources, 1))
+    cand_pid = [my_index * number + jnp.arange(number, dtype=jnp.int32)]
+    cand_pid.append(lax.dynamic_index_in_dim(send_pid, partner, 0, keepdims=False)[0])
+    for core in (my_index % 2, partner % 2):
+        for m in range(1, chips):
+            source = (my_chip ^ m) * 2 + core
+            cand_pid.append(lax.dynamic_index_in_dim(send_pid, source, 0, keepdims=False)[m])
+    cand_pid = jnp.concatenate(cand_pid)
+    candidates = jnp.concatenate(
+        [patches, direct, received, forwarded, jnp.zeros((1, extent, extent), patches.dtype)],
+        axis=0,
+    )
+    flat_owner = row_owner.reshape(-1)
+    hits = (flat_owner == my_index).astype(jnp.int32)
+    rank_in = jnp.cumsum(hits) - hits
     slot_ids = jnp.arange(CAP, dtype=jnp.int32)
-    picked = position[None, :] == slot_ids[:, None]
-    received_row = jnp.sum(jnp.where(picked, targets[None, :], 0), axis=1)
-    take_table = jnp.where(jnp.any(picked, axis=1), received_row, sources * SLOT)
-    my_columns = lax.dynamic_slice_in_dim(send_table, my_index * SLOT, SLOT, 1)
-    row_of = jnp.where(
-        my_columns < number, owner_ids[:, None] * number + my_columns, sources * number
-    ).reshape(-1)
-    row_of = jnp.concatenate([row_of, jnp.full((1,), sources * number, jnp.int32)])
-    slot_row = jnp.take(row_of, take_table)
-    my_send = lax.dynamic_slice_in_dim(send_table, my_index, 1, 0)[0]
-    return (my_send, take_table, slot_row)
+    wanted = (hits[None, :] == 1) & (rank_in[None, :] == slot_ids[:, None])
+    patch_ids = jnp.arange(sources * number, dtype=jnp.int32)
+    slot_pid = jnp.sum(jnp.where(wanted, patch_ids[None, :], 0), axis=1)
+    present = jnp.any(wanted, axis=1)
+    cand_ids = jnp.arange(cand_pid.shape[0], dtype=jnp.int32)
+    found = cand_pid[None, :] == slot_pid[:, None]
+    take_idx = jnp.sum(jnp.where(found, cand_ids[None, :], 0), axis=1)
+    take_idx = jnp.where(present, take_idx, cand_pid.shape[0])
+    my_slots = jnp.take(candidates, take_idx, axis=0)
+    return my_slots, jnp.where(present, slot_pid, sources * number)
 
 
 def make_spectra(images, focus_values, cosine, sine):
@@ -190,18 +214,7 @@
     number, extent = (patches.shape[0], patches.shape[1])
     cosine, sine = dft_tables(extent)
     row_owner = owner_of_patch.reshape(sources, number)
-    my_send, take_table, slot_row = routing(row_owner, my_index)
-    padded = jnp.concatenate([patches, jnp.zeros((1, extent, extent), jnp.bfloat16)], axis=0)
-    outgoing = jnp.take(padded, my_send, axis=0).reshape(sources, SLOT, extent, extent)
-    incoming = lax.all_to_all(outgoing, "patch", split_axis=0, concat_axis=0, tiled=True)
-    flattened = jnp.concatenate(
-        [
-            incoming.reshape(sources * SLOT, extent, extent),
-            jnp.zeros((1, extent, extent), jnp.bfloat16),
-        ],
-        axis=0,
-    )
-    my_slots = jnp.take(flattened, take_table, axis=0)
+    my_slots, slot_row = route_patches(patches, row_owner, my_index)
     groups = jnp.take(jnp.concatenate([group_of_patch, jnp.zeros((1,), jnp.int32)]), slot_row)
     focus_values = jnp.take(defocus, groups)
     spec_re, spec_im = make_spectra(my_slots, focus_values, cosine, sine)

time: 168 us -> 139 us (0.83)
  the two profiles are of different devices: /device:TPU:0 before, /device:TPU:9 now
where the time goes in v2:
time: 139 us; the launch traced here: 137 us
  Pallas kernels  69.7 us (50%)
  local copies, waits for them, and re-layouts  24 us (17%)
  starting transfers between devices  12.7 us (9%)
  matrix products  11.7 us (8%)
  other arithmetic  9.45 us (7%)
  waiting for transfers between devices  8.55 us (6%)
    pallas_call x4, Pallas kernels, correlate_chunk(): pl.pallas_call(functools.partial(corr_kernel, first), grid=(count, tiles)...  69.7 us
    ppermute x3, waiting for transfers between devices, route_patches(): lax.ppermute(outgoing[m], 'patch', xor_pairs(sources, 2 * m))  8.53 us
    unnamed x33, local copies, waits for them, and re-layouts  6.34 us
    dot_general x1, matrix products, make_spectra(): jnp.einsum('xk,nky->nxy', left_imag, half_stack, preferred_element_type=j...  4.61 us
    dot_general x1, matrix products, make_spectra(): jnp.einsum('xk,nky->nxy', left_real, half_stack, preferred_element_type=j...  4.58 us
    slice x4, local copies, waits for them, and re-layouts, correlate_chunk(): return (outs[:3], outs[3][:, :, 0, 0])  3.83 us
    ppermute x3, starting transfers between devices, correlate_all(): got_re = lax.ppermute(templ_re, 'blk', pairs)  3.73 us
    sub x1, other arithmetic, correlate_all(): var_map = squares / orient_total - mean_map * mean_map  3.1 us
  transfers between devices with their start and end apart: 11, of which 1 were waited for; matrix products, arithmetic and copies ran while one was open for 27% of the time, Pallas kernels for 38%

profile of v2, /device:TPU:9, one launch (start us, length us, event | category | flops | bytes accessed | tf_op | source)
XLA Modules:
  0.0 137.2 jit_solution(8033522407677645370)
XLA Ops:
  0.6 1.3 collective-permute-start.9
  1.9 1.2 collective-permute-start.7
  3.2 0.7 reshape.509
  4.9 1.0 concatenate.26
  5.8 0.6 gather_fusion
  7.0 2.3 %collective-permute-start.2 = (bf16[2,256,256]{2,1,0:T(8,128)(2,1)S(1)}, bf16[2,256,256]{2,1,0:T(8,128)(2,1)S(1)}, u32[]{:S(2)}, u32[]{:S(2)}) collective-permute-start(bf16[2,256,256]{2,1,0:T(8,128)(2,1)S(1)} %get-tuple-element.67), channel_id=1, source_target_pairs={{0,4},{1,5},{2,6},{3,7},{4,0},{5,1},{6,2},{7,3},{8,12},{9,13},{10,... | collective-permute-start | bytes 786440 | tf_op jit(solution)/shard_map/ppermute | solution.py:63
  9.5 0.7 constant_dynamic-update-slice_fusion.5
  10.7 1.1 sine_convert_fusion
  11.8 1.0 fusion.14
  13.7 0.6 gather_fusion.2
  14.4 0.6 gather_fusion.4
  15.6 0.6 gather_fusion.5
  16.2 0.6 compare_select_fusion.7
  16.8 0.6 gather_fusion.6
  18.0 0.6 gather_fusion.7
  18.6 0.6 compare_select_fusion.5
  19.2 0.6 gather_fusion.3
  20.4 2.1 %collective-permute-start = (bf16[2,256,256]{2,1,0:T(8,128)(2,1)S(1)}, bf16[2,256,256]{2,1,0:T(8,128)(2,1)S(1)}, u32[]{:S(2)}, u32[]{:S(2)}) collective-permute-start(bf16[2,256,256]{2,1,0:T(8,128)(2,1)S(1)} %get-tuple-element.69), channel_id=1, source_target_pairs={{0,1},{1,0},{2,3},{3,2},{4,5},{5,4},{6,7},{7,6},{8,9},{9,8},{10,11... | collective-permute-start | bytes 786440 | tf_op jit(solution)/shard_map/ppermute | solution.py:60
  22.7 8.5 %collective-permute-done.3 = bf16[2,256,256]{2,1,0:T(8,128)(2,1)S(1)} collective-permute-done((bf16[2,256,256]{2,1,0:T(8,128)(2,1)S(1)}, bf16[2,256,256]{2,1,0:T(8,128)(2,1)S(1)}, u32[]{:S(2)}, u32[]{:S(2)}) %collective-permute-start.3) | collective-permute-done | bytes 262176 | tf_op jit(solution)/shard_map/ppermute | solution.py:63
  31.3 2.5 %collective-permute-start.4 = (bf16[6,256,256]{2,1,0:T(8,128)(2,1)S(1)}, bf16[6,256,256]{2,1,0:T(8,128)(2,1)S(1)}, u32[]{:S(2)}, u32[]{:S(2)}) collective-permute-start(bf16[6,256,256]{2,1,0:T(8,128)(2,1)S(1)} %pad_maximum_fusion.1), channel_id=1, source_target_pairs={{0,1},{1,0},{2,3},{3,2},{4,5},{5,4},{6,7},{7,6},{8,9},{9,8},{10,11... | collective-permute-start | bytes 2359304 | tf_op jit(solution)/shard_map/ppermute | solution.py:65
  34.3 0.7 constant_dynamic-update-slice_fusion.4
  35.0 0.7 constant_dynamic-update-slice_fusion.3
  35.7 0.7 constant_dynamic-update-slice_fusion.2
  36.5 0.7 constant_dynamic-update-slice_fusion.1
  37.2 1.2 collective-permute-start.5
  38.4 1.0 constant_dynamic-update-slice_fusion
  39.4 0.7 broadcast_dynamic-update-slice_fusion
  40.1 2.2 %gather_fusion.1 = bf16[4,256,256]{2,1,0:T(8,128)(2,1)S(1)} fusion(bf16[17,256,256]{2,1,0:T(8,128)(2,1)} %broadcast_dynamic-update-slice_fusion, s32[1024]{0:T(1024)S(1)} %pad_clamp_fusion.6), kind=kCustom, calls=%fused_computation.5 | custom fusion | bytes 1048592 | tf_op jit(solution)/shard_map/jit(_take)/gather | solution.py:89
  42.5 1.2 convolution_convert_fusion.1
  43.7 1.2 convolution_convert_fusion
  45.4 4.6 %fusion.2.refs_1_ = bf16[4,256,256]{2,1,0:T(8,128)(2,1)} fusion(bf16[4,256,256]{1,2,0:T(8,128)(2,1)S(1)} %copy.80, bf16[4,256,256]{1,2,0:T(8,128)(2,1)S(1)} %copy.79, f32[256,256]{1,0:T(8,128)S(1)} %broadcast_add_fusion, f32[4]{0:T(128)S(1)} %copy-done.9, bf16[256,256]{1,0:T(8,128)(2,1)S(1)} %get-tuple-element.89.refs_4_, bf16[256,256]{1,0:T(8,128)(2,1)S(1)} %fusion.14), kind=kOutput, calls=%fused_computation.18 | convolution fusion | flops 272629760 | bytes 2097168 | tf_op jit(solution)/shard_map/xk,nky->nxy/dot_general | solution.py:104
  50.0 4.6 %fusion.3.refs_0_ = bf16[4,256,256]{2,1,0:T(8,128)(2,1)} fusion(bf16[4,256,256]{1,2,0:T(8,128)(2,1)S(1)} %copy.80, bf16[4,256,256]{1,2,0:T(8,128)(2,1)S(1)} %copy.79, f32[256,256]{1,0:T(8,128)S(1)} %broadcast_add_fusion, f32[4]{0:T(128)S(1)} %copy-done.9, bf16[256,256]{1,0:T(8,128)(2,1)S(1)} %get-tuple-element.88.refs_5_, ...), kind=kOutput, calls=%fused_computation.19 | convolution fusion | flops 272629760 | bytes 2097168 | tf_op jit(solution)/shard_map/xk,nky->nxy/dot_general | solution.py:103
  54.6 17.0 %shard_map.102 = (f32[4,256,256]{2,1,0:T(8,128)}, f32[4,256,256]{2,1,0:T(8,128)}, f32[4,256,256]{2,1,0:T(8,128)}, f32[4,4,8,128]{3,2,1,0:T(8,128)}) custom-call(bf16[4,256,256]{2,1,0:T(8,128)(2,1)} %fusion.3.refs_0_, bf16[4,256,256]{2,1,0:T(8,128)(2,1)} %fusion.2.refs_1_, bf16[4,256,256]{2,1,0:T(8,128)(2,1)} %refs_2_.1, bf16[4,256,256]{2,1,0:T(8,128)(2,1)} %refs_3_.1, ...), custom_call_target="tpu_custom_call" | custom-call | flops 3221225472 | bytes 14680064 | tf_op jit(solution)/shard_map/pallas_call | solution.py:170
  71.6 1.2 collective-permute-start.6
  72.8 17.6 %shard_map.103 = (f32[4,256,256]{2,1,0:T(8,128)}, f32[4,256,256]{2,1,0:T(8,128)}, f32[4,256,256]{2,1,0:T(8,128)}, f32[4,4,8,128]{3,2,1,0:T(8,128)}) custom-call(bf16[4,256,256]{2,1,0:T(8,128)(2,1)} %fusion.3.refs_0_, bf16[4,256,256]{2,1,0:T(8,128)(2,1)} %fusion.2.refs_1_, ...), custom_call_target="tpu_custom_call", output_to_operand_aliasing={{0}: (6, {}), {1}: (7, {}), {2}: (8, {})} | custom-call | flops 3221225472 | bytes 14680064 | tf_op jit(solution)/shard_map/pallas_call | solution.py:170
  90.4 1.0 slice_reduce_fusion.2
  91.5 1.0 slice_reduce_fusion.3
  92.5 17.6 %shard_map.104 = (f32[4,256,256]{2,1,0:T(8,128)}, f32[4,256,256]{2,1,0:T(8,128)}, f32[4,256,256]{2,1,0:T(8,128)}, f32[4,4,8,128]{3,2,1,0:T(8,128)}) custom-call(bf16[4,256,256]{2,1,0:T(8,128)(2,1)} %fusion.3.refs_0_, bf16[4,256,256]{2,1,0:T(8,128)(2,1)} %fusion.2.refs_1_, ...), custom_call_target="tpu_custom_call", output_to_operand_aliasing={{0}: (6, {}), {1}: (7, {}), {2}: (8, {})} | custom-call | flops 3221225472 | bytes 14680064 | tf_op jit(solution)/shard_map/pallas_call | solution.py:170
  110.1 1.0 slice_reduce_fusion.1
  111.2 0.8 copy-done.10
  112.2 17.6 %shard_map.105 = (f32[4,256,256]{2,1,0:T(8,128)}, f32[4,256,256]{2,1,0:T(8,128)}, f32[4,256,256]{2,1,0:T(8,128)}, f32[4,4,8,128]{3,2,1,0:T(8,128)}) custom-call(bf16[4,256,256]{2,1,0:T(8,128)(2,1)} %fusion.3.refs_0_, bf16[4,256,256]{2,1,0:T(8,128)(2,1)} %fusion.2.refs_1_, ...), custom_call_target="tpu_custom_call", output_to_operand_aliasing={{0}: (6, {}), {1}: (7, {}), {2}: (8, {})} | custom-call | flops 3221225472 | bytes 14680064 | tf_op jit(solution)/shard_map/pallas_call | solution.py:170
  129.8 1.0 slice_reduce_fusion
  130.8 0.7 scatter_custom_fusion
  131.6 0.6 scatter_fusion
  132.2 0.6 scatter_fusion.1
  132.8 0.6 scatter_fusion.2
  133.4 0.7 copy.87
  134.1 3.1 %multiply_subtract_fusion = (f32[4,256,256]{2,1,0:T(8,128)}, f32[4,256,256]{2,1,0:T(8,128)}) fusion(f32[4,256,256]{2,1,0:T(8,128)} %get-tuple-element.32, f32[4,256,256]{2,1,0:T(8,128)} %get-tuple-element.31), kind=kLoop, calls=%fused_computation.21 | loop fusion | flops 1048576 | bytes 4194304 | tf_op jit(solution)/shard_map/sub | solution.py:207
  (98 shorter events, 6.6 us)
Async XLA Ops:
  0.6 13.8 %copy-start = (s32[16]{0:T(128)S(1)}, s32[16]{0:T(128)}, u32[]{:S(2)}) copy-start(s32[16]{0:T(128)} %param.15) | copy-start | bytes 196
  0.6 72.2 %collective-permute-start.9 = (bf16[4,256,256]{2,1,0:T(8,128)(2,1)}, bf16[4,256,256]{2,1,0:T(8,128)(2,1)}, u32[]{:S(2)}, u32[]{:S(2)}) collective-permute-start(bf16[4,256,256]{2,1,0:T(8,128)(2,1)} %refs_2_.1), channel_id=1, source_target_pairs={{0,8},{8,0},{16,24},{24,16},{1,9},{9,1},{17,25},{25,17},{2,10},{10... | collective-permute-start | bytes 1572872 | tf_op jit(solution)/shard_map/ppermute | solution.py:194
  1.9 90.6 %collective-permute-start.7 = (bf16[4,256,256]{2,1,0:T(8,128)(2,1)}, bf16[4,256,256]{2,1,0:T(8,128)(2,1)}, u32[]{:S(2)}, u32[]{:S(2)}) collective-permute-start(bf16[4,256,256]{2,1,0:T(8,128)(2,1)} %refs_2_.1), channel_id=1, source_target_pairs={{0,16},{8,24},{16,0},{24,8},{1,17},{9,25},{17,1},{25,9},{2,18},{10... | collective-permute-start | bytes 1572872 | tf_op jit(solution)/shard_map/ppermute | solution.py:194
  6.5 3.0 %copy-start.2 = (bf16[2,256,256]{2,1,0:T(8,128)(2,1)S(1)}, bf16[2,256,256]{2,1,0:T(8,128)(2,1)}, u32[]{:S(2)}) copy-start(bf16[2,256,256]{2,1,0:T(8,128)(2,1)} %param.9) | copy-start | bytes 786436
  6.5 3.7 %copy-start.5 = (s32[16]{0:T(128)S(1)}, s32[16]{0:T(128)}, u32[]{:S(2)}) copy-start(s32[16]{0:T(128)} %param.10) | copy-start | bytes 196
  6.5 7.1 %copy-start.12 = (s32[16]{0:T(128)S(1)}, s32[16]{0:T(128)}, u32[]{:S(2)}) copy-start(s32[16]{0:T(128)} %param.11) | copy-start | bytes 196
  6.7 12.5 %copy-start.1 = (f32[32]{0:T(128)S(1)}, f32[32]{0:T(128)}, u32[]{:S(2)}) copy-start(f32[32]{0:T(128)} %param.12) | copy-start | bytes 388
  6.8 13.6 %collective-permute-start.1 = (bf16[2,256,256]{2,1,0:T(8,128)(2,1)S(1)}, bf16[2,256,256]{2,1,0:T(8,128)(2,1)S(1)}, u32[]{:S(2)}, u32[]{:S(2)}) collective-permute-start(bf16[2,256,256]{2,1,0:T(8,128)(2,1)S(1)} %get-tuple-element.68), channel_id=1, source_target_pairs={{0,2},{1,3},{2,0},{3,1},{4,6},{5,7},{6,4},{7,5},{8,10},{9,11},{10,... | collective-permute-start | bytes 786440 | tf_op jit(solution)/shard_map/ppermute | solution.py:63
  7.0 15.5 %collective-permute-start.2 = (bf16[2,256,256]{2,1,0:T(8,128)(2,1)S(1)}, bf16[2,256,256]{2,1,0:T(8,128)(2,1)S(1)}, u32[]{:S(2)}, u32[]{:S(2)}) collective-permute-start(bf16[2,256,256]{2,1,0:T(8,128)(2,1)S(1)} %get-tuple-element.67), channel_id=1, source_target_pairs={{0,4},{1,5},{2,6},{3,7},{4,0},{5,1},{6,2},{7,3},{8,12},{9,13},{10,... | collective-permute-start | bytes 786440 | tf_op jit(solution)/shard_map/ppermute | solution.py:63
  9.3 21.9 %collective-permute-start.3 = (bf16[2,256,256]{2,1,0:T(8,128)(2,1)S(1)}, bf16[2,256,256]{2,1,0:T(8,128)(2,1)S(1)}, u32[]{:S(2)}, u32[]{:S(2)}) collective-permute-start(bf16[2,256,256]{2,1,0:T(8,128)(2,1)S(1)} %get-tuple-element.66), channel_id=1, source_target_pairs={{0,6},{1,7},{2,4},{3,5},{4,2},{5,3},{6,0},{7,1},{8,14},{9,15},{10,... | collective-permute-start | bytes 786440 | tf_op jit(solution)/shard_map/ppermute | solution.py:63
  11.8 38.2 %copy-start.3 = (bf16[256,256]{1,0:T(8,128)(2,1)}, bf16[256,256]{1,0:T(8,128)(2,1)S(1)}, u32[]{:S(2)}) copy-start(bf16[256,256]{1,0:T(8,128)(2,1)S(1)} %get-tuple-element.88.refs_5_) | copy-start | bytes 393220
  11.8 38.2 %copy-start.4 = (bf16[256,256]{1,0:T(8,128)(2,1)}, bf16[256,256]{1,0:T(8,128)(2,1)S(1)}, u32[]{:S(2)}) copy-start(bf16[256,256]{1,0:T(8,128)(2,1)S(1)} %get-tuple-element.89.refs_4_) | copy-start | bytes 393220
  20.4 13.6 %collective-permute-start = (bf16[2,256,256]{2,1,0:T(8,128)(2,1)S(1)}, bf16[2,256,256]{2,1,0:T(8,128)(2,1)S(1)}, u32[]{:S(2)}, u32[]{:S(2)}) collective-permute-start(bf16[2,256,256]{2,1,0:T(8,128)(2,1)S(1)} %get-tuple-element.69), channel_id=1, source_target_pairs={{0,1},{1,0},{2,3},{3,2},{4,5},{5,4},{6,7},{7,6},{8,9},{9,8},{10,11... | collective-permute-start | bytes 786440 | tf_op jit(solution)/shard_map/ppermute | solution.py:60
  22.5 49.2 %collective-permute-start.10 = (bf16[4,256,256]{2,1,0:T(8,128)(2,1)}, bf16[4,256,256]{2,1,0:T(8,128)(2,1)}, u32[]{:S(2)}, u32[]{:S(2)}) collective-permute-start(bf16[4,256,256]{2,1,0:T(8,128)(2,1)} %refs_3_.1), channel_id=1, source_target_pairs={{0,8},{8,0},{16,24},{24,16},{1,9},{9,1},{17,25},{25,17},{2,10},{10... | collective-permute-start | bytes 1572872 | tf_op jit(solution)/shard_map/ppermute | solution.py:195
  31.3 5.9 %collective-permute-start.4 = (bf16[6,256,256]{2,1,0:T(8,128)(2,1)S(1)}, bf16[6,256,256]{2,1,0:T(8,128)(2,1)S(1)}, u32[]{:S(2)}, u32[]{:S(2)}) collective-permute-start(bf16[6,256,256]{2,1,0:T(8,128)(2,1)S(1)} %pad_maximum_fusion.1), channel_id=1, source_target_pairs={{0,1},{1,0},{2,3},{3,2},{4,5},{5,4},{6,7},{7,6},{8,9},{9,8},{10,11... | collective-permute-start | bytes 2359304 | tf_op jit(solution)/shard_map/ppermute | solution.py:65
  34.0 58.5 %collective-permute-start.8 = (bf16[4,256,256]{2,1,0:T(8,128)(2,1)}, bf16[4,256,256]{2,1,0:T(8,128)(2,1)}, u32[]{:S(2)}, u32[]{:S(2)}) collective-permute-start(bf16[4,256,256]{2,1,0:T(8,128)(2,1)} %refs_3_.1), channel_id=1, source_target_pairs={{0,16},{8,24},{16,0},{24,8},{1,17},{9,25},{17,1},{25,9},{2,18},{10... | collective-permute-start | bytes 1572872 | tf_op jit(solution)/shard_map/ppermute | solution.py:195
  37.2 74.0 %collective-permute-start.5 = (bf16[4,256,256]{2,1,0:T(8,128)(2,1)}, bf16[4,256,256]{2,1,0:T(8,128)(2,1)S(1)}, u32[]{:S(2)}, u32[]{:S(2)}) collective-permute-start(bf16[4,256,256]{2,1,0:T(8,128)(2,1)} %refs_2_.1), channel_id=1, source_target_pairs={{0,24},{8,16},{16,8},{24,0},{1,25},{9,17},{17,9},{25,1},{2,26},{10... | collective-permute-start | bytes 1572872 | tf_op jit(solution)/shard_map/ppermute | solution.py:194
  43.7 1.7 %copy-start.9 = (f32[4]{0:T(128)S(1)}, f32[4]{0:T(128)}, u32[]{:S(2)}) copy-start(f32[4]{0:T(128)} %fusion.38) | copy-start | bytes 52
  71.6 39.6 %collective-permute-start.6 = (bf16[4,256,256]{2,1,0:T(8,128)(2,1)}, bf16[4,256,256]{2,1,0:T(8,128)(2,1)S(1)}, u32[]{:S(2)}, u32[]{:S(2)}) collective-permute-start(bf16[4,256,256]{2,1,0:T(8,128)(2,1)} %refs_3_.1), channel_id=1, source_target_pairs={{0,24},{8,16},{16,8},{24,0},{1,25},{9,17},{17,9},{25,1},{2,26},{10... | collective-permute-start | bytes 1572872 | tf_op jit(solution)/shard_map/ppermute | solution.py:195
  111.2 0.8 copy-start.10
  111.2 1.0 copy-start.11
  112.2 19.4 %copy-start.6 = (s32[4]{0:T(128)S(1)}, s32[4]{0:T(128)}, u32[]{:S(2)}) copy-start(s32[4]{0:T(128)} %compare_select_fusion.7) | copy-start | bytes 52
  112.2 20.0 %copy-start.7 = (s32[4]{0:T(128)S(1)}, s32[4]{0:T(128)}, u32[]{:S(2)}) copy-start(s32[4]{0:T(128)} %compare_select_fusion.6) | copy-start | bytes 52
  112.2 20.6 %copy-start.8 = (s32[4]{0:T(128)S(1)}, s32[4]{0:T(128)}, u32[]{:S(2)}) copy-start(s32[4]{0:T(128)} %compare_select_fusion.5) | copy-start | bytes 52

commit v3 on v2

--- a/solution.py
+++ b/solution.py
@@ -106,60 +106,54 @@
     return ((real * scale).astype(jnp.bfloat16), (imag * scale).astype(jnp.bfloat16))
 
 
-def corr_kernel(first, *refs):
+def corr_kernel(first, tiles, *refs):
     if first:
-        (sr_ref, si_ref, tr_ref, ti_ref, c_ref, s_ref, top_ref, sum_ref, sq_ref, peak_ref) = refs
+        (sr_ref, si_ref, tr_ref, ti_ref, fw_ref, inv_ref, top_ref, sum_ref, sq_ref, peak_ref) = refs
     else:
-        (sr_ref, si_ref, tr_ref, ti_ref, c_ref, s_ref, top_in, sum_in, sq_in,
+        (sr_ref, si_ref, tr_ref, ti_ref, fw_ref, inv_ref, top_in, sum_in, sq_in,
          top_ref, sum_ref, sq_ref, peak_ref) = refs
-    t = pl.program_id(1)
     extent = sr_ref.shape[-1]
     sr = sr_ref[0].astype(jnp.float32)
     si = si_ref[0].astype(jnp.float32)
-    tr = tr_ref[0].astype(jnp.float32)
-    ti = ti_ref[0].astype(jnp.float32)
-    pre = (sr * tr + si * ti).astype(jnp.bfloat16)
-    pim = (si * tr - sr * ti).astype(jnp.bfloat16)
-    cos_t = c_ref[...]
-    sin_t = s_ref[...]
-
-    def mm(a, b):
-        return jnp.dot(a, b, preferred_element_type=jnp.float32)
-
-    q_re = (mm(pre, cos_t) - mm(pim, sin_t)).astype(jnp.bfloat16)
-    q_im = (mm(pre, sin_t) + mm(pim, cos_t)).astype(jnp.bfloat16)
-    corr = (mm(cos_t, q_re) - mm(sin_t, q_im)) / extent
-    peak_ref[...] = jnp.full(peak_ref.shape, jnp.max(corr), jnp.float32)
-
+    forward = fw_ref[...]
+    inverse = inv_ref[...]
+    top = total = square = None
+    for t in range(tiles):
+        tr = tr_ref[t].astype(jnp.float32)
+        ti = ti_ref[t].astype(jnp.float32)
+        pre = (sr * tr + si * ti).astype(jnp.bfloat16)
+        pim = (si * tr - sr * ti).astype(jnp.bfloat16)
+        prod = jnp.concatenate([pre, pim], axis=1)
+        q = jnp.dot(prod, forward, preferred_element_type=jnp.float32).astype(jnp.bfloat16)
+        q_stack = jnp.concatenate([q[:, :extent], q[:, extent:]], axis=0)
+        corr = jnp.dot(inverse, q_stack, preferred_element_type=jnp.float32)
+        peak_ref[0, t] = jnp.full(peak_ref.shape[2:], jnp.max(corr), jnp.float32)
+        if top is None:
+            top, total, square = corr, corr, corr * corr
+        else:
+            top = jnp.maximum(top, corr)
+            total = total + corr
+            square = square + corr * corr
     if first:
-        @pl.when(t == 0)
-        def _():
-            top_ref[0] = corr
-            sum_ref[0] = corr
-            sq_ref[0] = corr * corr
+        top_ref[0] = top
+        sum_ref[0] = total
+        sq_ref[0] = square
     else:
-        @pl.when(t == 0)
-        def _():
-            top_ref[0] = jnp.maximum(top_in[0], corr)
-            sum_ref[0] = sum_in[0] + corr
-            sq_ref[0] = sq_in[0] + corr * corr
-
-    @pl.when(t > 0)
-    def _():
-        top_ref[0] = jnp.maximum(top_ref[0], corr)
-        sum_ref[0] = sum_ref[0] + corr
-        sq_ref[0] = sq_ref[0] + corr * corr
-
-
-def correlate_chunk(spec_re, spec_im, templ_re, templ_im, cosine, sine, stats):
+        top_ref[0] = jnp.maximum(top_in[0], top)
+        sum_ref[0] = sum_in[0] + total
+        sq_ref[0] = sq_in[0] + square
+
+
+def correlate_chunk(spec_re, spec_im, templ_re, templ_im, forward, inverse, stats):
     count, extent = (spec_re.shape[0], spec_re.shape[-1])
     tiles = templ_re.shape[0]
     first = stats is None
-    plane = pl.BlockSpec((1, extent, extent), lambda s, t: (s, 0, 0))
-    templ_spec = pl.BlockSpec((1, extent, extent), lambda s, t: (t, 0, 0))
-    table = pl.BlockSpec((extent, extent), lambda s, t: (0, 0))
-    in_specs = [plane, plane, templ_spec, templ_spec, table, table]
-    operands = [spec_re, spec_im, templ_re, templ_im, cosine, sine]
+    plane = pl.BlockSpec((1, extent, extent), lambda s: (s, 0, 0))
+    templ_spec = pl.BlockSpec((tiles, extent, extent), lambda s: (0, 0, 0))
+    fw_spec = pl.BlockSpec(forward.shape, lambda s: (0, 0))
+    inv_spec = pl.BlockSpec(inverse.shape, lambda s: (0, 0))
+    in_specs = [plane, plane, templ_spec, templ_spec, fw_spec, inv_spec]
+    operands = [spec_re, spec_im, templ_re, templ_im, forward, inverse]
     aliases = {}
     if not first:
         in_specs += [plane, plane, plane]
@@ -168,17 +162,18 @@
     map_shape = jax.ShapeDtypeStruct((count, extent, extent), jnp.float32)
     flops = tiles * count * 12 * extent * extent * extent
     outs = pl.pallas_call(
-        functools.partial(corr_kernel, first),
-        grid=(count, tiles),
+        functools.partial(corr_kernel, first, tiles),
+        grid=(count,),
         in_specs=in_specs,
-        out_specs=[plane, plane, plane, pl.BlockSpec((1, 1, 8, 128), lambda s, t: (s, t, 0, 0))],
+        out_specs=[plane, plane, plane,
+                   pl.BlockSpec((1, tiles, 8, 128), lambda s: (s, 0, 0, 0))],
         out_shape=[map_shape, map_shape, map_shape,
                    jax.ShapeDtypeStruct((count, tiles, 8, 128), jnp.float32)],
         input_output_aliases=aliases,
-        compiler_params=pltpu.CompilerParams(dimension_semantics=("parallel", "arbitrary")),
+        compiler_params=pltpu.CompilerParams(dimension_semantics=("arbitrary",)),
         cost_estimate=pl.CostEstimate(
             flops=flops, transcendentals=0,
-            bytes_accessed=tiles * count * 4 * extent * extent * 2 + count * 6 * extent * extent * 4),
+            bytes_accessed=tiles * 4 * extent * extent * 2 + count * 10 * extent * extent * 4),
     )(*operands)
     return outs[:3], outs[3][:, :, 0, 0]
 
@@ -187,13 +182,19 @@
     blocks = lax.axis_size("blk")
     me = lax.axis_index("blk")
     tiles = templ_re.shape[0]
-    stats, peak = correlate_chunk(spec_re, spec_im, templ_re, templ_im, cosine, sine, None)
+    extent = cosine.shape[0]
+    forward = jnp.concatenate(
+        [jnp.concatenate([cosine, sine], axis=1), jnp.concatenate([-sine, cosine], axis=1)], axis=0
+    )
+    scale = jnp.asarray(1.0 / extent, jnp.bfloat16)
+    inverse = jnp.concatenate([cosine * scale, -sine * scale], axis=1)
+    stats, peak = correlate_chunk(spec_re, spec_im, templ_re, templ_im, forward, inverse, None)
     peaks = [(me, peak)]
     for k in range(1, blocks):
         pairs = [(b, b ^ k) for b in range(blocks)]
         got_re = lax.ppermute(templ_re, "blk", pairs)
         got_im = lax.ppermute(templ_im, "blk", pairs)
-        stats, peak = correlate_chunk(spec_re, spec_im, got_re, got_im, cosine, sine, stats)
+        stats, peak = correlate_chunk(spec_re, spec_im, got_re, got_im, forward, inverse, stats)
         peaks.append((me ^ k, peak))
     top_map, totals, squares = stats
     orient_total = orientation.shape[0]

time: 139 us -> 106 us (0.76); the launches traced: 137 us -> 106 us
  Pallas kernels: 69.7 us -> 38.2 us
  waiting for transfers between devices: 8.55 us -> 5.8 us
  other arithmetic: 9.45 us -> 12.2 us
    pallas_call x4, Pallas kernels: 69.7 us -> 38.2 us  [correlate_chunk(): pl.pallas_call(functools.partial(corr_kernel, first, tiles), grid=(count,...]
    ppermute x3, waiting for transfers between devices: 8.53 us -> 5.78 us  [route_patches(): lax.ppermute(outgoing[m], 'patch', xor_pairs(sources, 2 * m))]
    concatenate x0 -> x2, other arithmetic: none -> 1.57 us  [the longest x1 0.83 us: correlate_all(): jnp.concatenate([jnp.concatenate([cosine, sine], axis=1), jnp.concatenate...]
    unnamed x33 -> x29, local copies, waits for them, and re-layouts: 6.34 us -> 6.33 us
  transfers between devices with their start and end apart: 11 -> 11, of which waited for: 1 -> 1; matrix products, arithmetic and copies ran while one was open for 27% -> 37% of each run, Pallas kernels for 38% -> 27%
where the time goes in v3:
time: 106 us
  Pallas kernels  38.2 us (36%)
  local copies, waits for them, and re-layouts  24 us (23%)
  starting transfers between devices  12.7 us (12%)
  other arithmetic  12.2 us (12%)
  matrix products  11.7 us (11%)
  waiting for transfers between devices  5.8 us (5%)
  between operations  1.06 us (1%)
    pallas_call x4, Pallas kernels, correlate_chunk(): pl.pallas_call(functools.partial(corr_kernel, first, tiles), grid=(count,...  38.2 us
    unnamed x29, local copies, waits for them, and re-layouts  6.33 us
    ppermute x3, waiting for transfers between devices, route_patches(): lax.ppermute(outgoing[m], 'patch', xor_pairs(sources, 2 * m))  5.78 us
    dot_general x1, matrix products, make_spectra(): jnp.einsum('xk,nky->nxy', left_imag, half_stack, preferred_element_type=j...  4.61 us
    dot_general x1, matrix products, make_spectra(): jnp.einsum('xk,nky->nxy', left_real, half_stack, preferred_element_type=j...  4.57 us
    slice x4, local copies, waits for them, and re-layouts, correlate_chunk(): return (outs[:3], outs[3][:, :, 0, 0])  3.83 us
    ppermute x3, starting transfers between devices, correlate_all(): got_re = lax.ppermute(templ_re, 'blk', pairs)  3.73 us
    sub x1, other arithmetic, correlate_all(): var_map = squares / orient_total - mean_map * mean_map  3.1 us
  transfers between devices with their start and end apart: 11, of which 1 were waited for; matrix products, arithmetic and copies ran while one was open for 37% of the time, Pallas kernels for 27%

profile of v3, /device:TPU:9, one launch (start us, length us, event | category | flops | bytes accessed | tf_op | source)
XLA Modules:
  0.0 105.7 jit_solution(552685305678415403)
XLA Ops:
  0.6 1.3 %collective-permute-start.9 = (bf16[4,256,256]{2,1,0:T(8,128)(2,1)}, bf16[4,256,256]{2,1,0:T(8,128)(2,1)}, u32[]{:S(2)}, u32[]{:S(2)}) collective-permute-start(bf16[4,256,256]{2,1,0:T(8,128)(2,1)} %refs_2_.1), channel_id=1, source_target_pairs={{0,8},{8,0},{16,24},{24,16},{1,9},{9,1},{17,25},{25,17},{2,10},{10... | collective-permute-start | bytes 1572872 | tf_op jit(solution)/shard_map/ppermute | solution.py:195
  1.9 1.2 %collective-permute-start.7 = (bf16[4,256,256]{2,1,0:T(8,128)(2,1)}, bf16[4,256,256]{2,1,0:T(8,128)(2,1)}, u32[]{:S(2)}, u32[]{:S(2)}) collective-permute-start(bf16[4,256,256]{2,1,0:T(8,128)(2,1)} %refs_2_.1), channel_id=1, source_target_pairs={{0,16},{8,24},{16,0},{24,8},{1,17},{9,25},{17,1},{25,9},{2,18},{10... | collective-permute-start | bytes 1572872 | tf_op jit(solution)/shard_map/ppermute | solution.py:195
  3.2 0.7 reshape.509
  4.9 1.0 concatenate.34
  5.8 0.6 gather_fusion
  7.0 2.3 %collective-permute-start.2 = (bf16[2,256,256]{2,1,0:T(8,128)(2,1)S(1)}, bf16[2,256,256]{2,1,0:T(8,128)(2,1)S(1)}, u32[]{:S(2)}, u32[]{:S(2)}) collective-permute-start(bf16[2,256,256]{2,1,0:T(8,128)(2,1)S(1)} %get-tuple-element.67), channel_id=1, source_target_pairs={{0,4},{1,5},{2,6},{3,7},{4,0},{5,1},{6,2},{7,3},{8,12},{9,13},{10,... | collective-permute-start | bytes 786440 | tf_op jit(solution)/shard_map/ppermute | solution.py:63
  9.5 0.7 constant_dynamic-update-slice_fusion.5
  10.7 1.1 %sine_convert_fusion = (bf16[256,256]{1,0:T(8,128)(2,1)S(1)}, bf16[256,256]{1,0:T(8,128)(2,1)S(1)}) fusion(), kind=kLoop, calls=%fused_computation.41 | loop fusion | flops 1048576 | bytes 262144 | tf_op jit(solution)/shard_map/convert_element_type | solution.py:23
  11.8 1.0 fusion.15
  12.8 1.1 %fusion.14 = (bf16[256,256]{1,0:T(8,128)(2,1)S(1)}, bf16[256,256]{1,0:T(8,128)(2,1)S(1)}) fusion(), kind=kLoop, calls=%fused_computation.47 | loop fusion | flops 1572864 | bytes 262144 | tf_op jit(solution)/shard_map/mul | solution.py:190
  14.8 0.6 gather_fusion.2
  15.5 0.6 gather_fusion.4
  16.7 0.6 gather_fusion.5
  17.9 0.6 gather_fusion.6
  19.2 0.6 gather_fusion.7
  20.4 0.7 pad_maximum_fusion.4.refs_5_
  21.1 0.8 maximum_maximum_fusion.refs_4_
  21.9 0.6 gather_fusion.3
  23.1 2.1 %collective-permute-start = (bf16[2,256,256]{2,1,0:T(8,128)(2,1)S(1)}, bf16[2,256,256]{2,1,0:T(8,128)(2,1)S(1)}, u32[]{:S(2)}, u32[]{:S(2)}) collective-permute-start(bf16[2,256,256]{2,1,0:T(8,128)(2,1)S(1)} %get-tuple-element.69), channel_id=1, source_target_pairs={{0,1},{1,0},{2,3},{3,2},{4,5},{5,4},{6,7},{7,6},{8,9},{9,8},{10,11... | collective-permute-start | bytes 786440 | tf_op jit(solution)/shard_map/ppermute | solution.py:60
  25.5 5.8 %collective-permute-done.3 = bf16[2,256,256]{2,1,0:T(8,128)(2,1)S(1)} collective-permute-done((bf16[2,256,256]{2,1,0:T(8,128)(2,1)S(1)}, bf16[2,256,256]{2,1,0:T(8,128)(2,1)S(1)}, u32[]{:S(2)}, u32[]{:S(2)}) %collective-permute-start.3) | collective-permute-done | bytes 262176 | tf_op jit(solution)/shard_map/ppermute | solution.py:63
  31.3 2.5 %collective-permute-start.4 = (bf16[6,256,256]{2,1,0:T(8,128)(2,1)S(1)}, bf16[6,256,256]{2,1,0:T(8,128)(2,1)S(1)}, u32[]{:S(2)}, u32[]{:S(2)}) collective-permute-start(bf16[6,256,256]{2,1,0:T(8,128)(2,1)S(1)} %pad_maximum_fusion.1), channel_id=1, source_target_pairs={{0,1},{1,0},{2,3},{3,2},{4,5},{5,4},{6,7},{7,6},{8,9},{9,8},{10,11... | collective-permute-start | bytes 2359304 | tf_op jit(solution)/shard_map/ppermute | solution.py:65
  34.3 0.7 constant_dynamic-update-slice_fusion.4
  35.0 0.7 constant_dynamic-update-slice_fusion.3
  35.7 0.7 constant_dynamic-update-slice_fusion.2
  36.4 0.7 constant_dynamic-update-slice_fusion.1
  37.2 1.2 %collective-permute-start.5 = (bf16[4,256,256]{2,1,0:T(8,128)(2,1)}, bf16[4,256,256]{2,1,0:T(8,128)(2,1)S(1)}, u32[]{:S(2)}, u32[]{:S(2)}) collective-permute-start(bf16[4,256,256]{2,1,0:T(8,128)(2,1)} %refs_2_.1), channel_id=1, source_target_pairs={{0,24},{8,16},{16,8},{24,0},{1,25},{9,17},{17,9},{25,1},{2,26},{10... | collective-permute-start | bytes 1572872 | tf_op jit(solution)/shard_map/ppermute | solution.py:195
  38.4 1.0 constant_dynamic-update-slice_fusion
  39.4 0.7 broadcast_dynamic-update-slice_fusion
  40.0 2.2 %gather_fusion.1 = bf16[4,256,256]{2,1,0:T(8,128)(2,1)S(1)} fusion(bf16[17,256,256]{2,1,0:T(8,128)(2,1)} %broadcast_dynamic-update-slice_fusion, s32[1024]{0:T(1024)S(1)} %pad_clamp_fusion.6), kind=kCustom, calls=%fused_computation.5 | custom fusion | bytes 1048592 | tf_op jit(solution)/shard_map/jit(_take)/gather | solution.py:89
  42.5 1.2 %convolution_convert_fusion.1 = bf16[1024,256]{1,0:T(8,128)(2,1)S(1)} fusion(bf16[1024,256]{1,0:T(8,128)(2,1)S(1)} %bitcast_select_fusion), kind=kOutput, calls=%fused_computation.17 | convolution fusion | flops 135462912 | bytes 1048576 | tf_op jit(solution)/shard_map/dot_general | solution.py:96
  43.7 1.3 %convolution_convert_fusion = bf16[1024,256]{1,0:T(8,128)(2,1)S(1)} fusion(bf16[1024,256]{1,0:T(8,128)(2,1)S(1)} %bitcast_select_fusion), kind=kOutput, calls=%fused_computation.16 | convolution fusion | flops 135659520 | bytes 1048576 | tf_op jit(solution)/shard_map/dot_general | solution.py:97
  45.4 4.6 %fusion.2.refs_1_ = bf16[4,256,256]{2,1,0:T(8,128)(2,1)} fusion(bf16[4,256,256]{1,2,0:T(8,128)(2,1)S(1)} %copy.80, bf16[4,256,256]{1,2,0:T(8,128)(2,1)S(1)} %copy.79, f32[256,256]{1,0:T(8,128)S(1)} %broadcast_add_fusion, f32[4]{0:T(128)S(1)} %copy-done.7, bf16[256,256]{1,0:T(8,128)(2,1)S(1)} %get-tuple-element.89, bf16[256,256]{1,0:T(8,128)(2,1)S(1)} %fusion.15), kind=kOutput, calls=%fused_computation.18 | convolution fusion | flops 272629760 | bytes 2097168 | tf_op jit(solution)/shard_map/xk,nky->nxy/dot_general | solution.py:104
  50.0 4.6 %fusion.3.refs_0_ = bf16[4,256,256]{2,1,0:T(8,128)(2,1)} fusion(bf16[4,256,256]{1,2,0:T(8,128)(2,1)S(1)} %copy.80, bf16[4,256,256]{1,2,0:T(8,128)(2,1)S(1)} %copy.79, f32[256,256]{1,0:T(8,128)S(1)} %broadcast_add_fusion, f32[4]{0:T(128)S(1)} %copy-done.7, bf16[256,256]{1,0:T(8,128)(2,1)S(1)} %get-tuple-element.88, bf16[256,256]{1,0:T(8,128)(2,1)S(1)} %get-tuple-element.89), kind=kOutput, calls=%fused_computation.19 | convolution fusion | flops 272629760 | bytes 2097168 | tf_op jit(solution)/shard_map/xk,nky->nxy/dot_general | solution.py:103
  54.6 9.2 %shard_map.102 = (f32[4,256,256]{2,1,0:T(8,128)}, f32[4,256,256]{2,1,0:T(8,128)}, f32[4,256,256]{2,1,0:T(8,128)}, f32[4,4,8,128]{3,2,1,0:T(8,128)}) custom-call(bf16[4,256,256]{2,1,0:T(8,128)(2,1)} %fusion.3.refs_0_, bf16[4,256,256]{2,1,0:T(8,128)(2,1)} %fusion.2.refs_1_, bf16[4,256,256]{2,1,0:T(8,128)(2,1)} %refs_2_.1, bf16[4,256,256]{2,1,0:T(8,128)(2,1)} %refs_3_.1, ...), custom_call_target="tpu_custom_call" | custom-call | flops 3221225472 | bytes 12582912 | tf_op jit(solution)/shard_map/pallas_call | solution.py:164
  63.8 1.2 %collective-permute-start.6 = (bf16[4,256,256]{2,1,0:T(8,128)(2,1)}, bf16[4,256,256]{2,1,0:T(8,128)(2,1)S(1)}, u32[]{:S(2)}, u32[]{:S(2)}) collective-permute-start(bf16[4,256,256]{2,1,0:T(8,128)(2,1)} %refs_3_.1), channel_id=1, source_target_pairs={{0,24},{8,16},{16,8},{24,0},{1,25},{9,17},{17,9},{25,1},{2,26},{10... | collective-permute-start | bytes 1572872 | tf_op jit(solution)/shard_map/ppermute | solution.py:196
  65.0 9.7 %shard_map.103 = (f32[4,256,256]{2,1,0:T(8,128)}, f32[4,256,256]{2,1,0:T(8,128)}, f32[4,256,256]{2,1,0:T(8,128)}, f32[4,4,8,128]{3,2,1,0:T(8,128)}) custom-call(bf16[4,256,256]{2,1,0:T(8,128)(2,1)} %fusion.3.refs_0_, bf16[4,256,256]{2,1,0:T(8,128)(2,1)} %fusion.2.refs_1_, ...), custom_call_target="tpu_custom_call", output_to_operand_aliasing={{0}: (6, {}), {1}: (7, {}), {2}: (8, {})} | custom-call | flops 3221225472 | bytes 12582912 | tf_op jit(solution)/shard_map/pallas_call | solution.py:164
  74.7 1.0 slice_reduce_fusion.2
  75.8 1.0 slice_reduce_fusion.3
  76.8 9.7 %shard_map.104 = (f32[4,256,256]{2,1,0:T(8,128)}, f32[4,256,256]{2,1,0:T(8,128)}, f32[4,256,256]{2,1,0:T(8,128)}, f32[4,4,8,128]{3,2,1,0:T(8,128)}) custom-call(bf16[4,256,256]{2,1,0:T(8,128)(2,1)} %fusion.3.refs_0_, bf16[4,256,256]{2,1,0:T(8,128)(2,1)} %fusion.2.refs_1_, ...), custom_call_target="tpu_custom_call", output_to_operand_aliasing={{0}: (6, {}), {1}: (7, {}), {2}: (8, {})} | custom-call | flops 3221225472 | bytes 12582912 | tf_op jit(solution)/shard_map/pallas_call | solution.py:164
  86.5 1.0 slice_reduce_fusion.1
  87.6 0.8 copy-done.8
  88.6 9.7 %shard_map.105 = (f32[4,256,256]{2,1,0:T(8,128)}, f32[4,256,256]{2,1,0:T(8,128)}, f32[4,256,256]{2,1,0:T(8,128)}, f32[4,4,8,128]{3,2,1,0:T(8,128)}) custom-call(bf16[4,256,256]{2,1,0:T(8,128)(2,1)} %fusion.3.refs_0_, bf16[4,256,256]{2,1,0:T(8,128)(2,1)} %fusion.2.refs_1_, ...), custom_call_target="tpu_custom_call", output_to_operand_aliasing={{0}: (6, {}), {1}: (7, {}), {2}: (8, {})} | custom-call | flops 3221225472 | bytes 12582912 | tf_op jit(solution)/shard_map/pallas_call | solution.py:164
  98.3 1.0 slice_reduce_fusion
  99.3 0.7 scatter_custom_fusion
  100.0 0.6 scatter_fusion
  100.7 0.6 scatter_fusion.1
  101.9 0.7 copy.87
  102.6 3.1 %multiply_subtract_fusion = (f32[4,256,256]{2,1,0:T(8,128)}, f32[4,256,256]{2,1,0:T(8,128)}) fusion(f32[4,256,256]{2,1,0:T(8,128)} %get-tuple-element.32, f32[4,256,256]{2,1,0:T(8,128)} %get-tuple-element.31), kind=kLoop, calls=%fused_computation.21 | loop fusion | flops 1048576 | bytes 4194304 | tf_op jit(solution)/shard_map/sub | solution.py:208
  (97 shorter events, 8.4 us)
Async XLA Ops:
  0.6 14.9 %copy-start = (s32[16]{0:T(128)S(1)}, s32[16]{0:T(128)}, u32[]{:S(2)}) copy-start(s32[16]{0:T(128)} %param.15) | copy-start | bytes 196
  0.6 64.4 %collective-permute-start.9 = (bf16[4,256,256]{2,1,0:T(8,128)(2,1)}, bf16[4,256,256]{2,1,0:T(8,128)(2,1)}, u32[]{:S(2)}, u32[]{:S(2)}) collective-permute-start(bf16[4,256,256]{2,1,0:T(8,128)(2,1)} %refs_2_.1), channel_id=1, source_target_pairs={{0,8},{8,0},{16,24},{24,16},{1,9},{9,1},{17,25},{25,17},{2,10},{10... | collective-permute-start | bytes 1572872 | tf_op jit(solution)/shard_map/ppermute | solution.py:195
  1.9 74.9 %collective-permute-start.7 = (bf16[4,256,256]{2,1,0:T(8,128)(2,1)}, bf16[4,256,256]{2,1,0:T(8,128)(2,1)}, u32[]{:S(2)}, u32[]{:S(2)}) collective-permute-start(bf16[4,256,256]{2,1,0:T(8,128)(2,1)} %refs_2_.1), channel_id=1, source_target_pairs={{0,16},{8,24},{16,0},{24,8},{1,17},{9,25},{17,1},{25,9},{2,18},{10... | collective-permute-start | bytes 1572872 | tf_op jit(solution)/shard_map/ppermute | solution.py:195
  6.5 3.0 %copy-start.2 = (bf16[2,256,256]{2,1,0:T(8,128)(2,1)S(1)}, bf16[2,256,256]{2,1,0:T(8,128)(2,1)}, u32[]{:S(2)}) copy-start(bf16[2,256,256]{2,1,0:T(8,128)(2,1)} %param.9) | copy-start | bytes 786436
  6.5 3.7 %copy-start.3 = (s32[16]{0:T(128)S(1)}, s32[16]{0:T(128)}, u32[]{:S(2)}) copy-start(s32[16]{0:T(128)} %param.10) | copy-start | bytes 196
  6.7 8.1 %copy-start.10 = (s32[16]{0:T(128)S(1)}, s32[16]{0:T(128)}, u32[]{:S(2)}) copy-start(s32[16]{0:T(128)} %param.11) | copy-start | bytes 196
  6.7 16.4 %collective-permute-start.1 = (bf16[2,256,256]{2,1,0:T(8,128)(2,1)S(1)}, bf16[2,256,256]{2,1,0:T(8,128)(2,1)S(1)}, u32[]{:S(2)}, u32[]{:S(2)}) collective-permute-start(bf16[2,256,256]{2,1,0:T(8,128)(2,1)S(1)} %get-tuple-element.68), channel_id=1, source_target_pairs={{0,2},{1,3},{2,0},{3,1},{4,6},{5,7},{6,4},{7,5},{8,10},{9,11},{10,... | collective-permute-start | bytes 786440 | tf_op jit(solution)/shard_map/ppermute | solution.py:63
  7.0 18.2 %collective-permute-start.2 = (bf16[2,256,256]{2,1,0:T(8,128)(2,1)S(1)}, bf16[2,256,256]{2,1,0:T(8,128)(2,1)S(1)}, u32[]{:S(2)}, u32[]{:S(2)}) collective-permute-start(bf16[2,256,256]{2,1,0:T(8,128)(2,1)S(1)} %get-tuple-element.67), channel_id=1, source_target_pairs={{0,4},{1,5},{2,6},{3,7},{4,0},{5,1},{6,2},{7,3},{8,12},{9,13},{10,... | collective-permute-start | bytes 786440 | tf_op jit(solution)/shard_map/ppermute | solution.py:63
  9.3 21.9 %collective-permute-start.3 = (bf16[2,256,256]{2,1,0:T(8,128)(2,1)S(1)}, bf16[2,256,256]{2,1,0:T(8,128)(2,1)S(1)}, u32[]{:S(2)}, u32[]{:S(2)}) collective-permute-start(bf16[2,256,256]{2,1,0:T(8,128)(2,1)S(1)} %get-tuple-element.66), channel_id=1, source_target_pairs={{0,6},{1,7},{2,4},{3,5},{4,2},{5,3},{6,0},{7,1},{8,14},{9,15},{10,... | collective-permute-start | bytes 786440 | tf_op jit(solution)/shard_map/ppermute | solution.py:63
  12.8 9.2 %copy-start.1 = (f32[32]{0:T(128)S(1)}, f32[32]{0:T(128)}, u32[]{:S(2)}) copy-start(f32[32]{0:T(128)} %param.12) | copy-start | bytes 388
  23.1 10.9 %collective-permute-start = (bf16[2,256,256]{2,1,0:T(8,128)(2,1)S(1)}, bf16[2,256,256]{2,1,0:T(8,128)(2,1)S(1)}, u32[]{:S(2)}, u32[]{:S(2)}) collective-permute-start(bf16[2,256,256]{2,1,0:T(8,128)(2,1)S(1)} %get-tuple-element.69), channel_id=1, source_target_pairs={{0,1},{1,0},{2,3},{3,2},{4,5},{5,4},{6,7},{7,6},{8,9},{9,8},{10,11... | collective-permute-start | bytes 786440 | tf_op jit(solution)/shard_map/ppermute | solution.py:60
  25.2 38.6 %collective-permute-start.10 = (bf16[4,256,256]{2,1,0:T(8,128)(2,1)}, bf16[4,256,256]{2,1,0:T(8,128)(2,1)}, u32[]{:S(2)}, u32[]{:S(2)}) collective-permute-start(bf16[4,256,256]{2,1,0:T(8,128)(2,1)} %refs_3_.1), channel_id=1, source_target_pairs={{0,8},{8,0},{16,24},{24,16},{1,9},{9,1},{17,25},{25,17},{2,10},{10... | collective-permute-start | bytes 1572872 | tf_op jit(solution)/shard_map/ppermute | solution.py:196
  31.3 5.9 %collective-permute-start.4 = (bf16[6,256,256]{2,1,0:T(8,128)(2,1)S(1)}, bf16[6,256,256]{2,1,0:T(8,128)(2,1)S(1)}, u32[]{:S(2)}, u32[]{:S(2)}) collective-permute-start(bf16[6,256,256]{2,1,0:T(8,128)(2,1)S(1)} %pad_maximum_fusion.1), channel_id=1, source_target_pairs={{0,1},{1,0},{2,3},{3,2},{4,5},{5,4},{6,7},{7,6},{8,9},{9,8},{10,11... | collective-permute-start | bytes 2359304 | tf_op jit(solution)/shard_map/ppermute | solution.py:65
  34.0 42.8 %collective-permute-start.8 = (bf16[4,256,256]{2,1,0:T(8,128)(2,1)}, bf16[4,256,256]{2,1,0:T(8,128)(2,1)}, u32[]{:S(2)}, u32[]{:S(2)}) collective-permute-start(bf16[4,256,256]{2,1,0:T(8,128)(2,1)} %refs_3_.1), channel_id=1, source_target_pairs={{0,16},{8,24},{16,0},{24,8},{1,17},{9,25},{17,1},{25,9},{2,18},{10... | collective-permute-start | bytes 1572872 | tf_op jit(solution)/shard_map/ppermute | solution.py:196
  37.2 50.4 %collective-permute-start.5 = (bf16[4,256,256]{2,1,0:T(8,128)(2,1)}, bf16[4,256,256]{2,1,0:T(8,128)(2,1)S(1)}, u32[]{:S(2)}, u32[]{:S(2)}) collective-permute-start(bf16[4,256,256]{2,1,0:T(8,128)(2,1)} %refs_2_.1), channel_id=1, source_target_pairs={{0,24},{8,16},{16,8},{24,0},{1,25},{9,17},{17,9},{25,1},{2,26},{10... | collective-permute-start | bytes 1572872 | tf_op jit(solution)/shard_map/ppermute | solution.py:195
  43.7 1.7 %copy-start.7 = (f32[4]{0:T(128)S(1)}, f32[4]{0:T(128)}, u32[]{:S(2)}) copy-start(f32[4]{0:T(128)} %fusion.39) | copy-start | bytes 52
  63.8 23.7 %collective-permute-start.6 = (bf16[4,256,256]{2,1,0:T(8,128)(2,1)}, bf16[4,256,256]{2,1,0:T(8,128)(2,1)S(1)}, u32[]{:S(2)}, u32[]{:S(2)}) collective-permute-start(bf16[4,256,256]{2,1,0:T(8,128)(2,1)} %refs_3_.1), channel_id=1, source_target_pairs={{0,24},{8,16},{16,8},{24,0},{1,25},{9,17},{17,9},{25,1},{2,26},{10... | collective-permute-start | bytes 1572872 | tf_op jit(solution)/shard_map/ppermute | solution.py:196
  87.5 0.8 copy-start.8
  87.6 1.0 copy-start.9
  88.6 11.5 %copy-start.4 = (s32[4]{0:T(128)S(1)}, s32[4]{0:T(128)}, u32[]{:S(2)}) copy-start(s32[4]{0:T(128)} %compare_select_fusion.7) | copy-start | bytes 52
  88.6 12.1 %copy-start.5 = (s32[4]{0:T(128)S(1)}, s32[4]{0:T(128)}, u32[]{:S(2)}) copy-start(s32[4]{0:T(128)} %compare_select_fusion.6) | copy-start | bytes 52
  88.6 12.7 %copy-start.6 = (s32[4]{0:T(128)S(1)}, s32[4]{0:T(128)}, u32[]{:S(2)}) copy-start(s32[4]{0:T(128)} %compare_select_fusion.5) | copy-start | bytes 52

commit v4 on v3

v4 whole, which is shorter than its diff:
```python
import functools
import math

import jax
import jax.numpy as jnp
from jax import lax
from jax.experimental import pallas as pl
from jax.experimental.pallas import tpu as pltpu
from jax.sharding import PartitionSpec as P

SLOT = 2
CAP = 4
TILE_T = 4


AMPLITUDE = 0.07


def dft_tables(extent):
    indices = jnp.arange(extent, dtype=jnp.int32)
    turn_count = indices[:, None] * indices[None, :] % extent
    angles = turn_count.astype(jnp.float32) * (2.0 * math.pi / extent)
    return (jnp.cos(angles).astype(jnp.bfloat16), jnp.sin(angles).astype(jnp.bfloat16))


def ctf_filter(defocus_values, extent):
    indices = jnp.arange(extent, dtype=jnp.int32)
    signed = (
        jnp.where(indices < extent // 2, indices, indices - extent).astype(jnp.float32) / extent
    )
    radius = signed[:, None] * signed[:, None] + signed[None, :] * signed[None, :]
    phases = math.pi * defocus_values[:, None, None] * radius[None, :, :] - AMPLITUDE
    return -jnp.sin(phases)


def xor_pairs(count, shift):
    return [(d, d ^ shift) for d in range(count)]


def route_patches(patches, row_owner, my_index):
    sources, number = row_owner.shape
    extent = patches.shape[-1]
    chips = sources // 2
    devs = jnp.arange(sources, dtype=jnp.int32)
    chip_of = devs // 2
    owner_chip = row_owner // 2
    masks = [row_owner == (devs ^ 1)[:, None]]
    for m in range(1, chips):
        masks.append(owner_chip == (chip_of ^ m)[:, None])
    match = jnp.stack(masks, axis=1)
    first = jnp.where(match[..., 0], 0, jnp.where(match[..., 1], 1, number))
    second = jnp.where(match[..., 0] & match[..., 1], 1, number)
    send_sel = jnp.stack([first, second], axis=-1)
    send_pid = jnp.where(send_sel < number, devs[:, None, None] * number + send_sel, -1)
    padded = jnp.concatenate([patches, jnp.zeros((1, extent, extent), patches.dtype)], axis=0)
    my_sel = lax.dynamic_index_in_dim(send_sel, my_index, 0, keepdims=False)
    outgoing = jnp.take(padded, my_sel.reshape(-1), axis=0).reshape(chips, 2, extent, extent)
    partner = my_index ^ 1
    my_chip = my_index // 2
    direct = lax.ppermute(outgoing[0], "patch", xor_pairs(sources, 1))
    received = []
    for m in range(1, chips):
        received.append(lax.ppermute(outgoing[m], "patch", xor_pairs(sources, 2 * m)))
    received = jnp.concatenate(received, axis=0)
    forwarded = lax.ppermute(received, "patch", xor_pairs(sources, 1))
    cand_pid = [my_index * number + jnp.arange(number, dtype=jnp.int32)]
    cand_pid.append(lax.dynamic_index_in_dim(send_pid, partner, 0, keepdims=False)[0])
    for core in (my_index % 2, partner % 2):
        for m in range(1, chips):
            source = (my_chip ^ m) * 2 + core
            cand_pid.append(lax.dynamic_index_in_dim(send_pid, source, 0, keepdims=False)[m])
    cand_pid = jnp.concatenate(cand_pid)
    flat_owner = row_owner.reshape(-1)
    hits = (flat_owner == my_index).astype(jnp.int32)
    rank_in = jnp.cumsum(hits) - hits
    slot_ids = jnp.arange(CAP, dtype=jnp.int32)
    wanted = (hits[None, :] == 1) & (rank_in[None, :] == slot_ids[:, None])
    patch_ids = jnp.arange(sources * number, dtype=jnp.int32)
    slot_pid = jnp.sum(jnp.where(wanted, patch_ids[None, :], 0), axis=1)
    present = jnp.any(wanted, axis=1)
    cand_ids = jnp.arange(cand_pid.shape[0], dtype=jnp.int32)
    found = cand_pid[None, :] == slot_pid[:, None]
    take_idx = jnp.sum(jnp.where(found, cand_ids[None, :], 0), axis=1)
    take_idx = jnp.where(present, take_idx, cand_pid.shape[0])
    pieces = (patches, direct, received, forwarded)
    return take_idx, pieces, jnp.where(present, slot_pid, sources * number)


def spectra_kernel(rows, take_ref, own_ref, direct_ref, recv_ref, fwd_ref, scale_ref, half_ref,
                   full_ref, re_ref, im_ref):
    s = pl.program_id(0)
    idx = take_ref[s]
    number = own_ref.shape[0]
    pick_own = own_ref[jnp.clip(idx, 0, number - 1)]
    pick_direct = direct_ref[jnp.clip(idx - number, 0, number - 1)]
    pick_recv = recv_ref[jnp.clip(idx - 2 * number, 0, rows - 1)]
    pick_fwd = fwd_ref[jnp.clip(idx - 2 * number - rows, 0, rows - 1)]
    zero = jnp.zeros_like(pick_own)
    image = jnp.where(
        idx < number, pick_own,
        jnp.where(idx < 2 * number, pick_direct,
                  jnp.where(idx < 2 * number + rows, pick_recv,
                            jnp.where(idx < 2 * number + 2 * rows, pick_fwd, zero))))
    extent = image.shape[-1]
    half = jnp.dot(image, half_ref[...], preferred_element_type=jnp.float32).astype(jnp.bfloat16)
    half_stack = jnp.concatenate([half[:, :extent], half[:, extent:]], axis=0)
    spec = jnp.dot(full_ref[...], half_stack, preferred_element_type=jnp.float32)
    scale = scale_ref[0]
    re_ref[0] = (spec[:extent] * scale).astype(jnp.bfloat16)
    im_ref[0] = (spec[extent:] * scale).astype(jnp.bfloat16)


def make_spectra(take_idx, own, direct, received, forwarded, scale, half_table, full_table):
    count, extent = (scale.shape[0], scale.shape[-1])
    rows = received.shape[0]
    whole = pl.BlockSpec(memory_space=pltpu.VMEM)
    plane = pl.BlockSpec((1, extent, extent), lambda s: (s, 0, 0))
    spec_shape = jax.ShapeDtypeStruct((count, extent, extent), jnp.bfloat16)
    return pl.pallas_call(
        functools.partial(spectra_kernel, rows),
        grid=(count,),
        in_specs=[pl.BlockSpec(memory_space=pltpu.SMEM), whole, whole, whole, whole, plane,
                  pl.BlockSpec(half_table.shape, lambda s: (0, 0)),
                  pl.BlockSpec(full_table.shape, lambda s: (0, 0))],
        out_specs=[plane, plane],
        out_shape=[spec_shape, spec_shape],
        compiler_params=pltpu.CompilerParams(dimension_semantics=("arbitrary",)),
        cost_estimate=pl.CostEstimate(
            flops=count * 6 * extent * extent * extent, transcendentals=0,
            bytes_accessed=count * 10 * extent * extent),
    )(take_idx, own, direct, received, forwarded, scale, half_table, full_table)


def corr_kernel(first, last, tiles, orient_total, *refs):
    if first:
        (orient_ref, sr_ref, si_ref, tr_ref, ti_ref, fw_ref, inv_ref,
         top_ref, sum_ref, sq_ref, peak_ref) = refs
    else:
        (orient_ref, sr_ref, si_ref, tr_ref, ti_ref, fw_ref, inv_ref, top_in, sum_in, sq_in, peak_in,
         top_ref, sum_ref, sq_ref, peak_ref) = refs
    extent = sr_ref.shape[-1]
    sr = sr_ref[0].astype(jnp.float32)
    si = si_ref[0].astype(jnp.float32)
    forward = fw_ref[...]
    inverse = inv_ref[...]
    lanes = lax.broadcasted_iota(jnp.int32, peak_ref.shape[1:], 1)
    peak_row = jnp.zeros(peak_ref.shape[1:], jnp.float32) if first else peak_in[0]
    top = total = square = None
    for t in range(tiles):
        tr = tr_ref[t].astype(jnp.float32)
        ti = ti_ref[t].astype(jnp.float32)
        pre = (sr * tr + si * ti).astype(jnp.bfloat16)
        pim = (si * tr - sr * ti).astype(jnp.bfloat16)
        prod = jnp.concatenate([pre, pim], axis=1)
        q = jnp.dot(prod, forward, preferred_element_type=jnp.float32).astype(jnp.bfloat16)
        q_stack = jnp.concatenate([q[:, :extent], q[:, extent:]], axis=0)
        corr = jnp.dot(inverse, q_stack, preferred_element_type=jnp.float32)
        peak_row = jnp.where(lanes == orient_ref[t], jnp.max(corr), peak_row)
        if top is None:
            top, total, square = corr, corr, corr * corr
        else:
            top = jnp.maximum(top, corr)
            total = total + corr
            square = square + corr * corr
    if not first:
        top = jnp.maximum(top_in[0], top)
        total = sum_in[0] + total
        square = sq_in[0] + square
    top_ref[0] = top
    peak_ref[0] = peak_row
    if last:
        mean = total / orient_total
        sum_ref[0] = mean
        sq_ref[0] = square / orient_total - mean * mean
    else:
        sum_ref[0] = total
        sq_ref[0] = square


def correlate_chunk(spec_re, spec_im, templ_re, templ_im, forward, inverse, orient_chunk,
                    orient_total, stats, last):
    count, extent = (spec_re.shape[0], spec_re.shape[-1])
    tiles = templ_re.shape[0]
    first = stats is None
    lanes = 128 * ((orient_total + 127) // 128)
    plane = pl.BlockSpec((1, extent, extent), lambda s: (s, 0, 0))
    peak_spec = pl.BlockSpec((1, 8, lanes), lambda s: (s, 0, 0))
    templ_spec = pl.BlockSpec((tiles, extent, extent), lambda s: (0, 0, 0))
    fw_spec = pl.BlockSpec(forward.shape, lambda s: (0, 0))
    inv_spec = pl.BlockSpec(inverse.shape, lambda s: (0, 0))
    in_specs = [pl.BlockSpec(memory_space=pltpu.SMEM), plane, plane, templ_spec, templ_spec,
                fw_spec, inv_spec]
    operands = [orient_chunk, spec_re, spec_im, templ_re, templ_im, forward, inverse]
    aliases = {}
    if not first:
        in_specs += [plane, plane, plane, peak_spec]
        operands += list(stats)
        aliases = {7: 0, 8: 1, 9: 2, 10: 3}
    map_shape = jax.ShapeDtypeStruct((count, extent, extent), jnp.float32)
    flops = tiles * count * 12 * extent * extent * extent
    return pl.pallas_call(
        functools.partial(corr_kernel, first, last, tiles, orient_total),
        grid=(count,),
        in_specs=in_specs,
        out_specs=[plane, plane, plane, peak_spec],
        out_shape=[map_shape, map_shape, map_shape,
                   jax.ShapeDtypeStruct((count, 8, lanes), jnp.float32)],
        input_output_aliases=aliases,
        compiler_params=pltpu.CompilerParams(dimension_semantics=("arbitrary",)),
        cost_estimate=pl.CostEstimate(
            flops=flops, transcendentals=0,
            bytes_accessed=tiles * 4 * extent * extent * 2 + count * 10 * extent * extent * 4),
    )(*operands)


def correlate_all(spec_re, spec_im, templ_re, templ_im, orientation, forward, inverse):
    blocks = lax.axis_size("blk")
    me = lax.axis_index("blk")
    tiles = templ_re.shape[0]
    orient_total = orientation.shape[0]
    within = jnp.arange(tiles, dtype=jnp.int32)
    chunks = [(me, templ_re, templ_im)]
    for k in range(1, blocks):
        pairs = [(b, b ^ k) for b in range(blocks)]
        chunks.append((me ^ k, lax.ppermute(templ_re, "blk", pairs),
                       lax.ppermute(templ_im, "blk", pairs)))
    stats = None
    for n, (source, got_re, got_im) in enumerate(chunks):
        orient_chunk = jnp.take(orientation, source * tiles + within)
        stats = correlate_chunk(spec_re, spec_im, got_re, got_im, forward, inverse, orient_chunk,
                                orient_total, stats, n == len(chunks) - 1)
    top_map, mean_map, var_map, peak = stats
    return (top_map, mean_map, var_map, peak[:, 0, :orient_total])


def body(patches, owner_of_patch, group_of_patch, defocus, templ_re, templ_im, orientation):
    sources = lax.axis_size("patch")
    my_index = lax.axis_index("patch")
    number, extent = (patches.shape[0], patches.shape[1])
    cosine, sine = dft_tables(extent)
    row_owner = owner_of_patch.reshape(sources, number)
    take_idx, pieces, slot_row = route_patches(patches, row_owner, my_index)
    groups = jnp.take(jnp.concatenate([group_of_patch, jnp.zeros((1,), jnp.int32)]), slot_row)
    focus_values = jnp.take(defocus, groups)
    scale = ctf_filter(focus_values, extent) / extent
    forward = jnp.concatenate(
        [jnp.concatenate([cosine, sine], axis=1), jnp.concatenate([-sine, cosine], axis=1)], axis=0
    )
    half_table = jnp.concatenate([cosine, -sine], axis=1)
    inverse = half_table * jnp.asarray(1.0 / extent, jnp.bfloat16)
    spec_re, spec_im = make_spectra(take_idx, *pieces, scale, half_table, forward)
    return correlate_all(spec_re, spec_im, templ_re, templ_im, orientation, forward, inverse)


def solution(mesh):
    placed = (
        P(("blk", "patch"), None, None),
        P("blk"),
        P("blk"),
        P(),
        P("blk", None, None),
        P("blk", None, None),
        P(),
    )
    return jax.shard_map(
        body,
        mesh=mesh,
        in_specs=placed,
        out_specs=(
            P(("blk", "patch"), None, None),
            P(("blk", "patch"), None, None),
            P(("blk", "patch"), None, None),
            P(("blk", "patch"), None),
        ),
        check_vma=False,
    )
```

time: 106 us -> 98.1 us (0.925)
  local copies, waits for them, and re-layouts: 24 us -> 10.5 us
  matrix products: 11.7 us -> 0 us
  waiting for transfers between devices: 5.8 us -> 17.5 us
  Pallas kernels: 38.2 us -> 43.4 us
    dot_general x4 -> x0, matrix products: 11.7 us -> none  [the longest x1 4.61 us: make_spectra(): jnp.einsum('xk,nky->nxy', left_imag, half_stack, preferred_element_type=j...]
    ppermute x6, waiting for transfers between devices: 0.02 us -> 9.28 us  [the longest x3 9.27 us: correlate_all(): lax.ppermute(templ_im, 'blk', pairs)]
    pallas_call x4 -> x5, Pallas kernels: 38.2 us -> 43.4 us  [the longest x4 38.3 us: correlate_chunk(): pl.pallas_call(functools.partial(corr_kernel, first, last, tiles, orient_...]
    div x0 -> x1, other arithmetic: none -> 4.38 us  [body(): scale = ctf_filter(focus_values, extent) / extent]
    unnamed x29 -> x26, local copies, waits for them, and re-layouts: 6.33 us -> 2.31 us
    sub x1 -> x0, other arithmetic: 3.1 us -> none  [correlate_all(): var_map = squares / orient_total - mean_map * mean_map]
    scatter x4 -> x0, local copies, waits for them, and re-layouts: 2.53 us -> none  [correlate_all(): peak_rows = peak_rows.at[:, columns].set(peak)]
    slice x4 -> x1, local copies, waits for them, and re-layouts: 3.83 us -> 1.3 us  [correlate_all(): return (top_map, mean_map, var_map, peak[:, 0, :orient_total])]
  transfers between devices with their start and end apart: 11 -> 11, of which waited for: 1 -> 2; matrix products, arithmetic and copies ran while one was open for 37% -> 20% of each run, Pallas kernels for 27% -> 35%
where the time goes in v4:
time: 98.1 us; the launch traced here: 97.5 us
  Pallas kernels  43.4 us (44%)
  waiting for transfers between devices  17.5 us (18%)
  starting transfers between devices  12.8 us (13%)
  other arithmetic  12.2 us (12%)
  local copies, waits for them, and re-layouts  10.5 us (11%)
  between operations  1.02 us (1%)
    pallas_call x4, Pallas kernels, correlate_chunk(): pl.pallas_call(functools.partial(corr_kernel, first, last, tiles, orient_...  38.3 us
    ppermute x3, waiting for transfers between devices, correlate_all(): lax.ppermute(templ_im, 'blk', pairs)  9.27 us
    ppermute x3, waiting for transfers between devices, route_patches(): lax.ppermute(outgoing[m], 'patch', xor_pairs(sources, 2 * m))  8.24 us
    pallas_call x1, Pallas kernels, make_spectra(): pl.pallas_call(functools.partial(spectra_kernel, rows), grid=(count,), in...  5.13 us
    div x1, other arithmetic, body(): scale = ctf_filter(focus_values, extent) / extent  4.38 us
    ppermute x3, starting transfers between devices, correlate_all(): lax.ppermute(templ_re, 'blk', pairs)  3.79 us
    ppermute x3, starting transfers between devices, route_patches(): lax.ppermute(outgoing[m], 'patch', xor_pairs(sources, 2 * m))  2.71 us
    gather x4, local copies, waits for them, and re-layouts, correlate_all(): orient_chunk = jnp.take(orientation, source * tiles + within)  2.56 us
  transfers between devices with their start and end apart: 11, of which 2 were waited for; matrix products, arithmetic and copies ran while one was open for 20% of the time, Pallas kernels for 35%

profile of v4, /device:TPU:9, one launch (start us, length us, event | category | flops | bytes accessed | tf_op | source)
XLA Modules:
  0.0 97.5 jit_solution(9635672132563674736)
XLA Ops:
  0.6 1.3 %collective-permute-start.9 = (bf16[4,256,256]{2,1,0:T(8,128)(2,1)}, bf16[4,256,256]{2,1,0:T(8,128)(2,1)}, u32[]{:S(2)}, u32[]{:S(2)}) collective-permute-start(bf16[4,256,256]{2,1,0:T(8,128)(2,1)} %refs_3_.1), channel_id=1, source_target_pairs={{0,8},{8,0},{16,24},{24,16},{1,9},{9,1},{17,25},{25,17},{2,10},{10... | collective-permute-start | bytes 1572872 | tf_op jit(solution)/shard_map/ppermute | solution.py:225
  1.9 1.2 %collective-permute-start.7 = (bf16[4,256,256]{2,1,0:T(8,128)(2,1)}, bf16[4,256,256]{2,1,0:T(8,128)(2,1)}, u32[]{:S(2)}, u32[]{:S(2)}) collective-permute-start(bf16[4,256,256]{2,1,0:T(8,128)(2,1)} %refs_3_.1), channel_id=1, source_target_pairs={{0,16},{8,24},{16,0},{24,8},{1,17},{9,25},{17,1},{25,9},{2,18},{10... | collective-permute-start | bytes 1572872 | tf_op jit(solution)/shard_map/ppermute | solution.py:225
  3.2 0.7 copy-done.5
  4.5 0.1 copy.44
  4.9 1.0 %concatenate.25 = bf16[3,256,256]{2,1,0:T(8,128)(2,1)S(1)} pad(bf16[2,256,256]{2,1,0:T(8,128)(2,1)} %own_ref.1, bf16[]{:T(256)} %constant.173.clone.1), padding=0_1x0_0x0_0 | pad | bytes 655362 | tf_op jit(solution)/shard_map/concatenate | solution.py:55
  5.8 0.6 gather_fusion
  6.5 0.2 broadcast_select_fusion
  6.7 0.2 collective-permute-start.1
  7.0 2.3 %collective-permute-start.2 = (bf16[2,256,256]{2,1,0:T(8,128)(2,1)S(1)}, bf16[2,256,256]{2,1,0:T(8,128)(2,1)S(1)}, u32[]{:S(2)}, u32[]{:S(2)}) collective-permute-start(bf16[2,256,256]{2,1,0:T(8,128)(2,1)S(1)} %get-tuple-element.49), channel_id=1, source_target_pairs={{0,4},{1,5},{2,6},{3,7},{4,0},{5,1},{6,2},{7,3},{8,12},{9,13},{10,... | collective-permute-start | bytes 786440 | tf_op jit(solution)/shard_map/ppermute | solution.py:63
  9.3 0.2 collective-permute-start.3
  9.6 0.1 reduce
  9.7 0.1 fusion.11
  9.8 0.1 select_reduce_fusion.1
  10.0 1.1 %sine_convert_fusion = (bf16[256,256]{1,0:T(8,128)(2,1)S(1)}, bf16[256,256]{1,0:T(8,128)(2,1)S(1)}) fusion(), kind=kLoop, calls=%fused_computation.17 | loop fusion | flops 1048576 | bytes 262144 | tf_op jit(solution)/shard_map/convert_element_type | solution.py:23
  11.1 1.0 %fusion.6 = bf16[256,256]{1,0:T(8,128)(2,1)S(1)} fusion(), kind=kLoop, calls=%fused_computation.24 | loop fusion | flops 1179648 | bytes 131072 | tf_op jit(solution)/shard_map/neg | solution.py:249
  12.1 0.6 copy-done.11
  12.9 0.6 gather_fusion.1
  13.5 0.6 gather_fusion.2
  14.4 0.4 fusion.18
  14.9 0.2 select_reduce_fusion
  15.1 0.6 broadcast_select_fusion.2.take_ref
  15.7 0.6 gather_fusion.6
  16.3 0.6 and_select_fusion.refs_0_
  16.9 0.6 gather_fusion.5
  17.6 0.6 and_select_fusion.1.refs_0_
  18.1 0.8 broadcast_multiply_fusion
  19.0 0.8 maximum_maximum_fusion.full_ref.refs_5_
  19.8 0.6 gather_fusion.4
  20.5 2.1 %collective-permute-start = (bf16[2,256,256]{2,1,0:T(8,128)(2,1)S(1)}, bf16[2,256,256]{2,1,0:T(8,128)(2,1)S(1)}, u32[]{:S(2)}, u32[]{:S(2)}) collective-permute-start(bf16[2,256,256]{2,1,0:T(8,128)(2,1)S(1)} %get-tuple-element.51), channel_id=1, source_target_pairs={{0,1},{1,0},{2,3},{3,2},{4,5},{5,4},{6,7},{7,6},{8,9},{9,8},{10,11... | collective-permute-start | bytes 786440 | tf_op jit(solution)/shard_map/ppermute | solution.py:60
  22.6 0.3 collective-permute-start.10
  23.0 8.2 %collective-permute-done.3 = bf16[2,256,256]{2,1,0:T(8,128)(2,1)S(1)} collective-permute-done((bf16[2,256,256]{2,1,0:T(8,128)(2,1)S(1)}, bf16[2,256,256]{2,1,0:T(8,128)(2,1)S(1)}, u32[]{:S(2)}, u32[]{:S(2)}) %collective-permute-start.3) | collective-permute-done | bytes 262176 | tf_op jit(solution)/shard_map/ppermute | solution.py:63
  31.2 2.5 %collective-permute-start.4 = (bf16[6,256,256]{2,1,0:T(8,128)(2,1)S(1)}, bf16[6,256,256]{2,1,0:T(8,128)(2,1)S(1)}, u32[]{:S(2)}, u32[]{:S(2)}) collective-permute-start(bf16[6,256,256]{2,1,0:T(8,128)(2,1)S(1)} %constant_dynamic-update-slice_fusion.recv_ref), channel_id=1, source_target_pairs={{0,1},{1,0},{2,3},{3,2},{4,5},{5,4},{6,7},{7,6},{8,9},{9,8},{10,11... | collective-permute-start | bytes 2359304 | tf_op jit(solution)/shard_map/ppermute | solution.py:65
  33.7 0.5 and_select_fusion.2.refs_0_
  34.2 4.4 %negate_multiply_fusion.scale_ref = f32[4,256,256]{2,1,0:T(8,128)} fusion(f32[256,256]{1,0:T(8,128)S(1)} %broadcast_add_fusion, f32[4]{0:T(128)S(1)} %fusion.24), kind=kLoop, calls=%fused_computation.7 | loop fusion | flops 1048576 | bytes 1310736 | tf_op jit(solution)/shard_map/div | solution.py:245
  38.6 0.6 gather_fusion.3
  39.3 0.5 and_select_fusion.3.refs_0_
  39.8 0.2 collective-permute-start.8
  40.0 1.3 %collective-permute-start.5 = (bf16[4,256,256]{2,1,0:T(8,128)(2,1)S(1)}, bf16[4,256,256]{2,1,0:T(8,128)(2,1)S(1)}, u32[]{:S(2)}, u32[]{:S(2)}) collective-permute-start(bf16[4,256,256]{2,1,0:T(8,128)(2,1)S(1)} %copy-done.6), channel_id=1, source_target_pairs={{0,24},{8,16},{16,8},{24,0},{1,25},{9,17},{17,9},{25,1},{2,26},{10... | collective-permute-start | bytes 1572872 | tf_op jit(solution)/shard_map/ppermute | solution.py:225
  41.3 5.1 %shard_map.102 = (bf16[4,256,256]{2,1,0:T(8,128)(2,1)}, bf16[4,256,256]{2,1,0:T(8,128)(2,1)}) custom-call(s32[4]{0:T(128)} %broadcast_select_fusion.2.take_ref, bf16[2,256,256]{2,1,0:T(8,128)(2,1)} %own_ref.1, bf16[2,256,256]{2,1,0:T(8,128)(2,1)} %copy-done.4, bf16[6,256,256]{2,1,0:T(8,128)(2,1)} %copy-done.2, bf16[6,256,256]{2,1,0:T(8,128)(2,1)} %copy-done.3, ...), custom_call_target="tpu_custom_call" | custom-call | flops 402653184 | bytes 2621440 | tf_op jit(solution)/shard_map/pallas_call | solution.py:119
  46.4 9.2 %shard_map.103 = (f32[4,256,256]{2,1,0:T(8,128)}, f32[4,256,256]{2,1,0:T(8,128)}, f32[4,256,256]{2,1,0:T(8,128)}, f32[4,8,128]{2,1,0:T(8,128)}) custom-call(s32[4]{0:T(128)} %and_select_fusion.refs_0_, bf16[4,256,256]{2,1,0:T(8,128)(2,1)} %get-tuple-element.23.refs_1_, bf16[4,256,256]{2,1,0:T(8,128)(2,1)} %get-tuple-element.24.refs_2_, ...), custom_call_target="tpu_custom_call" | custom-call | flops 3221225472 | bytes 12582912 | tf_op jit(solution)/shard_map/pallas_call | solution.py:201
  55.7 1.2 %collective-permute-start.6 = (bf16[4,256,256]{2,1,0:T(8,128)(2,1)S(1)}, bf16[4,256,256]{2,1,0:T(8,128)(2,1)S(1)}, u32[]{:S(2)}, u32[]{:S(2)}) collective-permute-start(bf16[4,256,256]{2,1,0:T(8,128)(2,1)S(1)} %copy-done.8), channel_id=1, source_target_pairs={{0,24},{8,16},{16,8},{24,0},{1,25},{9,17},{17,9},{25,1},{2,26},{10... | collective-permute-start | bytes 1572872 | tf_op jit(solution)/shard_map/ppermute | solution.py:226
  56.9 9.7 %shard_map.104 = (f32[4,256,256]{2,1,0:T(8,128)}, f32[4,256,256]{2,1,0:T(8,128)}, f32[4,256,256]{2,1,0:T(8,128)}, f32[4,8,128]{2,1,0:T(8,128)}) custom-call(s32[4]{0:T(128)} %and_select_fusion.1.refs_0_, bf16[4,256,256]{2,1,0:T(8,128)(2,1)} %get-tuple-element.23.refs_1_, ...), custom_call_target="tpu_custom_call", output_to_operand_aliasing={{0}: (7, {}), {1}: (8, {}), {2}: (9, {}), {3}: (10, {})} | custom-call | flops 3221225472 | bytes 12582912 | tf_op jit(solution)/shard_map/pallas_call | solution.py:201
  66.6 9.3 %collective-permute-done.8.refs_4_ = bf16[4,256,256]{2,1,0:T(8,128)(2,1)} collective-permute-done((bf16[4,256,256]{2,1,0:T(8,128)(2,1)S(1)}, bf16[4,256,256]{2,1,0:T(8,128)(2,1)}, u32[]{:S(2)}, u32[]{:S(2)}) %collective-permute-start.8) | collective-permute-done | bytes 524320 | tf_op jit(solution)/shard_map/ppermute | solution.py:226
  75.8 9.7 %shard_map.105 = (f32[4,256,256]{2,1,0:T(8,128)}, f32[4,256,256]{2,1,0:T(8,128)}, f32[4,256,256]{2,1,0:T(8,128)}, f32[4,8,128]{2,1,0:T(8,128)}) custom-call(s32[4]{0:T(128)} %and_select_fusion.2.refs_0_, bf16[4,256,256]{2,1,0:T(8,128)(2,1)} %get-tuple-element.23.refs_1_, ...), custom_call_target="tpu_custom_call", output_to_operand_aliasing={{0}: (7, {}), {1}: (8, {}), {2}: (9, {}), {3}: (10, {})} | custom-call | flops 3221225472 | bytes 12582912 | tf_op jit(solution)/shard_map/pallas_call | solution.py:201
  85.5 0.8 copy-done.9
  86.3 0.2 copy-done.10
  86.5 9.8 %shard_map.106 = (f32[4,256,256]{2,1,0:T(8,128)}, f32[4,256,256]{2,1,0:T(8,128)}, f32[4,256,256]{2,1,0:T(8,128)}, f32[4,8,128]{2,1,0:T(8,128)}) custom-call(s32[4]{0:T(128)} %and_select_fusion.3.refs_0_, bf16[4,256,256]{2,1,0:T(8,128)(2,1)} %get-tuple-element.23.refs_1_, ...), custom_call_target="tpu_custom_call", output_to_operand_aliasing={{0}: (7, {}), {1}: (8, {}), {2}: (9, {}), {3}: (10, {})} | custom-call | flops 3221225472 | bytes 12582912 | tf_op jit(solution)/shard_map/pallas_call | solution.py:201
  96.2 1.3 %slice.68 = f32[4,1,16]{2,1,0:T(1,128)} slice(f32[4,8,128]{2,1,0:T(8,128)} %get-tuple-element.40), slice={[0:4], [0:1], [0:16]} | slice | bytes 512 | tf_op jit(solution)/shard_map/slice | solution.py:233
  (71 shorter events, 1.6 us)
Async XLA Ops:
  0.6 15.0 %copy-start = (s32[16]{0:T(128)S(1)}, s32[16]{0:T(128)}, u32[]{:S(2)}) copy-start(s32[16]{0:T(128)} %param.15) | copy-start | bytes 196
  0.6 56.3 %collective-permute-start.9 = (bf16[4,256,256]{2,1,0:T(8,128)(2,1)}, bf16[4,256,256]{2,1,0:T(8,128)(2,1)}, u32[]{:S(2)}, u32[]{:S(2)}) collective-permute-start(bf16[4,256,256]{2,1,0:T(8,128)(2,1)} %refs_3_.1), channel_id=1, source_target_pairs={{0,8},{8,0},{16,24},{24,16},{1,9},{9,1},{17,25},{25,17},{2,10},{10... | collective-permute-start | bytes 1572872 | tf_op jit(solution)/shard_map/ppermute | solution.py:225
  1.9 64.7 %collective-permute-start.7 = (bf16[4,256,256]{2,1,0:T(8,128)(2,1)}, bf16[4,256,256]{2,1,0:T(8,128)(2,1)}, u32[]{:S(2)}, u32[]{:S(2)}) collective-permute-start(bf16[4,256,256]{2,1,0:T(8,128)(2,1)} %refs_3_.1), channel_id=1, source_target_pairs={{0,16},{8,24},{16,0},{24,8},{1,17},{9,25},{17,1},{25,9},{2,18},{10... | collective-permute-start | bytes 1572872 | tf_op jit(solution)/shard_map/ppermute | solution.py:225
  3.2 0.7 copy-start.5
  6.7 13.7 %collective-permute-start.1 = (bf16[2,256,256]{2,1,0:T(8,128)(2,1)S(1)}, bf16[2,256,256]{2,1,0:T(8,128)(2,1)S(1)}, u32[]{:S(2)}, u32[]{:S(2)}) collective-permute-start(bf16[2,256,256]{2,1,0:T(8,128)(2,1)S(1)} %get-tuple-element.50), channel_id=1, source_target_pairs={{0,2},{1,3},{2,0},{3,1},{4,6},{5,7},{6,4},{7,5},{8,10},{9,11},{10,... | collective-permute-start | bytes 786440 | tf_op jit(solution)/shard_map/ppermute | solution.py:63
  7.0 15.7 %collective-permute-start.2 = (bf16[2,256,256]{2,1,0:T(8,128)(2,1)S(1)}, bf16[2,256,256]{2,1,0:T(8,128)(2,1)S(1)}, u32[]{:S(2)}, u32[]{:S(2)}) collective-permute-start(bf16[2,256,256]{2,1,0:T(8,128)(2,1)S(1)} %get-tuple-element.49), channel_id=1, source_target_pairs={{0,4},{1,5},{2,6},{3,7},{4,0},{5,1},{6,2},{7,3},{8,12},{9,13},{10,... | collective-permute-start | bytes 786440 | tf_op jit(solution)/shard_map/ppermute | solution.py:63
  9.3 21.9 %collective-permute-start.3 = (bf16[2,256,256]{2,1,0:T(8,128)(2,1)S(1)}, bf16[2,256,256]{2,1,0:T(8,128)(2,1)S(1)}, u32[]{:S(2)}, u32[]{:S(2)}) collective-permute-start(bf16[2,256,256]{2,1,0:T(8,128)(2,1)S(1)} %get-tuple-element.48), channel_id=1, source_target_pairs={{0,6},{1,7},{2,4},{3,5},{4,2},{5,3},{6,0},{7,1},{8,14},{9,15},{10,... | collective-permute-start | bytes 786440 | tf_op jit(solution)/shard_map/ppermute | solution.py:63
  12.1 0.7 copy-start.11
  12.9 0.7 copy-start.1
  19.8 2.8 %copy-start.7 = (bf16[4,256,256]{2,1,0:T(8,128)(2,1)S(1)}, bf16[4,256,256]{2,1,0:T(8,128)(2,1)}, u32[]{:S(2)}) copy-start(bf16[4,256,256]{2,1,0:T(8,128)(2,1)} %refs_4_.1) | copy-start | bytes 1572868
  20.5 19.3 %collective-permute-start = (bf16[2,256,256]{2,1,0:T(8,128)(2,1)S(1)}, bf16[2,256,256]{2,1,0:T(8,128)(2,1)S(1)}, u32[]{:S(2)}, u32[]{:S(2)}) collective-permute-start(bf16[2,256,256]{2,1,0:T(8,128)(2,1)S(1)} %get-tuple-element.51), channel_id=1, source_target_pairs={{0,1},{1,0},{2,3},{3,2},{4,5},{5,4},{6,7},{7,6},{8,9},{9,8},{10,11... | collective-permute-start | bytes 786440 | tf_op jit(solution)/shard_map/ppermute | solution.py:60
  22.6 33.1 %collective-permute-start.10 = (bf16[4,256,256]{2,1,0:T(8,128)(2,1)S(1)}, bf16[4,256,256]{2,1,0:T(8,128)(2,1)}, u32[]{:S(2)}, u32[]{:S(2)}) collective-permute-start(bf16[4,256,256]{2,1,0:T(8,128)(2,1)S(1)} %copy-done.7), channel_id=1, source_target_pairs={{0,8},{8,0},{16,24},{24,16},{1,9},{9,1},{17,25},{25,17},{2,10},{10... | collective-permute-start | bytes 1572872 | tf_op jit(solution)/shard_map/ppermute | solution.py:226
  31.2 8.0 %copy-start.2 = (bf16[6,256,256]{2,1,0:T(8,128)(2,1)}, bf16[6,256,256]{2,1,0:T(8,128)(2,1)S(1)}, u32[]{:S(2)}) copy-start(bf16[6,256,256]{2,1,0:T(8,128)(2,1)S(1)} %constant_dynamic-update-slice_fusion.recv_ref) | copy-start | bytes 2359300
  31.2 8.8 %collective-permute-start.4 = (bf16[6,256,256]{2,1,0:T(8,128)(2,1)S(1)}, bf16[6,256,256]{2,1,0:T(8,128)(2,1)S(1)}, u32[]{:S(2)}, u32[]{:S(2)}) collective-permute-start(bf16[6,256,256]{2,1,0:T(8,128)(2,1)S(1)} %constant_dynamic-update-slice_fusion.recv_ref), channel_id=1, source_target_pairs={{0,1},{1,0},{2,3},{3,2},{4,5},{5,4},{6,7},{7,6},{8,9},{9,8},{10,11... | collective-permute-start | bytes 2359304 | tf_op jit(solution)/shard_map/ppermute | solution.py:65
  38.6 1.4 %copy-start.6 = (bf16[4,256,256]{2,1,0:T(8,128)(2,1)S(1)}, bf16[4,256,256]{2,1,0:T(8,128)(2,1)}, u32[]{:S(2)}) copy-start(bf16[4,256,256]{2,1,0:T(8,128)(2,1)} %refs_3_.1) | copy-start | bytes 1572868
  39.8 1.5 %copy-start.4 = (bf16[2,256,256]{2,1,0:T(8,128)(2,1)}, bf16[2,256,256]{2,1,0:T(8,128)(2,1)S(1)}, u32[]{:S(2)}) copy-start(bf16[2,256,256]{2,1,0:T(8,128)(2,1)S(1)} %collective-permute-done.direct_ref) | copy-start | bytes 786436
  39.8 36.1 %collective-permute-start.8 = (bf16[4,256,256]{2,1,0:T(8,128)(2,1)S(1)}, bf16[4,256,256]{2,1,0:T(8,128)(2,1)}, u32[]{:S(2)}, u32[]{:S(2)}) collective-permute-start(bf16[4,256,256]{2,1,0:T(8,128)(2,1)S(1)} %copy-done.7), channel_id=1, source_target_pairs={{0,16},{8,24},{16,0},{24,8},{1,17},{9,25},{17,1},{25,9},{2,18},{10... | collective-permute-start | bytes 1572872 | tf_op jit(solution)/shard_map/ppermute | solution.py:226
  40.0 1.3 %copy-start.3 = (bf16[6,256,256]{2,1,0:T(8,128)(2,1)}, bf16[6,256,256]{2,1,0:T(8,128)(2,1)S(1)}, u32[]{:S(2)}) copy-start(bf16[6,256,256]{2,1,0:T(8,128)(2,1)S(1)} %collective-permute-done.4.fwd_ref) | copy-start | bytes 2359300
  40.0 45.5 %collective-permute-start.5 = (bf16[4,256,256]{2,1,0:T(8,128)(2,1)S(1)}, bf16[4,256,256]{2,1,0:T(8,128)(2,1)S(1)}, u32[]{:S(2)}, u32[]{:S(2)}) collective-permute-start(bf16[4,256,256]{2,1,0:T(8,128)(2,1)S(1)} %copy-done.6), channel_id=1, source_target_pairs={{0,24},{8,16},{16,8},{24,0},{1,25},{9,17},{17,9},{25,1},{2,26},{10... | collective-permute-start | bytes 1572872 | tf_op jit(solution)/shard_map/ppermute | solution.py:225
  46.4 9.2 %copy-start.8 = (bf16[4,256,256]{2,1,0:T(8,128)(2,1)S(1)}, bf16[4,256,256]{2,1,0:T(8,128)(2,1)}, u32[]{:S(2)}) copy-start(bf16[4,256,256]{2,1,0:T(8,128)(2,1)} %refs_4_.1) | copy-start | bytes 1572868
  55.7 29.8 %collective-permute-start.6 = (bf16[4,256,256]{2,1,0:T(8,128)(2,1)S(1)}, bf16[4,256,256]{2,1,0:T(8,128)(2,1)S(1)}, u32[]{:S(2)}, u32[]{:S(2)}) collective-permute-start(bf16[4,256,256]{2,1,0:T(8,128)(2,1)S(1)} %copy-done.8), channel_id=1, source_target_pairs={{0,24},{8,16},{16,8},{24,0},{1,25},{9,17},{17,9},{25,1},{2,26},{10... | collective-permute-start | bytes 1572872 | tf_op jit(solution)/shard_map/ppermute | solution.py:226
  85.5 0.8 copy-start.9
  85.5 0.9 copy-start.10

commit v5 on v4

--- a/solution.py
+++ b/solution.py
@@ -31,6 +31,21 @@
     radius = signed[:, None] * signed[:, None] + signed[None, :] * signed[None, :]
     phases = math.pi * defocus_values[:, None, None] * radius[None, :, :] - AMPLITUDE
     return -jnp.sin(phases)
+
+
+def ctf_scale(defocus_values, extent):
+    indices = jnp.arange(extent, dtype=jnp.int32)
+    signed = (
+        jnp.where(indices < extent // 2, indices, indices - extent).astype(jnp.float32) / extent
+    )
+    square = signed * signed
+    turn = math.pi * defocus_values[:, None]
+    row_phase = turn * square[None, :] - AMPLITUDE
+    col_phase = turn * square[None, :]
+    row_sin, row_cos = jnp.sin(row_phase), jnp.cos(row_phase)
+    col_sin, col_cos = jnp.sin(col_phase), jnp.cos(col_phase)
+    ctf = -(row_sin[:, :, None] * col_cos[:, None, :] + row_cos[:, :, None] * col_sin[:, None, :])
+    return ctf / extent
 
 
 def xor_pairs(count, shift):
@@ -126,7 +141,7 @@
         out_shape=[spec_shape, spec_shape],
         compiler_params=pltpu.CompilerParams(dimension_semantics=("arbitrary",)),
         cost_estimate=pl.CostEstimate(
-            flops=count * 6 * extent * extent * extent, transcendentals=0,
+            flops=3 * count * 6 * extent * extent * extent, transcendentals=0,
             bytes_accessed=count * 10 * extent * extent),
     )(take_idx, own, direct, received, forwarded, scale, half_table, full_table)
 
@@ -197,7 +212,7 @@
         operands += list(stats)
         aliases = {7: 0, 8: 1, 9: 2, 10: 3}
     map_shape = jax.ShapeDtypeStruct((count, extent, extent), jnp.float32)
-    flops = tiles * count * 12 * extent * extent * extent
+    flops = 3 * tiles * count * 12 * extent * extent * extent
     return pl.pallas_call(
         functools.partial(corr_kernel, first, last, tiles, orient_total),
         grid=(count,),
@@ -242,7 +257,7 @@
     take_idx, pieces, slot_row = route_patches(patches, row_owner, my_index)
     groups = jnp.take(jnp.concatenate([group_of_patch, jnp.zeros((1,), jnp.int32)]), slot_row)
     focus_values = jnp.take(defocus, groups)
-    scale = ctf_filter(focus_values, extent) / extent
+    scale = ctf_scale(focus_values, extent)
     forward = jnp.concatenate(
         [jnp.concatenate([cosine, sine], axis=1), jnp.concatenate([-sine, cosine], axis=1)], axis=0
     )

time: 98.1 us -> 95.1 us (0.969)
  other arithmetic: 12.2 us -> 9.11 us
    div x1, other arithmetic: 4.38 us -> 1.31 us  [ctf_scale(): return ctf / extent]
    unnamed x26 -> x22, local copies, waits for them, and re-layouts: 2.31 us -> 2.3 us
  transfers between devices with their start and end apart: 11 -> 11, of which waited for: 2 -> 2; matrix products, arithmetic and copies ran while one was open for 20% -> 17% of each run, Pallas kernels for 35% -> 36%
where the time goes in v5:
time: 95.1 us; the launch traced here: 94.5 us
  Pallas kernels  43.4 us (46%)
  waiting for transfers between devices  17.6 us (19%)
  starting transfers between devices  12.9 us (14%)
  local copies, waits for them, and re-layouts  10.5 us (11%)
  other arithmetic  9.11 us (10%)
  between operations  0.99 us (1%)
    pallas_call x4, Pallas kernels, correlate_chunk(): pl.pallas_call(functools.partial(corr_kernel, first, last, tiles, orient_...  38.3 us
    ppermute x3, waiting for transfers between devices, correlate_all(): lax.ppermute(templ_im, 'blk', pairs)  9.52 us
    ppermute x3, waiting for transfers between devices, route_patches(): lax.ppermute(outgoing[m], 'patch', xor_pairs(sources, 2 * m))  8.07 us
    pallas_call x1, Pallas kernels, make_spectra(): pl.pallas_call(functools.partial(spectra_kernel, rows), grid=(count,), in...  5.13 us
    ppermute x3, starting transfers between devices, correlate_all(): lax.ppermute(templ_re, 'blk', pairs)  3.79 us
    ppermute x3, starting transfers between devices, route_patches(): lax.ppermute(outgoing[m], 'patch', xor_pairs(sources, 2 * m))  2.71 us
    gather x4, local copies, waits for them, and re-layouts, correlate_all(): orient_chunk = jnp.take(orientation, source * tiles + within)  2.55 us
    ppermute x1, starting transfers between devices, route_patches(): forwarded = lax.ppermute(received, 'patch', xor_pairs(sources, 1))  2.46 us
  transfers between devices with their start and end apart: 11, of which 2 were waited for; matrix products, arithmetic and copies ran while one was open for 17% of the time, Pallas kernels for 36%

profile of v5, /device:TPU:9, one launch (start us, length us, event | category | flops | bytes accessed | tf_op | source)
XLA Modules:
  0.0 94.5 jit_solution(2199363652717423137)
XLA Ops:
  0.6 1.3 %collective-permute-start.9 = (bf16[4,256,256]{2,1,0:T(8,128)(2,1)}, bf16[4,256,256]{2,1,0:T(8,128)(2,1)}, u32[]{:S(2)}, u32[]{:S(2)}) collective-permute-start(bf16[4,256,256]{2,1,0:T(8,128)(2,1)} %refs_3_.1), channel_id=1, source_target_pairs={{0,8},{8,0},{16,24},{24,16},{1,9},{9,1},{17,25},{25,17},{2,10},{10... | collective-permute-start | bytes 1572872 | tf_op jit(solution)/shard_map/ppermute | solution.py:240
  1.9 1.2 %collective-permute-start.7 = (bf16[4,256,256]{2,1,0:T(8,128)(2,1)}, bf16[4,256,256]{2,1,0:T(8,128)(2,1)}, u32[]{:S(2)}, u32[]{:S(2)}) collective-permute-start(bf16[4,256,256]{2,1,0:T(8,128)(2,1)} %refs_3_.1), channel_id=1, source_target_pairs={{0,16},{8,24},{16,0},{24,8},{1,17},{9,25},{17,1},{25,9},{2,18},{10... | collective-permute-start | bytes 1572872 | tf_op jit(solution)/shard_map/ppermute | solution.py:240
  3.2 0.7 copy-done.3
  4.9 1.0 %concatenate.25 = bf16[3,256,256]{2,1,0:T(8,128)(2,1)S(1)} pad(bf16[2,256,256]{2,1,0:T(8,128)(2,1)} %own_ref.1, bf16[]{:T(256)} %constant.173.clone.1), padding=0_1x0_0x0_0 | pad | bytes 655362 | tf_op jit(solution)/shard_map/concatenate | solution.py:70
  5.8 0.6 gather_fusion
  6.5 0.2 broadcast_select_fusion
  6.7 0.2 collective-permute-start.1
  7.0 2.3 %collective-permute-start.2 = (bf16[2,256,256]{2,1,0:T(8,128)(2,1)S(1)}, bf16[2,256,256]{2,1,0:T(8,128)(2,1)S(1)}, u32[]{:S(2)}, u32[]{:S(2)}) collective-permute-start(bf16[2,256,256]{2,1,0:T(8,128)(2,1)S(1)} %get-tuple-element.49), channel_id=1, source_target_pairs={{0,4},{1,5},{2,6},{3,7},{4,0},{5,1},{6,2},{7,3},{8,12},{9,13},{10,... | collective-permute-start | bytes 786440 | tf_op jit(solution)/shard_map/ppermute | solution.py:78
  9.3 0.2 collective-permute-start.3
  9.6 0.1 reduce
  9.7 0.1 fusion.13
  9.8 0.1 select_reduce_fusion.1
  10.0 1.1 %sine_convert_fusion = (bf16[256,256]{1,0:T(8,128)(2,1)S(1)}, bf16[256,256]{1,0:T(8,128)(2,1)S(1)}) fusion(), kind=kLoop, calls=%fused_computation.17 | loop fusion | flops 1048576 | bytes 262144 | tf_op jit(solution)/shard_map/convert_element_type | solution.py:23
  11.1 1.0 %fusion.6 = bf16[256,256]{1,0:T(8,128)(2,1)S(1)} fusion(), kind=kLoop, calls=%fused_computation.23 | loop fusion | flops 1179648 | bytes 131072 | tf_op jit(solution)/shard_map/neg | solution.py:264
  12.1 0.6 copy-done.9
  12.9 0.6 gather_fusion.1
  13.5 0.6 gather_fusion.2
  14.2 0.4 fusion.20
  14.8 0.2 select_reduce_fusion
  14.9 0.6 broadcast_select_fusion.2.take_ref
  15.6 0.6 gather_fusion.6
  16.2 0.6 and_select_fusion.refs_0_
  16.8 0.6 gather_fusion.5
  17.4 0.5 and_select_fusion.1.refs_0_
  18.0 0.6 gather_fusion.4
  18.6 0.5 and_select_fusion.2.refs_0_
  19.2 0.8 broadcast_multiply_fusion
  20.0 0.6 gather_fusion.3
  20.6 2.1 %collective-permute-start = (bf16[2,256,256]{2,1,0:T(8,128)(2,1)S(1)}, bf16[2,256,256]{2,1,0:T(8,128)(2,1)S(1)}, u32[]{:S(2)}, u32[]{:S(2)}) collective-permute-start(bf16[2,256,256]{2,1,0:T(8,128)(2,1)S(1)} %get-tuple-element.51), channel_id=1, source_target_pairs={{0,1},{1,0},{2,3},{3,2},{4,5},{5,4},{6,7},{7,6},{8,9},{9,8},{10,11... | collective-permute-start | bytes 786440 | tf_op jit(solution)/shard_map/ppermute | solution.py:75
  22.8 0.3 collective-permute-start.10
  23.1 8.1 %collective-permute-done.3 = bf16[2,256,256]{2,1,0:T(8,128)(2,1)S(1)} collective-permute-done((bf16[2,256,256]{2,1,0:T(8,128)(2,1)S(1)}, bf16[2,256,256]{2,1,0:T(8,128)(2,1)S(1)}, u32[]{:S(2)}, u32[]{:S(2)}) %collective-permute-start.3) | collective-permute-done | bytes 262176 | tf_op jit(solution)/shard_map/ppermute | solution.py:78
  31.2 2.5 %collective-permute-start.4 = (bf16[6,256,256]{2,1,0:T(8,128)(2,1)S(1)}, bf16[6,256,256]{2,1,0:T(8,128)(2,1)S(1)}, u32[]{:S(2)}, u32[]{:S(2)}) collective-permute-start(bf16[6,256,256]{2,1,0:T(8,128)(2,1)S(1)} %constant_dynamic-update-slice_fusion.recv_ref), channel_id=1, source_target_pairs={{0,1},{1,0},{2,3},{3,2},{4,5},{5,4},{6,7},{7,6},{8,9},{9,8},{10,11... | collective-permute-start | bytes 2359304 | tf_op jit(solution)/shard_map/ppermute | solution.py:80
  33.7 0.5 and_select_fusion.3.refs_0_
  34.2 0.1 fusion.8
  34.3 0.8 maximum_maximum_fusion.full_ref.refs_5_
  35.2 1.3 %negate_multiply_fusion.scale_ref = f32[4,256,256]{2,1,0:T(8,128)} fusion(f32[4,256]{1,0:T(4,128)S(1)} %get-tuple-element.59, f32[4,256]{1,0:T(4,128)S(1)} %get-tuple-element.61, f32[4,256]{1,0:T(4,128)S(1)} %get-tuple-element.60, f32[4,256]{1,0:T(4,128)S(1)} %get-tuple-element.58), kind=kLoop, calls=%fused_computation.7 | loop fusion | flops 1310720 | bytes 1064960 | tf_op jit(solution)/shard_map/div | solution.py:48
  36.5 0.3 collective-permute-start.8
  36.8 1.3 %collective-permute-start.5 = (bf16[4,256,256]{2,1,0:T(8,128)(2,1)S(1)}, bf16[4,256,256]{2,1,0:T(8,128)(2,1)S(1)}, u32[]{:S(2)}, u32[]{:S(2)}) collective-permute-start(bf16[4,256,256]{2,1,0:T(8,128)(2,1)S(1)} %copy-done.5), channel_id=1, source_target_pairs={{0,24},{8,16},{16,8},{24,0},{1,25},{9,17},{17,9},{25,1},{2,26},{10... | collective-permute-start | bytes 1572872 | tf_op jit(solution)/shard_map/ppermute | solution.py:240
  38.1 5.1 %shard_map.102 = (bf16[4,256,256]{2,1,0:T(8,128)(2,1)}, bf16[4,256,256]{2,1,0:T(8,128)(2,1)}) custom-call(s32[4]{0:T(128)} %broadcast_select_fusion.2.take_ref, bf16[2,256,256]{2,1,0:T(8,128)(2,1)} %own_ref.1, bf16[2,256,256]{2,1,0:T(8,128)(2,1)} %copy-done.8, bf16[6,256,256]{2,1,0:T(8,128)(2,1)} %copy-done.2, bf16[6,256,256]{2,1,0:T(8,128)(2,1)} %copy-done.4, ...), custom_call_target="tpu_custom_call" | custom-call | flops 1207959552 | bytes 2621440 | tf_op jit(solution)/shard_map/pallas_call | solution.py:134
  43.2 9.2 %shard_map.103 = (f32[4,256,256]{2,1,0:T(8,128)}, f32[4,256,256]{2,1,0:T(8,128)}, f32[4,256,256]{2,1,0:T(8,128)}, f32[4,8,128]{2,1,0:T(8,128)}) custom-call(s32[4]{0:T(128)} %and_select_fusion.refs_0_, bf16[4,256,256]{2,1,0:T(8,128)(2,1)} %get-tuple-element.23.refs_1_, bf16[4,256,256]{2,1,0:T(8,128)(2,1)} %get-tuple-element.24.refs_2_, ...), custom_call_target="tpu_custom_call" | custom-call | flops 9663676416 | bytes 12582912 | tf_op jit(solution)/shard_map/pallas_call | solution.py:216
  52.4 1.2 %collective-permute-start.6 = (bf16[4,256,256]{2,1,0:T(8,128)(2,1)}, bf16[4,256,256]{2,1,0:T(8,128)(2,1)S(1)}, u32[]{:S(2)}, u32[]{:S(2)}) collective-permute-start(bf16[4,256,256]{2,1,0:T(8,128)(2,1)} %refs_4_.1), channel_id=1, source_target_pairs={{0,24},{8,16},{16,8},{24,0},{1,25},{9,17},{17,9},{25,1},{2,26},{10... | collective-permute-start | bytes 1572872 | tf_op jit(solution)/shard_map/ppermute | solution.py:241
  53.7 9.7 %shard_map.104 = (f32[4,256,256]{2,1,0:T(8,128)}, f32[4,256,256]{2,1,0:T(8,128)}, f32[4,256,256]{2,1,0:T(8,128)}, f32[4,8,128]{2,1,0:T(8,128)}) custom-call(s32[4]{0:T(128)} %and_select_fusion.1.refs_0_, bf16[4,256,256]{2,1,0:T(8,128)(2,1)} %get-tuple-element.23.refs_1_, ...), custom_call_target="tpu_custom_call", output_to_operand_aliasing={{0}: (7, {}), {1}: (8, {}), {2}: (9, {}), {3}: (10, {})} | custom-call | flops 9663676416 | bytes 12582912 | tf_op jit(solution)/shard_map/pallas_call | solution.py:216
  63.3 9.5 %collective-permute-done.8.refs_4_ = bf16[4,256,256]{2,1,0:T(8,128)(2,1)} collective-permute-done((bf16[4,256,256]{2,1,0:T(8,128)(2,1)}, bf16[4,256,256]{2,1,0:T(8,128)(2,1)}, u32[]{:S(2)}, u32[]{:S(2)}) %collective-permute-start.8) | collective-permute-done | bytes 524320 | tf_op jit(solution)/shard_map/ppermute | solution.py:241
  72.8 9.7 %shard_map.105 = (f32[4,256,256]{2,1,0:T(8,128)}, f32[4,256,256]{2,1,0:T(8,128)}, f32[4,256,256]{2,1,0:T(8,128)}, f32[4,8,128]{2,1,0:T(8,128)}) custom-call(s32[4]{0:T(128)} %and_select_fusion.2.refs_0_, bf16[4,256,256]{2,1,0:T(8,128)(2,1)} %get-tuple-element.23.refs_1_, ...), custom_call_target="tpu_custom_call", output_to_operand_aliasing={{0}: (7, {}), {1}: (8, {}), {2}: (9, {}), {3}: (10, {})} | custom-call | flops 9663676416 | bytes 12582912 | tf_op jit(solution)/shard_map/pallas_call | solution.py:216
  82.5 0.8 copy-done.6
  83.3 0.2 copy-done.7
  83.5 9.8 %shard_map.106 = (f32[4,256,256]{2,1,0:T(8,128)}, f32[4,256,256]{2,1,0:T(8,128)}, f32[4,256,256]{2,1,0:T(8,128)}, f32[4,8,128]{2,1,0:T(8,128)}) custom-call(s32[4]{0:T(128)} %and_select_fusion.3.refs_0_, bf16[4,256,256]{2,1,0:T(8,128)(2,1)} %get-tuple-element.23.refs_1_, ...), custom_call_target="tpu_custom_call", output_to_operand_aliasing={{0}: (7, {}), {1}: (8, {}), {2}: (9, {}), {3}: (10, {})} | custom-call | flops 9663676416 | bytes 12582912 | tf_op jit(solution)/shard_map/pallas_call | solution.py:216
  93.2 1.3 %slice.68 = f32[4,1,16]{2,1,0:T(1,128)} slice(f32[4,8,128]{2,1,0:T(8,128)} %get-tuple-element.40), slice={[0:4], [0:1], [0:16]} | slice | bytes 512 | tf_op jit(solution)/shard_map/slice | solution.py:248
  (67 shorter events, 1.6 us)
Async XLA Ops:
  0.6 14.9 %copy-start = (s32[16]{0:T(128)S(1)}, s32[16]{0:T(128)}, u32[]{:S(2)}) copy-start(s32[16]{0:T(128)} %param.15) | copy-start | bytes 196
  0.6 53.0 %collective-permute-start.9 = (bf16[4,256,256]{2,1,0:T(8,128)(2,1)}, bf16[4,256,256]{2,1,0:T(8,128)(2,1)}, u32[]{:S(2)}, u32[]{:S(2)}) collective-permute-start(bf16[4,256,256]{2,1,0:T(8,128)(2,1)} %refs_3_.1), channel_id=1, source_target_pairs={{0,8},{8,0},{16,24},{24,16},{1,9},{9,1},{17,25},{25,17},{2,10},{10... | collective-permute-start | bytes 1572872 | tf_op jit(solution)/shard_map/ppermute | solution.py:240
  1.9 61.4 %collective-permute-start.7 = (bf16[4,256,256]{2,1,0:T(8,128)(2,1)}, bf16[4,256,256]{2,1,0:T(8,128)(2,1)}, u32[]{:S(2)}, u32[]{:S(2)}) collective-permute-start(bf16[4,256,256]{2,1,0:T(8,128)(2,1)} %refs_3_.1), channel_id=1, source_target_pairs={{0,16},{8,24},{16,0},{24,8},{1,17},{9,25},{17,1},{25,9},{2,18},{10... | collective-permute-start | bytes 1572872 | tf_op jit(solution)/shard_map/ppermute | solution.py:240
  3.2 0.7 copy-start.3
  6.7 13.9 %collective-permute-start.1 = (bf16[2,256,256]{2,1,0:T(8,128)(2,1)S(1)}, bf16[2,256,256]{2,1,0:T(8,128)(2,1)S(1)}, u32[]{:S(2)}, u32[]{:S(2)}) collective-permute-start(bf16[2,256,256]{2,1,0:T(8,128)(2,1)S(1)} %get-tuple-element.50), channel_id=1, source_target_pairs={{0,2},{1,3},{2,0},{3,1},{4,6},{5,7},{6,4},{7,5},{8,10},{9,11},{10,... | collective-permute-start | bytes 786440 | tf_op jit(solution)/shard_map/ppermute | solution.py:78
  7.0 15.8 %collective-permute-start.2 = (bf16[2,256,256]{2,1,0:T(8,128)(2,1)S(1)}, bf16[2,256,256]{2,1,0:T(8,128)(2,1)S(1)}, u32[]{:S(2)}, u32[]{:S(2)}) collective-permute-start(bf16[2,256,256]{2,1,0:T(8,128)(2,1)S(1)} %get-tuple-element.49), channel_id=1, source_target_pairs={{0,4},{1,5},{2,6},{3,7},{4,0},{5,1},{6,2},{7,3},{8,12},{9,13},{10,... | collective-permute-start | bytes 786440 | tf_op jit(solution)/shard_map/ppermute | solution.py:78
  9.3 21.9 %collective-permute-start.3 = (bf16[2,256,256]{2,1,0:T(8,128)(2,1)S(1)}, bf16[2,256,256]{2,1,0:T(8,128)(2,1)S(1)}, u32[]{:S(2)}, u32[]{:S(2)}) collective-permute-start(bf16[2,256,256]{2,1,0:T(8,128)(2,1)S(1)} %get-tuple-element.48), channel_id=1, source_target_pairs={{0,6},{1,7},{2,4},{3,5},{4,2},{5,3},{6,0},{7,1},{8,14},{9,15},{10,... | collective-permute-start | bytes 786440 | tf_op jit(solution)/shard_map/ppermute | solution.py:78
  12.1 0.7 copy-start.9
  12.8 0.7 copy-start.1
  20.6 15.9 %collective-permute-start = (bf16[2,256,256]{2,1,0:T(8,128)(2,1)S(1)}, bf16[2,256,256]{2,1,0:T(8,128)(2,1)S(1)}, u32[]{:S(2)}, u32[]{:S(2)}) collective-permute-start(bf16[2,256,256]{2,1,0:T(8,128)(2,1)S(1)} %get-tuple-element.51), channel_id=1, source_target_pairs={{0,1},{1,0},{2,3},{3,2},{4,5},{5,4},{6,7},{7,6},{8,9},{9,8},{10,11... | collective-permute-start | bytes 786440 | tf_op jit(solution)/shard_map/ppermute | solution.py:75
  22.8 29.6 %collective-permute-start.10 = (bf16[4,256,256]{2,1,0:T(8,128)(2,1)}, bf16[4,256,256]{2,1,0:T(8,128)(2,1)}, u32[]{:S(2)}, u32[]{:S(2)}) collective-permute-start(bf16[4,256,256]{2,1,0:T(8,128)(2,1)} %refs_4_.1), channel_id=1, source_target_pairs={{0,8},{8,0},{16,24},{24,16},{1,9},{9,1},{17,25},{25,17},{2,10},{10... | collective-permute-start | bytes 1572872 | tf_op jit(solution)/shard_map/ppermute | solution.py:241
  31.2 5.3 %copy-start.2 = (bf16[6,256,256]{2,1,0:T(8,128)(2,1)}, bf16[6,256,256]{2,1,0:T(8,128)(2,1)S(1)}, u32[]{:S(2)}) copy-start(bf16[6,256,256]{2,1,0:T(8,128)(2,1)S(1)} %constant_dynamic-update-slice_fusion.recv_ref) | copy-start | bytes 2359300
  31.2 5.6 %collective-permute-start.4 = (bf16[6,256,256]{2,1,0:T(8,128)(2,1)S(1)}, bf16[6,256,256]{2,1,0:T(8,128)(2,1)S(1)}, u32[]{:S(2)}, u32[]{:S(2)}) collective-permute-start(bf16[6,256,256]{2,1,0:T(8,128)(2,1)S(1)} %constant_dynamic-update-slice_fusion.recv_ref), channel_id=1, source_target_pairs={{0,1},{1,0},{2,3},{3,2},{4,5},{5,4},{6,7},{7,6},{8,9},{9,8},{10,11... | collective-permute-start | bytes 2359304 | tf_op jit(solution)/shard_map/ppermute | solution.py:80
  35.2 1.6 %copy-start.5 = (bf16[4,256,256]{2,1,0:T(8,128)(2,1)S(1)}, bf16[4,256,256]{2,1,0:T(8,128)(2,1)}, u32[]{:S(2)}) copy-start(bf16[4,256,256]{2,1,0:T(8,128)(2,1)} %refs_3_.1) | copy-start | bytes 1572868
  36.5 1.6 %copy-start.8 = (bf16[2,256,256]{2,1,0:T(8,128)(2,1)}, bf16[2,256,256]{2,1,0:T(8,128)(2,1)S(1)}, u32[]{:S(2)}) copy-start(bf16[2,256,256]{2,1,0:T(8,128)(2,1)S(1)} %collective-permute-done.direct_ref) | copy-start | bytes 786436
  36.5 36.3 %collective-permute-start.8 = (bf16[4,256,256]{2,1,0:T(8,128)(2,1)}, bf16[4,256,256]{2,1,0:T(8,128)(2,1)}, u32[]{:S(2)}, u32[]{:S(2)}) collective-permute-start(bf16[4,256,256]{2,1,0:T(8,128)(2,1)} %refs_4_.1), channel_id=1, source_target_pairs={{0,16},{8,24},{16,0},{24,8},{1,17},{9,25},{17,1},{25,9},{2,18},{10... | collective-permute-start | bytes 1572872 | tf_op jit(solution)/shard_map/ppermute | solution.py:241
  36.8 1.3 %copy-start.4 = (bf16[6,256,256]{2,1,0:T(8,128)(2,1)}, bf16[6,256,256]{2,1,0:T(8,128)(2,1)S(1)}, u32[]{:S(2)}) copy-start(bf16[6,256,256]{2,1,0:T(8,128)(2,1)S(1)} %collective-permute-done.4.fwd_ref) | copy-start | bytes 2359300
  36.8 45.7 %collective-permute-start.5 = (bf16[4,256,256]{2,1,0:T(8,128)(2,1)S(1)}, bf16[4,256,256]{2,1,0:T(8,128)(2,1)S(1)}, u32[]{:S(2)}, u32[]{:S(2)}) collective-permute-start(bf16[4,256,256]{2,1,0:T(8,128)(2,1)S(1)} %copy-done.5), channel_id=1, source_target_pairs={{0,24},{8,16},{16,8},{24,0},{1,25},{9,17},{17,9},{25,1},{2,26},{10... | collective-permute-start | bytes 1572872 | tf_op jit(solution)/shard_map/ppermute | solution.py:240
  52.4 30.1 %collective-permute-start.6 = (bf16[4,256,256]{2,1,0:T(8,128)(2,1)}, bf16[4,256,256]{2,1,0:T(8,128)(2,1)S(1)}, u32[]{:S(2)}, u32[]{:S(2)}) collective-permute-start(bf16[4,256,256]{2,1,0:T(8,128)(2,1)} %refs_4_.1), channel_id=1, source_target_pairs={{0,24},{8,16},{16,8},{24,0},{1,25},{9,17},{17,9},{25,1},{2,26},{10... | collective-permute-start | bytes 1572872 | tf_op jit(solution)/shard_map/ppermute | solution.py:241
  82.5 0.8 copy-start.6
  82.5 0.9 copy-start.7

commit v6 on v5

--- a/solution.py
+++ b/solution.py
@@ -146,13 +146,16 @@
     )(take_idx, own, direct, received, forwarded, scale, half_table, full_table)
 
 
-def corr_kernel(first, last, tiles, orient_total, *refs):
+def corr_kernel(first, last, counts, orient_total, *refs):
+    groups = len(counts)
+    orient_ref, sr_ref, si_ref = refs[:3]
+    templ_refs = refs[3:3 + groups]
+    fw_ref, inv_ref = refs[3 + groups:5 + groups]
+    rest = refs[5 + groups:]
     if first:
-        (orient_ref, sr_ref, si_ref, tr_ref, ti_ref, fw_ref, inv_ref,
-         top_ref, sum_ref, sq_ref, peak_ref) = refs
+        top_ref, sum_ref, sq_ref, peak_ref = rest
     else:
-        (orient_ref, sr_ref, si_ref, tr_ref, ti_ref, fw_ref, inv_ref, top_in, sum_in, sq_in, peak_in,
-         top_ref, sum_ref, sq_ref, peak_ref) = refs
+        top_in, sum_in, sq_in, peak_in, top_ref, sum_ref, sq_ref, peak_ref = rest
     extent = sr_ref.shape[-1]
     sr = sr_ref[0].astype(jnp.float32)
     si = si_ref[0].astype(jnp.float32)
@@ -161,22 +164,25 @@
     lanes = lax.broadcasted_iota(jnp.int32, peak_ref.shape[1:], 1)
     peak_row = jnp.zeros(peak_ref.shape[1:], jnp.float32) if first else peak_in[0]
     top = total = square = None
-    for t in range(tiles):
-        tr = tr_ref[t].astype(jnp.float32)
-        ti = ti_ref[t].astype(jnp.float32)
-        pre = (sr * tr + si * ti).astype(jnp.bfloat16)
-        pim = (si * tr - sr * ti).astype(jnp.bfloat16)
-        prod = jnp.concatenate([pre, pim], axis=1)
-        q = jnp.dot(prod, forward, preferred_element_type=jnp.float32).astype(jnp.bfloat16)
-        q_stack = jnp.concatenate([q[:, :extent], q[:, extent:]], axis=0)
-        corr = jnp.dot(inverse, q_stack, preferred_element_type=jnp.float32)
-        peak_row = jnp.where(lanes == orient_ref[t], jnp.max(corr), peak_row)
-        if top is None:
-            top, total, square = corr, corr, corr * corr
-        else:
-            top = jnp.maximum(top, corr)
-            total = total + corr
-            square = square + corr * corr
+    position = 0
+    for templ_ref, count in zip(templ_refs, counts):
+        for t in range(count):
+            tr = templ_ref[t].astype(jnp.float32)
+            ti = templ_ref[count + t].astype(jnp.float32)
+            pre = (sr * tr + si * ti).astype(jnp.bfloat16)
+            pim = (si * tr - sr * ti).astype(jnp.bfloat16)
+            prod = jnp.concatenate([pre, pim], axis=1)
+            q = jnp.dot(prod, forward, preferred_element_type=jnp.float32).astype(jnp.bfloat16)
+            q_stack = jnp.concatenate([q[:, :extent], q[:, extent:]], axis=0)
+            corr = jnp.dot(inverse, q_stack, preferred_element_type=jnp.float32)
+            peak_row = jnp.where(lanes == orient_ref[position], jnp.max(corr), peak_row)
+            position += 1
+            if top is None:
+                top, total, square = corr, corr, corr * corr
+            else:
+                top = jnp.maximum(top, corr)
+                total = total + corr
+                square = square + corr * corr
     if not first:
         top = jnp.maximum(top_in[0], top)
         total = sum_in[0] + total
@@ -192,29 +198,31 @@
         sq_ref[0] = square
 
 
-def correlate_chunk(spec_re, spec_im, templ_re, templ_im, forward, inverse, orient_chunk,
+def correlate_chunk(spec_re, spec_im, templ_groups, forward, inverse, orient_chunk,
                     orient_total, stats, last):
     count, extent = (spec_re.shape[0], spec_re.shape[-1])
-    tiles = templ_re.shape[0]
+    counts = tuple(group.shape[0] // 2 for group in templ_groups)
+    tiles = sum(counts)
     first = stats is None
     lanes = 128 * ((orient_total + 127) // 128)
     plane = pl.BlockSpec((1, extent, extent), lambda s: (s, 0, 0))
     peak_spec = pl.BlockSpec((1, 8, lanes), lambda s: (s, 0, 0))
-    templ_spec = pl.BlockSpec((tiles, extent, extent), lambda s: (0, 0, 0))
+    templ_specs = [pl.BlockSpec(group.shape, lambda s: (0, 0, 0)) for group in templ_groups]
     fw_spec = pl.BlockSpec(forward.shape, lambda s: (0, 0))
     inv_spec = pl.BlockSpec(inverse.shape, lambda s: (0, 0))
-    in_specs = [pl.BlockSpec(memory_space=pltpu.SMEM), plane, plane, templ_spec, templ_spec,
-                fw_spec, inv_spec]
-    operands = [orient_chunk, spec_re, spec_im, templ_re, templ_im, forward, inverse]
+    in_specs = [pl.BlockSpec(memory_space=pltpu.SMEM), plane, plane] + templ_specs + [
+        fw_spec, inv_spec]
+    operands = [orient_chunk, spec_re, spec_im] + list(templ_groups) + [forward, inverse]
     aliases = {}
     if not first:
+        base = len(operands)
         in_specs += [plane, plane, plane, peak_spec]
         operands += list(stats)
-        aliases = {7: 0, 8: 1, 9: 2, 10: 3}
+        aliases = {base: 0, base + 1: 1, base + 2: 2, base + 3: 3}
     map_shape = jax.ShapeDtypeStruct((count, extent, extent), jnp.float32)
     flops = 3 * tiles * count * 12 * extent * extent * extent
     return pl.pallas_call(
-        functools.partial(corr_kernel, first, last, tiles, orient_total),
+        functools.partial(corr_kernel, first, last, counts, orient_total),
         grid=(count,),
         in_specs=in_specs,
         out_specs=[plane, plane, plane, peak_spec],
@@ -231,18 +239,28 @@
 def correlate_all(spec_re, spec_im, templ_re, templ_im, orientation, forward, inverse):
     blocks = lax.axis_size("blk")
     me = lax.axis_index("blk")
+    sources = lax.axis_size("patch")
+    core = lax.axis_index("patch") % 2
     tiles = templ_re.shape[0]
+    half = tiles // 2
     orient_total = orientation.shape[0]
-    within = jnp.arange(tiles, dtype=jnp.int32)
-    chunks = [(me, templ_re, templ_im)]
+    local = jnp.concatenate([templ_re, templ_im], axis=0)
+    mine = jnp.concatenate(
+        [lax.dynamic_slice_in_dim(templ_re, core * half, half, 0),
+         lax.dynamic_slice_in_dim(templ_im, core * half, half, 0)], axis=0)
+    within = jnp.arange(half, dtype=jnp.int32)
+    chunks = [([local], me * tiles + jnp.arange(tiles, dtype=jnp.int32))]
     for k in range(1, blocks):
-        pairs = [(b, b ^ k) for b in range(blocks)]
-        chunks.append((me ^ k, lax.ppermute(templ_re, "blk", pairs),
-                       lax.ppermute(templ_im, "blk", pairs)))
+        source = me ^ k
+        got = lax.ppermute(mine, "blk", [(b, b ^ k) for b in range(blocks)])
+        passed = lax.ppermute(got, "patch", xor_pairs(sources, 1))
+        index = jnp.concatenate(
+            [source * tiles + core * half + within, source * tiles + (1 - core) * half + within])
+        chunks.append(([got, passed], index))
     stats = None
-    for n, (source, got_re, got_im) in enumerate(chunks):
-        orient_chunk = jnp.take(orientation, source * tiles + within)
-        stats = correlate_chunk(spec_re, spec_im, got_re, got_im, forward, inverse, orient_chunk,
+    for n, (groups, index) in enumerate(chunks):
+        orient_chunk = jnp.take(orientation, index)
+        stats = correlate_chunk(spec_re, spec_im, groups, forward, inverse, orient_chunk,
                                 orient_total, stats, n == len(chunks) - 1)
     top_map, mean_map, var_map, peak = stats
     return (top_map, mean_map, var_map, peak[:, 0, :orient_total])

time: 95.1 us -> 87.6 us (0.921)
  waiting for transfers between devices: 17.6 us -> 2.62 us
  starting transfers between devices: 12.9 us -> 17.4 us
  local copies, waits for them, and re-layouts: 10.5 us -> 12.1 us
  other arithmetic: 9.11 us -> 10.6 us
    ppermute x6, waiting for transfers between devices: 9.53 us -> 0.02 us  [the longest x3 0.01 us: correlate_all(): got = lax.ppermute(mine, 'blk', [(b, b ^ k) for b in range(blocks)])]
    ppermute x1, starting transfers between devices: 2.11 us -> 9.04 us  [route_patches(): direct = lax.ppermute(outgoing[0], 'patch', xor_pairs(sources, 1))]
    ppermute x3, waiting for transfers between devices: 8.07 us -> 2.6 us  [route_patches(): lax.ppermute(outgoing[m], 'patch', xor_pairs(sources, 2 * m))]
    ppermute x6, starting transfers between devices: 5.64 us -> 3.3 us  [the longest x3 2.71 us: correlate_all(): got = lax.ppermute(mine, 'blk', [(b, b ^ k) for b in range(blocks)])]
    unnamed x22 -> x26, local copies, waits for them, and re-layouts: 2.3 us -> 3.76 us
    concatenate x0 -> x2, other arithmetic: none -> 1.12 us  [the longest x1 1.07 us: correlate_all(): local = jnp.concatenate([templ_re, templ_im], axis=0)]
    dynamic_slice x0 -> x1, local copies, waits for them, and re-layouts: none -> 1.07 us  [correlate_all(): lax.dynamic_slice_in_dim(templ_im, core * half, half, 0)]
    concatenate x1, local copies, waits for them, and re-layouts: 0.98 us -> 0.03 us  [route_patches(): jnp.concatenate([patches, jnp.zeros((1, extent, extent), patches.dtype)],...]
  transfers between devices with their start and end apart: 11 -> 11, of which waited for: 2 -> 2; matrix products, arithmetic and copies ran while one was open for 17% -> 19% of each run, Pallas kernels for 36% -> 39%
where the time goes in v6:
time: 87.6 us; the launch traced here: 87.2 us
  Pallas kernels  43.5 us (50%)
  starting transfers between devices  17.4 us (20%)
  local copies, waits for them, and re-layouts  12.1 us (14%)
  other arithmetic  10.6 us (12%)
  waiting for transfers between devices  2.62 us (3%)
  between operations  1.07 us (1%)
    pallas_call x4, Pallas kernels, correlate_chunk(): pl.pallas_call(functools.partial(corr_kernel, first, last, counts, orient...  38.3 us
    ppermute x1, starting transfers between devices, route_patches(): direct = lax.ppermute(outgoing[0], 'patch', xor_pairs(sources, 1))  9.04 us
    pallas_call x1, Pallas kernels, make_spectra(): pl.pallas_call(functools.partial(spectra_kernel, rows), grid=(count,), in...  5.11 us
    unnamed x26, local copies, waits for them, and re-layouts  3.76 us
    ppermute x3, starting transfers between devices, correlate_all(): got = lax.ppermute(mine, 'blk', [(b, b ^ k) for b in range(blocks)])  2.71 us
    ppermute x3, starting transfers between devices, route_patches(): lax.ppermute(outgoing[m], 'patch', xor_pairs(sources, 2 * m))  2.71 us
    select_n x8, other arithmetic, correlate_all(): orient_chunk = jnp.take(orientation, index)  2.61 us
    ppermute x3, waiting for transfers between devices, route_patches(): lax.ppermute(outgoing[m], 'patch', xor_pairs(sources, 2 * m))  2.6 us
  transfers between devices with their start and end apart: 11, of which 2 were waited for; matrix products, arithmetic and copies ran while one was open for 19% of the time, Pallas kernels for 39%

profile of v6, /device:TPU:9, one launch (start us, length us, event | category | flops | bytes accessed | tf_op | source)
XLA Modules:
  0.0 87.2 jit_solution(17584665090730306026)
XLA Ops:
  0.7 1.1 %constant_dynamic-slice_fusion = (bf16[2,256,256]{2,1,0:T(8,128)(2,1)S(1)}, bf16[2,256,256]{2,1,0:T(8,128)(2,1)S(1)}) fusion(bf16[4,256,256]{2,1,0:T(8,128)(2,1)} %param.14, s32[]{:T(128)S(6)} %select_n.292, bf16[4,256,256]{2,1,0:T(8,128)(2,1)} %param.13), kind=kLoop, calls=%fused_computation.65 | loop fusion | bytes 1048580 | tf_op jit(solution)/shard_map/dynamic_slice | solution.py:250
  1.8 1.3 %collective-permute-start.9 = (bf16[4,256,256]{2,1,0:T(8,128)(2,1)S(1)}, bf16[4,256,256]{2,1,0:T(8,128)(2,1)}, u32[]{:S(2)}, u32[]{:S(2)}) collective-permute-start(bf16[4,256,256]{2,1,0:T(8,128)(2,1)S(1)} %pad_maximum_fusion.1), channel_id=1, source_target_pairs={{0,8},{8,0},{16,24},{24,16},{1,9},{9,1},{17,25},{25,17},{2,10},{10... | collective-permute-start | bytes 1572872 | tf_op jit(solution)/shard_map/ppermute | solution.py:255
  3.1 1.2 %collective-permute-start.7 = (bf16[4,256,256]{2,1,0:T(8,128)(2,1)S(1)}, bf16[4,256,256]{2,1,0:T(8,128)(2,1)S(1)}, u32[]{:S(2)}, u32[]{:S(2)}) collective-permute-start(bf16[4,256,256]{2,1,0:T(8,128)(2,1)S(1)} %pad_maximum_fusion.1), channel_id=1, source_target_pairs={{0,16},{8,24},{16,0},{24,8},{1,17},{9,25},{17,1},{25,9},{2,18},{10... | collective-permute-start | bytes 1572872 | tf_op jit(solution)/shard_map/ppermute | solution.py:255
  4.3 0.7 copy-done.6
  6.1 0.6 gather_fusion
  6.7 0.2 broadcast_select_fusion
  6.9 0.2 collective-permute-start.1
  7.2 2.3 %collective-permute-start.2 = (bf16[2,256,256]{2,1,0:T(8,128)(2,1)S(1)}, bf16[2,256,256]{2,1,0:T(8,128)(2,1)S(1)}, u32[]{:S(2)}, u32[]{:S(2)}) collective-permute-start(bf16[2,256,256]{2,1,0:T(8,128)(2,1)S(1)} %get-tuple-element.49), channel_id=1, source_target_pairs={{0,4},{1,5},{2,6},{3,7},{4,0},{5,1},{6,2},{7,3},{8,12},{9,13},{10,... | collective-permute-start | bytes 786440 | tf_op jit(solution)/shard_map/ppermute | solution.py:78
  9.5 0.2 collective-permute-start.3
  9.8 0.1 reduce
  9.9 0.1 fusion.13
  10.3 0.6 copy-done.11
  11.0 0.6 gather_fusion.1
  11.8 0.7 copy-done.1
  12.4 0.6 gather_fusion.2
  13.1 0.4 fusion.20
  13.7 0.2 select_reduce_fusion
  13.8 0.5 broadcast_select_fusion.2.take_ref
  14.5 0.6 gather_fusion.6
  15.1 0.5 and_select_fusion.refs_0_
  15.6 0.6 gather_fusion.5
  16.3 0.6 and_select_fusion.1.refs_0_
  16.9 0.6 gather_fusion.4
  17.5 0.7 and_select_fusion.2.refs_0_
  18.2 0.1 fusion.8
  18.4 0.6 gather_fusion.3
  19.1 0.6 and_select_fusion.3.refs_0_
  19.7 0.2 collective-permute-start.5
  19.9 0.4 collective-permute-done.2
  20.2 9.0 %collective-permute-start = (bf16[2,256,256]{2,1,0:T(8,128)(2,1)S(1)}, bf16[2,256,256]{2,1,0:T(8,128)(2,1)S(1)}, u32[]{:S(2)}, u32[]{:S(2)}) collective-permute-start(bf16[2,256,256]{2,1,0:T(8,128)(2,1)S(1)} %get-tuple-element.51), channel_id=1, source_target_pairs={{0,1},{1,0},{2,3},{3,2},{4,5},{5,4},{6,7},{7,6},{8,9},{9,8},{10,11... | collective-permute-start | bytes 786440 | tf_op jit(solution)/shard_map/ppermute | solution.py:75
  29.3 2.2 %collective-permute-done.3 = bf16[2,256,256]{2,1,0:T(8,128)(2,1)S(1)} collective-permute-done((bf16[2,256,256]{2,1,0:T(8,128)(2,1)S(1)}, bf16[2,256,256]{2,1,0:T(8,128)(2,1)S(1)}, u32[]{:S(2)}, u32[]{:S(2)}) %collective-permute-start.3) | collective-permute-done | bytes 262176 | tf_op jit(solution)/shard_map/ppermute | solution.py:78
  31.6 2.4 %collective-permute-start.4 = (bf16[6,256,256]{2,1,0:T(8,128)(2,1)S(1)}, bf16[6,256,256]{2,1,0:T(8,128)(2,1)S(1)}, u32[]{:S(2)}, u32[]{:S(2)}) collective-permute-start(bf16[6,256,256]{2,1,0:T(8,128)(2,1)S(1)} %constant_dynamic-update-slice_fusion.recv_ref), channel_id=1, source_target_pairs={{0,1},{1,0},{2,3},{3,2},{4,5},{5,4},{6,7},{7,6},{8,9},{9,8},{10,11... | collective-permute-start | bytes 2359304 | tf_op jit(solution)/shard_map/ppermute | solution.py:80
  33.9 1.0 %fusion.6 = bf16[256,256]{1,0:T(8,128)(2,1)S(1)} fusion(), kind=kLoop, calls=%fused_computation.25 | loop fusion | flops 1179648 | bytes 131072 | tf_op jit(solution)/shard_map/neg | solution.py:282
  34.9 1.1 %sine_convert_fusion = (bf16[256,256]{1,0:T(8,128)(2,1)S(1)}, bf16[256,256]{1,0:T(8,128)(2,1)S(1)}) fusion(), kind=kLoop, calls=%fused_computation.19 | loop fusion | flops 1048576 | bytes 262144 | tf_op jit(solution)/shard_map/convert_element_type | solution.py:23
  36.0 0.8 broadcast_multiply_fusion
  36.9 1.1 %pad_maximum_fusion.refs_3_ = bf16[8,256,256]{2,1,0:T(8,128)(2,1)} fusion(bf16[4,256,256]{2,1,0:T(8,128)(2,1)S(1)} %copy-done.2, bf16[4,256,256]{2,1,0:T(8,128)(2,1)S(1)} %copy-done.3), kind=kLoop, calls=%fused_computation.7 | loop fusion | flops 524288 | bytes 2097152 | tf_op jit(solution)/shard_map/concatenate | solution.py:247
  37.9 0.8 maximum_maximum_fusion.full_ref.refs_4_.refs_5_
  38.8 1.3 %negate_multiply_fusion.scale_ref = f32[4,256,256]{2,1,0:T(8,128)} fusion(f32[4,256]{1,0:T(4,128)S(1)} %get-tuple-element.59, f32[4,256]{1,0:T(4,128)S(1)} %get-tuple-element.61, f32[4,256]{1,0:T(4,128)S(1)} %get-tuple-element.60, f32[4,256]{1,0:T(4,128)S(1)} %get-tuple-element.58), kind=kLoop, calls=%fused_computation.8 | loop fusion | flops 1310720 | bytes 1064960 | tf_op jit(solution)/shard_map/div | solution.py:48
  40.1 0.5 collective-permute-start.8
  40.7 0.7 copy-done.10
  41.4 0.3 copy-done.7
  41.7 5.1 %shard_map.102 = (bf16[4,256,256]{2,1,0:T(8,128)(2,1)}, bf16[4,256,256]{2,1,0:T(8,128)(2,1)}) custom-call(s32[4]{0:T(128)} %broadcast_select_fusion.2.take_ref, bf16[2,256,256]{2,1,0:T(8,128)(2,1)} %own_ref.1, bf16[2,256,256]{2,1,0:T(8,128)(2,1)} %copy-done.10, bf16[6,256,256]{2,1,0:T(8,128)(2,1)} %copy-done.5, bf16[6,256,256]{2,1,0:T(8,128)(2,1)} %copy-done.7, ...), custom_call_target="tpu_custom_call" | custom-call | flops 1207959552 | bytes 2621440 | tf_op jit(solution)/shard_map/pallas_call | solution.py:134
  46.8 9.2 %shard_map.103 = (f32[4,256,256]{2,1,0:T(8,128)}, f32[4,256,256]{2,1,0:T(8,128)}, f32[4,256,256]{2,1,0:T(8,128)}, f32[4,8,128]{2,1,0:T(8,128)}) custom-call(s32[4]{0:T(128)} %and_select_fusion.refs_0_, bf16[4,256,256]{2,1,0:T(8,128)(2,1)} %get-tuple-element.23.refs_1_, bf16[4,256,256]{2,1,0:T(8,128)(2,1)} %get-tuple-element.24.refs_2_, ...), custom_call_target="tpu_custom_call" | custom-call | flops 9663676416 | bytes 12582912 | tf_op jit(solution)/shard_map/pallas_call | solution.py:224
  56.0 9.7 %shard_map.104 = (f32[4,256,256]{2,1,0:T(8,128)}, f32[4,256,256]{2,1,0:T(8,128)}, f32[4,256,256]{2,1,0:T(8,128)}, f32[4,8,128]{2,1,0:T(8,128)}) custom-call(s32[4]{0:T(128)} %and_select_fusion.1.refs_0_, bf16[4,256,256]{2,1,0:T(8,128)(2,1)} %get-tuple-element.23.refs_1_, ...), custom_call_target="tpu_custom_call", output_to_operand_aliasing={{0}: (7, {}), {1}: (8, {}), {2}: (9, {}), {3}: (10, {})} | custom-call | flops 9663676416 | bytes 12582912 | tf_op jit(solution)/shard_map/pallas_call | solution.py:224
  65.7 9.7 %shard_map.105 = (f32[4,256,256]{2,1,0:T(8,128)}, f32[4,256,256]{2,1,0:T(8,128)}, f32[4,256,256]{2,1,0:T(8,128)}, f32[4,8,128]{2,1,0:T(8,128)}) custom-call(s32[4]{0:T(128)} %and_select_fusion.2.refs_0_, bf16[4,256,256]{2,1,0:T(8,128)(2,1)} %get-tuple-element.23.refs_1_, ...), custom_call_target="tpu_custom_call", output_to_operand_aliasing={{0}: (7, {}), {1}: (8, {}), {2}: (9, {}), {3}: (10, {})} | custom-call | flops 9663676416 | bytes 12582912 | tf_op jit(solution)/shard_map/pallas_call | solution.py:224
  75.4 0.8 copy-done.9
  76.2 9.8 %shard_map.106 = (f32[4,256,256]{2,1,0:T(8,128)}, f32[4,256,256]{2,1,0:T(8,128)}, f32[4,256,256]{2,1,0:T(8,128)}, f32[4,8,128]{2,1,0:T(8,128)}) custom-call(s32[4]{0:T(128)} %and_select_fusion.3.refs_0_, bf16[4,256,256]{2,1,0:T(8,128)(2,1)} %get-tuple-element.23.refs_1_, ...), custom_call_target="tpu_custom_call", output_to_operand_aliasing={{0}: (7, {}), {1}: (8, {}), {2}: (9, {}), {3}: (10, {})} | custom-call | flops 9663676416 | bytes 12582912 | tf_op jit(solution)/shard_map/pallas_call | solution.py:224
  85.9 1.3 %slice.68 = f32[4,1,16]{2,1,0:T(1,128)} slice(f32[4,8,128]{2,1,0:T(8,128)} %get-tuple-element.40), slice={[0:4], [0:1], [0:16]} | slice | bytes 512 | tf_op jit(solution)/shard_map/slice | solution.py:266
  (80 shorter events, 2.1 us)
Async XLA Ops:
  0.6 13.9 %copy-start = (s32[16]{0:T(128)S(1)}, s32[16]{0:T(128)}, u32[]{:S(2)}) copy-start(s32[16]{0:T(128)} %param.15) | copy-start | bytes 196
  1.7 4.3 %copy-start.4 = (bf16[2,256,256]{2,1,0:T(8,128)(2,1)S(1)}, bf16[2,256,256]{2,1,0:T(8,128)(2,1)}, u32[]{:S(2)}) copy-start(bf16[2,256,256]{2,1,0:T(8,128)(2,1)} %own_ref.1) | copy-start | bytes 786436
  1.8 38.3 %collective-permute-start.9 = (bf16[4,256,256]{2,1,0:T(8,128)(2,1)S(1)}, bf16[4,256,256]{2,1,0:T(8,128)(2,1)}, u32[]{:S(2)}, u32[]{:S(2)}) collective-permute-start(bf16[4,256,256]{2,1,0:T(8,128)(2,1)S(1)} %pad_maximum_fusion.1), channel_id=1, source_target_pairs={{0,8},{8,0},{16,24},{24,16},{1,9},{9,1},{17,25},{25,17},{2,10},{10... | collective-permute-start | bytes 1572872 | tf_op jit(solution)/shard_map/ppermute | solution.py:255
  3.1 37.0 %collective-permute-start.7 = (bf16[4,256,256]{2,1,0:T(8,128)(2,1)S(1)}, bf16[4,256,256]{2,1,0:T(8,128)(2,1)S(1)}, u32[]{:S(2)}, u32[]{:S(2)}) collective-permute-start(bf16[4,256,256]{2,1,0:T(8,128)(2,1)S(1)} %pad_maximum_fusion.1), channel_id=1, source_target_pairs={{0,16},{8,24},{16,0},{24,8},{1,17},{9,25},{17,1},{25,9},{2,18},{10... | collective-permute-start | bytes 1572872 | tf_op jit(solution)/shard_map/ppermute | solution.py:255
  4.3 0.7 copy-start.6
  6.9 12.7 %collective-permute-start.1 = (bf16[2,256,256]{2,1,0:T(8,128)(2,1)S(1)}, bf16[2,256,256]{2,1,0:T(8,128)(2,1)S(1)}, u32[]{:S(2)}, u32[]{:S(2)}) collective-permute-start(bf16[2,256,256]{2,1,0:T(8,128)(2,1)S(1)} %get-tuple-element.50), channel_id=1, source_target_pairs={{0,2},{1,3},{2,0},{3,1},{4,6},{5,7},{6,4},{7,5},{8,10},{9,11},{10,... | collective-permute-start | bytes 786440 | tf_op jit(solution)/shard_map/ppermute | solution.py:78
  7.2 13.1 %collective-permute-start.2 = (bf16[2,256,256]{2,1,0:T(8,128)(2,1)S(1)}, bf16[2,256,256]{2,1,0:T(8,128)(2,1)S(1)}, u32[]{:S(2)}, u32[]{:S(2)}) collective-permute-start(bf16[2,256,256]{2,1,0:T(8,128)(2,1)S(1)} %get-tuple-element.49), channel_id=1, source_target_pairs={{0,4},{1,5},{2,6},{3,7},{4,0},{5,1},{6,2},{7,3},{8,12},{9,13},{10,... | collective-permute-start | bytes 786440 | tf_op jit(solution)/shard_map/ppermute | solution.py:78
  9.5 22.0 %collective-permute-start.3 = (bf16[2,256,256]{2,1,0:T(8,128)(2,1)S(1)}, bf16[2,256,256]{2,1,0:T(8,128)(2,1)S(1)}, u32[]{:S(2)}, u32[]{:S(2)}) collective-permute-start(bf16[2,256,256]{2,1,0:T(8,128)(2,1)S(1)} %get-tuple-element.48), channel_id=1, source_target_pairs={{0,6},{1,7},{2,4},{3,5},{4,2},{5,3},{6,0},{7,1},{8,14},{9,15},{10,... | collective-permute-start | bytes 786440 | tf_op jit(solution)/shard_map/ppermute | solution.py:78
  10.3 0.7 copy-start.11
  11.8 0.7 copy-start.1
  19.7 20.9 %collective-permute-start.5 = (bf16[4,256,256]{2,1,0:T(8,128)(2,1)S(1)}, bf16[4,256,256]{2,1,0:T(8,128)(2,1)}, u32[]{:S(2)}, u32[]{:S(2)}) collective-permute-start(bf16[4,256,256]{2,1,0:T(8,128)(2,1)S(1)} %pad_maximum_fusion.1), channel_id=1, source_target_pairs={{0,24},{8,16},{16,8},{24,0},{1,25},{9,17},{17,9},{25,1},{2,26},{10... | collective-permute-start | bytes 1572872 | tf_op jit(solution)/shard_map/ppermute | solution.py:255
  20.2 20.4 %collective-permute-start = (bf16[2,256,256]{2,1,0:T(8,128)(2,1)S(1)}, bf16[2,256,256]{2,1,0:T(8,128)(2,1)S(1)}, u32[]{:S(2)}, u32[]{:S(2)}) collective-permute-start(bf16[2,256,256]{2,1,0:T(8,128)(2,1)S(1)} %get-tuple-element.51), channel_id=1, source_target_pairs={{0,1},{1,0},{2,3},{3,2},{4,5},{5,4},{6,7},{7,6},{8,9},{9,8},{10,11... | collective-permute-start | bytes 786440 | tf_op jit(solution)/shard_map/ppermute | solution.py:75
  31.5 6.4 %copy-start.5 = (bf16[6,256,256]{2,1,0:T(8,128)(2,1)}, bf16[6,256,256]{2,1,0:T(8,128)(2,1)S(1)}, u32[]{:S(2)}) copy-start(bf16[6,256,256]{2,1,0:T(8,128)(2,1)S(1)} %constant_dynamic-update-slice_fusion.recv_ref) | copy-start | bytes 2359300
  31.6 9.1 %collective-permute-start.4 = (bf16[6,256,256]{2,1,0:T(8,128)(2,1)S(1)}, bf16[6,256,256]{2,1,0:T(8,128)(2,1)S(1)}, u32[]{:S(2)}, u32[]{:S(2)}) collective-permute-start(bf16[6,256,256]{2,1,0:T(8,128)(2,1)S(1)} %constant_dynamic-update-slice_fusion.recv_ref), channel_id=1, source_target_pairs={{0,1},{1,0},{2,3},{3,2},{4,5},{5,4},{6,7},{7,6},{8,9},{9,8},{10,11... | collective-permute-start | bytes 2359304 | tf_op jit(solution)/shard_map/ppermute | solution.py:80
  34.9 2.0 %copy-start.2 = (bf16[4,256,256]{2,1,0:T(8,128)(2,1)S(1)}, bf16[4,256,256]{2,1,0:T(8,128)(2,1)}, u32[]{:S(2)}) copy-start(bf16[4,256,256]{2,1,0:T(8,128)(2,1)} %param.14) | copy-start | bytes 1572868
  34.9 2.0 %copy-start.3 = (bf16[4,256,256]{2,1,0:T(8,128)(2,1)S(1)}, bf16[4,256,256]{2,1,0:T(8,128)(2,1)}, u32[]{:S(2)}) copy-start(bf16[4,256,256]{2,1,0:T(8,128)(2,1)} %param.13) | copy-start | bytes 1572868
  40.1 15.9 %collective-permute-start.10 = (bf16[4,256,256]{2,1,0:T(8,128)(2,1)}, bf16[4,256,256]{2,1,0:T(8,128)(2,1)}, u32[]{:S(2)}, u32[]{:S(2)}) collective-permute-start(bf16[4,256,256]{2,1,0:T(8,128)(2,1)} %collective-permute-done.9.refs_3_), channel_id=1, source_target_pairs={{0,1},{1,0},{2,3},{3,2},{4,5},{5,4},{6,7},{7,6},{8,9},{9,8},{10,11... | collective-permute-start | bytes 1572872 | tf_op jit(solution)/shard_map/ppermute | solution.py:256
  40.1 6.7 %copy-start.8 = (bf16[4,256,256]{2,1,0:T(8,128)(2,1)}, bf16[4,256,256]{2,1,0:T(8,128)(2,1)S(1)}, u32[]{:S(2)}) copy-start(bf16[4,256,256]{2,1,0:T(8,128)(2,1)S(1)} %collective-permute-done.7.refs_3_) | copy-start | bytes 1572868
  40.1 25.6 %collective-permute-start.8 = (bf16[4,256,256]{2,1,0:T(8,128)(2,1)S(1)}, bf16[4,256,256]{2,1,0:T(8,128)(2,1)}, u32[]{:S(2)}, u32[]{:S(2)}) collective-permute-start(bf16[4,256,256]{2,1,0:T(8,128)(2,1)S(1)} %collective-permute-done.7.refs_3_), channel_id=1, source_target_pairs={{0,1},{1,0},{2,3},{3,2},{4,5},{5,4},{6,7},{7,6},{8,9},{9,8},{10,11... | collective-permute-start | bytes 1572872 | tf_op jit(solution)/shard_map/ppermute | solution.py:256
  40.6 34.8 %collective-permute-start.6 = (bf16[4,256,256]{2,1,0:T(8,128)(2,1)}, bf16[4,256,256]{2,1,0:T(8,128)(2,1)S(1)}, u32[]{:S(2)}, u32[]{:S(2)}) collective-permute-start(bf16[4,256,256]{2,1,0:T(8,128)(2,1)} %collective-permute-done.5.refs_3_), channel_id=1, source_target_pairs={{0,1},{1,0},{2,3},{3,2},{4,5},{5,4},{6,7},{7,6},{8,9},{9,8},{10,11... | collective-permute-start | bytes 1572872 | tf_op jit(solution)/shard_map/ppermute | solution.py:256
  40.7 0.7 copy-start.10
  40.7 1.0 %copy-start.7 = (bf16[6,256,256]{2,1,0:T(8,128)(2,1)}, bf16[6,256,256]{2,1,0:T(8,128)(2,1)S(1)}, u32[]{:S(2)}) copy-start(bf16[6,256,256]{2,1,0:T(8,128)(2,1)S(1)} %collective-permute-done.4.fwd_ref) | copy-start | bytes 2359300
  75.4 0.8 copy-start.9

commit v7 on v6

--- a/solution.py
+++ b/solution.py
@@ -2,6 +2,8 @@
 import math
 
 import jax
+import ml_dtypes
+import numpy as np
 import jax.numpy as jnp
 from jax import lax
 from jax.experimental import pallas as pl
@@ -17,10 +19,17 @@
 
 
 def dft_tables(extent):
-    indices = jnp.arange(extent, dtype=jnp.int32)
+    indices = np.arange(extent, dtype=np.int64)
     turn_count = indices[:, None] * indices[None, :] % extent
-    angles = turn_count.astype(jnp.float32) * (2.0 * math.pi / extent)
-    return (jnp.cos(angles).astype(jnp.bfloat16), jnp.sin(angles).astype(jnp.bfloat16))
+    angles = turn_count.astype(np.float32) * np.float32(2.0 * math.pi / extent)
+    cosine = np.cos(angles).astype(ml_dtypes.bfloat16)
+    sine = np.sin(angles).astype(ml_dtypes.bfloat16)
+    forward = np.concatenate(
+        [np.concatenate([cosine, sine], axis=1), np.concatenate([-sine, cosine], axis=1)], axis=0
+    )
+    half_table = np.concatenate([cosine, -sine], axis=1)
+    inverse = (half_table.astype(np.float32) / extent).astype(ml_dtypes.bfloat16)
+    return forward, half_table, inverse
 
 
 def ctf_filter(defocus_values, extent):
@@ -98,7 +107,7 @@
     take_idx = jnp.sum(jnp.where(found, cand_ids[None, :], 0), axis=1)
     take_idx = jnp.where(present, take_idx, cand_pid.shape[0])
     pieces = (patches, direct, received, forwarded)
-    return take_idx, pieces, jnp.where(present, slot_pid, sources * number)
+    return take_idx, pieces, jnp.where(present, slot_pid, sources * number), outgoing
 
 
 def spectra_kernel(rows, take_ref, own_ref, direct_ref, recv_ref, fwd_ref, scale_ref, half_ref,
@@ -270,17 +279,13 @@
     sources = lax.axis_size("patch")
     my_index = lax.axis_index("patch")
     number, extent = (patches.shape[0], patches.shape[1])
-    cosine, sine = dft_tables(extent)
+    forward, half_table, inverse = (jnp.asarray(table) for table in dft_tables(extent))
     row_owner = owner_of_patch.reshape(sources, number)
-    take_idx, pieces, slot_row = route_patches(patches, row_owner, my_index)
+    take_idx, pieces, slot_row, outgoing = route_patches(patches, row_owner, my_index)
+    templ_re, templ_im, unused = lax.optimization_barrier((templ_re, templ_im, outgoing))
     groups = jnp.take(jnp.concatenate([group_of_patch, jnp.zeros((1,), jnp.int32)]), slot_row)
     focus_values = jnp.take(defocus, groups)
     scale = ctf_scale(focus_values, extent)
-    forward = jnp.concatenate(
-        [jnp.concatenate([cosine, sine], axis=1), jnp.concatenate([-sine, cosine], axis=1)], axis=0
-    )
-    half_table = jnp.concatenate([cosine, -sine], axis=1)
-    inverse = half_table * jnp.asarray(1.0 / extent, jnp.bfloat16)
     spec_re, spec_im = make_spectra(take_idx, *pieces, scale, half_table, forward)
     return correlate_all(spec_re, spec_im, templ_re, templ_im, orientation, forward, inverse)
 

time: 87.6 us -> 85.7 us (0.978)
  other arithmetic: 10.6 us -> 6.88 us
  waiting for transfers between devices: 2.62 us -> 3.8 us
    ppermute x3, waiting for transfers between devices: 2.6 us -> 3.77 us  [route_patches(): lax.ppermute(outgoing[m], 'patch', xor_pairs(sources, 2 * m))]
    convert_element_type x1 -> x0, other arithmetic: 1.1 us -> none  [dft_tables(): jnp.sin(angles).astype(jnp.bfloat16)]
    neg x1 -> x0, other arithmetic: 0.99 us -> none  [body(): half_table = jnp.concatenate([cosine, -sine], axis=1)]
  transfers between devices with their start and end apart: 11 -> 11, of which waited for: 2 -> 2; matrix products, arithmetic and copies ran while one was open for 19% -> 15% of each run, Pallas kernels for 39% -> 39%
where the time goes in v7:
time: 85.7 us; the launch traced here: 85.3 us
  Pallas kernels  43.4 us (51%)
  starting transfers between devices  17.5 us (20%)
  local copies, waits for them, and re-layouts  12.7 us (15%)
  other arithmetic  6.88 us (8%)
  waiting for transfers between devices  3.8 us (4%)
  between operations  1.04 us (1%)
    pallas_call x4, Pallas kernels, correlate_chunk(): pl.pallas_call(functools.partial(corr_kernel, first, last, counts, orient...  38.3 us
    ppermute x1, starting transfers between devices, route_patches(): direct = lax.ppermute(outgoing[0], 'patch', xor_pairs(sources, 1))  9.04 us
    pallas_call x1, Pallas kernels, make_spectra(): pl.pallas_call(functools.partial(spectra_kernel, rows), grid=(count,), in...  5.09 us
    unnamed x26, local copies, waits for them, and re-layouts  4.38 us
    ppermute x3, waiting for transfers between devices, route_patches(): lax.ppermute(outgoing[m], 'patch', xor_pairs(sources, 2 * m))  3.77 us
    ppermute x3, starting transfers between devices, correlate_all(): got = lax.ppermute(mine, 'blk', [(b, b ^ k) for b in range(blocks)])  2.75 us
    ppermute x3, starting transfers between devices, route_patches(): lax.ppermute(outgoing[m], 'patch', xor_pairs(sources, 2 * m))  2.71 us
    select_n x8, other arithmetic, correlate_all(): orient_chunk = jnp.take(orientation, index)  2.62 us
  transfers between devices with their start and end apart: 11, of which 2 were waited for; matrix products, arithmetic and copies ran while one was open for 15% of the time, Pallas kernels for 39%

profile of v7, /device:TPU:9, one launch (start us, length us, event | category | flops | bytes accessed | tf_op | source)
XLA Modules:
  0.0 85.3 jit_solution(9338109597525889742)
XLA Ops:
  0.7 1.1 %constant_dynamic-slice_fusion = (bf16[2,256,256]{2,1,0:T(8,128)(2,1)S(1)}, bf16[2,256,256]{2,1,0:T(8,128)(2,1)S(1)}) fusion(bf16[4,256,256]{2,1,0:T(8,128)(2,1)} %param.17, s32[]{:T(128)S(6)} %select_n.275, bf16[4,256,256]{2,1,0:T(8,128)(2,1)} %param.16), kind=kLoop, calls=%fused_computation.50 | loop fusion | bytes 1048580 | tf_op jit(solution)/shard_map/dynamic_slice | solution.py:259
  1.8 1.3 %collective-permute-start.9 = (bf16[4,256,256]{2,1,0:T(8,128)(2,1)S(1)}, bf16[4,256,256]{2,1,0:T(8,128)(2,1)}, u32[]{:S(2)}, u32[]{:S(2)}) collective-permute-start(bf16[4,256,256]{2,1,0:T(8,128)(2,1)S(1)} %pad_maximum_fusion.1), channel_id=1, source_target_pairs={{0,8},{8,0},{16,24},{24,16},{1,9},{9,1},{17,25},{25,17},{2,10},{10... | collective-permute-start | bytes 1572872 | tf_op jit(solution)/shard_map/ppermute | solution.py:264
  3.1 1.2 %collective-permute-start.7 = (bf16[4,256,256]{2,1,0:T(8,128)(2,1)S(1)}, bf16[4,256,256]{2,1,0:T(8,128)(2,1)S(1)}, u32[]{:S(2)}, u32[]{:S(2)}) collective-permute-start(bf16[4,256,256]{2,1,0:T(8,128)(2,1)S(1)} %pad_maximum_fusion.1), channel_id=1, source_target_pairs={{0,16},{8,24},{16,0},{24,8},{1,17},{9,25},{17,1},{25,9},{2,18},{10... | collective-permute-start | bytes 1572872 | tf_op jit(solution)/shard_map/ppermute | solution.py:264
  4.3 0.7 copy-done.6
  5.1 0.1 copy.43
  5.3 0.1 copy.44
  5.7 0.1 copy.47
  6.1 0.6 gather_fusion
  6.7 0.2 broadcast_select_fusion
  6.9 0.2 collective-permute-start.1
  7.2 2.3 %collective-permute-start.2 = (bf16[2,256,256]{2,1,0:T(8,128)(2,1)S(1)}, bf16[2,256,256]{2,1,0:T(8,128)(2,1)S(1)}, u32[]{:S(2)}, u32[]{:S(2)}) collective-permute-start(bf16[2,256,256]{2,1,0:T(8,128)(2,1)S(1)} %get-tuple-element.53), channel_id=1, source_target_pairs={{0,4},{1,5},{2,6},{3,7},{4,0},{5,1},{6,2},{7,3},{8,12},{9,13},{10,... | collective-permute-start | bytes 786440 | tf_op jit(solution)/shard_map/ppermute | solution.py:87
  9.5 0.2 collective-permute-start.3
  9.8 0.1 reduce
  9.9 0.1 fusion.6
  10.0 0.1 select_reduce_fusion.1
  10.3 0.6 copy-done.11
  11.0 0.6 gather_fusion.1
  11.8 0.7 copy-done.1
  12.4 0.6 gather_fusion.2
  13.1 0.4 fusion.13
  13.7 0.2 select_reduce_fusion
  13.8 0.5 broadcast_select_fusion.2.take_ref
  14.5 0.6 gather_fusion.6
  15.1 0.6 and_select_fusion.refs_0_
  15.7 0.6 gather_fusion.5
  16.3 0.6 and_select_fusion.1.refs_0_
  16.9 0.1 fusion.1
  17.2 0.6 gather_fusion.4
  17.8 0.6 gather_fusion.3
  18.4 0.2 collective-permute-start.5
  18.7 1.6 %collective-permute-done.2 = bf16[2,256,256]{2,1,0:T(8,128)(2,1)S(1)} collective-permute-done((bf16[2,256,256]{2,1,0:T(8,128)(2,1)S(1)}, bf16[2,256,256]{2,1,0:T(8,128)(2,1)S(1)}, u32[]{:S(2)}, u32[]{:S(2)}) %collective-permute-start.2) | collective-permute-done | bytes 262176 | tf_op jit(solution)/shard_map/ppermute | solution.py:87
  20.2 9.0 %collective-permute-start = (bf16[2,256,256]{2,1,0:T(8,128)(2,1)S(1)}, bf16[2,256,256]{2,1,0:T(8,128)(2,1)S(1)}, u32[]{:S(2)}, u32[]{:S(2)}) collective-permute-start(bf16[2,256,256]{2,1,0:T(8,128)(2,1)S(1)} %get-tuple-element.55), channel_id=1, source_target_pairs={{0,1},{1,0},{2,3},{3,2},{4,5},{5,4},{6,7},{7,6},{8,9},{9,8},{10,11... | collective-permute-start | bytes 786440 | tf_op jit(solution)/shard_map/ppermute | solution.py:84
  29.3 2.2 %collective-permute-done.3 = bf16[2,256,256]{2,1,0:T(8,128)(2,1)S(1)} collective-permute-done((bf16[2,256,256]{2,1,0:T(8,128)(2,1)S(1)}, bf16[2,256,256]{2,1,0:T(8,128)(2,1)S(1)}, u32[]{:S(2)}, u32[]{:S(2)}) %collective-permute-start.3) | collective-permute-done | bytes 262176 | tf_op jit(solution)/shard_map/ppermute | solution.py:87
  31.6 2.4 %collective-permute-start.4 = (bf16[6,256,256]{2,1,0:T(8,128)(2,1)S(1)}, bf16[6,256,256]{2,1,0:T(8,128)(2,1)S(1)}, u32[]{:S(2)}, u32[]{:S(2)}) collective-permute-start(bf16[6,256,256]{2,1,0:T(8,128)(2,1)S(1)} %constant_dynamic-update-slice_fusion.recv_ref), channel_id=1, source_target_pairs={{0,1},{1,0},{2,3},{3,2},{4,5},{5,4},{6,7},{7,6},{8,9},{9,8},{10,11... | collective-permute-start | bytes 2359304 | tf_op jit(solution)/shard_map/ppermute | solution.py:89
  33.9 0.7 and_select_fusion.2.refs_0_
  34.6 0.6 and_select_fusion.3.refs_0_
  35.2 1.1 %pad_maximum_fusion.refs_3_ = bf16[8,256,256]{2,1,0:T(8,128)(2,1)} fusion(bf16[4,256,256]{2,1,0:T(8,128)(2,1)S(1)} %copy-done.2, bf16[4,256,256]{2,1,0:T(8,128)(2,1)S(1)} %copy-done.3), kind=kLoop, calls=%fused_computation.7 | loop fusion | flops 524288 | bytes 2097152 | tf_op jit(solution)/shard_map/concatenate | solution.py:256
  36.2 1.3 %negate_multiply_fusion.scale_ref = f32[4,256,256]{2,1,0:T(8,128)} fusion(f32[4,256]{1,0:T(4,128)S(1)} %get-tuple-element.61, f32[4,256]{1,0:T(4,128)S(1)} %get-tuple-element.63, f32[4,256]{1,0:T(4,128)S(1)} %get-tuple-element.62, f32[4,256]{1,0:T(4,128)S(1)} %get-tuple-element.60), kind=kLoop, calls=%fused_computation.8 | loop fusion | flops 1310720 | bytes 1064960 | tf_op jit(solution)/shard_map/div | solution.py:57
  37.7 0.4 collective-permute-start.8
  38.2 0.7 copy-done.10
  38.9 0.9 %copy-done.7 = bf16[6,256,256]{2,1,0:T(8,128)(2,1)} copy-done((bf16[6,256,256]{2,1,0:T(8,128)(2,1)}, bf16[6,256,256]{2,1,0:T(8,128)(2,1)S(1)}, u32[]{:S(2)}) %copy-start.7) | copy-done | bytes 786456
  39.8 5.1 %shard_map.129 = (bf16[4,256,256]{2,1,0:T(8,128)(2,1)}, bf16[4,256,256]{2,1,0:T(8,128)(2,1)}) custom-call(s32[4]{0:T(128)} %broadcast_select_fusion.2.take_ref, bf16[2,256,256]{2,1,0:T(8,128)(2,1)} %own_ref.1, bf16[2,256,256]{2,1,0:T(8,128)(2,1)} %copy-done.10, bf16[6,256,256]{2,1,0:T(8,128)(2,1)} %copy-done.5, bf16[6,256,256]{2,1,0:T(8,128)(2,1)} %copy-done.7, ...), custom_call_target="tpu_custom_call" | custom-call | flops 1207959552 | bytes 2621440 | tf_op jit(solution)/shard_map/pallas_call | solution.py:143
  44.9 9.2 %shard_map.130 = (f32[4,256,256]{2,1,0:T(8,128)}, f32[4,256,256]{2,1,0:T(8,128)}, f32[4,256,256]{2,1,0:T(8,128)}, f32[4,8,128]{2,1,0:T(8,128)}) custom-call(s32[4]{0:T(128)} %and_select_fusion.refs_0_, bf16[4,256,256]{2,1,0:T(8,128)(2,1)} %get-tuple-element.25.refs_1_, bf16[4,256,256]{2,1,0:T(8,128)(2,1)} %get-tuple-element.26.refs_2_, ...), custom_call_target="tpu_custom_call" | custom-call | flops 9663676416 | bytes 12582912 | tf_op jit(solution)/shard_map/pallas_call | solution.py:233
  54.1 9.7 %shard_map.131 = (f32[4,256,256]{2,1,0:T(8,128)}, f32[4,256,256]{2,1,0:T(8,128)}, f32[4,256,256]{2,1,0:T(8,128)}, f32[4,8,128]{2,1,0:T(8,128)}) custom-call(s32[4]{0:T(128)} %and_select_fusion.1.refs_0_, bf16[4,256,256]{2,1,0:T(8,128)(2,1)} %get-tuple-element.25.refs_1_, ...), custom_call_target="tpu_custom_call", output_to_operand_aliasing={{0}: (7, {}), {1}: (8, {}), {2}: (9, {}), {3}: (10, {})} | custom-call | flops 9663676416 | bytes 12582912 | tf_op jit(solution)/shard_map/pallas_call | solution.py:233
  63.8 9.7 %shard_map.132 = (f32[4,256,256]{2,1,0:T(8,128)}, f32[4,256,256]{2,1,0:T(8,128)}, f32[4,256,256]{2,1,0:T(8,128)}, f32[4,8,128]{2,1,0:T(8,128)}) custom-call(s32[4]{0:T(128)} %and_select_fusion.2.refs_0_, bf16[4,256,256]{2,1,0:T(8,128)(2,1)} %get-tuple-element.25.refs_1_, ...), custom_call_target="tpu_custom_call", output_to_operand_aliasing={{0}: (7, {}), {1}: (8, {}), {2}: (9, {}), {3}: (10, {})} | custom-call | flops 9663676416 | bytes 12582912 | tf_op jit(solution)/shard_map/pallas_call | solution.py:233
  73.5 0.8 copy-done.9
  74.3 9.8 %shard_map.133 = (f32[4,256,256]{2,1,0:T(8,128)}, f32[4,256,256]{2,1,0:T(8,128)}, f32[4,256,256]{2,1,0:T(8,128)}, f32[4,8,128]{2,1,0:T(8,128)}) custom-call(s32[4]{0:T(128)} %and_select_fusion.3.refs_0_, bf16[4,256,256]{2,1,0:T(8,128)(2,1)} %get-tuple-element.25.refs_1_, ...), custom_call_target="tpu_custom_call", output_to_operand_aliasing={{0}: (7, {}), {1}: (8, {}), {2}: (9, {}), {3}: (10, {})} | custom-call | flops 9663676416 | bytes 12582912 | tf_op jit(solution)/shard_map/pallas_call | solution.py:233
  84.0 1.3 %slice.68 = f32[4,1,16]{2,1,0:T(1,128)} slice(f32[4,8,128]{2,1,0:T(8,128)} %get-tuple-element.44), slice={[0:4], [0:1], [0:16]} | slice | bytes 512 | tf_op jit(solution)/shard_map/slice | solution.py:275
  (76 shorter events, 1.8 us)
Async XLA Ops:
  0.6 13.9 %copy-start = (s32[16]{0:T(128)S(1)}, s32[16]{0:T(128)}, u32[]{:S(2)}) copy-start(s32[16]{0:T(128)} %param.18) | copy-start | bytes 196
  1.7 4.3 %copy-start.4 = (bf16[2,256,256]{2,1,0:T(8,128)(2,1)S(1)}, bf16[2,256,256]{2,1,0:T(8,128)(2,1)}, u32[]{:S(2)}) copy-start(bf16[2,256,256]{2,1,0:T(8,128)(2,1)} %own_ref.1) | copy-start | bytes 786436
  1.8 35.7 %collective-permute-start.9 = (bf16[4,256,256]{2,1,0:T(8,128)(2,1)S(1)}, bf16[4,256,256]{2,1,0:T(8,128)(2,1)}, u32[]{:S(2)}, u32[]{:S(2)}) collective-permute-start(bf16[4,256,256]{2,1,0:T(8,128)(2,1)S(1)} %pad_maximum_fusion.1), channel_id=1, source_target_pairs={{0,8},{8,0},{16,24},{24,16},{1,9},{9,1},{17,25},{25,17},{2,10},{10... | collective-permute-start | bytes 1572872 | tf_op jit(solution)/shard_map/ppermute | solution.py:264
  3.1 34.6 %collective-permute-start.7 = (bf16[4,256,256]{2,1,0:T(8,128)(2,1)S(1)}, bf16[4,256,256]{2,1,0:T(8,128)(2,1)S(1)}, u32[]{:S(2)}, u32[]{:S(2)}) collective-permute-start(bf16[4,256,256]{2,1,0:T(8,128)(2,1)S(1)} %pad_maximum_fusion.1), channel_id=1, source_target_pairs={{0,16},{8,24},{16,0},{24,8},{1,17},{9,25},{17,1},{25,9},{2,18},{10... | collective-permute-start | bytes 1572872 | tf_op jit(solution)/shard_map/ppermute | solution.py:264
  4.3 0.7 copy-start.6
  6.9 11.5 %collective-permute-start.1 = (bf16[2,256,256]{2,1,0:T(8,128)(2,1)S(1)}, bf16[2,256,256]{2,1,0:T(8,128)(2,1)S(1)}, u32[]{:S(2)}, u32[]{:S(2)}) collective-permute-start(bf16[2,256,256]{2,1,0:T(8,128)(2,1)S(1)} %get-tuple-element.54), channel_id=1, source_target_pairs={{0,2},{1,3},{2,0},{3,1},{4,6},{5,7},{6,4},{7,5},{8,10},{9,11},{10,... | collective-permute-start | bytes 786440 | tf_op jit(solution)/shard_map/ppermute | solution.py:87
  7.2 13.1 %collective-permute-start.2 = (bf16[2,256,256]{2,1,0:T(8,128)(2,1)S(1)}, bf16[2,256,256]{2,1,0:T(8,128)(2,1)S(1)}, u32[]{:S(2)}, u32[]{:S(2)}) collective-permute-start(bf16[2,256,256]{2,1,0:T(8,128)(2,1)S(1)} %get-tuple-element.53), channel_id=1, source_target_pairs={{0,4},{1,5},{2,6},{3,7},{4,0},{5,1},{6,2},{7,3},{8,12},{9,13},{10,... | collective-permute-start | bytes 786440 | tf_op jit(solution)/shard_map/ppermute | solution.py:87
  9.5 22.0 %collective-permute-start.3 = (bf16[2,256,256]{2,1,0:T(8,128)(2,1)S(1)}, bf16[2,256,256]{2,1,0:T(8,128)(2,1)S(1)}, u32[]{:S(2)}, u32[]{:S(2)}) collective-permute-start(bf16[2,256,256]{2,1,0:T(8,128)(2,1)S(1)} %get-tuple-element.52), channel_id=1, source_target_pairs={{0,6},{1,7},{2,4},{3,5},{4,2},{5,3},{6,0},{7,1},{8,14},{9,15},{10,... | collective-permute-start | bytes 786440 | tf_op jit(solution)/shard_map/ppermute | solution.py:87
  10.3 0.7 copy-start.11
  11.8 0.7 copy-start.1
  18.4 19.6 %collective-permute-start.5 = (bf16[4,256,256]{2,1,0:T(8,128)(2,1)S(1)}, bf16[4,256,256]{2,1,0:T(8,128)(2,1)}, u32[]{:S(2)}, u32[]{:S(2)}) collective-permute-start(bf16[4,256,256]{2,1,0:T(8,128)(2,1)S(1)} %pad_maximum_fusion.1), channel_id=1, source_target_pairs={{0,24},{8,16},{16,8},{24,0},{1,25},{9,17},{17,9},{25,1},{2,26},{10... | collective-permute-start | bytes 1572872 | tf_op jit(solution)/shard_map/ppermute | solution.py:264
  20.2 14.9 %copy-start.2 = (bf16[4,256,256]{2,1,0:T(8,128)(2,1)S(1)}, bf16[4,256,256]{2,1,0:T(8,128)(2,1)}, u32[]{:S(2)}) copy-start(bf16[4,256,256]{2,1,0:T(8,128)(2,1)} %param.17) | copy-start | bytes 1572868
  20.2 14.9 %copy-start.3 = (bf16[4,256,256]{2,1,0:T(8,128)(2,1)S(1)}, bf16[4,256,256]{2,1,0:T(8,128)(2,1)}, u32[]{:S(2)}) copy-start(bf16[4,256,256]{2,1,0:T(8,128)(2,1)} %param.16) | copy-start | bytes 1572868
  20.2 17.9 %collective-permute-start = (bf16[2,256,256]{2,1,0:T(8,128)(2,1)S(1)}, bf16[2,256,256]{2,1,0:T(8,128)(2,1)S(1)}, u32[]{:S(2)}, u32[]{:S(2)}) collective-permute-start(bf16[2,256,256]{2,1,0:T(8,128)(2,1)S(1)} %get-tuple-element.55), channel_id=1, source_target_pairs={{0,1},{1,0},{2,3},{3,2},{4,5},{5,4},{6,7},{7,6},{8,9},{9,8},{10,11... | collective-permute-start | bytes 786440 | tf_op jit(solution)/shard_map/ppermute | solution.py:84
  31.5 4.7 %copy-start.5 = (bf16[6,256,256]{2,1,0:T(8,128)(2,1)}, bf16[6,256,256]{2,1,0:T(8,128)(2,1)S(1)}, u32[]{:S(2)}) copy-start(bf16[6,256,256]{2,1,0:T(8,128)(2,1)S(1)} %constant_dynamic-update-slice_fusion.recv_ref) | copy-start | bytes 2359300
  31.6 6.6 %collective-permute-start.4 = (bf16[6,256,256]{2,1,0:T(8,128)(2,1)S(1)}, bf16[6,256,256]{2,1,0:T(8,128)(2,1)S(1)}, u32[]{:S(2)}, u32[]{:S(2)}) collective-permute-start(bf16[6,256,256]{2,1,0:T(8,128)(2,1)S(1)} %constant_dynamic-update-slice_fusion.recv_ref), channel_id=1, source_target_pairs={{0,1},{1,0},{2,3},{3,2},{4,5},{5,4},{6,7},{7,6},{8,9},{9,8},{10,11... | collective-permute-start | bytes 2359304 | tf_op jit(solution)/shard_map/ppermute | solution.py:89
  37.5 16.6 %collective-permute-start.10 = (bf16[4,256,256]{2,1,0:T(8,128)(2,1)}, bf16[4,256,256]{2,1,0:T(8,128)(2,1)}, u32[]{:S(2)}, u32[]{:S(2)}) collective-permute-start(bf16[4,256,256]{2,1,0:T(8,128)(2,1)} %collective-permute-done.9.refs_3_), channel_id=1, source_target_pairs={{0,1},{1,0},{2,3},{3,2},{4,5},{5,4},{6,7},{7,6},{8,9},{9,8},{10,11... | collective-permute-start | bytes 1572872 | tf_op jit(solution)/shard_map/ppermute | solution.py:265
  37.7 7.2 %copy-start.8 = (bf16[4,256,256]{2,1,0:T(8,128)(2,1)}, bf16[4,256,256]{2,1,0:T(8,128)(2,1)S(1)}, u32[]{:S(2)}) copy-start(bf16[4,256,256]{2,1,0:T(8,128)(2,1)S(1)} %collective-permute-done.7.refs_3_) | copy-start | bytes 1572868
  37.7 26.1 %collective-permute-start.8 = (bf16[4,256,256]{2,1,0:T(8,128)(2,1)S(1)}, bf16[4,256,256]{2,1,0:T(8,128)(2,1)}, u32[]{:S(2)}, u32[]{:S(2)}) collective-permute-start(bf16[4,256,256]{2,1,0:T(8,128)(2,1)S(1)} %collective-permute-done.7.refs_3_), channel_id=1, source_target_pairs={{0,1},{1,0},{2,3},{3,2},{4,5},{5,4},{6,7},{7,6},{8,9},{9,8},{10,11... | collective-permute-start | bytes 1572872 | tf_op jit(solution)/shard_map/ppermute | solution.py:265
  38.1 35.4 %collective-permute-start.6 = (bf16[4,256,256]{2,1,0:T(8,128)(2,1)}, bf16[4,256,256]{2,1,0:T(8,128)(2,1)S(1)}, u32[]{:S(2)}, u32[]{:S(2)}) collective-permute-start(bf16[4,256,256]{2,1,0:T(8,128)(2,1)} %collective-permute-done.5.refs_3_), channel_id=1, source_target_pairs={{0,1},{1,0},{2,3},{3,2},{4,5},{5,4},{6,7},{7,6},{8,9},{9,8},{10,11... | collective-permute-start | bytes 1572872 | tf_op jit(solution)/shard_map/ppermute | solution.py:265
  38.2 0.7 copy-start.10
  38.9 0.9 %copy-start.7 = (bf16[6,256,256]{2,1,0:T(8,128)(2,1)}, bf16[6,256,256]{2,1,0:T(8,128)(2,1)S(1)}, u32[]{:S(2)}) copy-start(bf16[6,256,256]{2,1,0:T(8,128)(2,1)S(1)} %collective-permute-done.4.fwd_ref) | copy-start | bytes 2359300
  73.5 0.8 copy-start.9

commit v8 on v7

--- a/solution.py
+++ b/solution.py
@@ -112,43 +112,40 @@
 
 def spectra_kernel(rows, take_ref, own_ref, direct_ref, recv_ref, fwd_ref, scale_ref, half_ref,
                    full_ref, re_ref, im_ref):
-    s = pl.program_id(0)
-    idx = take_ref[s]
     number = own_ref.shape[0]
-    pick_own = own_ref[jnp.clip(idx, 0, number - 1)]
-    pick_direct = direct_ref[jnp.clip(idx - number, 0, number - 1)]
-    pick_recv = recv_ref[jnp.clip(idx - 2 * number, 0, rows - 1)]
-    pick_fwd = fwd_ref[jnp.clip(idx - 2 * number - rows, 0, rows - 1)]
-    zero = jnp.zeros_like(pick_own)
-    image = jnp.where(
-        idx < number, pick_own,
-        jnp.where(idx < 2 * number, pick_direct,
-                  jnp.where(idx < 2 * number + rows, pick_recv,
-                            jnp.where(idx < 2 * number + 2 * rows, pick_fwd, zero))))
-    extent = image.shape[-1]
-    half = jnp.dot(image, half_ref[...], preferred_element_type=jnp.float32).astype(jnp.bfloat16)
-    half_stack = jnp.concatenate([half[:, :extent], half[:, extent:]], axis=0)
-    spec = jnp.dot(full_ref[...], half_stack, preferred_element_type=jnp.float32)
-    scale = scale_ref[0]
-    re_ref[0] = (spec[:extent] * scale).astype(jnp.bfloat16)
-    im_ref[0] = (spec[extent:] * scale).astype(jnp.bfloat16)
+    extent = own_ref.shape[-1]
+    half_table = half_ref[...]
+    full_table = full_ref[...]
+    for s in range(re_ref.shape[0]):
+        idx = take_ref[s]
+        pick_own = own_ref[jnp.clip(idx, 0, number - 1)]
+        pick_direct = direct_ref[jnp.clip(idx - number, 0, number - 1)]
+        pick_recv = recv_ref[jnp.clip(idx - 2 * number, 0, rows - 1)]
+        pick_fwd = fwd_ref[jnp.clip(idx - 2 * number - rows, 0, rows - 1)]
+        zero = jnp.zeros_like(pick_own)
+        image = jnp.where(
+            idx < number, pick_own,
+            jnp.where(idx < 2 * number, pick_direct,
+                      jnp.where(idx < 2 * number + rows, pick_recv,
+                                jnp.where(idx < 2 * number + 2 * rows, pick_fwd, zero))))
+        half = jnp.dot(image, half_table, preferred_element_type=jnp.float32).astype(jnp.bfloat16)
+        half_stack = jnp.concatenate([half[:, :extent], half[:, extent:]], axis=0)
+        spec = jnp.dot(full_table, half_stack, preferred_element_type=jnp.float32)
+        scale = scale_ref[s]
+        re_ref[s] = (spec[:extent] * scale).astype(jnp.bfloat16)
+        im_ref[s] = (spec[extent:] * scale).astype(jnp.bfloat16)
 
 
 def make_spectra(take_idx, own, direct, received, forwarded, scale, half_table, full_table):
     count, extent = (scale.shape[0], scale.shape[-1])
     rows = received.shape[0]
     whole = pl.BlockSpec(memory_space=pltpu.VMEM)
-    plane = pl.BlockSpec((1, extent, extent), lambda s: (s, 0, 0))
     spec_shape = jax.ShapeDtypeStruct((count, extent, extent), jnp.bfloat16)
     return pl.pallas_call(
         functools.partial(spectra_kernel, rows),
-        grid=(count,),
-        in_specs=[pl.BlockSpec(memory_space=pltpu.SMEM), whole, whole, whole, whole, plane,
-                  pl.BlockSpec(half_table.shape, lambda s: (0, 0)),
-                  pl.BlockSpec(full_table.shape, lambda s: (0, 0))],
-        out_specs=[plane, plane],
+        in_specs=[pl.BlockSpec(memory_space=pltpu.SMEM)] + [whole] * 7,
+        out_specs=[whole, whole],
         out_shape=[spec_shape, spec_shape],
-        compiler_params=pltpu.CompilerParams(dimension_semantics=("arbitrary",)),
         cost_estimate=pl.CostEstimate(
             flops=3 * count * 6 * extent * extent * extent, transcendentals=0,
             bytes_accessed=count * 10 * extent * extent),
@@ -173,25 +170,27 @@
     lanes = lax.broadcasted_iota(jnp.int32, peak_ref.shape[1:], 1)
     peak_row = jnp.zeros(peak_ref.shape[1:], jnp.float32) if first else peak_in[0]
     top = total = square = None
-    position = 0
+    prods = []
     for templ_ref, count in zip(templ_refs, counts):
         for t in range(count):
             tr = templ_ref[t].astype(jnp.float32)
             ti = templ_ref[count + t].astype(jnp.float32)
             pre = (sr * tr + si * ti).astype(jnp.bfloat16)
             pim = (si * tr - sr * ti).astype(jnp.bfloat16)
-            prod = jnp.concatenate([pre, pim], axis=1)
-            q = jnp.dot(prod, forward, preferred_element_type=jnp.float32).astype(jnp.bfloat16)
-            q_stack = jnp.concatenate([q[:, :extent], q[:, extent:]], axis=0)
-            corr = jnp.dot(inverse, q_stack, preferred_element_type=jnp.float32)
-            peak_row = jnp.where(lanes == orient_ref[position], jnp.max(corr), peak_row)
-            position += 1
-            if top is None:
-                top, total, square = corr, corr, corr * corr
-            else:
-                top = jnp.maximum(top, corr)
-                total = total + corr
-                square = square + corr * corr
+            prods.append(jnp.concatenate([pre, pim], axis=1))
+    q_all = jnp.dot(jnp.concatenate(prods, axis=0), forward,
+                    preferred_element_type=jnp.float32).astype(jnp.bfloat16)
+    for position in range(len(prods)):
+        q = q_all[position * extent:(position + 1) * extent]
+        q_stack = jnp.concatenate([q[:, :extent], q[:, extent:]], axis=0)
+        corr = jnp.dot(inverse, q_stack, preferred_element_type=jnp.float32)
+        peak_row = jnp.where(lanes == orient_ref[position], jnp.max(corr), peak_row)
+        if top is None:
+            top, total, square = corr, corr, corr * corr
+        else:
+            top = jnp.maximum(top, corr)
+            total = total + corr
+            square = square + corr * corr
     if not first:
         top = jnp.maximum(top_in[0], top)
         total = sum_in[0] + total

time: 85.7 us -> 76.9 us (0.90)
  Pallas kernels: 43.4 us -> 34.5 us
    pallas_call x4, Pallas kernels: 38.3 us -> 30.4 us  [correlate_chunk(): pl.pallas_call(functools.partial(corr_kernel, first, last, counts, orient...]
    pallas_call x1, Pallas kernels: 5.09 us -> 4.12 us  [make_spectra(): pl.pallas_call(functools.partial(spectra_kernel, rows), in_specs=[pl.Bloc...]
  transfers between devices with their start and end apart: 11 -> 11, of which waited for: 2 -> 2; matrix products, arithmetic and copies ran while one was open for 15% -> 17% of each run, Pallas kernels for 39% -> 35%
where the time goes in v8:
time: 76.9 us; the launch traced here: 76.4 us
  Pallas kernels  34.5 us (45%)
  starting transfers between devices  17.5 us (23%)
  local copies, waits for them, and re-layouts  12.7 us (17%)
  other arithmetic  6.88 us (9%)
  waiting for transfers between devices  3.8 us (5%)
  between operations  1.04 us (1%)
    pallas_call x4, Pallas kernels, correlate_chunk(): pl.pallas_call(functools.partial(corr_kernel, first, last, counts, orient...  30.4 us
    ppermute x1, starting transfers between devices, route_patches(): direct = lax.ppermute(outgoing[0], 'patch', xor_pairs(sources, 1))  9.04 us
    unnamed x26, local copies, waits for them, and re-layouts  4.38 us
    pallas_call x1, Pallas kernels, make_spectra(): pl.pallas_call(functools.partial(spectra_kernel, rows), in_specs=[pl.Bloc...  4.12 us
    ppermute x3, waiting for transfers between devices, route_patches(): lax.ppermute(outgoing[m], 'patch', xor_pairs(sources, 2 * m))  3.77 us
    ppermute x3, starting transfers between devices, correlate_all(): got = lax.ppermute(mine, 'blk', [(b, b ^ k) for b in range(blocks)])  2.75 us
    ppermute x3, starting transfers between devices, route_patches(): lax.ppermute(outgoing[m], 'patch', xor_pairs(sources, 2 * m))  2.71 us
    select_n x8, other arithmetic, correlate_all(): orient_chunk = jnp.take(orientation, index)  2.62 us
  transfers between devices with their start and end apart: 11, of which 2 were waited for; matrix products, arithmetic and copies ran while one was open for 17% of the time, Pallas kernels for 35%

profile of v8, /device:TPU:9, one launch (start us, length us, event | category | flops | bytes accessed | tf_op | source)
XLA Modules:
  0.0 76.4 jit_solution(6227086757593952198)
XLA Ops:
  0.7 1.1 %constant_dynamic-slice_fusion = (bf16[2,256,256]{2,1,0:T(8,128)(2,1)S(1)}, bf16[2,256,256]{2,1,0:T(8,128)(2,1)S(1)}) fusion(bf16[4,256,256]{2,1,0:T(8,128)(2,1)} %param.17, s32[]{:T(128)S(6)} %select_n.275, bf16[4,256,256]{2,1,0:T(8,128)(2,1)} %param.16), kind=kLoop, calls=%fused_computation.50 | loop fusion | bytes 1048580 | tf_op jit(solution)/shard_map/dynamic_slice | solution.py:258
  1.8 1.3 %collective-permute-start.9 = (bf16[4,256,256]{2,1,0:T(8,128)(2,1)S(1)}, bf16[4,256,256]{2,1,0:T(8,128)(2,1)}, u32[]{:S(2)}, u32[]{:S(2)}) collective-permute-start(bf16[4,256,256]{2,1,0:T(8,128)(2,1)S(1)} %pad_maximum_fusion.1), channel_id=1, source_target_pairs={{0,8},{8,0},{16,24},{24,16},{1,9},{9,1},{17,25},{25,17},{2,10},{10... | collective-permute-start | bytes 1572872 | tf_op jit(solution)/shard_map/ppermute | solution.py:263
  3.1 1.2 %collective-permute-start.7 = (bf16[4,256,256]{2,1,0:T(8,128)(2,1)S(1)}, bf16[4,256,256]{2,1,0:T(8,128)(2,1)S(1)}, u32[]{:S(2)}, u32[]{:S(2)}) collective-permute-start(bf16[4,256,256]{2,1,0:T(8,128)(2,1)S(1)} %pad_maximum_fusion.1), channel_id=1, source_target_pairs={{0,16},{8,24},{16,0},{24,8},{1,17},{9,25},{17,1},{25,9},{2,18},{10... | collective-permute-start | bytes 1572872 | tf_op jit(solution)/shard_map/ppermute | solution.py:263
  4.3 0.7 copy-done.6
  5.1 0.1 copy.43
  5.3 0.1 copy.44
  5.7 0.1 copy.47
  6.1 0.6 gather_fusion
  6.7 0.2 broadcast_select_fusion
  6.9 0.2 collective-permute-start.1
  7.2 2.3 %collective-permute-start.2 = (bf16[2,256,256]{2,1,0:T(8,128)(2,1)S(1)}, bf16[2,256,256]{2,1,0:T(8,128)(2,1)S(1)}, u32[]{:S(2)}, u32[]{:S(2)}) collective-permute-start(bf16[2,256,256]{2,1,0:T(8,128)(2,1)S(1)} %get-tuple-element.53), channel_id=1, source_target_pairs={{0,4},{1,5},{2,6},{3,7},{4,0},{5,1},{6,2},{7,3},{8,12},{9,13},{10,... | collective-permute-start | bytes 786440 | tf_op jit(solution)/shard_map/ppermute | solution.py:87
  9.5 0.2 collective-permute-start.3
  9.8 0.1 reduce
  9.9 0.1 fusion.6
  10.0 0.1 select_reduce_fusion.1
  10.3 0.6 copy-done.11
  11.0 0.6 gather_fusion.1
  11.8 0.7 copy-done.1
  12.4 0.6 gather_fusion.2
  13.1 0.4 fusion.13
  13.7 0.2 select_reduce_fusion
  13.8 0.5 broadcast_select_fusion.2.take_ref
  14.5 0.6 gather_fusion.6
  15.1 0.6 and_select_fusion.refs_0_
  15.7 0.6 gather_fusion.5
  16.3 0.6 and_select_fusion.1.refs_0_
  16.9 0.1 fusion.1
  17.2 0.6 gather_fusion.4
  17.8 0.6 gather_fusion.3
  18.4 0.2 collective-permute-start.5
  18.7 1.6 %collective-permute-done.2 = bf16[2,256,256]{2,1,0:T(8,128)(2,1)S(1)} collective-permute-done((bf16[2,256,256]{2,1,0:T(8,128)(2,1)S(1)}, bf16[2,256,256]{2,1,0:T(8,128)(2,1)S(1)}, u32[]{:S(2)}, u32[]{:S(2)}) %collective-permute-start.2) | collective-permute-done | bytes 262176 | tf_op jit(solution)/shard_map/ppermute | solution.py:87
  20.2 9.0 %collective-permute-start = (bf16[2,256,256]{2,1,0:T(8,128)(2,1)S(1)}, bf16[2,256,256]{2,1,0:T(8,128)(2,1)S(1)}, u32[]{:S(2)}, u32[]{:S(2)}) collective-permute-start(bf16[2,256,256]{2,1,0:T(8,128)(2,1)S(1)} %get-tuple-element.55), channel_id=1, source_target_pairs={{0,1},{1,0},{2,3},{3,2},{4,5},{5,4},{6,7},{7,6},{8,9},{9,8},{10,11... | collective-permute-start | bytes 786440 | tf_op jit(solution)/shard_map/ppermute | solution.py:84
  29.3 2.2 %collective-permute-done.3 = bf16[2,256,256]{2,1,0:T(8,128)(2,1)S(1)} collective-permute-done((bf16[2,256,256]{2,1,0:T(8,128)(2,1)S(1)}, bf16[2,256,256]{2,1,0:T(8,128)(2,1)S(1)}, u32[]{:S(2)}, u32[]{:S(2)}) %collective-permute-start.3) | collective-permute-done | bytes 262176 | tf_op jit(solution)/shard_map/ppermute | solution.py:87
  31.6 2.4 %collective-permute-start.4 = (bf16[6,256,256]{2,1,0:T(8,128)(2,1)S(1)}, bf16[6,256,256]{2,1,0:T(8,128)(2,1)S(1)}, u32[]{:S(2)}, u32[]{:S(2)}) collective-permute-start(bf16[6,256,256]{2,1,0:T(8,128)(2,1)S(1)} %constant_dynamic-update-slice_fusion.recv_ref), channel_id=1, source_target_pairs={{0,1},{1,0},{2,3},{3,2},{4,5},{5,4},{6,7},{7,6},{8,9},{9,8},{10,11... | collective-permute-start | bytes 2359304 | tf_op jit(solution)/shard_map/ppermute | solution.py:89
  33.9 0.7 and_select_fusion.2.refs_0_
  34.6 0.6 and_select_fusion.3.refs_0_
  35.2 1.1 %pad_maximum_fusion.refs_3_ = bf16[8,256,256]{2,1,0:T(8,128)(2,1)} fusion(bf16[4,256,256]{2,1,0:T(8,128)(2,1)S(1)} %copy-done.2, bf16[4,256,256]{2,1,0:T(8,128)(2,1)S(1)} %copy-done.3), kind=kLoop, calls=%fused_computation.7 | loop fusion | flops 524288 | bytes 2097152 | tf_op jit(solution)/shard_map/concatenate | solution.py:255
  36.2 1.3 %negate_multiply_fusion.scale_ref = f32[4,256,256]{2,1,0:T(8,128)} fusion(f32[4,256]{1,0:T(4,128)S(1)} %get-tuple-element.61, f32[4,256]{1,0:T(4,128)S(1)} %get-tuple-element.63, f32[4,256]{1,0:T(4,128)S(1)} %get-tuple-element.62, f32[4,256]{1,0:T(4,128)S(1)} %get-tuple-element.60), kind=kLoop, calls=%fused_computation.8 | loop fusion | flops 1310720 | bytes 1064960 | tf_op jit(solution)/shard_map/div | solution.py:57
  37.7 0.4 collective-permute-start.8
  38.2 0.7 copy-done.10
  38.9 0.9 %copy-done.7 = bf16[6,256,256]{2,1,0:T(8,128)(2,1)} copy-done((bf16[6,256,256]{2,1,0:T(8,128)(2,1)}, bf16[6,256,256]{2,1,0:T(8,128)(2,1)S(1)}, u32[]{:S(2)}) %copy-start.7) | copy-done | bytes 786456
  39.8 4.1 %shard_map.129 = (bf16[4,256,256]{2,1,0:T(8,128)(2,1)}, bf16[4,256,256]{2,1,0:T(8,128)(2,1)}) custom-call(s32[4]{0:T(128)} %broadcast_select_fusion.2.take_ref, bf16[2,256,256]{2,1,0:T(8,128)(2,1)} %own_ref.1, bf16[2,256,256]{2,1,0:T(8,128)(2,1)} %copy-done.10, bf16[6,256,256]{2,1,0:T(8,128)(2,1)} %copy-done.5, bf16[6,256,256]{2,1,0:T(8,128)(2,1)} %copy-done.7, ...), custom_call_target="tpu_custom_call" | custom-call | flops 1207959552 | bytes 2621440 | tf_op jit(solution)/shard_map/pallas_call | solution.py:144
  43.9 7.1 %shard_map.130 = (f32[4,256,256]{2,1,0:T(8,128)}, f32[4,256,256]{2,1,0:T(8,128)}, f32[4,256,256]{2,1,0:T(8,128)}, f32[4,8,128]{2,1,0:T(8,128)}) custom-call(s32[4]{0:T(128)} %and_select_fusion.refs_0_, bf16[4,256,256]{2,1,0:T(8,128)(2,1)} %get-tuple-element.25.refs_1_, bf16[4,256,256]{2,1,0:T(8,128)(2,1)} %get-tuple-element.26.refs_2_, ...), custom_call_target="tpu_custom_call" | custom-call | flops 9663676416 | bytes 12582912 | tf_op jit(solution)/shard_map/pallas_call | solution.py:232
  51.0 7.7 %shard_map.131 = (f32[4,256,256]{2,1,0:T(8,128)}, f32[4,256,256]{2,1,0:T(8,128)}, f32[4,256,256]{2,1,0:T(8,128)}, f32[4,8,128]{2,1,0:T(8,128)}) custom-call(s32[4]{0:T(128)} %and_select_fusion.1.refs_0_, bf16[4,256,256]{2,1,0:T(8,128)(2,1)} %get-tuple-element.25.refs_1_, ...), custom_call_target="tpu_custom_call", output_to_operand_aliasing={{0}: (7, {}), {1}: (8, {}), {2}: (9, {}), {3}: (10, {})} | custom-call | flops 9663676416 | bytes 12582912 | tf_op jit(solution)/shard_map/pallas_call | solution.py:232
  58.8 7.7 %shard_map.132 = (f32[4,256,256]{2,1,0:T(8,128)}, f32[4,256,256]{2,1,0:T(8,128)}, f32[4,256,256]{2,1,0:T(8,128)}, f32[4,8,128]{2,1,0:T(8,128)}) custom-call(s32[4]{0:T(128)} %and_select_fusion.2.refs_0_, bf16[4,256,256]{2,1,0:T(8,128)(2,1)} %get-tuple-element.25.refs_1_, ...), custom_call_target="tpu_custom_call", output_to_operand_aliasing={{0}: (7, {}), {1}: (8, {}), {2}: (9, {}), {3}: (10, {})} | custom-call | flops 9663676416 | bytes 12582912 | tf_op jit(solution)/shard_map/pallas_call | solution.py:232
  66.5 0.8 %copy-done.9 = bf16[4,256,256]{2,1,0:T(8,128)(2,1)} copy-done((bf16[4,256,256]{2,1,0:T(8,128)(2,1)}, bf16[4,256,256]{2,1,0:T(8,128)(2,1)S(1)}, u32[]{:S(2)}) %copy-start.9) | copy-done | bytes 524312
  67.3 7.8 %shard_map.133 = (f32[4,256,256]{2,1,0:T(8,128)}, f32[4,256,256]{2,1,0:T(8,128)}, f32[4,256,256]{2,1,0:T(8,128)}, f32[4,8,128]{2,1,0:T(8,128)}) custom-call(s32[4]{0:T(128)} %and_select_fusion.3.refs_0_, bf16[4,256,256]{2,1,0:T(8,128)(2,1)} %get-tuple-element.25.refs_1_, ...), custom_call_target="tpu_custom_call", output_to_operand_aliasing={{0}: (7, {}), {1}: (8, {}), {2}: (9, {}), {3}: (10, {})} | custom-call | flops 9663676416 | bytes 12582912 | tf_op jit(solution)/shard_map/pallas_call | solution.py:232
  75.1 1.3 %slice.68 = f32[4,1,16]{2,1,0:T(1,128)} slice(f32[4,8,128]{2,1,0:T(8,128)} %get-tuple-element.44), slice={[0:4], [0:1], [0:16]} | slice | bytes 512 | tf_op jit(solution)/shard_map/slice | solution.py:274
  (76 shorter events, 1.8 us)
Async XLA Ops:
  0.6 13.9 %copy-start = (s32[16]{0:T(128)S(1)}, s32[16]{0:T(128)}, u32[]{:S(2)}) copy-start(s32[16]{0:T(128)} %param.18) | copy-start | bytes 196
  1.7 4.3 %copy-start.4 = (bf16[2,256,256]{2,1,0:T(8,128)(2,1)S(1)}, bf16[2,256,256]{2,1,0:T(8,128)(2,1)}, u32[]{:S(2)}) copy-start(bf16[2,256,256]{2,1,0:T(8,128)(2,1)} %own_ref.1) | copy-start | bytes 786436
  1.8 35.7 %collective-permute-start.9 = (bf16[4,256,256]{2,1,0:T(8,128)(2,1)S(1)}, bf16[4,256,256]{2,1,0:T(8,128)(2,1)}, u32[]{:S(2)}, u32[]{:S(2)}) collective-permute-start(bf16[4,256,256]{2,1,0:T(8,128)(2,1)S(1)} %pad_maximum_fusion.1), channel_id=1, source_target_pairs={{0,8},{8,0},{16,24},{24,16},{1,9},{9,1},{17,25},{25,17},{2,10},{10... | collective-permute-start | bytes 1572872 | tf_op jit(solution)/shard_map/ppermute | solution.py:263
  3.1 34.6 %collective-permute-start.7 = (bf16[4,256,256]{2,1,0:T(8,128)(2,1)S(1)}, bf16[4,256,256]{2,1,0:T(8,128)(2,1)S(1)}, u32[]{:S(2)}, u32[]{:S(2)}) collective-permute-start(bf16[4,256,256]{2,1,0:T(8,128)(2,1)S(1)} %pad_maximum_fusion.1), channel_id=1, source_target_pairs={{0,16},{8,24},{16,0},{24,8},{1,17},{9,25},{17,1},{25,9},{2,18},{10... | collective-permute-start | bytes 1572872 | tf_op jit(solution)/shard_map/ppermute | solution.py:263
  4.3 0.7 copy-start.6
  6.9 11.5 %collective-permute-start.1 = (bf16[2,256,256]{2,1,0:T(8,128)(2,1)S(1)}, bf16[2,256,256]{2,1,0:T(8,128)(2,1)S(1)}, u32[]{:S(2)}, u32[]{:S(2)}) collective-permute-start(bf16[2,256,256]{2,1,0:T(8,128)(2,1)S(1)} %get-tuple-element.54), channel_id=1, source_target_pairs={{0,2},{1,3},{2,0},{3,1},{4,6},{5,7},{6,4},{7,5},{8,10},{9,11},{10,... | collective-permute-start | bytes 786440 | tf_op jit(solution)/shard_map/ppermute | solution.py:87
  7.2 13.1 %collective-permute-start.2 = (bf16[2,256,256]{2,1,0:T(8,128)(2,1)S(1)}, bf16[2,256,256]{2,1,0:T(8,128)(2,1)S(1)}, u32[]{:S(2)}, u32[]{:S(2)}) collective-permute-start(bf16[2,256,256]{2,1,0:T(8,128)(2,1)S(1)} %get-tuple-element.53), channel_id=1, source_target_pairs={{0,4},{1,5},{2,6},{3,7},{4,0},{5,1},{6,2},{7,3},{8,12},{9,13},{10,... | collective-permute-start | bytes 786440 | tf_op jit(solution)/shard_map/ppermute | solution.py:87
  9.5 22.0 %collective-permute-start.3 = (bf16[2,256,256]{2,1,0:T(8,128)(2,1)S(1)}, bf16[2,256,256]{2,1,0:T(8,128)(2,1)S(1)}, u32[]{:S(2)}, u32[]{:S(2)}) collective-permute-start(bf16[2,256,256]{2,1,0:T(8,128)(2,1)S(1)} %get-tuple-element.52), channel_id=1, source_target_pairs={{0,6},{1,7},{2,4},{3,5},{4,2},{5,3},{6,0},{7,1},{8,14},{9,15},{10,... | collective-permute-start | bytes 786440 | tf_op jit(solution)/shard_map/ppermute | solution.py:87
  10.3 0.7 copy-start.11
  11.8 0.7 copy-start.1
  18.4 19.6 %collective-permute-start.5 = (bf16[4,256,256]{2,1,0:T(8,128)(2,1)S(1)}, bf16[4,256,256]{2,1,0:T(8,128)(2,1)}, u32[]{:S(2)}, u32[]{:S(2)}) collective-permute-start(bf16[4,256,256]{2,1,0:T(8,128)(2,1)S(1)} %pad_maximum_fusion.1), channel_id=1, source_target_pairs={{0,24},{8,16},{16,8},{24,0},{1,25},{9,17},{17,9},{25,1},{2,26},{10... | collective-permute-start | bytes 1572872 | tf_op jit(solution)/shard_map/ppermute | solution.py:263
  20.2 14.9 %copy-start.2 = (bf16[4,256,256]{2,1,0:T(8,128)(2,1)S(1)}, bf16[4,256,256]{2,1,0:T(8,128)(2,1)}, u32[]{:S(2)}) copy-start(bf16[4,256,256]{2,1,0:T(8,128)(2,1)} %param.17) | copy-start | bytes 1572868
  20.2 14.9 %copy-start.3 = (bf16[4,256,256]{2,1,0:T(8,128)(2,1)S(1)}, bf16[4,256,256]{2,1,0:T(8,128)(2,1)}, u32[]{:S(2)}) copy-start(bf16[4,256,256]{2,1,0:T(8,128)(2,1)} %param.16) | copy-start | bytes 1572868
  20.2 17.9 %collective-permute-start = (bf16[2,256,256]{2,1,0:T(8,128)(2,1)S(1)}, bf16[2,256,256]{2,1,0:T(8,128)(2,1)S(1)}, u32[]{:S(2)}, u32[]{:S(2)}) collective-permute-start(bf16[2,256,256]{2,1,0:T(8,128)(2,1)S(1)} %get-tuple-element.55), channel_id=1, source_target_pairs={{0,1},{1,0},{2,3},{3,2},{4,5},{5,4},{6,7},{7,6},{8,9},{9,8},{10,11... | collective-permute-start | bytes 786440 | tf_op jit(solution)/shard_map/ppermute | solution.py:84
  31.5 4.7 %copy-start.5 = (bf16[6,256,256]{2,1,0:T(8,128)(2,1)}, bf16[6,256,256]{2,1,0:T(8,128)(2,1)S(1)}, u32[]{:S(2)}) copy-start(bf16[6,256,256]{2,1,0:T(8,128)(2,1)S(1)} %constant_dynamic-update-slice_fusion.recv_ref) | copy-start | bytes 2359300
  31.6 6.6 %collective-permute-start.4 = (bf16[6,256,256]{2,1,0:T(8,128)(2,1)S(1)}, bf16[6,256,256]{2,1,0:T(8,128)(2,1)S(1)}, u32[]{:S(2)}, u32[]{:S(2)}) collective-permute-start(bf16[6,256,256]{2,1,0:T(8,128)(2,1)S(1)} %constant_dynamic-update-slice_fusion.recv_ref), channel_id=1, source_target_pairs={{0,1},{1,0},{2,3},{3,2},{4,5},{5,4},{6,7},{7,6},{8,9},{9,8},{10,11... | collective-permute-start | bytes 2359304 | tf_op jit(solution)/shard_map/ppermute | solution.py:89
  37.5 13.5 %collective-permute-start.10 = (bf16[4,256,256]{2,1,0:T(8,128)(2,1)}, bf16[4,256,256]{2,1,0:T(8,128)(2,1)}, u32[]{:S(2)}, u32[]{:S(2)}) collective-permute-start(bf16[4,256,256]{2,1,0:T(8,128)(2,1)} %collective-permute-done.9.refs_3_), channel_id=1, source_target_pairs={{0,1},{1,0},{2,3},{3,2},{4,5},{5,4},{6,7},{7,6},{8,9},{9,8},{10,11... | collective-permute-start | bytes 1572872 | tf_op jit(solution)/shard_map/ppermute | solution.py:264
  37.7 6.2 %copy-start.8 = (bf16[4,256,256]{2,1,0:T(8,128)(2,1)}, bf16[4,256,256]{2,1,0:T(8,128)(2,1)S(1)}, u32[]{:S(2)}) copy-start(bf16[4,256,256]{2,1,0:T(8,128)(2,1)S(1)} %collective-permute-done.7.refs_3_) | copy-start | bytes 1572868
  37.7 21.1 %collective-permute-start.8 = (bf16[4,256,256]{2,1,0:T(8,128)(2,1)S(1)}, bf16[4,256,256]{2,1,0:T(8,128)(2,1)}, u32[]{:S(2)}, u32[]{:S(2)}) collective-permute-start(bf16[4,256,256]{2,1,0:T(8,128)(2,1)S(1)} %collective-permute-done.7.refs_3_), channel_id=1, source_target_pairs={{0,1},{1,0},{2,3},{3,2},{4,5},{5,4},{6,7},{7,6},{8,9},{9,8},{10,11... | collective-permute-start | bytes 1572872 | tf_op jit(solution)/shard_map/ppermute | solution.py:264
  38.1 28.4 %collective-permute-start.6 = (bf16[4,256,256]{2,1,0:T(8,128)(2,1)}, bf16[4,256,256]{2,1,0:T(8,128)(2,1)S(1)}, u32[]{:S(2)}, u32[]{:S(2)}) collective-permute-start(bf16[4,256,256]{2,1,0:T(8,128)(2,1)} %collective-permute-done.5.refs_3_), channel_id=1, source_target_pairs={{0,1},{1,0},{2,3},{3,2},{4,5},{5,4},{6,7},{7,6},{8,9},{9,8},{10,11... | collective-permute-start | bytes 1572872 | tf_op jit(solution)/shard_map/ppermute | solution.py:264
  38.2 0.7 copy-start.10
  38.9 0.9 %copy-start.7 = (bf16[6,256,256]{2,1,0:T(8,128)(2,1)}, bf16[6,256,256]{2,1,0:T(8,128)(2,1)S(1)}, u32[]{:S(2)}) copy-start(bf16[6,256,256]{2,1,0:T(8,128)(2,1)S(1)} %collective-permute-done.4.fwd_ref) | copy-start | bytes 2359300
  66.5 0.8 %copy-start.9 = (bf16[4,256,256]{2,1,0:T(8,128)(2,1)}, bf16[4,256,256]{2,1,0:T(8,128)(2,1)S(1)}, u32[]{:S(2)}) copy-start(bf16[4,256,256]{2,1,0:T(8,128)(2,1)S(1)} %collective-permute-done.6.refs_4_) | copy-start | bytes 1572868

commit v9 on v8

--- a/solution.py
+++ b/solution.py
@@ -110,24 +110,40 @@
     return take_idx, pieces, jnp.where(present, slot_pid, sources * number), outgoing
 
 
-def spectra_kernel(rows, take_ref, own_ref, direct_ref, recv_ref, fwd_ref, scale_ref, half_ref,
-                   full_ref, re_ref, im_ref):
-    number = own_ref.shape[0]
-    extent = own_ref.shape[-1]
+def spectra_kernel(rows, take_ref, own_hbm, direct_hbm, recv_hbm, fwd_hbm, scale_ref, half_ref,
+                   full_ref, re_ref, im_ref, buf, sems):
+    number = own_hbm.shape[0]
+    extent = own_hbm.shape[-1]
+    count = re_ref.shape[0]
+    pieces = ((own_hbm, 0, number), (direct_hbm, number, number),
+              (recv_hbm, 2 * number, rows), (fwd_hbm, 2 * number + rows, rows))
+    limit = 2 * number + 2 * rows
+
+    def copies(s):
+        idx = take_ref[s]
+        found = []
+        for piece, base, size in pieces:
+            inside = (idx >= base) & (idx < base + size)
+            local = jnp.clip(idx - base, 0, size - 1)
+            found.append((inside, pltpu.make_async_copy(piece.at[local], buf.at[s], sems.at[s])))
+        return idx, found
+
+    for s in range(count):
+        idx, found = copies(s)
+        for inside, copy in found:
+            pl.when(inside)(copy.start)
+
+        @pl.when(idx >= limit)
+        def _():
+            buf[s] = jnp.zeros((extent, extent), buf.dtype)
+
     half_table = half_ref[...]
     full_table = full_ref[...]
-    for s in range(re_ref.shape[0]):
-        idx = take_ref[s]
-        pick_own = own_ref[jnp.clip(idx, 0, number - 1)]
-        pick_direct = direct_ref[jnp.clip(idx - number, 0, number - 1)]
-        pick_recv = recv_ref[jnp.clip(idx - 2 * number, 0, rows - 1)]
-        pick_fwd = fwd_ref[jnp.clip(idx - 2 * number - rows, 0, rows - 1)]
-        zero = jnp.zeros_like(pick_own)
-        image = jnp.where(
-            idx < number, pick_own,
-            jnp.where(idx < 2 * number, pick_direct,
-                      jnp.where(idx < 2 * number + rows, pick_recv,
-                                jnp.where(idx < 2 * number + 2 * rows, pick_fwd, zero))))
+    for s in range(count):
+        idx, found = copies(s)
+        for inside, copy in found:
+            pl.when(inside)(copy.wait)
+        image = buf[s]
         half = jnp.dot(image, half_table, preferred_element_type=jnp.float32).astype(jnp.bfloat16)
         half_stack = jnp.concatenate([half[:, :extent], half[:, extent:]], axis=0)
         spec = jnp.dot(full_table, half_stack, preferred_element_type=jnp.float32)
@@ -140,12 +156,15 @@
     count, extent = (scale.shape[0], scale.shape[-1])
     rows = received.shape[0]
     whole = pl.BlockSpec(memory_space=pltpu.VMEM)
+    far = pl.BlockSpec(memory_space=pl.ANY)
     spec_shape = jax.ShapeDtypeStruct((count, extent, extent), jnp.bfloat16)
     return pl.pallas_call(
         functools.partial(spectra_kernel, rows),
-        in_specs=[pl.BlockSpec(memory_space=pltpu.SMEM)] + [whole] * 7,
+        in_specs=[pl.BlockSpec(memory_space=pltpu.SMEM), far, far, far, far, whole, whole, whole],
         out_specs=[whole, whole],
         out_shape=[spec_shape, spec_shape],
+        scratch_shapes=[pltpu.VMEM((count, extent, extent), own.dtype),
+                        pltpu.SemaphoreType.DMA((count,))],
         cost_estimate=pl.CostEstimate(
             flops=3 * count * 6 * extent * extent * extent, transcendentals=0,
             bytes_accessed=count * 10 * extent * extent),
@@ -167,8 +186,9 @@
     si = si_ref[0].astype(jnp.float32)
     forward = fw_ref[...]
     inverse = inv_ref[...]
-    lanes = lax.broadcasted_iota(jnp.int32, peak_ref.shape[1:], 1)
-    peak_row = jnp.zeros(peak_ref.shape[1:], jnp.float32) if first else peak_in[0]
+    row_shape = (8, 128 * ((orient_total + 127) // 128))
+    lanes = lax.broadcasted_iota(jnp.int32, row_shape, 1)
+    peak_row = jnp.zeros(row_shape, jnp.float32) if first else peak_in[0]
     top = total = square = None
     prods = []
     for templ_ref, count in zip(templ_refs, counts):
@@ -196,7 +216,11 @@
         total = sum_in[0] + total
         square = sq_in[0] + square
     top_ref[0] = top
-    peak_ref[0] = peak_row
+    if last:
+        s = pl.program_id(0)
+        peak_ref[pl.ds(s, 1), :] = peak_row[0:1, :orient_total]
+    else:
+        peak_ref[0] = peak_row
     if last:
         mean = total / orient_total
         sum_ref[0] = mean
@@ -226,16 +250,20 @@
         base = len(operands)
         in_specs += [plane, plane, plane, peak_spec]
         operands += list(stats)
-        aliases = {base: 0, base + 1: 1, base + 2: 2, base + 3: 3}
+        aliases = {base: 0, base + 1: 1, base + 2: 2}
+        if not last:
+            aliases[base + 3] = 3
     map_shape = jax.ShapeDtypeStruct((count, extent, extent), jnp.float32)
     flops = 3 * tiles * count * 12 * extent * extent * extent
     return pl.pallas_call(
         functools.partial(corr_kernel, first, last, counts, orient_total),
         grid=(count,),
         in_specs=in_specs,
-        out_specs=[plane, plane, plane, peak_spec],
+        out_specs=[plane, plane, plane,
+                   pl.BlockSpec((count, orient_total), lambda s: (0, 0)) if last else peak_spec],
         out_shape=[map_shape, map_shape, map_shape,
-                   jax.ShapeDtypeStruct((count, 8, lanes), jnp.float32)],
+                   jax.ShapeDtypeStruct((count, orient_total) if last else (count, 8, lanes),
+                                        jnp.float32)],
         input_output_aliases=aliases,
         compiler_params=pltpu.CompilerParams(dimension_semantics=("arbitrary",)),
         cost_estimate=pl.CostEstimate(
@@ -271,7 +299,7 @@
         stats = correlate_chunk(spec_re, spec_im, groups, forward, inverse, orient_chunk,
                                 orient_total, stats, n == len(chunks) - 1)
     top_map, mean_map, var_map, peak = stats
-    return (top_map, mean_map, var_map, peak[:, 0, :orient_total])
+    return (top_map, mean_map, var_map, peak)
 
 
 def body(patches, owner_of_patch, group_of_patch, defocus, templ_re, templ_im, orientation):

time: 76.9 us -> 77.2 us (level)
  Pallas kernels: 34.5 us -> 36.1 us
  local copies, waits for them, and re-layouts: 12.7 us -> 11.4 us
    pallas_call x1, Pallas kernels: 4.12 us -> 5.73 us  [make_spectra(): pl.pallas_call(functools.partial(spectra_kernel, rows), in_specs=[pl.Bloc...]
    slice x1 -> x0, local copies, waits for them, and re-layouts: 1.3 us -> none  [correlate_all(): return (top_map, mean_map, var_map, peak[:, 0, :orient_total])]
  transfers between devices with their start and end apart: 11 -> 11, of which waited for: 2 -> 2; matrix products, arithmetic and copies ran while one was open for 17% -> 17% of each run, Pallas kernels for 35% -> 37%
where the time goes in v9:
time: 77.2 us; the launch traced here: 76.7 us
  Pallas kernels  36.1 us (47%)
  starting transfers between devices  17.5 us (23%)
  local copies, waits for them, and re-layouts  11.4 us (15%)
  other arithmetic  6.85 us (9%)
  waiting for transfers between devices  3.82 us (5%)
  between operations  1.06 us (1%)
    pallas_call x4, Pallas kernels, correlate_chunk(): pl.pallas_call(functools.partial(corr_kernel, first, last, counts, orient...  30.4 us
    ppermute x1, starting transfers between devices, route_patches(): direct = lax.ppermute(outgoing[0], 'patch', xor_pairs(sources, 1))  9.04 us
    pallas_call x1, Pallas kernels, make_spectra(): pl.pallas_call(functools.partial(spectra_kernel, rows), in_specs=[pl.Bloc...  5.73 us
    unnamed x26, local copies, waits for them, and re-layouts  4.37 us
    ppermute x3, waiting for transfers between devices, route_patches(): lax.ppermute(outgoing[m], 'patch', xor_pairs(sources, 2 * m))  3.8 us
    ppermute x3, starting transfers between devices, correlate_all(): got = lax.ppermute(mine, 'blk', [(b, b ^ k) for b in range(blocks)])  2.75 us
    ppermute x3, starting transfers between devices, route_patches(): lax.ppermute(outgoing[m], 'patch', xor_pairs(sources, 2 * m))  2.71 us
    select_n x8, other arithmetic, correlate_all(): orient_chunk = jnp.take(orientation, index)  2.61 us
  transfers between devices with their start and end apart: 11, of which 2 were waited for; matrix products, arithmetic and copies ran while one was open for 17% of the time, Pallas kernels for 37%

profile of v9, /device:TPU:9, one launch (start us, length us, event | category | flops | bytes accessed | tf_op | source)
XLA Modules:
  0.0 76.7 jit_solution(16354583955622355323)
XLA Ops:
  0.7 1.1 %constant_dynamic-slice_fusion = (bf16[2,256,256]{2,1,0:T(8,128)(2,1)S(1)}, bf16[2,256,256]{2,1,0:T(8,128)(2,1)S(1)}) fusion(bf16[4,256,256]{2,1,0:T(8,128)(2,1)} %param.17, s32[]{:T(128)S(6)} %select_n.275, bf16[4,256,256]{2,1,0:T(8,128)(2,1)} %param.16), kind=kLoop, calls=%fused_computation.50 | loop fusion | bytes 1048580 | tf_op jit(solution)/shard_map/dynamic_slice | solution.py:286
  1.8 1.3 %collective-permute-start.9 = (bf16[4,256,256]{2,1,0:T(8,128)(2,1)S(1)}, bf16[4,256,256]{2,1,0:T(8,128)(2,1)}, u32[]{:S(2)}, u32[]{:S(2)}) collective-permute-start(bf16[4,256,256]{2,1,0:T(8,128)(2,1)S(1)} %pad_maximum_fusion.1), channel_id=1, source_target_pairs={{0,8},{8,0},{16,24},{24,16},{1,9},{9,1},{17,25},{25,17},{2,10},{10... | collective-permute-start | bytes 1572872 | tf_op jit(solution)/shard_map/ppermute | solution.py:291
  3.1 1.2 %collective-permute-start.7 = (bf16[4,256,256]{2,1,0:T(8,128)(2,1)S(1)}, bf16[4,256,256]{2,1,0:T(8,128)(2,1)S(1)}, u32[]{:S(2)}, u32[]{:S(2)}) collective-permute-start(bf16[4,256,256]{2,1,0:T(8,128)(2,1)S(1)} %pad_maximum_fusion.1), channel_id=1, source_target_pairs={{0,16},{8,24},{16,0},{24,8},{1,17},{9,25},{17,1},{25,9},{2,18},{10... | collective-permute-start | bytes 1572872 | tf_op jit(solution)/shard_map/ppermute | solution.py:291
  4.3 0.7 copy-done.6
  5.1 0.1 copy.42
  5.3 0.1 copy.43
  5.4 0.1 copy.44
  5.7 0.1 copy.46
  6.1 0.6 gather_fusion
  6.7 0.2 broadcast_select_fusion
  6.9 0.2 collective-permute-start.1
  7.2 2.3 %collective-permute-start.2 = (bf16[2,256,256]{2,1,0:T(8,128)(2,1)S(1)}, bf16[2,256,256]{2,1,0:T(8,128)(2,1)S(1)}, u32[]{:S(2)}, u32[]{:S(2)}) collective-permute-start(bf16[2,256,256]{2,1,0:T(8,128)(2,1)S(1)} %get-tuple-element.45), channel_id=1, source_target_pairs={{0,4},{1,5},{2,6},{3,7},{4,0},{5,1},{6,2},{7,3},{8,12},{9,13},{10,... | collective-permute-start | bytes 786440 | tf_op jit(solution)/shard_map/ppermute | solution.py:87
  9.5 0.2 collective-permute-start.3
  9.8 0.1 reduce
  9.9 0.1 fusion.6
  10.0 0.1 select_reduce_fusion.1
  10.3 0.6 copy-done.11
  11.0 0.6 gather_fusion.1
  11.8 0.7 copy-done.1
  12.4 0.6 gather_fusion.2
  13.1 0.4 fusion.13
  13.7 0.2 select_reduce_fusion
  13.8 0.5 broadcast_select_fusion.2.take_ref
  14.5 0.6 gather_fusion.6
  15.1 0.6 and_select_fusion.refs_0_
  15.7 0.6 gather_fusion.5
  16.3 0.6 and_select_fusion.1.refs_0_
  16.9 0.1 fusion.1
  17.1 0.6 gather_fusion.4
  17.8 0.6 gather_fusion.3
  18.4 0.2 collective-permute-start.5
  18.7 1.6 %collective-permute-done.2 = bf16[2,256,256]{2,1,0:T(8,128)(2,1)S(1)} collective-permute-done((bf16[2,256,256]{2,1,0:T(8,128)(2,1)S(1)}, bf16[2,256,256]{2,1,0:T(8,128)(2,1)S(1)}, u32[]{:S(2)}, u32[]{:S(2)}) %collective-permute-start.2) | collective-permute-done | bytes 262176 | tf_op jit(solution)/shard_map/ppermute | solution.py:87
  20.2 9.0 %collective-permute-start = (bf16[2,256,256]{2,1,0:T(8,128)(2,1)S(1)}, bf16[2,256,256]{2,1,0:T(8,128)(2,1)S(1)}, u32[]{:S(2)}, u32[]{:S(2)}) collective-permute-start(bf16[2,256,256]{2,1,0:T(8,128)(2,1)S(1)} %get-tuple-element.47), channel_id=1, source_target_pairs={{0,1},{1,0},{2,3},{3,2},{4,5},{5,4},{6,7},{7,6},{8,9},{9,8},{10,11... | collective-permute-start | bytes 786440 | tf_op jit(solution)/shard_map/ppermute | solution.py:84
  29.3 2.2 %collective-permute-done.3 = bf16[2,256,256]{2,1,0:T(8,128)(2,1)S(1)} collective-permute-done((bf16[2,256,256]{2,1,0:T(8,128)(2,1)S(1)}, bf16[2,256,256]{2,1,0:T(8,128)(2,1)S(1)}, u32[]{:S(2)}, u32[]{:S(2)}) %collective-permute-start.3) | collective-permute-done | bytes 262176 | tf_op jit(solution)/shard_map/ppermute | solution.py:87
  31.6 2.4 %collective-permute-start.4 = (bf16[6,256,256]{2,1,0:T(8,128)(2,1)S(1)}, bf16[6,256,256]{2,1,0:T(8,128)(2,1)S(1)}, u32[]{:S(2)}, u32[]{:S(2)}) collective-permute-start(bf16[6,256,256]{2,1,0:T(8,128)(2,1)S(1)} %constant_dynamic-update-slice_fusion.recv_hbm), channel_id=1, source_target_pairs={{0,1},{1,0},{2,3},{3,2},{4,5},{5,4},{6,7},{7,6},{8,9},{9,8},{10,11... | collective-permute-start | bytes 2359304 | tf_op jit(solution)/shard_map/ppermute | solution.py:89
  33.9 0.7 and_select_fusion.2.refs_0_
  34.6 0.6 and_select_fusion.3.refs_0_
  35.2 1.1 %pad_maximum_fusion.refs_3_ = bf16[8,256,256]{2,1,0:T(8,128)(2,1)} fusion(bf16[4,256,256]{2,1,0:T(8,128)(2,1)S(1)} %copy-done.2, bf16[4,256,256]{2,1,0:T(8,128)(2,1)S(1)} %copy-done.3), kind=kLoop, calls=%fused_computation.7 | loop fusion | flops 524288 | bytes 2097152 | tf_op jit(solution)/shard_map/concatenate | solution.py:283
  36.2 1.3 %negate_multiply_fusion.scale_ref = f32[4,256,256]{2,1,0:T(8,128)} fusion(f32[4,256]{1,0:T(4,128)S(1)} %get-tuple-element.53, f32[4,256]{1,0:T(4,128)S(1)} %get-tuple-element.55, f32[4,256]{1,0:T(4,128)S(1)} %get-tuple-element.54, f32[4,256]{1,0:T(4,128)S(1)} %get-tuple-element.52), kind=kLoop, calls=%fused_computation.8 | loop fusion | flops 1310720 | bytes 1064960 | tf_op jit(solution)/shard_map/div | solution.py:57
  37.7 0.4 collective-permute-start.8
  38.2 0.7 copy-done.10
  38.9 0.9 %copy-done.7 = bf16[6,256,256]{2,1,0:T(8,128)(2,1)} copy-done((bf16[6,256,256]{2,1,0:T(8,128)(2,1)}, bf16[6,256,256]{2,1,0:T(8,128)(2,1)S(1)}, u32[]{:S(2)}) %copy-start.7) | copy-done | bytes 786456
  39.7 5.7 %shard_map.129 = (bf16[4,256,256]{2,1,0:T(8,128)(2,1)}, bf16[4,256,256]{2,1,0:T(8,128)(2,1)}) custom-call(s32[4]{0:T(128)} %broadcast_select_fusion.2.take_ref, bf16[2,256,256]{2,1,0:T(8,128)(2,1)} %own_hbm.1, bf16[2,256,256]{2,1,0:T(8,128)(2,1)} %copy-done.10, bf16[6,256,256]{2,1,0:T(8,128)(2,1)} %copy-done.5, bf16[6,256,256]{2,1,0:T(8,128)(2,1)} %copy-done.7, ...), custom_call_target="tpu_custom_call" | custom-call | flops 1207959552 | bytes 2621440 | tf_op jit(solution)/shard_map/pallas_call | solution.py:161
  45.5 7.1 %shard_map.130 = (f32[4,256,256]{2,1,0:T(8,128)}, f32[4,256,256]{2,1,0:T(8,128)}, f32[4,256,256]{2,1,0:T(8,128)}, f32[4,8,128]{2,1,0:T(8,128)}) custom-call(s32[4]{0:T(128)} %and_select_fusion.refs_0_, bf16[4,256,256]{2,1,0:T(8,128)(2,1)} %get-tuple-element.21.refs_1_, bf16[4,256,256]{2,1,0:T(8,128)(2,1)} %get-tuple-element.22.refs_2_, ...), custom_call_target="tpu_custom_call" | custom-call | flops 9663676416 | bytes 12582912 | tf_op jit(solution)/shard_map/pallas_call | solution.py:258
  52.6 7.7 %shard_map.131 = (f32[4,256,256]{2,1,0:T(8,128)}, f32[4,256,256]{2,1,0:T(8,128)}, f32[4,256,256]{2,1,0:T(8,128)}, f32[4,8,128]{2,1,0:T(8,128)}) custom-call(s32[4]{0:T(128)} %and_select_fusion.1.refs_0_, bf16[4,256,256]{2,1,0:T(8,128)(2,1)} %get-tuple-element.21.refs_1_, ...), custom_call_target="tpu_custom_call", output_to_operand_aliasing={{0}: (7, {}), {1}: (8, {}), {2}: (9, {}), {3}: (10, {})} | custom-call | flops 9663676416 | bytes 12582912 | tf_op jit(solution)/shard_map/pallas_call | solution.py:258
  60.4 7.7 %shard_map.132 = (f32[4,256,256]{2,1,0:T(8,128)}, f32[4,256,256]{2,1,0:T(8,128)}, f32[4,256,256]{2,1,0:T(8,128)}, f32[4,8,128]{2,1,0:T(8,128)}) custom-call(s32[4]{0:T(128)} %and_select_fusion.2.refs_0_, bf16[4,256,256]{2,1,0:T(8,128)(2,1)} %get-tuple-element.21.refs_1_, ...), custom_call_target="tpu_custom_call", output_to_operand_aliasing={{0}: (7, {}), {1}: (8, {}), {2}: (9, {}), {3}: (10, {})} | custom-call | flops 9663676416 | bytes 12582912 | tf_op jit(solution)/shard_map/pallas_call | solution.py:258
  68.2 0.8 %copy-done.9 = bf16[4,256,256]{2,1,0:T(8,128)(2,1)} copy-done((bf16[4,256,256]{2,1,0:T(8,128)(2,1)}, bf16[4,256,256]{2,1,0:T(8,128)(2,1)S(1)}, u32[]{:S(2)}) %copy-start.9) | copy-done | bytes 524312
  68.9 7.8 %shard_map.133 = (f32[4,256,256]{2,1,0:T(8,128)}, f32[4,256,256]{2,1,0:T(8,128)}, f32[4,256,256]{2,1,0:T(8,128)}, f32[4,16]{1,0:T(4,128)}) custom-call(s32[4]{0:T(128)} %and_select_fusion.3.refs_0_, bf16[4,256,256]{2,1,0:T(8,128)(2,1)} %get-tuple-element.21.refs_1_, ...), custom_call_target="tpu_custom_call", output_to_operand_aliasing={{0}: (7, {}), {1}: (8, {}), {2}: (9, {})} | custom-call | flops 9663676416 | bytes 12582912 | tf_op jit(solution)/shard_map/pallas_call | solution.py:258
  (75 shorter events, 1.7 us)
Async XLA Ops:
  0.6 13.8 %copy-start = (s32[16]{0:T(128)S(1)}, s32[16]{0:T(128)}, u32[]{:S(2)}) copy-start(s32[16]{0:T(128)} %param.18) | copy-start | bytes 196
  1.7 4.3 %copy-start.4 = (bf16[2,256,256]{2,1,0:T(8,128)(2,1)S(1)}, bf16[2,256,256]{2,1,0:T(8,128)(2,1)}, u32[]{:S(2)}) copy-start(bf16[2,256,256]{2,1,0:T(8,128)(2,1)} %own_hbm.1) | copy-start | bytes 786436
  1.8 35.7 %collective-permute-start.9 = (bf16[4,256,256]{2,1,0:T(8,128)(2,1)S(1)}, bf16[4,256,256]{2,1,0:T(8,128)(2,1)}, u32[]{:S(2)}, u32[]{:S(2)}) collective-permute-start(bf16[4,256,256]{2,1,0:T(8,128)(2,1)S(1)} %pad_maximum_fusion.1), channel_id=1, source_target_pairs={{0,8},{8,0},{16,24},{24,16},{1,9},{9,1},{17,25},{25,17},{2,10},{10... | collective-permute-start | bytes 1572872 | tf_op jit(solution)/shard_map/ppermute | solution.py:291
  3.1 34.6 %collective-permute-start.7 = (bf16[4,256,256]{2,1,0:T(8,128)(2,1)S(1)}, bf16[4,256,256]{2,1,0:T(8,128)(2,1)S(1)}, u32[]{:S(2)}, u32[]{:S(2)}) collective-permute-start(bf16[4,256,256]{2,1,0:T(8,128)(2,1)S(1)} %pad_maximum_fusion.1), channel_id=1, source_target_pairs={{0,16},{8,24},{16,0},{24,8},{1,17},{9,25},{17,1},{25,9},{2,18},{10... | collective-permute-start | bytes 1572872 | tf_op jit(solution)/shard_map/ppermute | solution.py:291
  4.3 0.7 copy-start.6
  6.9 11.5 %collective-permute-start.1 = (bf16[2,256,256]{2,1,0:T(8,128)(2,1)S(1)}, bf16[2,256,256]{2,1,0:T(8,128)(2,1)S(1)}, u32[]{:S(2)}, u32[]{:S(2)}) collective-permute-start(bf16[2,256,256]{2,1,0:T(8,128)(2,1)S(1)} %get-tuple-element.46), channel_id=1, source_target_pairs={{0,2},{1,3},{2,0},{3,1},{4,6},{5,7},{6,4},{7,5},{8,10},{9,11},{10,... | collective-permute-start | bytes 786440 | tf_op jit(solution)/shard_map/ppermute | solution.py:87
  7.2 13.1 %collective-permute-start.2 = (bf16[2,256,256]{2,1,0:T(8,128)(2,1)S(1)}, bf16[2,256,256]{2,1,0:T(8,128)(2,1)S(1)}, u32[]{:S(2)}, u32[]{:S(2)}) collective-permute-start(bf16[2,256,256]{2,1,0:T(8,128)(2,1)S(1)} %get-tuple-element.45), channel_id=1, source_target_pairs={{0,4},{1,5},{2,6},{3,7},{4,0},{5,1},{6,2},{7,3},{8,12},{9,13},{10,... | collective-permute-start | bytes 786440 | tf_op jit(solution)/shard_map/ppermute | solution.py:87
  9.5 22.0 %collective-permute-start.3 = (bf16[2,256,256]{2,1,0:T(8,128)(2,1)S(1)}, bf16[2,256,256]{2,1,0:T(8,128)(2,1)S(1)}, u32[]{:S(2)}, u32[]{:S(2)}) collective-permute-start(bf16[2,256,256]{2,1,0:T(8,128)(2,1)S(1)} %get-tuple-element.44), channel_id=1, source_target_pairs={{0,6},{1,7},{2,4},{3,5},{4,2},{5,3},{6,0},{7,1},{8,14},{9,15},{10,... | collective-permute-start | bytes 786440 | tf_op jit(solution)/shard_map/ppermute | solution.py:87
  10.3 0.7 copy-start.11
  11.8 0.7 copy-start.1
  18.4 19.7 %collective-permute-start.5 = (bf16[4,256,256]{2,1,0:T(8,128)(2,1)S(1)}, bf16[4,256,256]{2,1,0:T(8,128)(2,1)}, u32[]{:S(2)}, u32[]{:S(2)}) collective-permute-start(bf16[4,256,256]{2,1,0:T(8,128)(2,1)S(1)} %pad_maximum_fusion.1), channel_id=1, source_target_pairs={{0,24},{8,16},{16,8},{24,0},{1,25},{9,17},{17,9},{25,1},{2,26},{10... | collective-permute-start | bytes 1572872 | tf_op jit(solution)/shard_map/ppermute | solution.py:291
  20.2 14.9 %copy-start.2 = (bf16[4,256,256]{2,1,0:T(8,128)(2,1)S(1)}, bf16[4,256,256]{2,1,0:T(8,128)(2,1)}, u32[]{:S(2)}) copy-start(bf16[4,256,256]{2,1,0:T(8,128)(2,1)} %param.17) | copy-start | bytes 1572868
  20.2 14.9 %copy-start.3 = (bf16[4,256,256]{2,1,0:T(8,128)(2,1)S(1)}, bf16[4,256,256]{2,1,0:T(8,128)(2,1)}, u32[]{:S(2)}) copy-start(bf16[4,256,256]{2,1,0:T(8,128)(2,1)} %param.16) | copy-start | bytes 1572868
  20.2 17.9 %collective-permute-start = (bf16[2,256,256]{2,1,0:T(8,128)(2,1)S(1)}, bf16[2,256,256]{2,1,0:T(8,128)(2,1)S(1)}, u32[]{:S(2)}, u32[]{:S(2)}) collective-permute-start(bf16[2,256,256]{2,1,0:T(8,128)(2,1)S(1)} %get-tuple-element.47), channel_id=1, source_target_pairs={{0,1},{1,0},{2,3},{3,2},{4,5},{5,4},{6,7},{7,6},{8,9},{9,8},{10,11... | collective-permute-start | bytes 786440 | tf_op jit(solution)/shard_map/ppermute | solution.py:84
  31.5 4.7 %copy-start.5 = (bf16[6,256,256]{2,1,0:T(8,128)(2,1)}, bf16[6,256,256]{2,1,0:T(8,128)(2,1)S(1)}, u32[]{:S(2)}) copy-start(bf16[6,256,256]{2,1,0:T(8,128)(2,1)S(1)} %constant_dynamic-update-slice_fusion.recv_hbm) | copy-start | bytes 2359300
  31.6 6.6 %collective-permute-start.4 = (bf16[6,256,256]{2,1,0:T(8,128)(2,1)S(1)}, bf16[6,256,256]{2,1,0:T(8,128)(2,1)S(1)}, u32[]{:S(2)}, u32[]{:S(2)}) collective-permute-start(bf16[6,256,256]{2,1,0:T(8,128)(2,1)S(1)} %constant_dynamic-update-slice_fusion.recv_hbm), channel_id=1, source_target_pairs={{0,1},{1,0},{2,3},{3,2},{4,5},{5,4},{6,7},{7,6},{8,9},{9,8},{10,11... | collective-permute-start | bytes 2359304 | tf_op jit(solution)/shard_map/ppermute | solution.py:89
  37.5 15.1 %collective-permute-start.10 = (bf16[4,256,256]{2,1,0:T(8,128)(2,1)}, bf16[4,256,256]{2,1,0:T(8,128)(2,1)}, u32[]{:S(2)}, u32[]{:S(2)}) collective-permute-start(bf16[4,256,256]{2,1,0:T(8,128)(2,1)} %collective-permute-done.9.refs_3_), channel_id=1, source_target_pairs={{0,1},{1,0},{2,3},{3,2},{4,5},{5,4},{6,7},{7,6},{8,9},{9,8},{10,11... | collective-permute-start | bytes 1572872 | tf_op jit(solution)/shard_map/ppermute | solution.py:292
  37.7 7.8 %copy-start.8 = (bf16[4,256,256]{2,1,0:T(8,128)(2,1)}, bf16[4,256,256]{2,1,0:T(8,128)(2,1)S(1)}, u32[]{:S(2)}) copy-start(bf16[4,256,256]{2,1,0:T(8,128)(2,1)S(1)} %collective-permute-done.7.refs_3_) | copy-start | bytes 1572868
  37.7 22.7 %collective-permute-start.8 = (bf16[4,256,256]{2,1,0:T(8,128)(2,1)S(1)}, bf16[4,256,256]{2,1,0:T(8,128)(2,1)}, u32[]{:S(2)}, u32[]{:S(2)}) collective-permute-start(bf16[4,256,256]{2,1,0:T(8,128)(2,1)S(1)} %collective-permute-done.7.refs_3_), channel_id=1, source_target_pairs={{0,1},{1,0},{2,3},{3,2},{4,5},{5,4},{6,7},{7,6},{8,9},{9,8},{10,11... | collective-permute-start | bytes 1572872 | tf_op jit(solution)/shard_map/ppermute | solution.py:292
  38.1 30.1 %collective-permute-start.6 = (bf16[4,256,256]{2,1,0:T(8,128)(2,1)}, bf16[4,256,256]{2,1,0:T(8,128)(2,1)S(1)}, u32[]{:S(2)}, u32[]{:S(2)}) collective-permute-start(bf16[4,256,256]{2,1,0:T(8,128)(2,1)} %collective-permute-done.5.refs_3_), channel_id=1, source_target_pairs={{0,1},{1,0},{2,3},{3,2},{4,5},{5,4},{6,7},{7,6},{8,9},{9,8},{10,11... | collective-permute-start | bytes 1572872 | tf_op jit(solution)/shard_map/ppermute | solution.py:292
  38.2 0.7 copy-start.10
  38.9 0.9 %copy-start.7 = (bf16[6,256,256]{2,1,0:T(8,128)(2,1)}, bf16[6,256,256]{2,1,0:T(8,128)(2,1)S(1)}, u32[]{:S(2)}) copy-start(bf16[6,256,256]{2,1,0:T(8,128)(2,1)S(1)} %collective-permute-done.4.fwd_hbm) | copy-start | bytes 2359300
  68.1 0.8 %copy-start.9 = (bf16[4,256,256]{2,1,0:T(8,128)(2,1)}, bf16[4,256,256]{2,1,0:T(8,128)(2,1)S(1)}, u32[]{:S(2)}) copy-start(bf16[4,256,256]{2,1,0:T(8,128)(2,1)S(1)} %collective-permute-done.6.refs_4_) | copy-start | bytes 1572868

commit v10 on v8

--- a/solution.py
+++ b/solution.py
@@ -167,8 +167,9 @@
     si = si_ref[0].astype(jnp.float32)
     forward = fw_ref[...]
     inverse = inv_ref[...]
-    lanes = lax.broadcasted_iota(jnp.int32, peak_ref.shape[1:], 1)
-    peak_row = jnp.zeros(peak_ref.shape[1:], jnp.float32) if first else peak_in[0]
+    row_shape = (8, 128 * ((orient_total + 127) // 128))
+    lanes = lax.broadcasted_iota(jnp.int32, row_shape, 1)
+    peak_row = jnp.zeros(row_shape, jnp.float32) if first else peak_in[0]
     top = total = square = None
     prods = []
     for templ_ref, count in zip(templ_refs, counts):
@@ -196,7 +197,11 @@
         total = sum_in[0] + total
         square = sq_in[0] + square
     top_ref[0] = top
-    peak_ref[0] = peak_row
+    if last:
+        s = pl.program_id(0)
+        peak_ref[pl.ds(s, 1), :] = peak_row[0:1, :orient_total]
+    else:
+        peak_ref[0] = peak_row
     if last:
         mean = total / orient_total
         sum_ref[0] = mean
@@ -226,16 +231,20 @@
         base = len(operands)
         in_specs += [plane, plane, plane, peak_spec]
         operands += list(stats)
-        aliases = {base: 0, base + 1: 1, base + 2: 2, base + 3: 3}
+        aliases = {base: 0, base + 1: 1, base + 2: 2}
+        if not last:
+            aliases[base + 3] = 3
     map_shape = jax.ShapeDtypeStruct((count, extent, extent), jnp.float32)
     flops = 3 * tiles * count * 12 * extent * extent * extent
     return pl.pallas_call(
         functools.partial(corr_kernel, first, last, counts, orient_total),
         grid=(count,),
         in_specs=in_specs,
-        out_specs=[plane, plane, plane, peak_spec],
+        out_specs=[plane, plane, plane,
+                   pl.BlockSpec((count, orient_total), lambda s: (0, 0)) if last else peak_spec],
         out_shape=[map_shape, map_shape, map_shape,
-                   jax.ShapeDtypeStruct((count, 8, lanes), jnp.float32)],
+                   jax.ShapeDtypeStruct((count, orient_total) if last else (count, 8, lanes),
+                                        jnp.float32)],
         input_output_aliases=aliases,
         compiler_params=pltpu.CompilerParams(dimension_semantics=("arbitrary",)),
         cost_estimate=pl.CostEstimate(
@@ -271,7 +280,7 @@
         stats = correlate_chunk(spec_re, spec_im, groups, forward, inverse, orient_chunk,
                                 orient_total, stats, n == len(chunks) - 1)
     top_map, mean_map, var_map, peak = stats
-    return (top_map, mean_map, var_map, peak[:, 0, :orient_total])
+    return (top_map, mean_map, var_map, peak)
 
 
 def body(patches, owner_of_patch, group_of_patch, defocus, templ_re, templ_im, orientation):

time: 76.9 us -> 75.5 us (0.982)
  local copies, waits for them, and re-layouts: 12.7 us -> 11.4 us
    slice x1 -> x0, local copies, waits for them, and re-layouts: 1.3 us -> none  [correlate_all(): return (top_map, mean_map, var_map, peak[:, 0, :orient_total])]
  transfers between devices with their start and end apart: 11 -> 11, of which waited for: 2 -> 2; matrix products, arithmetic and copies ran while one was open for 17% -> 17% of each run, Pallas kernels for 35% -> 36%
where the time goes in v10:
time: 75.5 us; the launch traced here: 75.1 us
  Pallas kernels  34.5 us (46%)
  starting transfers between devices  17.5 us (23%)
  local copies, waits for them, and re-layouts  11.4 us (15%)
  other arithmetic  6.85 us (9%)
  waiting for transfers between devices  3.82 us (5%)
  between operations  1.04 us (1%)
    pallas_call x4, Pallas kernels, correlate_chunk(): pl.pallas_call(functools.partial(corr_kernel, first, last, counts, orient...  30.4 us
    ppermute x1, starting transfers between devices, route_patches(): direct = lax.ppermute(outgoing[0], 'patch', xor_pairs(sources, 1))  9.04 us
    unnamed x26, local copies, waits for them, and re-layouts  4.37 us
    pallas_call x1, Pallas kernels, make_spectra(): pl.pallas_call(functools.partial(spectra_kernel, rows), in_specs=[pl.Bloc...  4.12 us
    ppermute x3, waiting for transfers between devices, route_patches(): lax.ppermute(outgoing[m], 'patch', xor_pairs(sources, 2 * m))  3.8 us
    ppermute x3, starting transfers between devices, correlate_all(): got = lax.ppermute(mine, 'blk', [(b, b ^ k) for b in range(blocks)])  2.75 us
    ppermute x3, starting transfers between devices, route_patches(): lax.ppermute(outgoing[m], 'patch', xor_pairs(sources, 2 * m))  2.71 us
    select_n x8, other arithmetic, correlate_all(): orient_chunk = jnp.take(orientation, index)  2.61 us
  transfers between devices with their start and end apart: 11, of which 2 were waited for; matrix products, arithmetic and copies ran while one was open for 17% of the time, Pallas kernels for 36%

profile of v10, /device:TPU:9, one launch (start us, length us, event | category | flops | bytes accessed | tf_op | source)
XLA Modules:
  0.0 75.1 jit_solution(7020843748376494805)
XLA Ops:
  0.7 1.1 %constant_dynamic-slice_fusion = (bf16[2,256,256]{2,1,0:T(8,128)(2,1)S(1)}, bf16[2,256,256]{2,1,0:T(8,128)(2,1)S(1)}) fusion(bf16[4,256,256]{2,1,0:T(8,128)(2,1)} %param.17, s32[]{:T(128)S(6)} %select_n.275, bf16[4,256,256]{2,1,0:T(8,128)(2,1)} %param.16), kind=kLoop, calls=%fused_computation.50 | loop fusion | bytes 1048580 | tf_op jit(solution)/shard_map/dynamic_slice | solution.py:267
  1.8 1.3 %collective-permute-start.9 = (bf16[4,256,256]{2,1,0:T(8,128)(2,1)S(1)}, bf16[4,256,256]{2,1,0:T(8,128)(2,1)}, u32[]{:S(2)}, u32[]{:S(2)}) collective-permute-start(bf16[4,256,256]{2,1,0:T(8,128)(2,1)S(1)} %pad_maximum_fusion.1), channel_id=1, source_target_pairs={{0,8},{8,0},{16,24},{24,16},{1,9},{9,1},{17,25},{25,17},{2,10},{10... | collective-permute-start | bytes 1572872 | tf_op jit(solution)/shard_map/ppermute | solution.py:272
  3.1 1.2 %collective-permute-start.7 = (bf16[4,256,256]{2,1,0:T(8,128)(2,1)S(1)}, bf16[4,256,256]{2,1,0:T(8,128)(2,1)S(1)}, u32[]{:S(2)}, u32[]{:S(2)}) collective-permute-start(bf16[4,256,256]{2,1,0:T(8,128)(2,1)S(1)} %pad_maximum_fusion.1), channel_id=1, source_target_pairs={{0,16},{8,24},{16,0},{24,8},{1,17},{9,25},{17,1},{25,9},{2,18},{10... | collective-permute-start | bytes 1572872 | tf_op jit(solution)/shard_map/ppermute | solution.py:272
  4.3 0.7 copy-done.6
  5.1 0.1 copy.42
  5.3 0.1 copy.43
  5.4 0.1 copy.44
  5.7 0.1 copy.46
  6.1 0.6 gather_fusion
  6.7 0.2 broadcast_select_fusion
  6.9 0.2 collective-permute-start.1
  7.2 2.3 %collective-permute-start.2 = (bf16[2,256,256]{2,1,0:T(8,128)(2,1)S(1)}, bf16[2,256,256]{2,1,0:T(8,128)(2,1)S(1)}, u32[]{:S(2)}, u32[]{:S(2)}) collective-permute-start(bf16[2,256,256]{2,1,0:T(8,128)(2,1)S(1)} %get-tuple-element.45), channel_id=1, source_target_pairs={{0,4},{1,5},{2,6},{3,7},{4,0},{5,1},{6,2},{7,3},{8,12},{9,13},{10,... | collective-permute-start | bytes 786440 | tf_op jit(solution)/shard_map/ppermute | solution.py:87
  9.5 0.2 collective-permute-start.3
  9.8 0.1 reduce
  9.9 0.1 fusion.6
  10.0 0.1 select_reduce_fusion.1
  10.3 0.6 copy-done.11
  11.0 0.6 gather_fusion.1
  11.8 0.7 copy-done.1
  12.4 0.6 gather_fusion.2
  13.1 0.4 fusion.13
  13.7 0.2 select_reduce_fusion
  13.8 0.5 broadcast_select_fusion.2.take_ref
  14.5 0.6 gather_fusion.6
  15.1 0.6 and_select_fusion.refs_0_
  15.7 0.6 gather_fusion.5
  16.3 0.6 and_select_fusion.1.refs_0_
  16.9 0.1 fusion.1
  17.1 0.6 gather_fusion.4
  17.8 0.6 gather_fusion.3
  18.4 0.2 collective-permute-start.5
  18.7 1.6 %collective-permute-done.2 = bf16[2,256,256]{2,1,0:T(8,128)(2,1)S(1)} collective-permute-done((bf16[2,256,256]{2,1,0:T(8,128)(2,1)S(1)}, bf16[2,256,256]{2,1,0:T(8,128)(2,1)S(1)}, u32[]{:S(2)}, u32[]{:S(2)}) %collective-permute-start.2) | collective-permute-done | bytes 262176 | tf_op jit(solution)/shard_map/ppermute | solution.py:87
  20.2 9.0 %collective-permute-start = (bf16[2,256,256]{2,1,0:T(8,128)(2,1)S(1)}, bf16[2,256,256]{2,1,0:T(8,128)(2,1)S(1)}, u32[]{:S(2)}, u32[]{:S(2)}) collective-permute-start(bf16[2,256,256]{2,1,0:T(8,128)(2,1)S(1)} %get-tuple-element.47), channel_id=1, source_target_pairs={{0,1},{1,0},{2,3},{3,2},{4,5},{5,4},{6,7},{7,6},{8,9},{9,8},{10,11... | collective-permute-start | bytes 786440 | tf_op jit(solution)/shard_map/ppermute | solution.py:84
  29.3 2.2 %collective-permute-done.3 = bf16[2,256,256]{2,1,0:T(8,128)(2,1)S(1)} collective-permute-done((bf16[2,256,256]{2,1,0:T(8,128)(2,1)S(1)}, bf16[2,256,256]{2,1,0:T(8,128)(2,1)S(1)}, u32[]{:S(2)}, u32[]{:S(2)}) %collective-permute-start.3) | collective-permute-done | bytes 262176 | tf_op jit(solution)/shard_map/ppermute | solution.py:87
  31.6 2.4 %collective-permute-start.4 = (bf16[6,256,256]{2,1,0:T(8,128)(2,1)S(1)}, bf16[6,256,256]{2,1,0:T(8,128)(2,1)S(1)}, u32[]{:S(2)}, u32[]{:S(2)}) collective-permute-start(bf16[6,256,256]{2,1,0:T(8,128)(2,1)S(1)} %constant_dynamic-update-slice_fusion.recv_ref), channel_id=1, source_target_pairs={{0,1},{1,0},{2,3},{3,2},{4,5},{5,4},{6,7},{7,6},{8,9},{9,8},{10,11... | collective-permute-start | bytes 2359304 | tf_op jit(solution)/shard_map/ppermute | solution.py:89
  33.9 0.7 and_select_fusion.2.refs_0_
  34.6 0.6 and_select_fusion.3.refs_0_
  35.2 1.1 %pad_maximum_fusion.refs_3_ = bf16[8,256,256]{2,1,0:T(8,128)(2,1)} fusion(bf16[4,256,256]{2,1,0:T(8,128)(2,1)S(1)} %copy-done.2, bf16[4,256,256]{2,1,0:T(8,128)(2,1)S(1)} %copy-done.3), kind=kLoop, calls=%fused_computation.7 | loop fusion | flops 524288 | bytes 2097152 | tf_op jit(solution)/shard_map/concatenate | solution.py:264
  36.2 1.3 %negate_multiply_fusion.scale_ref = f32[4,256,256]{2,1,0:T(8,128)} fusion(f32[4,256]{1,0:T(4,128)S(1)} %get-tuple-element.53, f32[4,256]{1,0:T(4,128)S(1)} %get-tuple-element.55, f32[4,256]{1,0:T(4,128)S(1)} %get-tuple-element.54, f32[4,256]{1,0:T(4,128)S(1)} %get-tuple-element.52), kind=kLoop, calls=%fused_computation.8 | loop fusion | flops 1310720 | bytes 1064960 | tf_op jit(solution)/shard_map/div | solution.py:57
  37.7 0.4 collective-permute-start.8
  38.2 0.7 copy-done.10
  38.9 0.9 %copy-done.7 = bf16[6,256,256]{2,1,0:T(8,128)(2,1)} copy-done((bf16[6,256,256]{2,1,0:T(8,128)(2,1)}, bf16[6,256,256]{2,1,0:T(8,128)(2,1)S(1)}, u32[]{:S(2)}) %copy-start.7) | copy-done | bytes 786456
  39.7 4.1 %shard_map.129 = (bf16[4,256,256]{2,1,0:T(8,128)(2,1)}, bf16[4,256,256]{2,1,0:T(8,128)(2,1)}) custom-call(s32[4]{0:T(128)} %broadcast_select_fusion.2.take_ref, bf16[2,256,256]{2,1,0:T(8,128)(2,1)} %own_ref.1, bf16[2,256,256]{2,1,0:T(8,128)(2,1)} %copy-done.10, bf16[6,256,256]{2,1,0:T(8,128)(2,1)} %copy-done.5, bf16[6,256,256]{2,1,0:T(8,128)(2,1)} %copy-done.7, ...), custom_call_target="tpu_custom_call" | custom-call | flops 1207959552 | bytes 2621440 | tf_op jit(solution)/shard_map/pallas_call | solution.py:144
  43.9 7.1 %shard_map.130 = (f32[4,256,256]{2,1,0:T(8,128)}, f32[4,256,256]{2,1,0:T(8,128)}, f32[4,256,256]{2,1,0:T(8,128)}, f32[4,8,128]{2,1,0:T(8,128)}) custom-call(s32[4]{0:T(128)} %and_select_fusion.refs_0_, bf16[4,256,256]{2,1,0:T(8,128)(2,1)} %get-tuple-element.21.refs_1_, bf16[4,256,256]{2,1,0:T(8,128)(2,1)} %get-tuple-element.22.refs_2_, ...), custom_call_target="tpu_custom_call" | custom-call | flops 9663676416 | bytes 12582912 | tf_op jit(solution)/shard_map/pallas_call | solution.py:239
  51.0 7.7 %shard_map.131 = (f32[4,256,256]{2,1,0:T(8,128)}, f32[4,256,256]{2,1,0:T(8,128)}, f32[4,256,256]{2,1,0:T(8,128)}, f32[4,8,128]{2,1,0:T(8,128)}) custom-call(s32[4]{0:T(128)} %and_select_fusion.1.refs_0_, bf16[4,256,256]{2,1,0:T(8,128)(2,1)} %get-tuple-element.21.refs_1_, ...), custom_call_target="tpu_custom_call", output_to_operand_aliasing={{0}: (7, {}), {1}: (8, {}), {2}: (9, {}), {3}: (10, {})} | custom-call | flops 9663676416 | bytes 12582912 | tf_op jit(solution)/shard_map/pallas_call | solution.py:239
  58.8 7.7 %shard_map.132 = (f32[4,256,256]{2,1,0:T(8,128)}, f32[4,256,256]{2,1,0:T(8,128)}, f32[4,256,256]{2,1,0:T(8,128)}, f32[4,8,128]{2,1,0:T(8,128)}) custom-call(s32[4]{0:T(128)} %and_select_fusion.2.refs_0_, bf16[4,256,256]{2,1,0:T(8,128)(2,1)} %get-tuple-element.21.refs_1_, ...), custom_call_target="tpu_custom_call", output_to_operand_aliasing={{0}: (7, {}), {1}: (8, {}), {2}: (9, {}), {3}: (10, {})} | custom-call | flops 9663676416 | bytes 12582912 | tf_op jit(solution)/shard_map/pallas_call | solution.py:239
  66.5 0.8 %copy-done.9 = bf16[4,256,256]{2,1,0:T(8,128)(2,1)} copy-done((bf16[4,256,256]{2,1,0:T(8,128)(2,1)}, bf16[4,256,256]{2,1,0:T(8,128)(2,1)S(1)}, u32[]{:S(2)}) %copy-start.9) | copy-done | bytes 524312
  67.3 7.8 %shard_map.133 = (f32[4,256,256]{2,1,0:T(8,128)}, f32[4,256,256]{2,1,0:T(8,128)}, f32[4,256,256]{2,1,0:T(8,128)}, f32[4,16]{1,0:T(4,128)}) custom-call(s32[4]{0:T(128)} %and_select_fusion.3.refs_0_, bf16[4,256,256]{2,1,0:T(8,128)(2,1)} %get-tuple-element.21.refs_1_, ...), custom_call_target="tpu_custom_call", output_to_operand_aliasing={{0}: (7, {}), {1}: (8, {}), {2}: (9, {})} | custom-call | flops 9663676416 | bytes 12582912 | tf_op jit(solution)/shard_map/pallas_call | solution.py:239
  (75 shorter events, 1.7 us)
Async XLA Ops:
  0.6 13.8 %copy-start = (s32[16]{0:T(128)S(1)}, s32[16]{0:T(128)}, u32[]{:S(2)}) copy-start(s32[16]{0:T(128)} %param.18) | copy-start | bytes 196
  1.7 4.3 %copy-start.4 = (bf16[2,256,256]{2,1,0:T(8,128)(2,1)S(1)}, bf16[2,256,256]{2,1,0:T(8,128)(2,1)}, u32[]{:S(2)}) copy-start(bf16[2,256,256]{2,1,0:T(8,128)(2,1)} %own_ref.1) | copy-start | bytes 786436
  1.8 35.7 %collective-permute-start.9 = (bf16[4,256,256]{2,1,0:T(8,128)(2,1)S(1)}, bf16[4,256,256]{2,1,0:T(8,128)(2,1)}, u32[]{:S(2)}, u32[]{:S(2)}) collective-permute-start(bf16[4,256,256]{2,1,0:T(8,128)(2,1)S(1)} %pad_maximum_fusion.1), channel_id=1, source_target_pairs={{0,8},{8,0},{16,24},{24,16},{1,9},{9,1},{17,25},{25,17},{2,10},{10... | collective-permute-start | bytes 1572872 | tf_op jit(solution)/shard_map/ppermute | solution.py:272
  3.1 34.6 %collective-permute-start.7 = (bf16[4,256,256]{2,1,0:T(8,128)(2,1)S(1)}, bf16[4,256,256]{2,1,0:T(8,128)(2,1)S(1)}, u32[]{:S(2)}, u32[]{:S(2)}) collective-permute-start(bf16[4,256,256]{2,1,0:T(8,128)(2,1)S(1)} %pad_maximum_fusion.1), channel_id=1, source_target_pairs={{0,16},{8,24},{16,0},{24,8},{1,17},{9,25},{17,1},{25,9},{2,18},{10... | collective-permute-start | bytes 1572872 | tf_op jit(solution)/shard_map/ppermute | solution.py:272
  4.3 0.7 copy-start.6
  6.9 11.5 %collective-permute-start.1 = (bf16[2,256,256]{2,1,0:T(8,128)(2,1)S(1)}, bf16[2,256,256]{2,1,0:T(8,128)(2,1)S(1)}, u32[]{:S(2)}, u32[]{:S(2)}) collective-permute-start(bf16[2,256,256]{2,1,0:T(8,128)(2,1)S(1)} %get-tuple-element.46), channel_id=1, source_target_pairs={{0,2},{1,3},{2,0},{3,1},{4,6},{5,7},{6,4},{7,5},{8,10},{9,11},{10,... | collective-permute-start | bytes 786440 | tf_op jit(solution)/shard_map/ppermute | solution.py:87
  7.2 13.1 %collective-permute-start.2 = (bf16[2,256,256]{2,1,0:T(8,128)(2,1)S(1)}, bf16[2,256,256]{2,1,0:T(8,128)(2,1)S(1)}, u32[]{:S(2)}, u32[]{:S(2)}) collective-permute-start(bf16[2,256,256]{2,1,0:T(8,128)(2,1)S(1)} %get-tuple-element.45), channel_id=1, source_target_pairs={{0,4},{1,5},{2,6},{3,7},{4,0},{5,1},{6,2},{7,3},{8,12},{9,13},{10,... | collective-permute-start | bytes 786440 | tf_op jit(solution)/shard_map/ppermute | solution.py:87
  9.5 22.0 %collective-permute-start.3 = (bf16[2,256,256]{2,1,0:T(8,128)(2,1)S(1)}, bf16[2,256,256]{2,1,0:T(8,128)(2,1)S(1)}, u32[]{:S(2)}, u32[]{:S(2)}) collective-permute-start(bf16[2,256,256]{2,1,0:T(8,128)(2,1)S(1)} %get-tuple-element.44), channel_id=1, source_target_pairs={{0,6},{1,7},{2,4},{3,5},{4,2},{5,3},{6,0},{7,1},{8,14},{9,15},{10,... | collective-permute-start | bytes 786440 | tf_op jit(solution)/shard_map/ppermute | solution.py:87
  10.3 0.7 copy-start.11
  11.8 0.7 copy-start.1
  18.4 19.7 %collective-permute-start.5 = (bf16[4,256,256]{2,1,0:T(8,128)(2,1)S(1)}, bf16[4,256,256]{2,1,0:T(8,128)(2,1)}, u32[]{:S(2)}, u32[]{:S(2)}) collective-permute-start(bf16[4,256,256]{2,1,0:T(8,128)(2,1)S(1)} %pad_maximum_fusion.1), channel_id=1, source_target_pairs={{0,24},{8,16},{16,8},{24,0},{1,25},{9,17},{17,9},{25,1},{2,26},{10... | collective-permute-start | bytes 1572872 | tf_op jit(solution)/shard_map/ppermute | solution.py:272
  20.2 14.9 %copy-start.2 = (bf16[4,256,256]{2,1,0:T(8,128)(2,1)S(1)}, bf16[4,256,256]{2,1,0:T(8,128)(2,1)}, u32[]{:S(2)}) copy-start(bf16[4,256,256]{2,1,0:T(8,128)(2,1)} %param.17) | copy-start | bytes 1572868
  20.2 14.9 %copy-start.3 = (bf16[4,256,256]{2,1,0:T(8,128)(2,1)S(1)}, bf16[4,256,256]{2,1,0:T(8,128)(2,1)}, u32[]{:S(2)}) copy-start(bf16[4,256,256]{2,1,0:T(8,128)(2,1)} %param.16) | copy-start | bytes 1572868
  20.2 17.9 %collective-permute-start = (bf16[2,256,256]{2,1,0:T(8,128)(2,1)S(1)}, bf16[2,256,256]{2,1,0:T(8,128)(2,1)S(1)}, u32[]{:S(2)}, u32[]{:S(2)}) collective-permute-start(bf16[2,256,256]{2,1,0:T(8,128)(2,1)S(1)} %get-tuple-element.47), channel_id=1, source_target_pairs={{0,1},{1,0},{2,3},{3,2},{4,5},{5,4},{6,7},{7,6},{8,9},{9,8},{10,11... | collective-permute-start | bytes 786440 | tf_op jit(solution)/shard_map/ppermute | solution.py:84
  31.5 4.7 %copy-start.5 = (bf16[6,256,256]{2,1,0:T(8,128)(2,1)}, bf16[6,256,256]{2,1,0:T(8,128)(2,1)S(1)}, u32[]{:S(2)}) copy-start(bf16[6,256,256]{2,1,0:T(8,128)(2,1)S(1)} %constant_dynamic-update-slice_fusion.recv_ref) | copy-start | bytes 2359300
  31.6 6.6 %collective-permute-start.4 = (bf16[6,256,256]{2,1,0:T(8,128)(2,1)S(1)}, bf16[6,256,256]{2,1,0:T(8,128)(2,1)S(1)}, u32[]{:S(2)}, u32[]{:S(2)}) collective-permute-start(bf16[6,256,256]{2,1,0:T(8,128)(2,1)S(1)} %constant_dynamic-update-slice_fusion.recv_ref), channel_id=1, source_target_pairs={{0,1},{1,0},{2,3},{3,2},{4,5},{5,4},{6,7},{7,6},{8,9},{9,8},{10,11... | collective-permute-start | bytes 2359304 | tf_op jit(solution)/shard_map/ppermute | solution.py:89
  37.5 13.5 %collective-permute-start.10 = (bf16[4,256,256]{2,1,0:T(8,128)(2,1)}, bf16[4,256,256]{2,1,0:T(8,128)(2,1)}, u32[]{:S(2)}, u32[]{:S(2)}) collective-permute-start(bf16[4,256,256]{2,1,0:T(8,128)(2,1)} %collective-permute-done.9.refs_3_), channel_id=1, source_target_pairs={{0,1},{1,0},{2,3},{3,2},{4,5},{5,4},{6,7},{7,6},{8,9},{9,8},{10,11... | collective-permute-start | bytes 1572872 | tf_op jit(solution)/shard_map/ppermute | solution.py:273
  37.7 6.2 %copy-start.8 = (bf16[4,256,256]{2,1,0:T(8,128)(2,1)}, bf16[4,256,256]{2,1,0:T(8,128)(2,1)S(1)}, u32[]{:S(2)}) copy-start(bf16[4,256,256]{2,1,0:T(8,128)(2,1)S(1)} %collective-permute-done.7.refs_3_) | copy-start | bytes 1572868
  37.7 21.1 %collective-permute-start.8 = (bf16[4,256,256]{2,1,0:T(8,128)(2,1)S(1)}, bf16[4,256,256]{2,1,0:T(8,128)(2,1)}, u32[]{:S(2)}, u32[]{:S(2)}) collective-permute-start(bf16[4,256,256]{2,1,0:T(8,128)(2,1)S(1)} %collective-permute-done.7.refs_3_), channel_id=1, source_target_pairs={{0,1},{1,0},{2,3},{3,2},{4,5},{5,4},{6,7},{7,6},{8,9},{9,8},{10,11... | collective-permute-start | bytes 1572872 | tf_op jit(solution)/shard_map/ppermute | solution.py:273
  38.1 28.4 %collective-permute-start.6 = (bf16[4,256,256]{2,1,0:T(8,128)(2,1)}, bf16[4,256,256]{2,1,0:T(8,128)(2,1)S(1)}, u32[]{:S(2)}, u32[]{:S(2)}) collective-permute-start(bf16[4,256,256]{2,1,0:T(8,128)(2,1)} %collective-permute-done.5.refs_3_), channel_id=1, source_target_pairs={{0,1},{1,0},{2,3},{3,2},{4,5},{5,4},{6,7},{7,6},{8,9},{9,8},{10,11... | collective-permute-start | bytes 1572872 | tf_op jit(solution)/shard_map/ppermute | solution.py:273
  38.2 0.7 copy-start.10
  38.9 0.9 %copy-start.7 = (bf16[6,256,256]{2,1,0:T(8,128)(2,1)}, bf16[6,256,256]{2,1,0:T(8,128)(2,1)S(1)}, u32[]{:S(2)}) copy-start(bf16[6,256,256]{2,1,0:T(8,128)(2,1)S(1)} %collective-permute-done.4.fwd_ref) | copy-start | bytes 2359300
  66.5 0.8 %copy-start.9 = (bf16[4,256,256]{2,1,0:T(8,128)(2,1)}, bf16[4,256,256]{2,1,0:T(8,128)(2,1)S(1)}, u32[]{:S(2)}) copy-start(bf16[4,256,256]{2,1,0:T(8,128)(2,1)S(1)} %collective-permute-done.6.refs_4_) | copy-start | bytes 1572868

commit v11 on v10

--- a/solution.py
+++ b/solution.py
@@ -59,6 +59,72 @@
 
 def xor_pairs(count, shift):
     return [(d, d ^ shift) for d in range(count)]
+
+
+def two_matches(match, empty):
+    first = jnp.where(match[..., 0], 0, jnp.where(match[..., 1], 1, empty))
+    second = jnp.where(match[..., 0] & match[..., 1], 1, empty)
+    return jnp.stack([first, second], axis=-1)
+
+
+def route_relay(patches, row_owner, my_index):
+    sources, number = row_owner.shape
+    extent = patches.shape[-1]
+    devs = jnp.arange(sources, dtype=jnp.int32)
+    chip_of = devs // 2
+    flat_owner = row_owner.reshape(-1)
+    own_pid = devs[:, None] * number + jnp.arange(number, dtype=jnp.int32)[None, :]
+    owner_chip = row_owner // 2
+    sel_p = two_matches(row_owner == (devs ^ 1)[:, None], number)
+    sel_n = two_matches(owner_chip == (chip_of ^ 1)[:, None], number)
+    sel_f = two_matches((owner_chip ^ chip_of[:, None]) >= 2, number)
+
+    def pids_of(sel, base):
+        picked = jnp.take_along_axis(base, jnp.minimum(sel, number - 1), axis=1)
+        return jnp.where(sel < number, picked, -1)
+
+    pid_p = pids_of(sel_p, own_pid)
+    pid_n = pids_of(sel_n, own_pid)
+    pid_f = pids_of(sel_f, own_pid)
+    far_got = jnp.take(pid_f, devs ^ 4, axis=0)
+    far_chip = jnp.where(far_got >= 0, jnp.take(flat_owner, jnp.maximum(far_got, 0)) // 2, -1)
+    sel_r = two_matches(far_chip == (chip_of ^ 1)[:, None], number)
+    pid_r = pids_of(sel_r, far_got)
+    padded = jnp.concatenate([patches, jnp.zeros((1, extent, extent), patches.dtype)], axis=0)
+    my_sel = jnp.concatenate([lax.dynamic_index_in_dim(sel, my_index, 0, keepdims=False)
+                              for sel in (sel_p, sel_n, sel_f)])
+    outgoing = jnp.take(padded, my_sel, axis=0)
+    direct = lax.ppermute(outgoing[0:2], "patch", xor_pairs(sources, 1))
+    near_got = lax.ppermute(outgoing[2:4], "patch", xor_pairs(sources, 2))
+    far_slots = lax.ppermute(outgoing[4:6], "patch", xor_pairs(sources, 4))
+    far_padded = jnp.concatenate([far_slots, jnp.zeros((1, extent, extent), patches.dtype)], axis=0)
+    my_relay = lax.dynamic_index_in_dim(sel_r, my_index, 0, keepdims=False)
+    relay_got = lax.ppermute(jnp.take(far_padded, my_relay, axis=0), "patch",
+                             xor_pairs(sources, 2))
+    received = jnp.concatenate([near_got, far_slots, relay_got], axis=0)
+    forwarded = lax.ppermute(received, "patch", xor_pairs(sources, 1))
+    partner = my_index ^ 1
+
+    def row(table, device):
+        return lax.dynamic_index_in_dim(table, device, 0, keepdims=False)
+
+    cand_pid = jnp.concatenate([
+        row(own_pid, my_index), row(pid_p, partner),
+        row(pid_n, my_index ^ 2), row(pid_f, my_index ^ 4), row(pid_r, my_index ^ 2),
+        row(pid_n, partner ^ 2), row(pid_f, partner ^ 4), row(pid_r, partner ^ 2)])
+    hits = (flat_owner == my_index).astype(jnp.int32)
+    rank_in = jnp.cumsum(hits) - hits
+    slot_ids = jnp.arange(CAP, dtype=jnp.int32)
+    wanted = (hits[None, :] == 1) & (rank_in[None, :] == slot_ids[:, None])
+    patch_ids = jnp.arange(sources * number, dtype=jnp.int32)
+    slot_pid = jnp.sum(jnp.where(wanted, patch_ids[None, :], 0), axis=1)
+    present = jnp.any(wanted, axis=1)
+    cand_ids = jnp.arange(cand_pid.shape[0], dtype=jnp.int32)
+    found = cand_pid[None, :] == slot_pid[:, None]
+    take_idx = jnp.sum(jnp.where(found, cand_ids[None, :], 0), axis=1)
+    take_idx = jnp.where(present, take_idx, cand_pid.shape[0])
+    pieces = (patches, direct, received, forwarded)
+    return take_idx, pieces, jnp.where(present, slot_pid, sources * number), outgoing
 
 
 def route_patches(patches, row_owner, my_index):
@@ -289,7 +355,10 @@
     number, extent = (patches.shape[0], patches.shape[1])
     forward, half_table, inverse = (jnp.asarray(table) for table in dft_tables(extent))
     row_owner = owner_of_patch.reshape(sources, number)
-    take_idx, pieces, slot_row, outgoing = route_patches(patches, row_owner, my_index)
+    if sources == 8 and number == 2:
+        take_idx, pieces, slot_row, outgoing = route_relay(patches, row_owner, my_index)
+    else:
+        take_idx, pieces, slot_row, outgoing = route_patches(patches, row_owner, my_index)
     templ_re, templ_im, unused = lax.optimization_barrier((templ_re, templ_im, outgoing))
     groups = jnp.take(jnp.concatenate([group_of_patch, jnp.zeros((1,), jnp.int32)]), slot_row)
     focus_values = jnp.take(defocus, groups)

time: 75.5 us -> 77.8 us (1.030)
  the two profiles are of different devices: /device:TPU:9 before, /device:TPU:0 now
where the time goes in v11:
time: 77.8 us; the launch traced here: 77.3 us
  Pallas kernels  34.5 us (44%)
  local copies, waits for them, and re-layouts  18 us (23%)
  starting transfers between devices  10.8 us (14%)
  other arithmetic  8.08 us (10%)
  waiting for transfers between devices  4.83 us (6%)
  between operations  1.13 us (1%)
    pallas_call x4, Pallas kernels, correlate_chunk(): pl.pallas_call(functools.partial(corr_kernel, first, last, counts, orient...  30.4 us
    unnamed x24, local copies, waits for them, and re-layouts  6.15 us
    ppermute x1, waiting for transfers between devices, route_relay(): lax.ppermute(jnp.take(far_padded, my_relay, axis=0), 'patch', xor_pairs(s...  4.8 us
    ppermute x3, starting transfers between devices, correlate_all(): got = lax.ppermute(mine, 'blk', [(b, b ^ k) for b in range(blocks)])  4.55 us
    pallas_call x1, Pallas kernels, make_spectra(): pl.pallas_call(functools.partial(spectra_kernel, rows), in_specs=[pl.Bloc...  4.15 us
    gather x20, local copies, waits for them, and re-layouts, pids_of(): picked = jnp.take_along_axis(base, jnp.minimum(sel, number - 1), axis=1)  3.9 us
    select_n x8, other arithmetic, correlate_all(): orient_chunk = jnp.take(orientation, index)  2.77 us
    ppermute x1, starting transfers between devices, route_relay(): far_slots = lax.ppermute(outgoing[4:6], 'patch', xor_pairs(sources, 4))  2.59 us
  transfers between devices with their start and end apart: 11, of which 1 were waited for; matrix products, arithmetic and copies ran while one was open for 22% of the time, Pallas kernels for 35%

profile of v11, /device:TPU:0, one launch (start us, length us, event | category | flops | bytes accessed | tf_op | source)
XLA Modules:
  0.0 77.3 jit_solution(6286714817489326160)
XLA Ops:
  0.7 0.6 copy-done.1
  2.1 1.0 %concatenate.74 = bf16[3,256,256]{2,1,0:T(8,128)(2,1)S(1)} pad(bf16[2,256,256]{2,1,0:T(8,128)(2,1)} %own_ref.1, bf16[]{:T(256)} %constant.217.clone.1), padding=0_1x0_0x0_0 | pad | bytes 655362 | tf_op jit(solution)/shard_map/concatenate | solution.py:93
  3.1 0.6 gather_fusion.2
  3.8 0.1 broadcast_select_fusion
  4.0 0.9 %copy-done.3 = bf16[4,256,256]{2,1,0:T(8,128)(2,1)S(1)} copy-done((bf16[4,256,256]{2,1,0:T(8,128)(2,1)S(1)}, bf16[4,256,256]{2,1,0:T(8,128)(2,1)}, u32[]{:S(2)}) %copy-start.3) | copy-done | bytes 524312
  4.9 0.2 copy-done.4
  5.1 3.0 %collective-permute-start.9 = (bf16[4,256,256]{2,1,0:T(8,128)(2,1)S(1)}, bf16[4,256,256]{2,1,0:T(8,128)(2,1)}, u32[]{:S(2)}, u32[]{:S(2)}) collective-permute-start(bf16[4,256,256]{2,1,0:T(8,128)(2,1)S(1)} %pad_maximum_fusion.1), channel_id=1, source_target_pairs={{0,8},{8,0},{16,24},{24,16},{1,9},{9,1},{17,25},{25,17},{2,10},{10... | collective-permute-start | bytes 1572872 | tf_op jit(solution)/shard_map/ppermute | solution.py:338
  8.1 1.5 %collective-permute-start.7 = (bf16[4,256,256]{2,1,0:T(8,128)(2,1)S(1)}, bf16[4,256,256]{2,1,0:T(8,128)(2,1)}, u32[]{:S(2)}, u32[]{:S(2)}) collective-permute-start(bf16[4,256,256]{2,1,0:T(8,128)(2,1)S(1)} %pad_maximum_fusion.1), channel_id=1, source_target_pairs={{0,16},{8,24},{16,0},{24,8},{1,17},{9,25},{17,1},{25,9},{2,18},{10... | collective-permute-start | bytes 1572872 | tf_op jit(solution)/shard_map/ppermute | solution.py:338
  9.7 2.1 %collective-permute-start.1 = (bf16[2,256,256]{2,1,0:T(8,128)(2,1)S(1)}, bf16[2,256,256]{2,1,0:T(8,128)(2,1)S(1)}, u32[]{:S(2)}, u32[]{:S(2)}) collective-permute-start(bf16[2,256,256]{2,1,0:T(8,128)(2,1)S(1)} %get-tuple-element.49), channel_id=1, source_target_pairs={{0,2},{1,3},{2,0},{3,1},{4,6},{5,7},{6,4},{7,5},{8,10},{9,11},{10,... | collective-permute-start | bytes 786440 | tf_op jit(solution)/shard_map/ppermute | solution.py:98
  11.8 2.6 %collective-permute-start.2 = (bf16[2,256,256]{2,1,0:T(8,128)(2,1)S(1)}, bf16[2,256,256]{2,1,0:T(8,128)(2,1)S(1)}, u32[]{:S(2)}, u32[]{:S(2)}) collective-permute-start(bf16[2,256,256]{2,1,0:T(8,128)(2,1)S(1)} %get-tuple-element.48), channel_id=1, source_target_pairs={{0,4},{1,5},{2,6},{3,7},{4,0},{5,1},{6,2},{7,3},{8,12},{9,13},{10,... | collective-permute-start | bytes 786440 | tf_op jit(solution)/shard_map/ppermute | solution.py:99
  14.8 0.6 gather_fusion.9
  15.5 0.6 gather_fusion
  16.3 0.7 gather_fusion.1
  17.6 0.1 fusion.11
  18.0 0.6 copy-done.10
  18.7 0.6 gather_fusion.4
  19.5 0.7 copy-done.2
  20.1 0.6 gather_fusion.5
  21.0 0.6 gather_fusion.10
  22.0 0.6 gather_fusion.7
  23.0 0.7 gather_fusion.8
  23.9 0.2 select_reduce_fusion
  24.1 0.5 broadcast_select_fusion.4.take_ref
  24.8 0.6 gather_fusion.13
  25.4 0.6 and_select_fusion.4.refs_0_
  26.0 0.6 gather_fusion.12
  26.6 0.6 and_select_fusion.5.refs_0_
  27.3 0.1 fusion.1
  27.5 0.6 gather_fusion.3
  28.1 0.5 collective-permute-start.3
  28.7 0.6 gather_fusion.11
  29.3 0.6 gather_fusion.6
  30.1 4.8 %collective-permute-done.3 = bf16[2,256,256]{2,1,0:T(8,128)(2,1)S(1)} collective-permute-done((bf16[2,256,256]{2,1,0:T(8,128)(2,1)S(1)}, bf16[2,256,256]{2,1,0:T(8,128)(2,1)S(1)}, u32[]{:S(2)}, u32[]{:S(2)}) %collective-permute-start.3) | collective-permute-done | bytes 262176 | tf_op jit(solution)/shard_map/ppermute | solution.py:102
  35.0 0.7 and_select_fusion.6.refs_0_
  35.7 0.6 and_select_fusion.7.refs_0_
  36.3 1.1 %pad_maximum_fusion.refs_3_ = bf16[8,256,256]{2,1,0:T(8,128)(2,1)} fusion(bf16[4,256,256]{2,1,0:T(8,128)(2,1)S(1)} %copy-done.3, bf16[4,256,256]{2,1,0:T(8,128)(2,1)S(1)} %copy-done.4), kind=kLoop, calls=%fused_computation.14 | loop fusion | flops 524288 | bytes 2097152 | tf_op jit(solution)/shard_map/concatenate | solution.py:330
  37.4 1.3 %negate_multiply_fusion.scale_ref = f32[4,256,256]{2,1,0:T(8,128)} fusion(f32[4,256]{1,0:T(4,128)S(1)} %get-tuple-element.67, f32[4,256]{1,0:T(4,128)S(1)} %get-tuple-element.69, f32[4,256]{1,0:T(4,128)S(1)} %get-tuple-element.68, f32[4,256]{1,0:T(4,128)S(1)} %get-tuple-element.66), kind=kLoop, calls=%fused_computation.15 | loop fusion | flops 1310720 | bytes 1064960 | tf_op jit(solution)/shard_map/div | solution.py:57
  38.7 0.4 collective-permute-start.10
  39.2 0.4 collective-permute-start.6
  39.7 0.7 copy-done.9
  40.4 4.2 %shard_map.129 = (bf16[4,256,256]{2,1,0:T(8,128)(2,1)}, bf16[4,256,256]{2,1,0:T(8,128)(2,1)}) custom-call(s32[4]{0:T(128)} %broadcast_select_fusion.4.take_ref, bf16[2,256,256]{2,1,0:T(8,128)(2,1)} %own_ref.1, bf16[2,256,256]{2,1,0:T(8,128)(2,1)} %copy-done.9, bf16[6,256,256]{2,1,0:T(8,128)(2,1)} %copy-done.5, ...), custom_call_target="tpu_custom_call" | custom-call | flops 1207959552 | bytes 2621440 | tf_op jit(solution)/shard_map/pallas_call | solution.py:210
  44.5 7.1 %shard_map.130 = (f32[4,256,256]{2,1,0:T(8,128)}, f32[4,256,256]{2,1,0:T(8,128)}, f32[4,256,256]{2,1,0:T(8,128)}, f32[4,8,128]{2,1,0:T(8,128)}) custom-call(s32[4]{0:T(128)} %and_select_fusion.4.refs_0_, bf16[4,256,256]{2,1,0:T(8,128)(2,1)} %get-tuple-element.22.refs_1_, bf16[4,256,256]{2,1,0:T(8,128)(2,1)} %get-tuple-element.23.refs_2_, ...), custom_call_target="tpu_custom_call" | custom-call | flops 9663676416 | bytes 12582912 | tf_op jit(solution)/shard_map/pallas_call | solution.py:305
  51.6 0.8 %copy-done.8 = bf16[4,256,256]{2,1,0:T(8,128)(2,1)} copy-done((bf16[4,256,256]{2,1,0:T(8,128)(2,1)}, bf16[4,256,256]{2,1,0:T(8,128)(2,1)S(1)}, u32[]{:S(2)}) %copy-start.8) | copy-done | bytes 524312
  52.4 7.7 %shard_map.131 = (f32[4,256,256]{2,1,0:T(8,128)}, f32[4,256,256]{2,1,0:T(8,128)}, f32[4,256,256]{2,1,0:T(8,128)}, f32[4,8,128]{2,1,0:T(8,128)}) custom-call(s32[4]{0:T(128)} %and_select_fusion.5.refs_0_, bf16[4,256,256]{2,1,0:T(8,128)(2,1)} %get-tuple-element.22.refs_1_, ...), custom_call_target="tpu_custom_call", output_to_operand_aliasing={{0}: (7, {}), {1}: (8, {}), {2}: (9, {}), {3}: (10, {})} | custom-call | flops 9663676416 | bytes 12582912 | tf_op jit(solution)/shard_map/pallas_call | solution.py:305
  60.2 0.8 %copy-done.7 = bf16[4,256,256]{2,1,0:T(8,128)(2,1)} copy-done((bf16[4,256,256]{2,1,0:T(8,128)(2,1)}, bf16[4,256,256]{2,1,0:T(8,128)(2,1)S(1)}, u32[]{:S(2)}) %copy-start.7) | copy-done | bytes 524312
  61.0 7.7 %shard_map.132 = (f32[4,256,256]{2,1,0:T(8,128)}, f32[4,256,256]{2,1,0:T(8,128)}, f32[4,256,256]{2,1,0:T(8,128)}, f32[4,8,128]{2,1,0:T(8,128)}) custom-call(s32[4]{0:T(128)} %and_select_fusion.6.refs_0_, bf16[4,256,256]{2,1,0:T(8,128)(2,1)} %get-tuple-element.22.refs_1_, ...), custom_call_target="tpu_custom_call", output_to_operand_aliasing={{0}: (7, {}), {1}: (8, {}), {2}: (9, {}), {3}: (10, {})} | custom-call | flops 9663676416 | bytes 12582912 | tf_op jit(solution)/shard_map/pallas_call | solution.py:305
  68.7 0.8 %copy-done.6 = bf16[4,256,256]{2,1,0:T(8,128)(2,1)} copy-done((bf16[4,256,256]{2,1,0:T(8,128)(2,1)}, bf16[4,256,256]{2,1,0:T(8,128)(2,1)S(1)}, u32[]{:S(2)}) %copy-start.6) | copy-done | bytes 524312
  69.5 7.8 %shard_map.133 = (f32[4,256,256]{2,1,0:T(8,128)}, f32[4,256,256]{2,1,0:T(8,128)}, f32[4,256,256]{2,1,0:T(8,128)}, f32[4,16]{1,0:T(4,128)}) custom-call(s32[4]{0:T(128)} %and_select_fusion.7.refs_0_, bf16[4,256,256]{2,1,0:T(8,128)(2,1)} %get-tuple-element.22.refs_1_, ...), custom_call_target="tpu_custom_call", output_to_operand_aliasing={{0}: (7, {}), {1}: (8, {}), {2}: (9, {})} | custom-call | flops 9663676416 | bytes 12582912 | tf_op jit(solution)/shard_map/pallas_call | solution.py:305
  (122 shorter events, 4.5 us)
Async XLA Ops:
  0.6 24.1 %copy-start = (s32[16]{0:T(128)S(1)}, s32[16]{0:T(128)}, u32[]{:S(2)}) copy-start(s32[16]{0:T(128)} %param.20) | copy-start | bytes 196
  0.7 0.7 copy-start.1
  3.8 1.0 %copy-start.3 = (bf16[4,256,256]{2,1,0:T(8,128)(2,1)S(1)}, bf16[4,256,256]{2,1,0:T(8,128)(2,1)}, u32[]{:S(2)}) copy-start(bf16[4,256,256]{2,1,0:T(8,128)(2,1)} %param.19) | copy-start | bytes 1572868
  4.0 1.1 %copy-start.4 = (bf16[4,256,256]{2,1,0:T(8,128)(2,1)S(1)}, bf16[4,256,256]{2,1,0:T(8,128)(2,1)}, u32[]{:S(2)}) copy-start(bf16[4,256,256]{2,1,0:T(8,128)(2,1)} %param.18) | copy-start | bytes 1572868
  5.1 33.6 %collective-permute-start.9 = (bf16[4,256,256]{2,1,0:T(8,128)(2,1)S(1)}, bf16[4,256,256]{2,1,0:T(8,128)(2,1)}, u32[]{:S(2)}, u32[]{:S(2)}) collective-permute-start(bf16[4,256,256]{2,1,0:T(8,128)(2,1)S(1)} %pad_maximum_fusion.1), channel_id=1, source_target_pairs={{0,8},{8,0},{16,24},{24,16},{1,9},{9,1},{17,25},{25,17},{2,10},{10... | collective-permute-start | bytes 1572872 | tf_op jit(solution)/shard_map/ppermute | solution.py:338
  8.1 31.0 %collective-permute-start.7 = (bf16[4,256,256]{2,1,0:T(8,128)(2,1)S(1)}, bf16[4,256,256]{2,1,0:T(8,128)(2,1)}, u32[]{:S(2)}, u32[]{:S(2)}) collective-permute-start(bf16[4,256,256]{2,1,0:T(8,128)(2,1)S(1)} %pad_maximum_fusion.1), channel_id=1, source_target_pairs={{0,16},{8,24},{16,0},{24,8},{1,17},{9,25},{17,1},{25,9},{2,18},{10... | collective-permute-start | bytes 1572872 | tf_op jit(solution)/shard_map/ppermute | solution.py:338
  9.7 29.6 %collective-permute-start.5 = (bf16[4,256,256]{2,1,0:T(8,128)(2,1)S(1)}, bf16[4,256,256]{2,1,0:T(8,128)(2,1)}, u32[]{:S(2)}, u32[]{:S(2)}) collective-permute-start(bf16[4,256,256]{2,1,0:T(8,128)(2,1)S(1)} %pad_maximum_fusion.1), channel_id=1, source_target_pairs={{0,24},{8,16},{16,8},{24,0},{1,25},{9,17},{17,9},{25,1},{2,26},{10... | collective-permute-start | bytes 1572872 | tf_op jit(solution)/shard_map/ppermute | solution.py:338
  9.7 20.2 %collective-permute-start.1 = (bf16[2,256,256]{2,1,0:T(8,128)(2,1)S(1)}, bf16[2,256,256]{2,1,0:T(8,128)(2,1)S(1)}, u32[]{:S(2)}, u32[]{:S(2)}) collective-permute-start(bf16[2,256,256]{2,1,0:T(8,128)(2,1)S(1)} %get-tuple-element.49), channel_id=1, source_target_pairs={{0,2},{1,3},{2,0},{3,1},{4,6},{5,7},{6,4},{7,5},{8,10},{9,11},{10,... | collective-permute-start | bytes 786440 | tf_op jit(solution)/shard_map/ppermute | solution.py:98
  11.8 15.6 %collective-permute-start.2 = (bf16[2,256,256]{2,1,0:T(8,128)(2,1)S(1)}, bf16[2,256,256]{2,1,0:T(8,128)(2,1)S(1)}, u32[]{:S(2)}, u32[]{:S(2)}) collective-permute-start(bf16[2,256,256]{2,1,0:T(8,128)(2,1)S(1)} %get-tuple-element.48), channel_id=1, source_target_pairs={{0,4},{1,5},{2,6},{3,7},{4,0},{5,1},{6,2},{7,3},{8,12},{9,13},{10,... | collective-permute-start | bytes 786440 | tf_op jit(solution)/shard_map/ppermute | solution.py:99
  18.0 0.7 copy-start.10
  19.5 0.7 copy-start.2
  28.1 6.7 %collective-permute-start.3 = (bf16[2,256,256]{2,1,0:T(8,128)(2,1)S(1)}, bf16[2,256,256]{2,1,0:T(8,128)(2,1)S(1)}, u32[]{:S(2)}, u32[]{:S(2)}) collective-permute-start(bf16[2,256,256]{2,1,0:T(8,128)(2,1)S(1)} %broadcast_select_fusion.1), channel_id=1, source_target_pairs={{0,2},{1,3},{2,0},{3,1},{4,6},{5,7},{6,4},{7,5},{8,10},{9,11},{10,... | collective-permute-start | bytes 786440 | tf_op jit(solution)/shard_map/ppermute | solution.py:102
  30.0 9.7 %collective-permute-start = (bf16[2,256,256]{2,1,0:T(8,128)(2,1)S(1)}, bf16[2,256,256]{2,1,0:T(8,128)(2,1)S(1)}, u32[]{:S(2)}, u32[]{:S(2)}) collective-permute-start(bf16[2,256,256]{2,1,0:T(8,128)(2,1)S(1)} %get-tuple-element.50), channel_id=1, source_target_pairs={{0,1},{1,0},{2,3},{3,2},{4,5},{5,4},{6,7},{7,6},{8,9},{9,8},{10,11... | collective-permute-start | bytes 786440 | tf_op jit(solution)/shard_map/ppermute | solution.py:97
  34.9 2.5 %copy-start.5 = (bf16[6,256,256]{2,1,0:T(8,128)(2,1)}, bf16[6,256,256]{2,1,0:T(8,128)(2,1)S(1)}, u32[]{:S(2)}) copy-start(bf16[6,256,256]{2,1,0:T(8,128)(2,1)S(1)} %constant_dynamic-update-slice_fusion.recv_ref) | copy-start | bytes 2359300
  34.9 4.8 %collective-permute-start.4 = (bf16[6,256,256]{2,1,0:T(8,128)(2,1)S(1)}, bf16[6,256,256]{2,1,0:T(8,128)(2,1)}, u32[]{:S(2)}, u32[]{:S(2)}) collective-permute-start(bf16[6,256,256]{2,1,0:T(8,128)(2,1)S(1)} %constant_dynamic-update-slice_fusion.recv_ref), channel_id=1, source_target_pairs={{0,1},{1,0},{2,3},{3,2},{4,5},{5,4},{6,7},{7,6},{8,9},{9,8},{10,11... | collective-permute-start | bytes 2359304 | tf_op jit(solution)/shard_map/ppermute | solution.py:105
  38.7 12.9 %collective-permute-start.10 = (bf16[4,256,256]{2,1,0:T(8,128)(2,1)}, bf16[4,256,256]{2,1,0:T(8,128)(2,1)S(1)}, u32[]{:S(2)}, u32[]{:S(2)}) collective-permute-start(bf16[4,256,256]{2,1,0:T(8,128)(2,1)} %collective-permute-done.9.refs_3_), channel_id=1, source_target_pairs={{0,1},{1,0},{2,3},{3,2},{4,5},{5,4},{6,7},{7,6},{8,9},{9,8},{10,11... | collective-permute-start | bytes 1572872 | tf_op jit(solution)/shard_map/ppermute | solution.py:339
  39.1 21.0 %collective-permute-start.8 = (bf16[4,256,256]{2,1,0:T(8,128)(2,1)}, bf16[4,256,256]{2,1,0:T(8,128)(2,1)S(1)}, u32[]{:S(2)}, u32[]{:S(2)}) collective-permute-start(bf16[4,256,256]{2,1,0:T(8,128)(2,1)} %collective-permute-done.7.refs_3_), channel_id=1, source_target_pairs={{0,1},{1,0},{2,3},{3,2},{4,5},{5,4},{6,7},{7,6},{8,9},{9,8},{10,11... | collective-permute-start | bytes 1572872 | tf_op jit(solution)/shard_map/ppermute | solution.py:339
  39.2 29.5 %collective-permute-start.6 = (bf16[4,256,256]{2,1,0:T(8,128)(2,1)}, bf16[4,256,256]{2,1,0:T(8,128)(2,1)S(1)}, u32[]{:S(2)}, u32[]{:S(2)}) collective-permute-start(bf16[4,256,256]{2,1,0:T(8,128)(2,1)} %collective-permute-done.5.refs_3_), channel_id=1, source_target_pairs={{0,1},{1,0},{2,3},{3,2},{4,5},{5,4},{6,7},{7,6},{8,9},{9,8},{10,11... | collective-permute-start | bytes 1572872 | tf_op jit(solution)/shard_map/ppermute | solution.py:339
  39.7 0.7 copy-start.9
  51.6 0.8 %copy-start.8 = (bf16[4,256,256]{2,1,0:T(8,128)(2,1)}, bf16[4,256,256]{2,1,0:T(8,128)(2,1)S(1)}, u32[]{:S(2)}) copy-start(bf16[4,256,256]{2,1,0:T(8,128)(2,1)S(1)} %collective-permute-done.10.refs_4_) | copy-start | bytes 1572868
  60.2 0.8 %copy-start.7 = (bf16[4,256,256]{2,1,0:T(8,128)(2,1)}, bf16[4,256,256]{2,1,0:T(8,128)(2,1)S(1)}, u32[]{:S(2)}) copy-start(bf16[4,256,256]{2,1,0:T(8,128)(2,1)S(1)} %collective-permute-done.8.refs_4_) | copy-start | bytes 1572868
  68.7 0.8 %copy-start.6 = (bf16[4,256,256]{2,1,0:T(8,128)(2,1)}, bf16[4,256,256]{2,1,0:T(8,128)(2,1)S(1)}, u32[]{:S(2)}) copy-start(bf16[4,256,256]{2,1,0:T(8,128)(2,1)S(1)} %collective-permute-done.6.refs_4_) | copy-start | bytes 1572868

commit v12 on v10

--- a/solution.py
+++ b/solution.py
@@ -13,6 +13,7 @@
 SLOT = 2
 CAP = 4
 TILE_T = 4
+PER_STEP = 2
 
 
 AMPLITUDE = 0.07
@@ -163,52 +164,58 @@
     else:
         top_in, sum_in, sq_in, peak_in, top_ref, sum_ref, sq_ref, peak_ref = rest
     extent = sr_ref.shape[-1]
-    sr = sr_ref[0].astype(jnp.float32)
-    si = si_ref[0].astype(jnp.float32)
+    per_step = sr_ref.shape[0]
     forward = fw_ref[...]
     inverse = inv_ref[...]
     row_shape = (8, 128 * ((orient_total + 127) // 128))
     lanes = lax.broadcasted_iota(jnp.int32, row_shape, 1)
-    peak_row = jnp.zeros(row_shape, jnp.float32) if first else peak_in[0]
-    top = total = square = None
-    prods = []
+    templs = []
     for templ_ref, count in zip(templ_refs, counts):
         for t in range(count):
-            tr = templ_ref[t].astype(jnp.float32)
-            ti = templ_ref[count + t].astype(jnp.float32)
+            templs.append((templ_ref[t].astype(jnp.float32), templ_ref[count + t].astype(jnp.float32)))
+    prods = []
+    for j in range(per_step):
+        sr = sr_ref[j].astype(jnp.float32)
+        si = si_ref[j].astype(jnp.float32)
+        for tr, ti in templs:
             pre = (sr * tr + si * ti).astype(jnp.bfloat16)
             pim = (si * tr - sr * ti).astype(jnp.bfloat16)
             prods.append(jnp.concatenate([pre, pim], axis=1))
     q_all = jnp.dot(jnp.concatenate(prods, axis=0), forward,
                     preferred_element_type=jnp.float32).astype(jnp.bfloat16)
-    for position in range(len(prods)):
-        q = q_all[position * extent:(position + 1) * extent]
-        q_stack = jnp.concatenate([q[:, :extent], q[:, extent:]], axis=0)
-        corr = jnp.dot(inverse, q_stack, preferred_element_type=jnp.float32)
-        peak_row = jnp.where(lanes == orient_ref[position], jnp.max(corr), peak_row)
-        if top is None:
-            top, total, square = corr, corr, corr * corr
+    tiles = len(templs)
+    for j in range(per_step):
+        peak_row = jnp.zeros(row_shape, jnp.float32) if first else peak_in[j]
+        top = total = square = None
+        for position in range(tiles):
+            row = (j * tiles + position) * extent
+            q = q_all[row:row + extent]
+            q_stack = jnp.concatenate([q[:, :extent], q[:, extent:]], axis=0)
+            corr = jnp.dot(inverse, q_stack, preferred_element_type=jnp.float32)
+            peak_row = jnp.where(lanes == orient_ref[position], jnp.max(corr), peak_row)
+            if top is None:
+                top, total, square = corr, corr, corr * corr
+            else:
+                top = jnp.maximum(top, corr)
+                total = total + corr
+                square = square + corr * corr
+        if not first:
+            top = jnp.maximum(top_in[j], top)
+            total = sum_in[j] + total
+            square = sq_in[j] + square
+        top_ref[j] = top
+        if last:
+            s = pl.program_id(0) * per_step + j
+            peak_ref[pl.ds(s, 1), :] = peak_row[0:1, :orient_total]
         else:
-            top = jnp.maximum(top, corr)
-            total = total + corr
-            square = square + corr * corr
-    if not first:
-        top = jnp.maximum(top_in[0], top)
-        total = sum_in[0] + total
-        square = sq_in[0] + square
-    top_ref[0] = top
-    if last:
-        s = pl.program_id(0)
-        peak_ref[pl.ds(s, 1), :] = peak_row[0:1, :orient_total]
-    else:
-        peak_ref[0] = peak_row
-    if last:
-        mean = total / orient_total
-        sum_ref[0] = mean
-        sq_ref[0] = square / orient_total - mean * mean
-    else:
-        sum_ref[0] = total
-        sq_ref[0] = square
+            peak_ref[j] = peak_row
+        if last:
+            mean = total / orient_total
+            sum_ref[j] = mean
+            sq_ref[j] = square / orient_total - mean * mean
+        else:
+            sum_ref[j] = total
+            sq_ref[j] = square
 
 
 def correlate_chunk(spec_re, spec_im, templ_groups, forward, inverse, orient_chunk,
@@ -218,8 +225,9 @@
     tiles = sum(counts)
     first = stats is None
     lanes = 128 * ((orient_total + 127) // 128)
-    plane = pl.BlockSpec((1, extent, extent), lambda s: (s, 0, 0))
-    peak_spec = pl.BlockSpec((1, 8, lanes), lambda s: (s, 0, 0))
+    per_step = PER_STEP if count % PER_STEP == 0 else 1
+    plane = pl.BlockSpec((per_step, extent, extent), lambda s: (s, 0, 0))
+    peak_spec = pl.BlockSpec((per_step, 8, lanes), lambda s: (s, 0, 0))
     templ_specs = [pl.BlockSpec(group.shape, lambda s: (0, 0, 0)) for group in templ_groups]
     fw_spec = pl.BlockSpec(forward.shape, lambda s: (0, 0))
     inv_spec = pl.BlockSpec(inverse.shape, lambda s: (0, 0))
@@ -238,7 +246,7 @@
     flops = 3 * tiles * count * 12 * extent * extent * extent
     return pl.pallas_call(
         functools.partial(corr_kernel, first, last, counts, orient_total),
-        grid=(count,),
+        grid=(count // per_step,),
         in_specs=in_specs,
         out_specs=[plane, plane, plane,
                    pl.BlockSpec((count, orient_total), lambda s: (0, 0)) if last else peak_spec],

time: 75.5 us -> 75.3 us (level)
  transfers between devices with their start and end apart: 11 -> 11, of which waited for: 2 -> 2; matrix products, arithmetic and copies ran while one was open for 17% -> 17% of each run, Pallas kernels for 36% -> 35%
where the time goes in v12:
time: 75.3 us; the launch traced here: 75 us
  Pallas kernels  34.3 us (46%)
  starting transfers between devices  17.5 us (23%)
  local copies, waits for them, and re-layouts  11.4 us (15%)
  other arithmetic  6.85 us (9%)
  waiting for transfers between devices  3.82 us (5%)
  between operations  1.2 us (2%)
    pallas_call x4, Pallas kernels, correlate_chunk(): pl.pallas_call(functools.partial(corr_kernel, first, last, counts, orient...  30.2 us
    ppermute x1, starting transfers between devices, route_patches(): direct = lax.ppermute(outgoing[0], 'patch', xor_pairs(sources, 1))  9.04 us
    unnamed x26, local copies, waits for them, and re-layouts  4.37 us
    pallas_call x1, Pallas kernels, make_spectra(): pl.pallas_call(functools.partial(spectra_kernel, rows), in_specs=[pl.Bloc...  4.12 us
    ppermute x3, waiting for transfers between devices, route_patches(): lax.ppermute(outgoing[m], 'patch', xor_pairs(sources, 2 * m))  3.8 us
    ppermute x3, starting transfers between devices, correlate_all(): got = lax.ppermute(mine, 'blk', [(b, b ^ k) for b in range(blocks)])  2.75 us
    ppermute x3, starting transfers between devices, route_patches(): lax.ppermute(outgoing[m], 'patch', xor_pairs(sources, 2 * m))  2.71 us
    select_n x8, other arithmetic, correlate_all(): orient_chunk = jnp.take(orientation, index)  2.61 us
  transfers between devices with their start and end apart: 11, of which 2 were waited for; matrix products, arithmetic and copies ran while one was open for 17% of the time, Pallas kernels for 35%

profile of v12, /device:TPU:9, one launch (start us, length us, event | category | flops | bytes accessed | tf_op | source)
XLA Modules:
  0.0 75.0 jit_solution(13487435372498230753)
XLA Ops:
  0.7 1.1 %constant_dynamic-slice_fusion = (bf16[2,256,256]{2,1,0:T(8,128)(2,1)S(1)}, bf16[2,256,256]{2,1,0:T(8,128)(2,1)S(1)}) fusion(bf16[4,256,256]{2,1,0:T(8,128)(2,1)} %param.17, s32[]{:T(128)S(6)} %select_n.275, bf16[4,256,256]{2,1,0:T(8,128)(2,1)} %param.16), kind=kLoop, calls=%fused_computation.50 | loop fusion | bytes 1048580 | tf_op jit(solution)/shard_map/dynamic_slice | solution.py:275
  1.8 1.3 %collective-permute-start.9 = (bf16[4,256,256]{2,1,0:T(8,128)(2,1)S(1)}, bf16[4,256,256]{2,1,0:T(8,128)(2,1)}, u32[]{:S(2)}, u32[]{:S(2)}) collective-permute-start(bf16[4,256,256]{2,1,0:T(8,128)(2,1)S(1)} %pad_maximum_fusion.1), channel_id=1, source_target_pairs={{0,8},{8,0},{16,24},{24,16},{1,9},{9,1},{17,25},{25,17},{2,10},{10... | collective-permute-start | bytes 1572872 | tf_op jit(solution)/shard_map/ppermute | solution.py:280
  3.1 1.2 %collective-permute-start.7 = (bf16[4,256,256]{2,1,0:T(8,128)(2,1)S(1)}, bf16[4,256,256]{2,1,0:T(8,128)(2,1)S(1)}, u32[]{:S(2)}, u32[]{:S(2)}) collective-permute-start(bf16[4,256,256]{2,1,0:T(8,128)(2,1)S(1)} %pad_maximum_fusion.1), channel_id=1, source_target_pairs={{0,16},{8,24},{16,0},{24,8},{1,17},{9,25},{17,1},{25,9},{2,18},{10... | collective-permute-start | bytes 1572872 | tf_op jit(solution)/shard_map/ppermute | solution.py:280
  4.3 0.7 copy-done.6
  5.1 0.1 copy.42
  5.3 0.1 copy.43
  5.4 0.1 copy.44
  5.7 0.1 copy.46
  6.1 0.6 gather_fusion
  6.7 0.2 broadcast_select_fusion
  6.9 0.2 collective-permute-start.1
  7.2 2.3 %collective-permute-start.2 = (bf16[2,256,256]{2,1,0:T(8,128)(2,1)S(1)}, bf16[2,256,256]{2,1,0:T(8,128)(2,1)S(1)}, u32[]{:S(2)}, u32[]{:S(2)}) collective-permute-start(bf16[2,256,256]{2,1,0:T(8,128)(2,1)S(1)} %get-tuple-element.45), channel_id=1, source_target_pairs={{0,4},{1,5},{2,6},{3,7},{4,0},{5,1},{6,2},{7,3},{8,12},{9,13},{10,... | collective-permute-start | bytes 786440 | tf_op jit(solution)/shard_map/ppermute | solution.py:88
  9.5 0.2 collective-permute-start.3
  9.8 0.1 reduce
  9.9 0.1 fusion.6
  10.0 0.1 select_reduce_fusion.1
  10.3 0.6 copy-done.11
  11.0 0.6 gather_fusion.1
  11.8 0.7 copy-done.1
  12.4 0.6 gather_fusion.2
  13.1 0.4 fusion.13
  13.7 0.2 select_reduce_fusion
  13.8 0.5 broadcast_select_fusion.2.take_ref
  14.5 0.6 gather_fusion.6
  15.1 0.6 and_select_fusion.refs_0_
  15.7 0.6 gather_fusion.5
  16.3 0.6 and_select_fusion.1.refs_0_
  16.9 0.1 fusion.1
  17.1 0.6 gather_fusion.4
  17.8 0.6 gather_fusion.3
  18.4 0.2 collective-permute-start.5
  18.7 1.6 %collective-permute-done.2 = bf16[2,256,256]{2,1,0:T(8,128)(2,1)S(1)} collective-permute-done((bf16[2,256,256]{2,1,0:T(8,128)(2,1)S(1)}, bf16[2,256,256]{2,1,0:T(8,128)(2,1)S(1)}, u32[]{:S(2)}, u32[]{:S(2)}) %collective-permute-start.2) | collective-permute-done | bytes 262176 | tf_op jit(solution)/shard_map/ppermute | solution.py:88
  20.2 9.0 %collective-permute-start = (bf16[2,256,256]{2,1,0:T(8,128)(2,1)S(1)}, bf16[2,256,256]{2,1,0:T(8,128)(2,1)S(1)}, u32[]{:S(2)}, u32[]{:S(2)}) collective-permute-start(bf16[2,256,256]{2,1,0:T(8,128)(2,1)S(1)} %get-tuple-element.47), channel_id=1, source_target_pairs={{0,1},{1,0},{2,3},{3,2},{4,5},{5,4},{6,7},{7,6},{8,9},{9,8},{10,11... | collective-permute-start | bytes 786440 | tf_op jit(solution)/shard_map/ppermute | solution.py:85
  29.3 2.2 %collective-permute-done.3 = bf16[2,256,256]{2,1,0:T(8,128)(2,1)S(1)} collective-permute-done((bf16[2,256,256]{2,1,0:T(8,128)(2,1)S(1)}, bf16[2,256,256]{2,1,0:T(8,128)(2,1)S(1)}, u32[]{:S(2)}, u32[]{:S(2)}) %collective-permute-start.3) | collective-permute-done | bytes 262176 | tf_op jit(solution)/shard_map/ppermute | solution.py:88
  31.6 2.4 %collective-permute-start.4 = (bf16[6,256,256]{2,1,0:T(8,128)(2,1)S(1)}, bf16[6,256,256]{2,1,0:T(8,128)(2,1)S(1)}, u32[]{:S(2)}, u32[]{:S(2)}) collective-permute-start(bf16[6,256,256]{2,1,0:T(8,128)(2,1)S(1)} %constant_dynamic-update-slice_fusion.recv_ref), channel_id=1, source_target_pairs={{0,1},{1,0},{2,3},{3,2},{4,5},{5,4},{6,7},{7,6},{8,9},{9,8},{10,11... | collective-permute-start | bytes 2359304 | tf_op jit(solution)/shard_map/ppermute | solution.py:90
  33.9 0.7 and_select_fusion.2.refs_0_
  34.6 0.6 and_select_fusion.3.refs_0_
  35.2 1.1 %pad_maximum_fusion.refs_3_ = bf16[8,256,256]{2,1,0:T(8,128)(2,1)} fusion(bf16[4,256,256]{2,1,0:T(8,128)(2,1)S(1)} %copy-done.2, bf16[4,256,256]{2,1,0:T(8,128)(2,1)S(1)} %copy-done.3), kind=kLoop, calls=%fused_computation.7 | loop fusion | flops 524288 | bytes 2097152 | tf_op jit(solution)/shard_map/concatenate | solution.py:272
  36.2 1.3 %negate_multiply_fusion.scale_ref = f32[4,256,256]{2,1,0:T(8,128)} fusion(f32[4,256]{1,0:T(4,128)S(1)} %get-tuple-element.53, f32[4,256]{1,0:T(4,128)S(1)} %get-tuple-element.55, f32[4,256]{1,0:T(4,128)S(1)} %get-tuple-element.54, f32[4,256]{1,0:T(4,128)S(1)} %get-tuple-element.52), kind=kLoop, calls=%fused_computation.8 | loop fusion | flops 1310720 | bytes 1064960 | tf_op jit(solution)/shard_map/div | solution.py:58
  37.7 0.4 collective-permute-start.8
  38.2 0.7 copy-done.10
  38.9 0.9 %copy-done.7 = bf16[6,256,256]{2,1,0:T(8,128)(2,1)} copy-done((bf16[6,256,256]{2,1,0:T(8,128)(2,1)}, bf16[6,256,256]{2,1,0:T(8,128)(2,1)S(1)}, u32[]{:S(2)}) %copy-start.7) | copy-done | bytes 786456
  39.7 4.1 %shard_map.129 = (bf16[4,256,256]{2,1,0:T(8,128)(2,1)}, bf16[4,256,256]{2,1,0:T(8,128)(2,1)}) custom-call(s32[4]{0:T(128)} %broadcast_select_fusion.2.take_ref, bf16[2,256,256]{2,1,0:T(8,128)(2,1)} %own_ref.1, bf16[2,256,256]{2,1,0:T(8,128)(2,1)} %copy-done.10, bf16[6,256,256]{2,1,0:T(8,128)(2,1)} %copy-done.5, bf16[6,256,256]{2,1,0:T(8,128)(2,1)} %copy-done.7, ...), custom_call_target="tpu_custom_call" | custom-call | flops 1207959552 | bytes 2621440 | tf_op jit(solution)/shard_map/pallas_call | solution.py:145
  43.9 7.0 %shard_map.130 = (f32[4,256,256]{2,1,0:T(8,128)}, f32[4,256,256]{2,1,0:T(8,128)}, f32[4,256,256]{2,1,0:T(8,128)}, f32[4,8,128]{2,1,0:T(8,128)}) custom-call(s32[4]{0:T(128)} %and_select_fusion.refs_0_, bf16[4,256,256]{2,1,0:T(8,128)(2,1)} %get-tuple-element.21.refs_1_, bf16[4,256,256]{2,1,0:T(8,128)(2,1)} %get-tuple-element.22.refs_2_, ...), custom_call_target="tpu_custom_call" | custom-call | flops 9663676416 | bytes 12582912 | tf_op jit(solution)/shard_map/pallas_call | solution.py:247
  50.9 7.7 %shard_map.131 = (f32[4,256,256]{2,1,0:T(8,128)}, f32[4,256,256]{2,1,0:T(8,128)}, f32[4,256,256]{2,1,0:T(8,128)}, f32[4,8,128]{2,1,0:T(8,128)}) custom-call(s32[4]{0:T(128)} %and_select_fusion.1.refs_0_, bf16[4,256,256]{2,1,0:T(8,128)(2,1)} %get-tuple-element.21.refs_1_, ...), custom_call_target="tpu_custom_call", output_to_operand_aliasing={{0}: (7, {}), {1}: (8, {}), {2}: (9, {}), {3}: (10, {})} | custom-call | flops 9663676416 | bytes 12582912 | tf_op jit(solution)/shard_map/pallas_call | solution.py:247
  58.6 7.7 %shard_map.132 = (f32[4,256,256]{2,1,0:T(8,128)}, f32[4,256,256]{2,1,0:T(8,128)}, f32[4,256,256]{2,1,0:T(8,128)}, f32[4,8,128]{2,1,0:T(8,128)}) custom-call(s32[4]{0:T(128)} %and_select_fusion.2.refs_0_, bf16[4,256,256]{2,1,0:T(8,128)(2,1)} %get-tuple-element.21.refs_1_, ...), custom_call_target="tpu_custom_call", output_to_operand_aliasing={{0}: (7, {}), {1}: (8, {}), {2}: (9, {}), {3}: (10, {})} | custom-call | flops 9663676416 | bytes 12582912 | tf_op jit(solution)/shard_map/pallas_call | solution.py:247
  66.4 0.8 %copy-done.9 = bf16[4,256,256]{2,1,0:T(8,128)(2,1)} copy-done((bf16[4,256,256]{2,1,0:T(8,128)(2,1)}, bf16[4,256,256]{2,1,0:T(8,128)(2,1)S(1)}, u32[]{:S(2)}) %copy-start.9) | copy-done | bytes 524312
  67.2 7.7 %shard_map.133 = (f32[4,256,256]{2,1,0:T(8,128)}, f32[4,256,256]{2,1,0:T(8,128)}, f32[4,256,256]{2,1,0:T(8,128)}, f32[4,16]{1,0:T(4,128)}) custom-call(s32[4]{0:T(128)} %and_select_fusion.3.refs_0_, bf16[4,256,256]{2,1,0:T(8,128)(2,1)} %get-tuple-element.21.refs_1_, ...), custom_call_target="tpu_custom_call", output_to_operand_aliasing={{0}: (7, {}), {1}: (8, {}), {2}: (9, {})} | custom-call | flops 9663676416 | bytes 12582912 | tf_op jit(solution)/shard_map/pallas_call | solution.py:247
  (75 shorter events, 1.7 us)
Async XLA Ops:
  0.6 13.8 %copy-start = (s32[16]{0:T(128)S(1)}, s32[16]{0:T(128)}, u32[]{:S(2)}) copy-start(s32[16]{0:T(128)} %param.18) | copy-start | bytes 196
  1.7 4.3 %copy-start.4 = (bf16[2,256,256]{2,1,0:T(8,128)(2,1)S(1)}, bf16[2,256,256]{2,1,0:T(8,128)(2,1)}, u32[]{:S(2)}) copy-start(bf16[2,256,256]{2,1,0:T(8,128)(2,1)} %own_ref.1) | copy-start | bytes 786436
  1.8 35.7 %collective-permute-start.9 = (bf16[4,256,256]{2,1,0:T(8,128)(2,1)S(1)}, bf16[4,256,256]{2,1,0:T(8,128)(2,1)}, u32[]{:S(2)}, u32[]{:S(2)}) collective-permute-start(bf16[4,256,256]{2,1,0:T(8,128)(2,1)S(1)} %pad_maximum_fusion.1), channel_id=1, source_target_pairs={{0,8},{8,0},{16,24},{24,16},{1,9},{9,1},{17,25},{25,17},{2,10},{10... | collective-permute-start | bytes 1572872 | tf_op jit(solution)/shard_map/ppermute | solution.py:280
  3.1 34.6 %collective-permute-start.7 = (bf16[4,256,256]{2,1,0:T(8,128)(2,1)S(1)}, bf16[4,256,256]{2,1,0:T(8,128)(2,1)S(1)}, u32[]{:S(2)}, u32[]{:S(2)}) collective-permute-start(bf16[4,256,256]{2,1,0:T(8,128)(2,1)S(1)} %pad_maximum_fusion.1), channel_id=1, source_target_pairs={{0,16},{8,24},{16,0},{24,8},{1,17},{9,25},{17,1},{25,9},{2,18},{10... | collective-permute-start | bytes 1572872 | tf_op jit(solution)/shard_map/ppermute | solution.py:280
  4.3 0.7 copy-start.6
  6.9 11.5 %collective-permute-start.1 = (bf16[2,256,256]{2,1,0:T(8,128)(2,1)S(1)}, bf16[2,256,256]{2,1,0:T(8,128)(2,1)S(1)}, u32[]{:S(2)}, u32[]{:S(2)}) collective-permute-start(bf16[2,256,256]{2,1,0:T(8,128)(2,1)S(1)} %get-tuple-element.46), channel_id=1, source_target_pairs={{0,2},{1,3},{2,0},{3,1},{4,6},{5,7},{6,4},{7,5},{8,10},{9,11},{10,... | collective-permute-start | bytes 786440 | tf_op jit(solution)/shard_map/ppermute | solution.py:88
  7.2 13.1 %collective-permute-start.2 = (bf16[2,256,256]{2,1,0:T(8,128)(2,1)S(1)}, bf16[2,256,256]{2,1,0:T(8,128)(2,1)S(1)}, u32[]{:S(2)}, u32[]{:S(2)}) collective-permute-start(bf16[2,256,256]{2,1,0:T(8,128)(2,1)S(1)} %get-tuple-element.45), channel_id=1, source_target_pairs={{0,4},{1,5},{2,6},{3,7},{4,0},{5,1},{6,2},{7,3},{8,12},{9,13},{10,... | collective-permute-start | bytes 786440 | tf_op jit(solution)/shard_map/ppermute | solution.py:88
  9.5 22.0 %collective-permute-start.3 = (bf16[2,256,256]{2,1,0:T(8,128)(2,1)S(1)}, bf16[2,256,256]{2,1,0:T(8,128)(2,1)S(1)}, u32[]{:S(2)}, u32[]{:S(2)}) collective-permute-start(bf16[2,256,256]{2,1,0:T(8,128)(2,1)S(1)} %get-tuple-element.44), channel_id=1, source_target_pairs={{0,6},{1,7},{2,4},{3,5},{4,2},{5,3},{6,0},{7,1},{8,14},{9,15},{10,... | collective-permute-start | bytes 786440 | tf_op jit(solution)/shard_map/ppermute | solution.py:88
  10.3 0.7 copy-start.11
  11.8 0.7 copy-start.1
  18.4 19.7 %collective-permute-start.5 = (bf16[4,256,256]{2,1,0:T(8,128)(2,1)S(1)}, bf16[4,256,256]{2,1,0:T(8,128)(2,1)}, u32[]{:S(2)}, u32[]{:S(2)}) collective-permute-start(bf16[4,256,256]{2,1,0:T(8,128)(2,1)S(1)} %pad_maximum_fusion.1), channel_id=1, source_target_pairs={{0,24},{8,16},{16,8},{24,0},{1,25},{9,17},{17,9},{25,1},{2,26},{10... | collective-permute-start | bytes 1572872 | tf_op jit(solution)/shard_map/ppermute | solution.py:280
  20.2 14.9 %copy-start.2 = (bf16[4,256,256]{2,1,0:T(8,128)(2,1)S(1)}, bf16[4,256,256]{2,1,0:T(8,128)(2,1)}, u32[]{:S(2)}) copy-start(bf16[4,256,256]{2,1,0:T(8,128)(2,1)} %param.17) | copy-start | bytes 1572868
  20.2 14.9 %copy-start.3 = (bf16[4,256,256]{2,1,0:T(8,128)(2,1)S(1)}, bf16[4,256,256]{2,1,0:T(8,128)(2,1)}, u32[]{:S(2)}) copy-start(bf16[4,256,256]{2,1,0:T(8,128)(2,1)} %param.16) | copy-start | bytes 1572868
  20.2 17.9 %collective-permute-start = (bf16[2,256,256]{2,1,0:T(8,128)(2,1)S(1)}, bf16[2,256,256]{2,1,0:T(8,128)(2,1)S(1)}, u32[]{:S(2)}, u32[]{:S(2)}) collective-permute-start(bf16[2,256,256]{2,1,0:T(8,128)(2,1)S(1)} %get-tuple-element.47), channel_id=1, source_target_pairs={{0,1},{1,0},{2,3},{3,2},{4,5},{5,4},{6,7},{7,6},{8,9},{9,8},{10,11... | collective-permute-start | bytes 786440 | tf_op jit(solution)/shard_map/ppermute | solution.py:85
  31.5 4.7 %copy-start.5 = (bf16[6,256,256]{2,1,0:T(8,128)(2,1)}, bf16[6,256,256]{2,1,0:T(8,128)(2,1)S(1)}, u32[]{:S(2)}) copy-start(bf16[6,256,256]{2,1,0:T(8,128)(2,1)S(1)} %constant_dynamic-update-slice_fusion.recv_ref) | copy-start | bytes 2359300
  31.6 6.6 %collective-permute-start.4 = (bf16[6,256,256]{2,1,0:T(8,128)(2,1)S(1)}, bf16[6,256,256]{2,1,0:T(8,128)(2,1)S(1)}, u32[]{:S(2)}, u32[]{:S(2)}) collective-permute-start(bf16[6,256,256]{2,1,0:T(8,128)(2,1)S(1)} %constant_dynamic-update-slice_fusion.recv_ref), channel_id=1, source_target_pairs={{0,1},{1,0},{2,3},{3,2},{4,5},{5,4},{6,7},{7,6},{8,9},{9,8},{10,11... | collective-permute-start | bytes 2359304 | tf_op jit(solution)/shard_map/ppermute | solution.py:90
  37.5 13.4 %collective-permute-start.10 = (bf16[4,256,256]{2,1,0:T(8,128)(2,1)}, bf16[4,256,256]{2,1,0:T(8,128)(2,1)}, u32[]{:S(2)}, u32[]{:S(2)}) collective-permute-start(bf16[4,256,256]{2,1,0:T(8,128)(2,1)} %collective-permute-done.9.refs_3_), channel_id=1, source_target_pairs={{0,1},{1,0},{2,3},{3,2},{4,5},{5,4},{6,7},{7,6},{8,9},{9,8},{10,11... | collective-permute-start | bytes 1572872 | tf_op jit(solution)/shard_map/ppermute | solution.py:281
  37.7 6.2 %copy-start.8 = (bf16[4,256,256]{2,1,0:T(8,128)(2,1)}, bf16[4,256,256]{2,1,0:T(8,128)(2,1)S(1)}, u32[]{:S(2)}) copy-start(bf16[4,256,256]{2,1,0:T(8,128)(2,1)S(1)} %collective-permute-done.7.refs_3_) | copy-start | bytes 1572868
  37.7 21.0 %collective-permute-start.8 = (bf16[4,256,256]{2,1,0:T(8,128)(2,1)S(1)}, bf16[4,256,256]{2,1,0:T(8,128)(2,1)}, u32[]{:S(2)}, u32[]{:S(2)}) collective-permute-start(bf16[4,256,256]{2,1,0:T(8,128)(2,1)S(1)} %collective-permute-done.7.refs_3_), channel_id=1, source_target_pairs={{0,1},{1,0},{2,3},{3,2},{4,5},{5,4},{6,7},{7,6},{8,9},{9,8},{10,11... | collective-permute-start | bytes 1572872 | tf_op jit(solution)/shard_map/ppermute | solution.py:281
  38.1 28.3 %collective-permute-start.6 = (bf16[4,256,256]{2,1,0:T(8,128)(2,1)}, bf16[4,256,256]{2,1,0:T(8,128)(2,1)S(1)}, u32[]{:S(2)}, u32[]{:S(2)}) collective-permute-start(bf16[4,256,256]{2,1,0:T(8,128)(2,1)} %collective-permute-done.5.refs_3_), channel_id=1, source_target_pairs={{0,1},{1,0},{2,3},{3,2},{4,5},{5,4},{6,7},{7,6},{8,9},{9,8},{10,11... | collective-permute-start | bytes 1572872 | tf_op jit(solution)/shard_map/ppermute | solution.py:281
  38.2 0.7 copy-start.10
  38.9 0.9 %copy-start.7 = (bf16[6,256,256]{2,1,0:T(8,128)(2,1)}, bf16[6,256,256]{2,1,0:T(8,128)(2,1)S(1)}, u32[]{:S(2)}) copy-start(bf16[6,256,256]{2,1,0:T(8,128)(2,1)S(1)} %collective-permute-done.4.fwd_ref) | copy-start | bytes 2359300
  66.4 0.8 %copy-start.9 = (bf16[4,256,256]{2,1,0:T(8,128)(2,1)}, bf16[4,256,256]{2,1,0:T(8,128)(2,1)S(1)}, u32[]{:S(2)}) copy-start(bf16[4,256,256]{2,1,0:T(8,128)(2,1)S(1)} %collective-permute-done.6.refs_4_) | copy-start | bytes 1572868

commit v13 on v10

--- a/solution.py
+++ b/solution.py
@@ -274,6 +274,9 @@
         index = jnp.concatenate(
             [source * tiles + core * half + within, source * tiles + (1 - core) * half + within])
         chunks.append(([got, passed], index))
+    if len(chunks) > 2:
+        merged = (chunks[0][0] + chunks[1][0], jnp.concatenate([chunks[0][1], chunks[1][1]]))
+        chunks = [merged] + chunks[2:]
     stats = None
     for n, (groups, index) in enumerate(chunks):
         orient_chunk = jnp.take(orientation, index)

time: 75.5 us -> 71.8 us (0.951)
  Pallas kernels: 34.5 us -> 30.8 us
  waiting for transfers between devices: 3.82 us -> 5.01 us
    pallas_call x4 -> x3, Pallas kernels: 30.4 us -> 26.7 us  [correlate_chunk(): pl.pallas_call(functools.partial(corr_kernel, first, last, counts, orient...]
    ppermute x3, waiting for transfers between devices: 3.8 us -> 4.99 us  [route_patches(): lax.ppermute(outgoing[m], 'patch', xor_pairs(sources, 2 * m))]
    select_n x8 -> x5, other arithmetic: 2.61 us -> 1.98 us  [correlate_all(): orient_chunk = jnp.take(orientation, index)]
    gather x4 -> x3, local copies, waits for them, and re-layouts: 2.55 us -> 1.93 us  [correlate_all(): orient_chunk = jnp.take(orientation, index)]
  transfers between devices with their start and end apart: 11 -> 11, of which waited for: 2 -> 2; matrix products, arithmetic and copies ran while one was open for 17% -> 16% of each run, Pallas kernels for 36% -> 32%
where the time goes in v13:
time: 71.8 us; the launch traced here: 71.5 us
  Pallas kernels  30.8 us (43%)
  starting transfers between devices  17.5 us (24%)
  local copies, waits for them, and re-layouts  10.8 us (15%)
  other arithmetic  6.33 us (9%)
  waiting for transfers between devices  5.01 us (7%)
  between operations  1.05 us (1%)
    pallas_call x3, Pallas kernels, correlate_chunk(): pl.pallas_call(functools.partial(corr_kernel, first, last, counts, orient...  26.7 us
    ppermute x1, starting transfers between devices, route_patches(): direct = lax.ppermute(outgoing[0], 'patch', xor_pairs(sources, 1))  9.04 us
    ppermute x3, waiting for transfers between devices, route_patches(): lax.ppermute(outgoing[m], 'patch', xor_pairs(sources, 2 * m))  4.99 us
    unnamed x26, local copies, waits for them, and re-layouts  4.37 us
    pallas_call x1, Pallas kernels, make_spectra(): pl.pallas_call(functools.partial(spectra_kernel, rows), in_specs=[pl.Bloc...  4.12 us
    ppermute x3, starting transfers between devices, correlate_all(): got = lax.ppermute(mine, 'blk', [(b, b ^ k) for b in range(blocks)])  2.75 us
    ppermute x3, starting transfers between devices, route_patches(): lax.ppermute(outgoing[m], 'patch', xor_pairs(sources, 2 * m))  2.71 us
    ppermute x1, starting transfers between devices, route_patches(): forwarded = lax.ppermute(received, 'patch', xor_pairs(sources, 1))  2.35 us
  transfers between devices with their start and end apart: 11, of which 2 were waited for; matrix products, arithmetic and copies ran while one was open for 16% of the time, Pallas kernels for 32%

profile of v13, /device:TPU:9, one launch (start us, length us, event | category | flops | bytes accessed | tf_op | source)
XLA Modules:
  0.0 71.5 jit_solution(14253146382802127718)
XLA Ops:
  0.7 1.1 %constant_dynamic-slice_fusion = (bf16[2,256,256]{2,1,0:T(8,128)(2,1)S(1)}, bf16[2,256,256]{2,1,0:T(8,128)(2,1)S(1)}) fusion(bf16[4,256,256]{2,1,0:T(8,128)(2,1)} %param.17, s32[]{:T(128)S(6)} %select_n.294, bf16[4,256,256]{2,1,0:T(8,128)(2,1)} %param.16), kind=kLoop, calls=%fused_computation.48 | loop fusion | bytes 1048580 | tf_op jit(solution)/shard_map/dynamic_slice | solution.py:267
  1.8 1.3 %collective-permute-start.9 = (bf16[4,256,256]{2,1,0:T(8,128)(2,1)S(1)}, bf16[4,256,256]{2,1,0:T(8,128)(2,1)}, u32[]{:S(2)}, u32[]{:S(2)}) collective-permute-start(bf16[4,256,256]{2,1,0:T(8,128)(2,1)S(1)} %pad_maximum_fusion.1), channel_id=1, source_target_pairs={{0,8},{8,0},{16,24},{24,16},{1,9},{9,1},{17,25},{25,17},{2,10},{10... | collective-permute-start | bytes 1572872 | tf_op jit(solution)/shard_map/ppermute | solution.py:272
  3.1 1.2 %collective-permute-start.7 = (bf16[4,256,256]{2,1,0:T(8,128)(2,1)S(1)}, bf16[4,256,256]{2,1,0:T(8,128)(2,1)S(1)}, u32[]{:S(2)}, u32[]{:S(2)}) collective-permute-start(bf16[4,256,256]{2,1,0:T(8,128)(2,1)S(1)} %pad_maximum_fusion.1), channel_id=1, source_target_pairs={{0,16},{8,24},{16,0},{24,8},{1,17},{9,25},{17,1},{25,9},{2,18},{10... | collective-permute-start | bytes 1572872 | tf_op jit(solution)/shard_map/ppermute | solution.py:272
  4.4 0.6 copy-done.6
  5.2 0.1 copy.38
  5.3 0.1 copy.39
  5.4 0.1 copy.40
  5.5 0.1 copy.41
  5.7 0.1 copy.42
  6.2 0.6 gather_fusion
  6.8 0.2 broadcast_select_fusion
  7.1 0.2 collective-permute-start.1
  7.3 2.3 %collective-permute-start.2 = (bf16[2,256,256]{2,1,0:T(8,128)(2,1)S(1)}, bf16[2,256,256]{2,1,0:T(8,128)(2,1)S(1)}, u32[]{:S(2)}, u32[]{:S(2)}) collective-permute-start(bf16[2,256,256]{2,1,0:T(8,128)(2,1)S(1)} %get-tuple-element.37), channel_id=1, source_target_pairs={{0,4},{1,5},{2,6},{3,7},{4,0},{5,1},{6,2},{7,3},{8,12},{9,13},{10,... | collective-permute-start | bytes 786440 | tf_op jit(solution)/shard_map/ppermute | solution.py:87
  9.6 0.2 collective-permute-start.3
  9.9 0.1 reduce
  10.0 0.1 fusion.6
  10.1 0.1 select_reduce_fusion.1
  10.4 0.6 copy-done.11
  11.1 0.6 gather_fusion.1
  11.9 0.7 copy-done.1
  12.5 0.6 gather_fusion.2
  13.2 0.4 fusion.13
  13.8 0.2 select_reduce_fusion
  13.9 0.5 broadcast_select_fusion.2.take_ref
  14.5 0.6 gather_fusion.5
  15.1 0.6 and_select_fusion.refs_0_
  15.9 0.1 fusion.1
  16.0 0.6 gather_fusion.3
  16.7 0.6 gather_fusion.4
  17.3 0.2 collective-permute-start.5
  17.6 2.8 %collective-permute-done.2 = bf16[2,256,256]{2,1,0:T(8,128)(2,1)S(1)} collective-permute-done((bf16[2,256,256]{2,1,0:T(8,128)(2,1)S(1)}, bf16[2,256,256]{2,1,0:T(8,128)(2,1)S(1)}, u32[]{:S(2)}, u32[]{:S(2)}) %collective-permute-start.2) | collective-permute-done | bytes 262176 | tf_op jit(solution)/shard_map/ppermute | solution.py:87
  20.4 9.0 %collective-permute-start = (bf16[2,256,256]{2,1,0:T(8,128)(2,1)S(1)}, bf16[2,256,256]{2,1,0:T(8,128)(2,1)S(1)}, u32[]{:S(2)}, u32[]{:S(2)}) collective-permute-start(bf16[2,256,256]{2,1,0:T(8,128)(2,1)S(1)} %get-tuple-element.39), channel_id=1, source_target_pairs={{0,1},{1,0},{2,3},{3,2},{4,5},{5,4},{6,7},{7,6},{8,9},{9,8},{10,11... | collective-permute-start | bytes 786440 | tf_op jit(solution)/shard_map/ppermute | solution.py:84
  29.4 2.2 %collective-permute-done.3 = bf16[2,256,256]{2,1,0:T(8,128)(2,1)S(1)} collective-permute-done((bf16[2,256,256]{2,1,0:T(8,128)(2,1)S(1)}, bf16[2,256,256]{2,1,0:T(8,128)(2,1)S(1)}, u32[]{:S(2)}, u32[]{:S(2)}) %collective-permute-start.3) | collective-permute-done | bytes 262176 | tf_op jit(solution)/shard_map/ppermute | solution.py:87
  31.7 2.4 %collective-permute-start.4 = (bf16[6,256,256]{2,1,0:T(8,128)(2,1)S(1)}, bf16[6,256,256]{2,1,0:T(8,128)(2,1)S(1)}, u32[]{:S(2)}, u32[]{:S(2)}) collective-permute-start(bf16[6,256,256]{2,1,0:T(8,128)(2,1)S(1)} %constant_dynamic-update-slice_fusion.recv_ref), channel_id=1, source_target_pairs={{0,1},{1,0},{2,3},{3,2},{4,5},{5,4},{6,7},{7,6},{8,9},{9,8},{10,11... | collective-permute-start | bytes 2359304 | tf_op jit(solution)/shard_map/ppermute | solution.py:89
  34.0 0.6 and_select_fusion.1.refs_0_
  34.6 0.1 collective-permute-start.10
  34.7 0.6 and_select_fusion.2.refs_0_
  35.3 1.1 %pad_maximum_fusion.refs_3_ = bf16[8,256,256]{2,1,0:T(8,128)(2,1)} fusion(bf16[4,256,256]{2,1,0:T(8,128)(2,1)S(1)} %copy-done.2, bf16[4,256,256]{2,1,0:T(8,128)(2,1)S(1)} %copy-done.3), kind=kLoop, calls=%fused_computation.6 | loop fusion | flops 524288 | bytes 2097152 | tf_op jit(solution)/shard_map/concatenate | solution.py:264
  36.4 1.3 %negate_multiply_fusion.scale_ref = f32[4,256,256]{2,1,0:T(8,128)} fusion(f32[4,256]{1,0:T(4,128)S(1)} %get-tuple-element.45, f32[4,256]{1,0:T(4,128)S(1)} %get-tuple-element.47, f32[4,256]{1,0:T(4,128)S(1)} %get-tuple-element.46, f32[4,256]{1,0:T(4,128)S(1)} %get-tuple-element.44), kind=kLoop, calls=%fused_computation.7 | loop fusion | flops 1310720 | bytes 1064960 | tf_op jit(solution)/shard_map/div | solution.py:57
  37.7 0.4 collective-permute-start.8
  38.1 0.1 collective-permute-start.6
  38.2 0.7 copy-done.10
  38.9 0.9 %copy-done.7 = bf16[6,256,256]{2,1,0:T(8,128)(2,1)} copy-done((bf16[6,256,256]{2,1,0:T(8,128)(2,1)}, bf16[6,256,256]{2,1,0:T(8,128)(2,1)S(1)}, u32[]{:S(2)}) %copy-start.7) | copy-done | bytes 786456
  39.8 4.1 %shard_map.129 = (bf16[4,256,256]{2,1,0:T(8,128)(2,1)}, bf16[4,256,256]{2,1,0:T(8,128)(2,1)}) custom-call(s32[4]{0:T(128)} %broadcast_select_fusion.2.take_ref, bf16[2,256,256]{2,1,0:T(8,128)(2,1)} %own_ref.1, bf16[2,256,256]{2,1,0:T(8,128)(2,1)} %copy-done.10, bf16[6,256,256]{2,1,0:T(8,128)(2,1)} %copy-done.5, bf16[6,256,256]{2,1,0:T(8,128)(2,1)} %copy-done.7, ...), custom_call_target="tpu_custom_call" | custom-call | flops 1207959552 | bytes 2621440 | tf_op jit(solution)/shard_map/pallas_call | solution.py:144
  43.9 11.2 %shard_map.130 = (f32[4,256,256]{2,1,0:T(8,128)}, f32[4,256,256]{2,1,0:T(8,128)}, f32[4,256,256]{2,1,0:T(8,128)}, f32[4,8,128]{2,1,0:T(8,128)}) custom-call(s32[8]{0:T(128)} %and_select_fusion.2.refs_0_, bf16[4,256,256]{2,1,0:T(8,128)(2,1)} %get-tuple-element.17.refs_1_, bf16[4,256,256]{2,1,0:T(8,128)(2,1)} %get-tuple-element.18.refs_2_, ...), custom_call_target="tpu_custom_call" | custom-call | flops 19327352832 | bytes 14680064 | tf_op jit(solution)/shard_map/pallas_call | solution.py:239
  55.1 7.7 %shard_map.131 = (f32[4,256,256]{2,1,0:T(8,128)}, f32[4,256,256]{2,1,0:T(8,128)}, f32[4,256,256]{2,1,0:T(8,128)}, f32[4,8,128]{2,1,0:T(8,128)}) custom-call(s32[4]{0:T(128)} %and_select_fusion.refs_0_, bf16[4,256,256]{2,1,0:T(8,128)(2,1)} %get-tuple-element.17.refs_1_, ...), custom_call_target="tpu_custom_call", output_to_operand_aliasing={{0}: (7, {}), {1}: (8, {}), {2}: (9, {}), {3}: (10, {})} | custom-call | flops 9663676416 | bytes 12582912 | tf_op jit(solution)/shard_map/pallas_call | solution.py:239
  62.9 0.8 %copy-done.9 = bf16[4,256,256]{2,1,0:T(8,128)(2,1)} copy-done((bf16[4,256,256]{2,1,0:T(8,128)(2,1)}, bf16[4,256,256]{2,1,0:T(8,128)(2,1)S(1)}, u32[]{:S(2)}) %copy-start.9) | copy-done | bytes 524312
  63.6 7.8 %shard_map.132 = (f32[4,256,256]{2,1,0:T(8,128)}, f32[4,256,256]{2,1,0:T(8,128)}, f32[4,256,256]{2,1,0:T(8,128)}, f32[4,16]{1,0:T(4,128)}) custom-call(s32[4]{0:T(128)} %and_select_fusion.1.refs_0_, bf16[4,256,256]{2,1,0:T(8,128)(2,1)} %get-tuple-element.17.refs_1_, ...), custom_call_target="tpu_custom_call", output_to_operand_aliasing={{0}: (7, {}), {1}: (8, {}), {2}: (9, {})} | custom-call | flops 9663676416 | bytes 12582912 | tf_op jit(solution)/shard_map/pallas_call | solution.py:239
  (76 shorter events, 1.4 us)
Async XLA Ops:
  0.6 13.8 %copy-start = (s32[16]{0:T(128)S(1)}, s32[16]{0:T(128)}, u32[]{:S(2)}) copy-start(s32[16]{0:T(128)} %param.18) | copy-start | bytes 196
  1.7 4.4 %copy-start.4 = (bf16[2,256,256]{2,1,0:T(8,128)(2,1)S(1)}, bf16[2,256,256]{2,1,0:T(8,128)(2,1)}, u32[]{:S(2)}) copy-start(bf16[2,256,256]{2,1,0:T(8,128)(2,1)} %own_ref.1) | copy-start | bytes 786436
  1.8 32.8 %collective-permute-start.9 = (bf16[4,256,256]{2,1,0:T(8,128)(2,1)S(1)}, bf16[4,256,256]{2,1,0:T(8,128)(2,1)}, u32[]{:S(2)}, u32[]{:S(2)}) collective-permute-start(bf16[4,256,256]{2,1,0:T(8,128)(2,1)S(1)} %pad_maximum_fusion.1), channel_id=1, source_target_pairs={{0,8},{8,0},{16,24},{24,16},{1,9},{9,1},{17,25},{25,17},{2,10},{10... | collective-permute-start | bytes 1572872 | tf_op jit(solution)/shard_map/ppermute | solution.py:272
  3.1 34.6 %collective-permute-start.7 = (bf16[4,256,256]{2,1,0:T(8,128)(2,1)S(1)}, bf16[4,256,256]{2,1,0:T(8,128)(2,1)S(1)}, u32[]{:S(2)}, u32[]{:S(2)}) collective-permute-start(bf16[4,256,256]{2,1,0:T(8,128)(2,1)S(1)} %pad_maximum_fusion.1), channel_id=1, source_target_pairs={{0,16},{8,24},{16,0},{24,8},{1,17},{9,25},{17,1},{25,9},{2,18},{10... | collective-permute-start | bytes 1572872 | tf_op jit(solution)/shard_map/ppermute | solution.py:272
  4.4 0.7 copy-start.6
  7.1 10.3 %collective-permute-start.1 = (bf16[2,256,256]{2,1,0:T(8,128)(2,1)S(1)}, bf16[2,256,256]{2,1,0:T(8,128)(2,1)S(1)}, u32[]{:S(2)}, u32[]{:S(2)}) collective-permute-start(bf16[2,256,256]{2,1,0:T(8,128)(2,1)S(1)} %get-tuple-element.38), channel_id=1, source_target_pairs={{0,2},{1,3},{2,0},{3,1},{4,6},{5,7},{6,4},{7,5},{8,10},{9,11},{10,... | collective-permute-start | bytes 786440 | tf_op jit(solution)/shard_map/ppermute | solution.py:87
  7.3 13.1 %collective-permute-start.2 = (bf16[2,256,256]{2,1,0:T(8,128)(2,1)S(1)}, bf16[2,256,256]{2,1,0:T(8,128)(2,1)S(1)}, u32[]{:S(2)}, u32[]{:S(2)}) collective-permute-start(bf16[2,256,256]{2,1,0:T(8,128)(2,1)S(1)} %get-tuple-element.37), channel_id=1, source_target_pairs={{0,4},{1,5},{2,6},{3,7},{4,0},{5,1},{6,2},{7,3},{8,12},{9,13},{10,... | collective-permute-start | bytes 786440 | tf_op jit(solution)/shard_map/ppermute | solution.py:87
  9.6 22.0 %collective-permute-start.3 = (bf16[2,256,256]{2,1,0:T(8,128)(2,1)S(1)}, bf16[2,256,256]{2,1,0:T(8,128)(2,1)S(1)}, u32[]{:S(2)}, u32[]{:S(2)}) collective-permute-start(bf16[2,256,256]{2,1,0:T(8,128)(2,1)S(1)} %get-tuple-element.36), channel_id=1, source_target_pairs={{0,6},{1,7},{2,4},{3,5},{4,2},{5,3},{6,0},{7,1},{8,14},{9,15},{10,... | collective-permute-start | bytes 786440 | tf_op jit(solution)/shard_map/ppermute | solution.py:87
  10.4 0.7 copy-start.11
  11.9 0.7 copy-start.1
  17.3 20.8 %collective-permute-start.5 = (bf16[4,256,256]{2,1,0:T(8,128)(2,1)S(1)}, bf16[4,256,256]{2,1,0:T(8,128)(2,1)}, u32[]{:S(2)}, u32[]{:S(2)}) collective-permute-start(bf16[4,256,256]{2,1,0:T(8,128)(2,1)S(1)} %pad_maximum_fusion.1), channel_id=1, source_target_pairs={{0,24},{8,16},{16,8},{24,0},{1,25},{9,17},{17,9},{25,1},{2,26},{10... | collective-permute-start | bytes 1572872 | tf_op jit(solution)/shard_map/ppermute | solution.py:272
  20.4 15.0 %copy-start.2 = (bf16[4,256,256]{2,1,0:T(8,128)(2,1)S(1)}, bf16[4,256,256]{2,1,0:T(8,128)(2,1)}, u32[]{:S(2)}) copy-start(bf16[4,256,256]{2,1,0:T(8,128)(2,1)} %param.17) | copy-start | bytes 1572868
  20.4 15.0 %copy-start.3 = (bf16[4,256,256]{2,1,0:T(8,128)(2,1)S(1)}, bf16[4,256,256]{2,1,0:T(8,128)(2,1)}, u32[]{:S(2)}) copy-start(bf16[4,256,256]{2,1,0:T(8,128)(2,1)} %param.16) | copy-start | bytes 1572868
  20.4 17.9 %collective-permute-start = (bf16[2,256,256]{2,1,0:T(8,128)(2,1)S(1)}, bf16[2,256,256]{2,1,0:T(8,128)(2,1)S(1)}, u32[]{:S(2)}, u32[]{:S(2)}) collective-permute-start(bf16[2,256,256]{2,1,0:T(8,128)(2,1)S(1)} %get-tuple-element.39), channel_id=1, source_target_pairs={{0,1},{1,0},{2,3},{3,2},{4,5},{5,4},{6,7},{7,6},{8,9},{9,8},{10,11... | collective-permute-start | bytes 786440 | tf_op jit(solution)/shard_map/ppermute | solution.py:84
  31.7 4.7 %copy-start.5 = (bf16[6,256,256]{2,1,0:T(8,128)(2,1)}, bf16[6,256,256]{2,1,0:T(8,128)(2,1)S(1)}, u32[]{:S(2)}) copy-start(bf16[6,256,256]{2,1,0:T(8,128)(2,1)S(1)} %constant_dynamic-update-slice_fusion.recv_ref) | copy-start | bytes 2359300
  31.7 6.6 %collective-permute-start.4 = (bf16[6,256,256]{2,1,0:T(8,128)(2,1)S(1)}, bf16[6,256,256]{2,1,0:T(8,128)(2,1)S(1)}, u32[]{:S(2)}, u32[]{:S(2)}) collective-permute-start(bf16[6,256,256]{2,1,0:T(8,128)(2,1)S(1)} %constant_dynamic-update-slice_fusion.recv_ref), channel_id=1, source_target_pairs={{0,1},{1,0},{2,3},{3,2},{4,5},{5,4},{6,7},{7,6},{8,9},{9,8},{10,11... | collective-permute-start | bytes 2359304 | tf_op jit(solution)/shard_map/ppermute | solution.py:89
  34.6 9.3 %collective-permute-start.10 = (bf16[4,256,256]{2,1,0:T(8,128)(2,1)}, bf16[4,256,256]{2,1,0:T(8,128)(2,1)}, u32[]{:S(2)}, u32[]{:S(2)}) collective-permute-start(bf16[4,256,256]{2,1,0:T(8,128)(2,1)} %collective-permute-done.9.refs_4_), channel_id=1, source_target_pairs={{0,1},{1,0},{2,3},{3,2},{4,5},{5,4},{6,7},{7,6},{8,9},{9,8},{10,11... | collective-permute-start | bytes 1572872 | tf_op jit(solution)/shard_map/ppermute | solution.py:273
  37.7 6.2 %copy-start.8 = (bf16[4,256,256]{2,1,0:T(8,128)(2,1)}, bf16[4,256,256]{2,1,0:T(8,128)(2,1)S(1)}, u32[]{:S(2)}) copy-start(bf16[4,256,256]{2,1,0:T(8,128)(2,1)S(1)} %collective-permute-done.7.refs_3_) | copy-start | bytes 1572868
  37.7 17.4 %collective-permute-start.8 = (bf16[4,256,256]{2,1,0:T(8,128)(2,1)S(1)}, bf16[4,256,256]{2,1,0:T(8,128)(2,1)}, u32[]{:S(2)}, u32[]{:S(2)}) collective-permute-start(bf16[4,256,256]{2,1,0:T(8,128)(2,1)S(1)} %collective-permute-done.7.refs_3_), channel_id=1, source_target_pairs={{0,1},{1,0},{2,3},{3,2},{4,5},{5,4},{6,7},{7,6},{8,9},{9,8},{10,11... | collective-permute-start | bytes 1572872 | tf_op jit(solution)/shard_map/ppermute | solution.py:273
  38.1 24.7 %collective-permute-start.6 = (bf16[4,256,256]{2,1,0:T(8,128)(2,1)}, bf16[4,256,256]{2,1,0:T(8,128)(2,1)S(1)}, u32[]{:S(2)}, u32[]{:S(2)}) collective-permute-start(bf16[4,256,256]{2,1,0:T(8,128)(2,1)} %collective-permute-done.5.refs_3_), channel_id=1, source_target_pairs={{0,1},{1,0},{2,3},{3,2},{4,5},{5,4},{6,7},{7,6},{8,9},{9,8},{10,11... | collective-permute-start | bytes 1572872 | tf_op jit(solution)/shard_map/ppermute | solution.py:273
  38.2 0.7 copy-start.10
  38.9 0.9 %copy-start.7 = (bf16[6,256,256]{2,1,0:T(8,128)(2,1)}, bf16[6,256,256]{2,1,0:T(8,128)(2,1)S(1)}, u32[]{:S(2)}) copy-start(bf16[6,256,256]{2,1,0:T(8,128)(2,1)S(1)} %collective-permute-done.4.fwd_ref) | copy-start | bytes 2359300
  62.9 0.8 %copy-start.9 = (bf16[4,256,256]{2,1,0:T(8,128)(2,1)}, bf16[4,256,256]{2,1,0:T(8,128)(2,1)S(1)}, u32[]{:S(2)}) copy-start(bf16[4,256,256]{2,1,0:T(8,128)(2,1)S(1)} %collective-permute-done.6.refs_4_) | copy-start | bytes 1572868

commit v14 on v10

--- a/solution.py
+++ b/solution.py
@@ -266,14 +266,24 @@
         [lax.dynamic_slice_in_dim(templ_re, core * half, half, 0),
          lax.dynamic_slice_in_dim(templ_im, core * half, half, 0)], axis=0)
     within = jnp.arange(half, dtype=jnp.int32)
-    chunks = [([local], me * tiles + jnp.arange(tiles, dtype=jnp.int32))]
+    first_groups = [local]
+    first_index = [me * tiles + jnp.arange(tiles, dtype=jnp.int32)]
+    late_groups, late_index = [], []
     for k in range(1, blocks):
         source = me ^ k
         got = lax.ppermute(mine, "blk", [(b, b ^ k) for b in range(blocks)])
         passed = lax.ppermute(got, "patch", xor_pairs(sources, 1))
-        index = jnp.concatenate(
-            [source * tiles + core * half + within, source * tiles + (1 - core) * half + within])
-        chunks.append(([got, passed], index))
+        first_groups.append(got)
+        first_index.append(source * tiles + core * half + within)
+        if k == 1:
+            first_groups.append(passed)
+            first_index.append(source * tiles + (1 - core) * half + within)
+        else:
+            late_groups.append(passed)
+            late_index.append(source * tiles + (1 - core) * half + within)
+    chunks = [(first_groups, jnp.concatenate(first_index))]
+    if late_groups:
+        chunks.append((late_groups, jnp.concatenate(late_index)))
     stats = None
     for n, (groups, index) in enumerate(chunks):
         orient_chunk = jnp.take(orientation, index)

time: 75.5 us -> 71.2 us (0.943)
  waiting for transfers between devices: 3.82 us -> 15.6 us
  Pallas kernels: 34.5 us -> 27.1 us
  starting transfers between devices: 17.5 us -> 11.9 us
  local copies, waits for them, and re-layouts: 11.4 us -> 9.69 us
  other arithmetic: 6.85 us -> 5.62 us
    ppermute x3, waiting for transfers between devices: 3.8 us -> 13.1 us  [route_patches(): lax.ppermute(outgoing[m], 'patch', xor_pairs(sources, 2 * m))]
    pallas_call x4 -> x2, Pallas kernels: 30.4 us -> 22.9 us  [correlate_chunk(): pl.pallas_call(functools.partial(corr_kernel, first, last, counts, orient...]
    ppermute x1, starting transfers between devices: 9.04 us -> 2.16 us  [route_patches(): direct = lax.ppermute(outgoing[0], 'patch', xor_pairs(sources, 1))]
    ppermute x3, starting transfers between devices: 0.62 us -> 3.44 us  [correlate_all(): passed = lax.ppermute(got, 'patch', xor_pairs(sources, 1))]
    ppermute x3, waiting for transfers between devices: 0.01 us -> 2.56 us  [correlate_all(): got = lax.ppermute(mine, 'blk', [(b, b ^ k) for b in range(blocks)])]
    ppermute x1, starting transfers between devices: 2.35 us -> 0.07 us  [route_patches(): forwarded = lax.ppermute(received, 'patch', xor_pairs(sources, 1))]
    gather x4 -> x2, local copies, waits for them, and re-layouts: 2.55 us -> 1.31 us  [correlate_all(): orient_chunk = jnp.take(orientation, index)]
    select_n x8 -> x4, other arithmetic: 2.61 us -> 1.38 us  [correlate_all(): orient_chunk = jnp.take(orientation, index)]
  transfers between devices with their start and end apart: 11 -> 11, of which waited for: 2 -> 3; matrix products, arithmetic and copies ran while one was open for 17% -> 15% of each run, Pallas kernels for 36% -> 27%
where the time goes in v14:
time: 71.2 us; the launch traced here: 71 us
  Pallas kernels  27.1 us (38%)
  waiting for transfers between devices  15.6 us (22%)
  starting transfers between devices  11.9 us (17%)
  local copies, waits for them, and re-layouts  9.69 us (14%)
  other arithmetic  5.62 us (8%)
  between operations  1.01 us (1%)
    pallas_call x2, Pallas kernels, correlate_chunk(): pl.pallas_call(functools.partial(corr_kernel, first, last, counts, orient...  22.9 us
    ppermute x3, waiting for transfers between devices, route_patches(): lax.ppermute(outgoing[m], 'patch', xor_pairs(sources, 2 * m))  13.1 us
    pallas_call x1, Pallas kernels, make_spectra(): pl.pallas_call(functools.partial(spectra_kernel, rows), in_specs=[pl.Bloc...  4.15 us
    unnamed x26, local copies, waits for them, and re-layouts  3.73 us
    ppermute x3, starting transfers between devices, route_patches(): lax.ppermute(outgoing[m], 'patch', xor_pairs(sources, 2 * m))  3.56 us
    ppermute x3, starting transfers between devices, correlate_all(): passed = lax.ppermute(got, 'patch', xor_pairs(sources, 1))  3.44 us
    ppermute x3, starting transfers between devices, correlate_all(): got = lax.ppermute(mine, 'blk', [(b, b ^ k) for b in range(blocks)])  2.71 us
    ppermute x3, waiting for transfers between devices, correlate_all(): got = lax.ppermute(mine, 'blk', [(b, b ^ k) for b in range(blocks)])  2.56 us
  transfers between devices with their start and end apart: 11, of which 3 were waited for; matrix products, arithmetic and copies ran while one was open for 15% of the time, Pallas kernels for 27%

profile of v14, /device:TPU:9, one launch (start us, length us, event | category | flops | bytes accessed | tf_op | source)
XLA Modules:
  0.0 71.0 jit_solution(2358697752601069303)
XLA Ops:
  0.7 1.1 %constant_dynamic-slice_fusion = (bf16[2,256,256]{2,1,0:T(8,128)(2,1)S(1)}, bf16[2,256,256]{2,1,0:T(8,128)(2,1)S(1)}) fusion(bf16[4,256,256]{2,1,0:T(8,128)(2,1)} %param.15, s32[]{:T(128)S(6)} %select_n.311, bf16[4,256,256]{2,1,0:T(8,128)(2,1)} %param.14), kind=kLoop, calls=%fused_computation.46 | loop fusion | bytes 1048580 | tf_op jit(solution)/shard_map/dynamic_slice | solution.py:267
  1.8 1.3 %collective-permute-start.9 = (bf16[4,256,256]{2,1,0:T(8,128)(2,1)S(1)}, bf16[4,256,256]{2,1,0:T(8,128)(2,1)S(1)}, u32[]{:S(2)}, u32[]{:S(2)}) collective-permute-start(bf16[4,256,256]{2,1,0:T(8,128)(2,1)S(1)} %pad_maximum_fusion.1), channel_id=1, source_target_pairs={{0,8},{8,0},{16,24},{24,16},{1,9},{9,1},{17,25},{25,17},{2,10},{10... | collective-permute-start | bytes 1572872 | tf_op jit(solution)/shard_map/ppermute | solution.py:274
  3.1 1.2 %collective-permute-start.7 = (bf16[4,256,256]{2,1,0:T(8,128)(2,1)S(1)}, bf16[4,256,256]{2,1,0:T(8,128)(2,1)}, u32[]{:S(2)}, u32[]{:S(2)}) collective-permute-start(bf16[4,256,256]{2,1,0:T(8,128)(2,1)S(1)} %pad_maximum_fusion.1), channel_id=1, source_target_pairs={{0,24},{8,16},{16,8},{24,0},{1,25},{9,17},{17,9},{25,1},{2,26},{10... | collective-permute-start | bytes 1572872 | tf_op jit(solution)/shard_map/ppermute | solution.py:274
  4.3 0.7 copy-done.6
  5.1 0.1 copy.34
  5.2 0.1 copy.36
  5.3 0.1 copy.37
  5.5 0.1 copy.35
  5.7 0.1 copy.38
  5.8 0.1 reshape.722
  5.9 0.1 reshape.721
  6.0 0.6 gather_fusion.1
  6.7 0.2 broadcast_select_fusion
  6.9 1.4 %collective-permute-start.3 = (bf16[2,256,256]{2,1,0:T(8,128)(2,1)S(1)}, bf16[2,256,256]{2,1,0:T(8,128)(2,1)S(1)}, u32[]{:S(2)}, u32[]{:S(2)}) collective-permute-start(bf16[2,256,256]{2,1,0:T(8,128)(2,1)S(1)} %get-tuple-element.27), channel_id=1, source_target_pairs={{0,6},{1,7},{2,4},{3,5},{4,2},{5,3},{6,0},{7,1},{8,14},{9,15},{10,... | collective-permute-start | bytes 786440 | tf_op jit(solution)/shard_map/ppermute | solution.py:87
  8.3 1.1 %collective-permute-start.2 = (bf16[2,256,256]{2,1,0:T(8,128)(2,1)S(1)}, bf16[2,256,256]{2,1,0:T(8,128)(2,1)S(1)}, u32[]{:S(2)}, u32[]{:S(2)}) collective-permute-start(bf16[2,256,256]{2,1,0:T(8,128)(2,1)S(1)} %get-tuple-element.28), channel_id=1, source_target_pairs={{0,4},{1,5},{2,6},{3,7},{4,0},{5,1},{6,2},{7,3},{8,12},{9,13},{10,... | collective-permute-start | bytes 786440 | tf_op jit(solution)/shard_map/ppermute | solution.py:87
  9.4 1.1 %collective-permute-start.1 = (bf16[2,256,256]{2,1,0:T(8,128)(2,1)S(1)}, bf16[2,256,256]{2,1,0:T(8,128)(2,1)S(1)}, u32[]{:S(2)}, u32[]{:S(2)}) collective-permute-start(bf16[2,256,256]{2,1,0:T(8,128)(2,1)S(1)} %get-tuple-element.29), channel_id=1, source_target_pairs={{0,2},{1,3},{2,0},{3,1},{4,6},{5,7},{6,4},{7,5},{8,10},{9,11},{10,... | collective-permute-start | bytes 786440 | tf_op jit(solution)/shard_map/ppermute | solution.py:87
  10.5 0.1 copy.33
  10.6 0.1 reduce
  10.8 0.1 select_reduce_fusion.1
  10.9 0.1 fusion.6
  11.1 0.1 concatenate.99
  11.2 0.4 fusion.13
  11.8 0.2 select_reduce_fusion
  12.0 0.5 broadcast_select_fusion.2.take_ref
  12.5 0.6 copy-done.11
  13.2 0.6 gather_fusion.2
  14.0 0.6 gather_fusion.3
  14.6 0.1 fusion.1
  14.8 0.7 gather_fusion.4
  15.5 0.6 gather_fusion
  16.2 10.9 %collective-permute-done.1 = bf16[2,256,256]{2,1,0:T(8,128)(2,1)S(1)} collective-permute-done((bf16[2,256,256]{2,1,0:T(8,128)(2,1)S(1)}, bf16[2,256,256]{2,1,0:T(8,128)(2,1)S(1)}, u32[]{:S(2)}, u32[]{:S(2)}) %collective-permute-start.1) | collective-permute-done | bytes 262176 | tf_op jit(solution)/shard_map/ppermute | solution.py:87
  27.0 0.2 collective-permute-start.5
  27.3 2.2 %collective-permute-done.2 = bf16[2,256,256]{2,1,0:T(8,128)(2,1)S(1)} collective-permute-done((bf16[2,256,256]{2,1,0:T(8,128)(2,1)S(1)}, bf16[2,256,256]{2,1,0:T(8,128)(2,1)S(1)}, u32[]{:S(2)}, u32[]{:S(2)}) %collective-permute-start.2) | collective-permute-done | bytes 262176 | tf_op jit(solution)/shard_map/ppermute | solution.py:87
  29.5 2.2 %collective-permute-start = (bf16[2,256,256]{2,1,0:T(8,128)(2,1)S(1)}, bf16[2,256,256]{2,1,0:T(8,128)(2,1)S(1)}, u32[]{:S(2)}, u32[]{:S(2)}) collective-permute-start(bf16[2,256,256]{2,1,0:T(8,128)(2,1)S(1)} %get-tuple-element.30), channel_id=1, source_target_pairs={{0,1},{1,0},{2,3},{3,2},{4,5},{5,4},{6,7},{7,6},{8,9},{9,8},{10,11... | collective-permute-start | bytes 786440 | tf_op jit(solution)/shard_map/ppermute | solution.py:84
  31.8 0.7 %and_select_fusion.refs_0_ = s32[12]{0:T(128)} fusion(s32[12]{0:T(128)S(1)} %gather_fusion.4, s32[12]{0:T(128)S(1)} %concatenate.93), kind=kLoop, calls=%fused_computation.64 | loop fusion | flops 84 | bytes 144 | tf_op jit(solution)/shard_map/jit(_take)/select_n | solution.py:289
  32.5 0.4 collective-permute-start.10
  32.9 0.6 and_select_fusion.6.refs_0_
  33.5 1.1 %pad_maximum_fusion.refs_3_ = bf16[8,256,256]{2,1,0:T(8,128)(2,1)} fusion(bf16[4,256,256]{2,1,0:T(8,128)(2,1)S(1)} %copy-done.2, bf16[4,256,256]{2,1,0:T(8,128)(2,1)S(1)} %copy-done.3), kind=kLoop, calls=%fused_computation.5 | loop fusion | flops 524288 | bytes 2097152 | tf_op jit(solution)/shard_map/concatenate | solution.py:264
  34.6 1.3 %negate_multiply_fusion.scale_ref = f32[4,256,256]{2,1,0:T(8,128)} fusion(f32[4,256]{1,0:T(4,128)S(1)} %get-tuple-element.36, f32[4,256]{1,0:T(4,128)S(1)} %get-tuple-element.38, f32[4,256]{1,0:T(4,128)S(1)} %get-tuple-element.37, f32[4,256]{1,0:T(4,128)S(1)} %get-tuple-element.35), kind=kLoop, calls=%fused_computation.6 | loop fusion | flops 1310720 | bytes 1064960 | tf_op jit(solution)/shard_map/div | solution.py:57
  35.9 0.1 collective-permute-start.8
  36.0 2.6 %collective-permute-done.5.refs_6_ = bf16[4,256,256]{2,1,0:T(8,128)(2,1)} collective-permute-done((bf16[4,256,256]{2,1,0:T(8,128)(2,1)S(1)}, bf16[4,256,256]{2,1,0:T(8,128)(2,1)}, u32[]{:S(2)}, u32[]{:S(2)}) %collective-permute-start.5) | collective-permute-done | bytes 524320 | tf_op jit(solution)/shard_map/ppermute | solution.py:274
  38.6 2.9 %collective-permute-start.6 = (bf16[4,256,256]{2,1,0:T(8,128)(2,1)}, bf16[4,256,256]{2,1,0:T(8,128)(2,1)S(1)}, u32[]{:S(2)}, u32[]{:S(2)}) collective-permute-start(bf16[4,256,256]{2,1,0:T(8,128)(2,1)} %collective-permute-done.5.refs_6_), channel_id=1, source_target_pairs={{0,1},{1,0},{2,3},{3,2},{4,5},{5,4},{6,7},{7,6},{8,9},{9,8},{10,11... | collective-permute-start | bytes 1572872 | tf_op jit(solution)/shard_map/ppermute | solution.py:275
  41.5 0.7 copy-done.10
  42.2 0.9 %copy-done.7 = bf16[6,256,256]{2,1,0:T(8,128)(2,1)} copy-done((bf16[6,256,256]{2,1,0:T(8,128)(2,1)}, bf16[6,256,256]{2,1,0:T(8,128)(2,1)S(1)}, u32[]{:S(2)}) %copy-start.7) | copy-done | bytes 786456
  43.1 4.2 %shard_map.129 = (bf16[4,256,256]{2,1,0:T(8,128)(2,1)}, bf16[4,256,256]{2,1,0:T(8,128)(2,1)}) custom-call(s32[4]{0:T(128)} %broadcast_select_fusion.2.take_ref, bf16[2,256,256]{2,1,0:T(8,128)(2,1)} %own_ref.1, bf16[2,256,256]{2,1,0:T(8,128)(2,1)} %copy-done.10, bf16[6,256,256]{2,1,0:T(8,128)(2,1)} %copy-done.5, bf16[6,256,256]{2,1,0:T(8,128)(2,1)} %copy-done.7, ...), custom_call_target="tpu_custom_call" | custom-call | flops 1207959552 | bytes 2621440 | tf_op jit(solution)/shard_map/pallas_call | solution.py:144
  47.2 15.1 %shard_map.130 = (f32[4,256,256]{2,1,0:T(8,128)}, f32[4,256,256]{2,1,0:T(8,128)}, f32[4,256,256]{2,1,0:T(8,128)}, f32[4,8,128]{2,1,0:T(8,128)}) custom-call(s32[12]{0:T(128)} %and_select_fusion.refs_0_, bf16[4,256,256]{2,1,0:T(8,128)(2,1)} %get-tuple-element.12.refs_1_, bf16[4,256,256]{2,1,0:T(8,128)(2,1)} %get-tuple-element.13.refs_2_, ...), custom_call_target="tpu_custom_call" | custom-call | flops 28991029248 | bytes 16777216 | tf_op jit(solution)/shard_map/pallas_call | solution.py:239
  62.4 0.8 %copy-done.9 = bf16[4,256,256]{2,1,0:T(8,128)(2,1)} copy-done((bf16[4,256,256]{2,1,0:T(8,128)(2,1)}, bf16[4,256,256]{2,1,0:T(8,128)(2,1)S(1)}, u32[]{:S(2)}) %copy-start.9) | copy-done | bytes 524312
  63.2 7.8 %shard_map.131 = (f32[4,256,256]{2,1,0:T(8,128)}, f32[4,256,256]{2,1,0:T(8,128)}, f32[4,256,256]{2,1,0:T(8,128)}, f32[4,16]{1,0:T(4,128)}) custom-call(s32[4]{0:T(128)} %and_select_fusion.6.refs_0_, bf16[4,256,256]{2,1,0:T(8,128)(2,1)} %get-tuple-element.12.refs_1_, ...), custom_call_target="tpu_custom_call", output_to_operand_aliasing={{0}: (7, {}), {1}: (8, {}), {2}: (9, {})} | custom-call | flops 9663676416 | bytes 12582912 | tf_op jit(solution)/shard_map/pallas_call | solution.py:239
  (73 shorter events, 1.1 us)
Async XLA Ops:
  0.6 14.2 %copy-start = (s32[16]{0:T(128)S(1)}, s32[16]{0:T(128)}, u32[]{:S(2)}) copy-start(s32[16]{0:T(128)} %param.16) | copy-start | bytes 196
  1.7 4.3 %copy-start.4 = (bf16[2,256,256]{2,1,0:T(8,128)(2,1)S(1)}, bf16[2,256,256]{2,1,0:T(8,128)(2,1)}, u32[]{:S(2)}) copy-start(bf16[2,256,256]{2,1,0:T(8,128)(2,1)} %own_ref.1) | copy-start | bytes 786436
  1.8 30.7 %collective-permute-start.9 = (bf16[4,256,256]{2,1,0:T(8,128)(2,1)S(1)}, bf16[4,256,256]{2,1,0:T(8,128)(2,1)S(1)}, u32[]{:S(2)}, u32[]{:S(2)}) collective-permute-start(bf16[4,256,256]{2,1,0:T(8,128)(2,1)S(1)} %pad_maximum_fusion.1), channel_id=1, source_target_pairs={{0,8},{8,0},{16,24},{24,16},{1,9},{9,1},{17,25},{25,17},{2,10},{10... | collective-permute-start | bytes 1572872 | tf_op jit(solution)/shard_map/ppermute | solution.py:274
  3.1 32.8 %collective-permute-start.7 = (bf16[4,256,256]{2,1,0:T(8,128)(2,1)S(1)}, bf16[4,256,256]{2,1,0:T(8,128)(2,1)}, u32[]{:S(2)}, u32[]{:S(2)}) collective-permute-start(bf16[4,256,256]{2,1,0:T(8,128)(2,1)S(1)} %pad_maximum_fusion.1), channel_id=1, source_target_pairs={{0,24},{8,16},{16,8},{24,0},{1,25},{9,17},{17,9},{25,1},{2,26},{10... | collective-permute-start | bytes 1572872 | tf_op jit(solution)/shard_map/ppermute | solution.py:274
  4.3 0.7 copy-start.6
  6.9 24.8 %collective-permute-start.3 = (bf16[2,256,256]{2,1,0:T(8,128)(2,1)S(1)}, bf16[2,256,256]{2,1,0:T(8,128)(2,1)S(1)}, u32[]{:S(2)}, u32[]{:S(2)}) collective-permute-start(bf16[2,256,256]{2,1,0:T(8,128)(2,1)S(1)} %get-tuple-element.27), channel_id=1, source_target_pairs={{0,6},{1,7},{2,4},{3,5},{4,2},{5,3},{6,0},{7,1},{8,14},{9,15},{10,... | collective-permute-start | bytes 786440 | tf_op jit(solution)/shard_map/ppermute | solution.py:87
  8.3 21.2 %collective-permute-start.2 = (bf16[2,256,256]{2,1,0:T(8,128)(2,1)S(1)}, bf16[2,256,256]{2,1,0:T(8,128)(2,1)S(1)}, u32[]{:S(2)}, u32[]{:S(2)}) collective-permute-start(bf16[2,256,256]{2,1,0:T(8,128)(2,1)S(1)} %get-tuple-element.28), channel_id=1, source_target_pairs={{0,4},{1,5},{2,6},{3,7},{4,0},{5,1},{6,2},{7,3},{8,12},{9,13},{10,... | collective-permute-start | bytes 786440 | tf_op jit(solution)/shard_map/ppermute | solution.py:87
  9.4 17.7 %collective-permute-start.1 = (bf16[2,256,256]{2,1,0:T(8,128)(2,1)S(1)}, bf16[2,256,256]{2,1,0:T(8,128)(2,1)S(1)}, u32[]{:S(2)}, u32[]{:S(2)}) collective-permute-start(bf16[2,256,256]{2,1,0:T(8,128)(2,1)S(1)} %get-tuple-element.29), channel_id=1, source_target_pairs={{0,2},{1,3},{2,0},{3,1},{4,6},{5,7},{6,4},{7,5},{8,10},{9,11},{10,... | collective-permute-start | bytes 786440 | tf_op jit(solution)/shard_map/ppermute | solution.py:87
  12.5 0.7 copy-start.11
  13.2 0.7 %copy-start.1 = (f32[32]{0:T(128)S(1)}, f32[32]{0:T(128)}, u32[]{:S(2)}) copy-start(f32[32]{0:T(128)} %param.13) | copy-start | bytes 388
  27.0 11.5 %collective-permute-start.5 = (bf16[4,256,256]{2,1,0:T(8,128)(2,1)S(1)}, bf16[4,256,256]{2,1,0:T(8,128)(2,1)}, u32[]{:S(2)}, u32[]{:S(2)}) collective-permute-start(bf16[4,256,256]{2,1,0:T(8,128)(2,1)S(1)} %pad_maximum_fusion.1), channel_id=1, source_target_pairs={{0,16},{8,24},{16,0},{24,8},{1,17},{9,25},{17,1},{25,9},{2,18},{10... | collective-permute-start | bytes 1572872 | tf_op jit(solution)/shard_map/ppermute | solution.py:274
  29.5 4.0 %copy-start.2 = (bf16[4,256,256]{2,1,0:T(8,128)(2,1)S(1)}, bf16[4,256,256]{2,1,0:T(8,128)(2,1)}, u32[]{:S(2)}) copy-start(bf16[4,256,256]{2,1,0:T(8,128)(2,1)} %param.15) | copy-start | bytes 1572868
  29.5 4.0 %copy-start.3 = (bf16[4,256,256]{2,1,0:T(8,128)(2,1)S(1)}, bf16[4,256,256]{2,1,0:T(8,128)(2,1)}, u32[]{:S(2)}) copy-start(bf16[4,256,256]{2,1,0:T(8,128)(2,1)} %param.14) | copy-start | bytes 1572868
  29.5 12.0 %collective-permute-start = (bf16[2,256,256]{2,1,0:T(8,128)(2,1)S(1)}, bf16[2,256,256]{2,1,0:T(8,128)(2,1)S(1)}, u32[]{:S(2)}, u32[]{:S(2)}) collective-permute-start(bf16[2,256,256]{2,1,0:T(8,128)(2,1)S(1)} %get-tuple-element.30), channel_id=1, source_target_pairs={{0,1},{1,0},{2,3},{3,2},{4,5},{5,4},{6,7},{7,6},{8,9},{9,8},{10,11... | collective-permute-start | bytes 786440 | tf_op jit(solution)/shard_map/ppermute | solution.py:84
  31.7 2.8 %copy-start.5 = (bf16[6,256,256]{2,1,0:T(8,128)(2,1)}, bf16[6,256,256]{2,1,0:T(8,128)(2,1)S(1)}, u32[]{:S(2)}) copy-start(bf16[6,256,256]{2,1,0:T(8,128)(2,1)S(1)} %constant_dynamic-update-slice_fusion.recv_ref) | copy-start | bytes 2359300
  31.7 9.8 %collective-permute-start.4 = (bf16[6,256,256]{2,1,0:T(8,128)(2,1)S(1)}, bf16[6,256,256]{2,1,0:T(8,128)(2,1)S(1)}, u32[]{:S(2)}, u32[]{:S(2)}) collective-permute-start(bf16[6,256,256]{2,1,0:T(8,128)(2,1)S(1)} %constant_dynamic-update-slice_fusion.recv_ref), channel_id=1, source_target_pairs={{0,1},{1,0},{2,3},{3,2},{4,5},{5,4},{6,7},{7,6},{8,9},{9,8},{10,11... | collective-permute-start | bytes 2359304 | tf_op jit(solution)/shard_map/ppermute | solution.py:89
  32.5 2.0 %copy-start.8 = (bf16[4,256,256]{2,1,0:T(8,128)(2,1)}, bf16[4,256,256]{2,1,0:T(8,128)(2,1)S(1)}, u32[]{:S(2)}) copy-start(bf16[4,256,256]{2,1,0:T(8,128)(2,1)S(1)} %collective-permute-done.9.refs_4_) | copy-start | bytes 1572868
  32.5 14.7 %collective-permute-start.10 = (bf16[4,256,256]{2,1,0:T(8,128)(2,1)S(1)}, bf16[4,256,256]{2,1,0:T(8,128)(2,1)}, u32[]{:S(2)}, u32[]{:S(2)}) collective-permute-start(bf16[4,256,256]{2,1,0:T(8,128)(2,1)S(1)} %collective-permute-done.9.refs_4_), channel_id=1, source_target_pairs={{0,1},{1,0},{2,3},{3,2},{4,5},{5,4},{6,7},{7,6},{8,9},{9,8},{10,11... | collective-permute-start | bytes 1572872 | tf_op jit(solution)/shard_map/ppermute | solution.py:275
  35.9 26.5 %collective-permute-start.8 = (bf16[4,256,256]{2,1,0:T(8,128)(2,1)}, bf16[4,256,256]{2,1,0:T(8,128)(2,1)}, u32[]{:S(2)}, u32[]{:S(2)}) collective-permute-start(bf16[4,256,256]{2,1,0:T(8,128)(2,1)} %collective-permute-done.7.refs_7_), channel_id=1, source_target_pairs={{0,1},{1,0},{2,3},{3,2},{4,5},{5,4},{6,7},{7,6},{8,9},{9,8},{10,11... | collective-permute-start | bytes 1572872 | tf_op jit(solution)/shard_map/ppermute | solution.py:275
  38.6 23.8 %collective-permute-start.6 = (bf16[4,256,256]{2,1,0:T(8,128)(2,1)}, bf16[4,256,256]{2,1,0:T(8,128)(2,1)S(1)}, u32[]{:S(2)}, u32[]{:S(2)}) collective-permute-start(bf16[4,256,256]{2,1,0:T(8,128)(2,1)} %collective-permute-done.5.refs_6_), channel_id=1, source_target_pairs={{0,1},{1,0},{2,3},{3,2},{4,5},{5,4},{6,7},{7,6},{8,9},{9,8},{10,11... | collective-permute-start | bytes 1572872 | tf_op jit(solution)/shard_map/ppermute | solution.py:275
  41.5 0.7 copy-start.10
  42.2 0.9 %copy-start.7 = (bf16[6,256,256]{2,1,0:T(8,128)(2,1)}, bf16[6,256,256]{2,1,0:T(8,128)(2,1)S(1)}, u32[]{:S(2)}) copy-start(bf16[6,256,256]{2,1,0:T(8,128)(2,1)S(1)} %collective-permute-done.4.fwd_ref) | copy-start | bytes 2359300
  62.4 0.8 %copy-start.9 = (bf16[4,256,256]{2,1,0:T(8,128)(2,1)}, bf16[4,256,256]{2,1,0:T(8,128)(2,1)S(1)}, u32[]{:S(2)}) copy-start(bf16[4,256,256]{2,1,0:T(8,128)(2,1)S(1)} %collective-permute-done.6.refs_3_) | copy-start | bytes 1572868

commit v15 on v14

--- a/solution.py
+++ b/solution.py
@@ -172,13 +172,14 @@
     peak_row = jnp.zeros(row_shape, jnp.float32) if first else peak_in[0]
     top = total = square = None
     prods = []
-    for templ_ref, count in zip(templ_refs, counts):
-        for t in range(count):
-            tr = templ_ref[t].astype(jnp.float32)
-            ti = templ_ref[count + t].astype(jnp.float32)
-            pre = (sr * tr + si * ti).astype(jnp.bfloat16)
-            pim = (si * tr - sr * ti).astype(jnp.bfloat16)
-            prods.append(jnp.concatenate([pre, pim], axis=1))
+    for templ_ref, (count, parts) in zip(templ_refs, counts):
+        for part in range(parts):
+            for t in range(count):
+                tr = templ_ref[2 * count * part + t].astype(jnp.float32)
+                ti = templ_ref[2 * count * part + count + t].astype(jnp.float32)
+                pre = (sr * tr + si * ti).astype(jnp.bfloat16)
+                pim = (si * tr - sr * ti).astype(jnp.bfloat16)
+                prods.append(jnp.concatenate([pre, pim], axis=1))
     q_all = jnp.dot(jnp.concatenate(prods, axis=0), forward,
                     preferred_element_type=jnp.float32).astype(jnp.bfloat16)
     for position in range(len(prods)):
@@ -211,11 +212,11 @@
         sq_ref[0] = square
 
 
-def correlate_chunk(spec_re, spec_im, templ_groups, forward, inverse, orient_chunk,
-                    orient_total, stats, last):
+def correlate_chunk(spec_re, spec_im, templ_groups, template_counts, forward, inverse,
+                    orient_chunk, orient_total, stats, last):
     count, extent = (spec_re.shape[0], spec_re.shape[-1])
-    counts = tuple(group.shape[0] // 2 for group in templ_groups)
-    tiles = sum(counts)
+    counts = tuple(template_counts)
+    tiles = sum(count * parts for count, parts in counts)
     first = stats is None
     lanes = 128 * ((orient_total + 127) // 128)
     plane = pl.BlockSpec((1, extent, extent), lambda s: (s, 0, 0))
@@ -266,29 +267,31 @@
         [lax.dynamic_slice_in_dim(templ_re, core * half, half, 0),
          lax.dynamic_slice_in_dim(templ_im, core * half, half, 0)], axis=0)
     within = jnp.arange(half, dtype=jnp.int32)
-    first_groups = [local]
+    first_groups = [(local, 1)]
     first_index = [me * tiles + jnp.arange(tiles, dtype=jnp.int32)]
-    late_groups, late_index = [], []
+    late_got, late_index = [], []
     for k in range(1, blocks):
         source = me ^ k
         got = lax.ppermute(mine, "blk", [(b, b ^ k) for b in range(blocks)])
-        passed = lax.ppermute(got, "patch", xor_pairs(sources, 1))
-        first_groups.append(got)
+        first_groups.append((got, 1))
         first_index.append(source * tiles + core * half + within)
         if k == 1:
-            first_groups.append(passed)
+            first_groups.append((lax.ppermute(got, "patch", xor_pairs(sources, 1)), 1))
             first_index.append(source * tiles + (1 - core) * half + within)
         else:
-            late_groups.append(passed)
+            late_got.append(got)
             late_index.append(source * tiles + (1 - core) * half + within)
     chunks = [(first_groups, jnp.concatenate(first_index))]
-    if late_groups:
-        chunks.append((late_groups, jnp.concatenate(late_index)))
+    if late_got:
+        passed = lax.ppermute(jnp.concatenate(late_got, axis=0), "patch", xor_pairs(sources, 1))
+        chunks.append(([(passed, len(late_got))], jnp.concatenate(late_index)))
     stats = None
     for n, (groups, index) in enumerate(chunks):
         orient_chunk = jnp.take(orientation, index)
-        stats = correlate_chunk(spec_re, spec_im, groups, forward, inverse, orient_chunk,
-                                orient_total, stats, n == len(chunks) - 1)
+        counts = [(group.shape[0] // (2 * parts), parts) for group, parts in groups]
+        stats = correlate_chunk(spec_re, spec_im, [group for group, parts in groups], counts,
+                                forward, inverse, orient_chunk, orient_total, stats,
+                                n == len(chunks) - 1)
     top_map, mean_map, var_map, peak = stats
     return (top_map, mean_map, var_map, peak)
 

time: 71.2 us -> 69.5 us (0.976)
  waiting for transfers between devices: 15.6 us -> 13.4 us
    ppermute x3, waiting for transfers between devices: 13.1 us -> 11.7 us  [route_patches(): lax.ppermute(outgoing[m], 'patch', xor_pairs(sources, 2 * m))]
    ppermute x3, waiting for transfers between devices: 2.56 us -> 1.66 us  [correlate_all(): got = lax.ppermute(mine, 'blk', [(b, b ^ k) for b in range(blocks)])]
    unnamed x26 -> x20, local copies, waits for them, and re-layouts: 3.73 us -> 3.47 us
    ppermute x3 -> x2, starting transfers between devices: 3.44 us -> 3.6 us  [the longest x1 3.03 us: correlate_all(): lax.ppermute(jnp.concatenate(late_got, axis=0), 'patch', xor_pairs(source...]
  transfers between devices with their start and end apart: 11 -> 10, of which waited for: 3 -> 3; matrix products, arithmetic and copies ran while one was open for 15% -> 18% of each run, Pallas kernels for 27% -> 28%
where the time goes in v15:
time: 69.5 us; the launch traced here: 69.2 us
  Pallas kernels  27.1 us (39%)
  waiting for transfers between devices  13.4 us (19%)
  starting transfers between devices  12 us (17%)
  local copies, waits for them, and re-layouts  10.1 us (15%)
  other arithmetic  5.6 us (8%)
  between operations  0.94 us (1%)
    pallas_call x2, Pallas kernels, correlate_chunk(): pl.pallas_call(functools.partial(corr_kernel, first, last, counts, orient...  23 us
    ppermute x3, waiting for transfers between devices, route_patches(): lax.ppermute(outgoing[m], 'patch', xor_pairs(sources, 2 * m))  11.7 us
    pallas_call x1, Pallas kernels, make_spectra(): pl.pallas_call(functools.partial(spectra_kernel, rows), in_specs=[pl.Bloc...  4.15 us
    ppermute x3, starting transfers between devices, route_patches(): lax.ppermute(outgoing[m], 'patch', xor_pairs(sources, 2 * m))  3.56 us
    unnamed x20, local copies, waits for them, and re-layouts  3.47 us
    ppermute x1, starting transfers between devices, correlate_all(): lax.ppermute(jnp.concatenate(late_got, axis=0), 'patch', xor_pairs(source...  3.03 us
    ppermute x3, starting transfers between devices, correlate_all(): got = lax.ppermute(mine, 'blk', [(b, b ^ k) for b in range(blocks)])  2.71 us
    ppermute x1, starting transfers between devices, route_patches(): direct = lax.ppermute(outgoing[0], 'patch', xor_pairs(sources, 1))  2.16 us
  transfers between devices with their start and end apart: 10, of which 3 were waited for; matrix products, arithmetic and copies ran while one was open for 18% of the time, Pallas kernels for 28%

profile of v15, /device:TPU:9, one launch (start us, length us, event | category | flops | bytes accessed | tf_op | source)
XLA Modules:
  0.0 69.2 jit_solution(15712366680512359576)
XLA Ops:
  0.7 1.1 %constant_dynamic-slice_fusion = (bf16[2,256,256]{2,1,0:T(8,128)(2,1)S(1)}, bf16[2,256,256]{2,1,0:T(8,128)(2,1)S(1)}) fusion(bf16[4,256,256]{2,1,0:T(8,128)(2,1)} %param.15, s32[]{:T(128)S(6)} %select_n.311, bf16[4,256,256]{2,1,0:T(8,128)(2,1)} %param.14), kind=kLoop, calls=%fused_computation.47 | loop fusion | bytes 1048580 | tf_op jit(solution)/shard_map/dynamic_slice | solution.py:268
  1.8 1.3 %collective-permute-start.8 = (bf16[4,256,256]{2,1,0:T(8,128)(2,1)S(1)}, bf16[4,256,256]{2,1,0:T(8,128)(2,1)}, u32[]{:S(2)}, u32[]{:S(2)}) collective-permute-start(bf16[4,256,256]{2,1,0:T(8,128)(2,1)S(1)} %pad_maximum_fusion.2), channel_id=1, source_target_pairs={{0,8},{8,0},{16,24},{24,16},{1,9},{9,1},{17,25},{25,17},{2,10},{10... | collective-permute-start | bytes 1572872 | tf_op jit(solution)/shard_map/ppermute | solution.py:275
  3.1 1.2 %collective-permute-start.6 = (bf16[4,256,256]{2,1,0:T(8,128)(2,1)S(1)}, bf16[4,256,256]{2,1,0:T(8,128)(2,1)S(1)}, u32[]{:S(2)}, u32[]{:S(2)}) collective-permute-start(bf16[4,256,256]{2,1,0:T(8,128)(2,1)S(1)} %pad_maximum_fusion.2), channel_id=1, source_target_pairs={{0,24},{8,16},{16,8},{24,0},{1,25},{9,17},{17,9},{25,1},{2,26},{10... | collective-permute-start | bytes 1572872 | tf_op jit(solution)/shard_map/ppermute | solution.py:275
  4.3 0.7 copy-done.7
  5.1 0.1 copy.34
  5.2 0.1 copy.36
  5.3 0.1 copy.37
  5.5 0.1 copy.35
  5.7 0.1 copy.38
  5.8 0.1 reshape.722
  6.0 0.6 gather_fusion.1
  6.7 0.2 broadcast_select_fusion
  6.9 1.4 %collective-permute-start.3 = (bf16[2,256,256]{2,1,0:T(8,128)(2,1)S(1)}, bf16[2,256,256]{2,1,0:T(8,128)(2,1)S(1)}, u32[]{:S(2)}, u32[]{:S(2)}) collective-permute-start(bf16[2,256,256]{2,1,0:T(8,128)(2,1)S(1)} %get-tuple-element.27), channel_id=1, source_target_pairs={{0,6},{1,7},{2,4},{3,5},{4,2},{5,3},{6,0},{7,1},{8,14},{9,15},{10,... | collective-permute-start | bytes 786440 | tf_op jit(solution)/shard_map/ppermute | solution.py:87
  8.3 1.1 %collective-permute-start.2 = (bf16[2,256,256]{2,1,0:T(8,128)(2,1)S(1)}, bf16[2,256,256]{2,1,0:T(8,128)(2,1)S(1)}, u32[]{:S(2)}, u32[]{:S(2)}) collective-permute-start(bf16[2,256,256]{2,1,0:T(8,128)(2,1)S(1)} %get-tuple-element.28), channel_id=1, source_target_pairs={{0,4},{1,5},{2,6},{3,7},{4,0},{5,1},{6,2},{7,3},{8,12},{9,13},{10,... | collective-permute-start | bytes 786440 | tf_op jit(solution)/shard_map/ppermute | solution.py:87
  9.4 1.1 %collective-permute-start.1 = (bf16[2,256,256]{2,1,0:T(8,128)(2,1)S(1)}, bf16[2,256,256]{2,1,0:T(8,128)(2,1)S(1)}, u32[]{:S(2)}, u32[]{:S(2)}) collective-permute-start(bf16[2,256,256]{2,1,0:T(8,128)(2,1)S(1)} %get-tuple-element.29), channel_id=1, source_target_pairs={{0,2},{1,3},{2,0},{3,1},{4,6},{5,7},{6,4},{7,5},{8,10},{9,11},{10,... | collective-permute-start | bytes 786440 | tf_op jit(solution)/shard_map/ppermute | solution.py:87
  10.5 0.1 copy.33
  10.6 0.1 reduce
  10.7 0.1 select_reduce_fusion.1
  10.9 0.1 fusion.6
  11.1 0.1 concatenate.103
  11.2 0.4 fusion.13
  11.7 0.2 select_reduce_fusion
  11.9 0.5 broadcast_select_fusion.2.take_ref
  12.5 0.6 copy-done.8
  13.2 0.6 gather_fusion.2
  13.9 0.6 gather_fusion.3
  14.6 0.1 fusion.1
  14.7 1.3 %negate_multiply_fusion.scale_ref = f32[4,256,256]{2,1,0:T(8,128)} fusion(f32[4,256]{1,0:T(4,128)S(1)} %get-tuple-element.36, f32[4,256]{1,0:T(4,128)S(1)} %get-tuple-element.38, f32[4,256]{1,0:T(4,128)S(1)} %get-tuple-element.37, f32[4,256]{1,0:T(4,128)S(1)} %get-tuple-element.35), kind=kLoop, calls=%fused_computation.7 | loop fusion | flops 1310720 | bytes 1064960 | tf_op jit(solution)/shard_map/div | solution.py:57
  16.1 0.7 gather_fusion.4
  16.8 10.1 %collective-permute-done.1 = bf16[2,256,256]{2,1,0:T(8,128)(2,1)S(1)} collective-permute-done((bf16[2,256,256]{2,1,0:T(8,128)(2,1)S(1)}, bf16[2,256,256]{2,1,0:T(8,128)(2,1)S(1)}, u32[]{:S(2)}, u32[]{:S(2)}) %collective-permute-start.1) | collective-permute-done | bytes 262176 | tf_op jit(solution)/shard_map/ppermute | solution.py:87
  26.9 0.2 collective-permute-start.5
  27.2 0.7 %constant_dynamic-update-slice_fusion.2 = bf16[6,256,256]{2,1,0:T(8,128)(2,1)} fusion(bf16[2,256,256]{2,1,0:T(8,128)(2,1)S(1)} %collective-permute-done.1), kind=kLoop, calls=%fused_computation.15 | loop fusion | bytes 524288
  27.9 1.6 %collective-permute-done.2 = bf16[2,256,256]{2,1,0:T(8,128)(2,1)S(1)} collective-permute-done((bf16[2,256,256]{2,1,0:T(8,128)(2,1)S(1)}, bf16[2,256,256]{2,1,0:T(8,128)(2,1)S(1)}, u32[]{:S(2)}, u32[]{:S(2)}) %collective-permute-start.2) | collective-permute-done | bytes 262176 | tf_op jit(solution)/shard_map/ppermute | solution.py:87
  29.5 2.2 %collective-permute-start = (bf16[2,256,256]{2,1,0:T(8,128)(2,1)S(1)}, bf16[2,256,256]{2,1,0:T(8,128)(2,1)}, u32[]{:S(2)}, u32[]{:S(2)}) collective-permute-start(bf16[2,256,256]{2,1,0:T(8,128)(2,1)S(1)} %get-tuple-element.30), channel_id=1, source_target_pairs={{0,1},{1,0},{2,3},{3,2},{4,5},{5,4},{6,7},{7,6},{8,9},{9,8},{10,11... | collective-permute-start | bytes 786440 | tf_op jit(solution)/shard_map/ppermute | solution.py:84
  31.7 0.7 %constant_dynamic-update-slice_fusion.1 = bf16[6,256,256]{2,1,0:T(8,128)(2,1)} fusion(bf16[6,256,256]{2,1,0:T(8,128)(2,1)} %constant_dynamic-update-slice_fusion.2, bf16[2,256,256]{2,1,0:T(8,128)(2,1)S(1)} %collective-permute-done.2), kind=kLoop, calls=%fused_computation.14 | loop fusion | bytes 524288
  32.4 0.7 %constant_dynamic-update-slice_fusion.recv_ref = bf16[6,256,256]{2,1,0:T(8,128)(2,1)} fusion(bf16[6,256,256]{2,1,0:T(8,128)(2,1)} %constant_dynamic-update-slice_fusion.1, bf16[2,256,256]{2,1,0:T(8,128)(2,1)S(1)} %collective-permute-done.3), kind=kLoop, calls=%fused_computation.13 | loop fusion | bytes 524288 | tf_op jit(solution)/shard_map/concatenate | solution.py:88
  33.1 0.5 and_select_fusion.refs_0_
  33.7 0.6 gather_fusion
  34.3 0.6 collective-permute-start.9
  34.9 0.6 and_select_fusion.6.refs_0_
  35.5 1.1 %pad_maximum_fusion.1.refs_3_ = bf16[8,256,256]{2,1,0:T(8,128)(2,1)} fusion(bf16[4,256,256]{2,1,0:T(8,128)(2,1)S(1)} %copy-done.2, bf16[4,256,256]{2,1,0:T(8,128)(2,1)S(1)} %copy-done.3), kind=kLoop, calls=%fused_computation.6 | loop fusion | flops 524288 | bytes 2097152 | tf_op jit(solution)/shard_map/concatenate | solution.py:265
  36.6 1.7 %collective-permute-done.5.refs_6_ = bf16[4,256,256]{2,1,0:T(8,128)(2,1)S(1)} collective-permute-done((bf16[4,256,256]{2,1,0:T(8,128)(2,1)S(1)}, bf16[4,256,256]{2,1,0:T(8,128)(2,1)S(1)}, u32[]{:S(2)}, u32[]{:S(2)}) %collective-permute-start.5) | collective-permute-done | bytes 524320 | tf_op jit(solution)/shard_map/ppermute | solution.py:275
  38.3 0.1 pad_maximum_fusion
  38.4 0.7 %copy-done.5 = bf16[4,256,256]{2,1,0:T(8,128)(2,1)} copy-done((bf16[4,256,256]{2,1,0:T(8,128)(2,1)}, bf16[4,256,256]{2,1,0:T(8,128)(2,1)S(1)}, u32[]{:S(2)}) %copy-start.5) | copy-done | bytes 524312
  39.1 3.0 %collective-permute-start.7 = (bf16[8,256,256]{2,1,0:T(8,128)(2,1)S(1)}, bf16[8,256,256]{2,1,0:T(8,128)(2,1)}, u32[]{:S(2)}, u32[]{:S(2)}) collective-permute-start(bf16[8,256,256]{2,1,0:T(8,128)(2,1)S(1)} %pad_maximum_fusion), channel_id=1, source_target_pairs={{0,1},{1,0},{2,3},{3,2},{4,5},{5,4},{6,7},{7,6},{8,9},{9,8},{10,11... | collective-permute-start | bytes 3145736 | tf_op jit(solution)/shard_map/ppermute | solution.py:286
  42.1 4.2 %shard_map.129 = (bf16[4,256,256]{2,1,0:T(8,128)(2,1)}, bf16[4,256,256]{2,1,0:T(8,128)(2,1)}) custom-call(s32[4]{0:T(128)} %broadcast_select_fusion.2.take_ref, bf16[2,256,256]{2,1,0:T(8,128)(2,1)} %own_ref.1, bf16[2,256,256]{2,1,0:T(8,128)(2,1)} %collective-permute-done.direct_ref, bf16[6,256,256]{2,1,0:T(8,128)(2,1)} %constant_dynamic-update-slice_fusion.recv_ref, ...), custom_call_target="tpu_custom_call" | custom-call | flops 1207959552 | bytes 2621440 | tf_op jit(solution)/shard_map/pallas_call | solution.py:144
  46.2 15.1 %shard_map.130 = (f32[4,256,256]{2,1,0:T(8,128)}, f32[4,256,256]{2,1,0:T(8,128)}, f32[4,256,256]{2,1,0:T(8,128)}, f32[4,8,128]{2,1,0:T(8,128)}) custom-call(s32[12]{0:T(128)} %and_select_fusion.refs_0_, bf16[4,256,256]{2,1,0:T(8,128)(2,1)} %get-tuple-element.12.refs_1_, bf16[4,256,256]{2,1,0:T(8,128)(2,1)} %get-tuple-element.13.refs_2_, ...), custom_call_target="tpu_custom_call" | custom-call | flops 28991029248 | bytes 16777216 | tf_op jit(solution)/shard_map/pallas_call | solution.py:240
  61.4 7.8 %shard_map.131 = (f32[4,256,256]{2,1,0:T(8,128)}, f32[4,256,256]{2,1,0:T(8,128)}, f32[4,256,256]{2,1,0:T(8,128)}, f32[4,16]{1,0:T(4,128)}) custom-call(s32[4]{0:T(128)} %and_select_fusion.6.refs_0_, bf16[4,256,256]{2,1,0:T(8,128)(2,1)} %get-tuple-element.12.refs_1_, ...), custom_call_target="tpu_custom_call", output_to_operand_aliasing={{0}: (6, {}), {1}: (7, {}), {2}: (8, {})} | custom-call | flops 9663676416 | bytes 12582912 | tf_op jit(solution)/shard_map/pallas_call | solution.py:240
  (66 shorter events, 1.0 us)
Async XLA Ops:
  0.6 15.4 %copy-start = (s32[16]{0:T(128)S(1)}, s32[16]{0:T(128)}, u32[]{:S(2)}) copy-start(s32[16]{0:T(128)} %param.16) | copy-start | bytes 196
  1.7 4.3 %copy-start.6 = (bf16[2,256,256]{2,1,0:T(8,128)(2,1)S(1)}, bf16[2,256,256]{2,1,0:T(8,128)(2,1)}, u32[]{:S(2)}) copy-start(bf16[2,256,256]{2,1,0:T(8,128)(2,1)} %own_ref.1) | copy-start | bytes 786436
  1.8 32.5 %collective-permute-start.8 = (bf16[4,256,256]{2,1,0:T(8,128)(2,1)S(1)}, bf16[4,256,256]{2,1,0:T(8,128)(2,1)}, u32[]{:S(2)}, u32[]{:S(2)}) collective-permute-start(bf16[4,256,256]{2,1,0:T(8,128)(2,1)S(1)} %pad_maximum_fusion.2), channel_id=1, source_target_pairs={{0,8},{8,0},{16,24},{24,16},{1,9},{9,1},{17,25},{25,17},{2,10},{10... | collective-permute-start | bytes 1572872 | tf_op jit(solution)/shard_map/ppermute | solution.py:275
  3.1 33.5 %collective-permute-start.6 = (bf16[4,256,256]{2,1,0:T(8,128)(2,1)S(1)}, bf16[4,256,256]{2,1,0:T(8,128)(2,1)S(1)}, u32[]{:S(2)}, u32[]{:S(2)}) collective-permute-start(bf16[4,256,256]{2,1,0:T(8,128)(2,1)S(1)} %pad_maximum_fusion.2), channel_id=1, source_target_pairs={{0,24},{8,16},{16,8},{24,0},{1,25},{9,17},{17,9},{25,1},{2,26},{10... | collective-permute-start | bytes 1572872 | tf_op jit(solution)/shard_map/ppermute | solution.py:275
  4.3 0.7 copy-start.7
  6.9 25.5 %collective-permute-start.3 = (bf16[2,256,256]{2,1,0:T(8,128)(2,1)S(1)}, bf16[2,256,256]{2,1,0:T(8,128)(2,1)S(1)}, u32[]{:S(2)}, u32[]{:S(2)}) collective-permute-start(bf16[2,256,256]{2,1,0:T(8,128)(2,1)S(1)} %get-tuple-element.27), channel_id=1, source_target_pairs={{0,6},{1,7},{2,4},{3,5},{4,2},{5,3},{6,0},{7,1},{8,14},{9,15},{10,... | collective-permute-start | bytes 786440 | tf_op jit(solution)/shard_map/ppermute | solution.py:87
  8.3 21.2 %collective-permute-start.2 = (bf16[2,256,256]{2,1,0:T(8,128)(2,1)S(1)}, bf16[2,256,256]{2,1,0:T(8,128)(2,1)S(1)}, u32[]{:S(2)}, u32[]{:S(2)}) collective-permute-start(bf16[2,256,256]{2,1,0:T(8,128)(2,1)S(1)} %get-tuple-element.28), channel_id=1, source_target_pairs={{0,4},{1,5},{2,6},{3,7},{4,0},{5,1},{6,2},{7,3},{8,12},{9,13},{10,... | collective-permute-start | bytes 786440 | tf_op jit(solution)/shard_map/ppermute | solution.py:87
  9.4 17.6 %collective-permute-start.1 = (bf16[2,256,256]{2,1,0:T(8,128)(2,1)S(1)}, bf16[2,256,256]{2,1,0:T(8,128)(2,1)S(1)}, u32[]{:S(2)}, u32[]{:S(2)}) collective-permute-start(bf16[2,256,256]{2,1,0:T(8,128)(2,1)S(1)} %get-tuple-element.29), channel_id=1, source_target_pairs={{0,2},{1,3},{2,0},{3,1},{4,6},{5,7},{6,4},{7,5},{8,10},{9,11},{10,... | collective-permute-start | bytes 786440 | tf_op jit(solution)/shard_map/ppermute | solution.py:87
  12.5 0.7 copy-start.8
  13.2 0.7 %copy-start.1 = (f32[32]{0:T(128)S(1)}, f32[32]{0:T(128)}, u32[]{:S(2)}) copy-start(f32[32]{0:T(128)} %param.13) | copy-start | bytes 388
  26.9 11.3 %collective-permute-start.5 = (bf16[4,256,256]{2,1,0:T(8,128)(2,1)S(1)}, bf16[4,256,256]{2,1,0:T(8,128)(2,1)S(1)}, u32[]{:S(2)}, u32[]{:S(2)}) collective-permute-start(bf16[4,256,256]{2,1,0:T(8,128)(2,1)S(1)} %pad_maximum_fusion.2), channel_id=1, source_target_pairs={{0,16},{8,24},{16,0},{24,8},{1,17},{9,25},{17,1},{25,9},{2,18},{10... | collective-permute-start | bytes 1572872 | tf_op jit(solution)/shard_map/ppermute | solution.py:275
  29.5 12.6 %collective-permute-start = (bf16[2,256,256]{2,1,0:T(8,128)(2,1)S(1)}, bf16[2,256,256]{2,1,0:T(8,128)(2,1)}, u32[]{:S(2)}, u32[]{:S(2)}) collective-permute-start(bf16[2,256,256]{2,1,0:T(8,128)(2,1)S(1)} %get-tuple-element.30), channel_id=1, source_target_pairs={{0,1},{1,0},{2,3},{3,2},{4,5},{5,4},{6,7},{7,6},{8,9},{9,8},{10,11... | collective-permute-start | bytes 786440 | tf_op jit(solution)/shard_map/ppermute | solution.py:84
  32.4 3.1 %copy-start.2 = (bf16[4,256,256]{2,1,0:T(8,128)(2,1)S(1)}, bf16[4,256,256]{2,1,0:T(8,128)(2,1)}, u32[]{:S(2)}) copy-start(bf16[4,256,256]{2,1,0:T(8,128)(2,1)} %param.15) | copy-start | bytes 1572868
  32.4 3.1 %copy-start.3 = (bf16[4,256,256]{2,1,0:T(8,128)(2,1)S(1)}, bf16[4,256,256]{2,1,0:T(8,128)(2,1)}, u32[]{:S(2)}) copy-start(bf16[4,256,256]{2,1,0:T(8,128)(2,1)} %param.14) | copy-start | bytes 1572868
  33.1 9.0 %collective-permute-start.4 = (bf16[6,256,256]{2,1,0:T(8,128)(2,1)}, bf16[6,256,256]{2,1,0:T(8,128)(2,1)}, u32[]{:S(2)}, u32[]{:S(2)}) collective-permute-start(bf16[6,256,256]{2,1,0:T(8,128)(2,1)} %constant_dynamic-update-slice_fusion.recv_ref), channel_id=1, source_target_pairs={{0,1},{1,0},{2,3},{3,2},{4,5},{5,4},{6,7},{7,6},{8,9},{9,8},{10,11... | collective-permute-start | bytes 2359304 | tf_op jit(solution)/shard_map/ppermute | solution.py:89
  34.3 11.9 %collective-permute-start.9 = (bf16[4,256,256]{2,1,0:T(8,128)(2,1)}, bf16[4,256,256]{2,1,0:T(8,128)(2,1)}, u32[]{:S(2)}, u32[]{:S(2)}) collective-permute-start(bf16[4,256,256]{2,1,0:T(8,128)(2,1)} %collective-permute-done.8.refs_4_), channel_id=1, source_target_pairs={{0,1},{1,0},{2,3},{3,2},{4,5},{5,4},{6,7},{7,6},{8,9},{9,8},{10,11... | collective-permute-start | bytes 1572872 | tf_op jit(solution)/shard_map/ppermute | solution.py:279
  36.6 1.8 %copy-start.4 = (bf16[4,256,256]{2,1,0:T(8,128)(2,1)}, bf16[4,256,256]{2,1,0:T(8,128)(2,1)S(1)}, u32[]{:S(2)}) copy-start(bf16[4,256,256]{2,1,0:T(8,128)(2,1)S(1)} %collective-permute-done.6.refs_7_) | copy-start | bytes 1572868
  38.2 0.8 %copy-start.5 = (bf16[4,256,256]{2,1,0:T(8,128)(2,1)}, bf16[4,256,256]{2,1,0:T(8,128)(2,1)S(1)}, u32[]{:S(2)}) copy-start(bf16[4,256,256]{2,1,0:T(8,128)(2,1)S(1)} %collective-permute-done.5.refs_6_) | copy-start | bytes 1572868
  39.1 22.3 %collective-permute-start.7 = (bf16[8,256,256]{2,1,0:T(8,128)(2,1)S(1)}, bf16[8,256,256]{2,1,0:T(8,128)(2,1)}, u32[]{:S(2)}, u32[]{:S(2)}) collective-permute-start(bf16[8,256,256]{2,1,0:T(8,128)(2,1)S(1)} %pad_maximum_fusion), channel_id=1, source_target_pairs={{0,1},{1,0},{2,3},{3,2},{4,5},{5,4},{6,7},{7,6},{8,9},{9,8},{10,11... | collective-permute-start | bytes 3145736 | tf_op jit(solution)/shard_map/ppermute | solution.py:286

commit v16 on v15

--- a/solution.py
+++ b/solution.py
@@ -275,12 +275,8 @@
         got = lax.ppermute(mine, "blk", [(b, b ^ k) for b in range(blocks)])
         first_groups.append((got, 1))
         first_index.append(source * tiles + core * half + within)
-        if k == 1:
-            first_groups.append((lax.ppermute(got, "patch", xor_pairs(sources, 1)), 1))
-            first_index.append(source * tiles + (1 - core) * half + within)
-        else:
-            late_got.append(got)
-            late_index.append(source * tiles + (1 - core) * half + within)
+        late_got.append(got)
+        late_index.append(source * tiles + (1 - core) * half + within)
     chunks = [(first_groups, jnp.concatenate(first_index))]
     if late_got:
         passed = lax.ppermute(jnp.concatenate(late_got, axis=0), "patch", xor_pairs(sources, 1))

time: 69.5 us -> 69.3 us (level)
    ppermute x3, waiting for transfers between devices: 1.66 us -> 0.53 us  [correlate_all(): got = lax.ppermute(mine, 'blk', [(b, b ^ k) for b in range(blocks)])]
    slice x1, local copies, waits for them, and re-layouts: 0.07 us -> 0.9 us  [route_patches(): outgoing[m]]
    ppermute x3, waiting for transfers between devices: 11.7 us -> 12.5 us  [route_patches(): lax.ppermute(outgoing[m], 'patch', xor_pairs(sources, 2 * m))]
    unnamed x20 -> x22, local copies, waits for them, and re-layouts: 3.47 us -> 3.39 us
  transfers between devices with their start and end apart: 10 -> 9, of which waited for: 3 -> 3; matrix products, arithmetic and copies ran while one was open for 18% -> 22% of each run, Pallas kernels for 28% -> 25%
where the time goes in v16:
time: 69.3 us; the launch traced here: 69 us
  Pallas kernels  27 us (39%)
  waiting for transfers between devices  13.1 us (19%)
  starting transfers between devices  11.5 us (17%)
  local copies, waits for them, and re-layouts  10.7 us (15%)
  other arithmetic  5.78 us (8%)
  between operations  0.98 us (1%)
    pallas_call x2, Pallas kernels, correlate_chunk(): pl.pallas_call(functools.partial(corr_kernel, first, last, counts, orient...  22.9 us
    ppermute x3, waiting for transfers between devices, route_patches(): lax.ppermute(outgoing[m], 'patch', xor_pairs(sources, 2 * m))  12.5 us
    pallas_call x1, Pallas kernels, make_spectra(): pl.pallas_call(functools.partial(spectra_kernel, rows), in_specs=[pl.Bloc...  4.16 us
    ppermute x3, starting transfers between devices, route_patches(): lax.ppermute(outgoing[m], 'patch', xor_pairs(sources, 2 * m))  3.49 us
    unnamed x22, local copies, waits for them, and re-layouts  3.39 us
    ppermute x1, starting transfers between devices, correlate_all(): lax.ppermute(jnp.concatenate(late_got, axis=0), 'patch', xor_pairs(source...  3.1 us
    ppermute x3, starting transfers between devices, correlate_all(): got = lax.ppermute(mine, 'blk', [(b, b ^ k) for b in range(blocks)])  2.71 us
    ppermute x1, starting transfers between devices, route_patches(): direct = lax.ppermute(outgoing[0], 'patch', xor_pairs(sources, 1))  2.16 us
  transfers between devices with their start and end apart: 9, of which 3 were waited for; matrix products, arithmetic and copies ran while one was open for 22% of the time, Pallas kernels for 25%

profile of v16, /device:TPU:9, one launch (start us, length us, event | category | flops | bytes accessed | tf_op | source)
XLA Modules:
  0.0 69.0 jit_solution(5623095629242753223)
XLA Ops:
  0.7 1.1 %constant_dynamic-slice_fusion = (bf16[2,256,256]{2,1,0:T(8,128)(2,1)S(1)}, bf16[2,256,256]{2,1,0:T(8,128)(2,1)S(1)}) fusion(bf16[4,256,256]{2,1,0:T(8,128)(2,1)} %param.15, s32[]{:T(128)S(6)} %select_n.312, bf16[4,256,256]{2,1,0:T(8,128)(2,1)} %param.14), kind=kLoop, calls=%fused_computation.47 | loop fusion | bytes 1048580 | tf_op jit(solution)/shard_map/dynamic_slice | solution.py:268
  1.9 2.2 %collective-permute-start.7 = (bf16[4,256,256]{2,1,0:T(8,128)(2,1)S(1)}, bf16[4,256,256]{2,1,0:T(8,128)(2,1)S(1)}, u32[]{:S(2)}, u32[]{:S(2)}) collective-permute-start(bf16[4,256,256]{2,1,0:T(8,128)(2,1)S(1)} %pad_maximum_fusion.2), channel_id=1, source_target_pairs={{0,24},{8,16},{16,8},{24,0},{1,25},{9,17},{17,9},{25,1},{2,26},{10... | collective-permute-start | bytes 1572872 | tf_op jit(solution)/shard_map/ppermute | solution.py:275
  4.1 0.2 collective-permute-start.6
  4.5 0.1 copy.34
  4.6 0.1 copy.36
  4.7 0.1 copy.37
  4.8 0.1 copy.35
  5.0 0.1 fusion.2
  5.1 0.1 copy.38
  5.2 0.1 reshape.722
  5.3 0.1 reshape.721
  5.4 0.6 gather_fusion.1
  6.0 0.2 broadcast_select_fusion
  6.2 0.9 %fusion.32 = (bf16[2,256,256]{2,1,0:T(8,128)(2,1)}, bf16[2,256,256]{2,1,0:T(8,128)(2,1)}, bf16[2,256,256]{2,1,0:T(8,128)(2,1)S(1)}, bf16[2,256,256]{2,1,0:T(8,128)(2,1)}) fusion(bf16[8,256,256]{2,1,0:T(8,128)(2,1)S(1)} %broadcast_select_fusion), kind=kLoop, calls=%fused_computation.120 | loop fusion | bytes 2097152 | tf_op jit(solution)/shard_map/slice | solution.py:87
  7.1 1.3 %collective-permute-start.3 = (bf16[2,256,256]{2,1,0:T(8,128)(2,1)}, bf16[2,256,256]{2,1,0:T(8,128)(2,1)S(1)}, u32[]{:S(2)}, u32[]{:S(2)}) collective-permute-start(bf16[2,256,256]{2,1,0:T(8,128)(2,1)} %get-tuple-element.27), channel_id=1, source_target_pairs={{0,6},{1,7},{2,4},{3,5},{4,2},{5,3},{6,0},{7,1},{8,14},{9,15},{10,... | collective-permute-start | bytes 786440 | tf_op jit(solution)/shard_map/ppermute | solution.py:87
  8.4 1.0 %collective-permute-start.2 = (bf16[2,256,256]{2,1,0:T(8,128)(2,1)}, bf16[2,256,256]{2,1,0:T(8,128)(2,1)}, u32[]{:S(2)}, u32[]{:S(2)}) collective-permute-start(bf16[2,256,256]{2,1,0:T(8,128)(2,1)} %get-tuple-element.28), channel_id=1, source_target_pairs={{0,4},{1,5},{2,6},{3,7},{4,0},{5,1},{6,2},{7,3},{8,12},{9,13},{10,... | collective-permute-start | bytes 786440 | tf_op jit(solution)/shard_map/ppermute | solution.py:87
  9.4 1.2 %collective-permute-start.1 = (bf16[2,256,256]{2,1,0:T(8,128)(2,1)S(1)}, bf16[2,256,256]{2,1,0:T(8,128)(2,1)}, u32[]{:S(2)}, u32[]{:S(2)}) collective-permute-start(bf16[2,256,256]{2,1,0:T(8,128)(2,1)S(1)} %get-tuple-element.29), channel_id=1, source_target_pairs={{0,2},{1,3},{2,0},{3,1},{4,6},{5,7},{6,4},{7,5},{8,10},{9,11},{10,... | collective-permute-start | bytes 786440 | tf_op jit(solution)/shard_map/ppermute | solution.py:87
  10.7 0.1 copy.33
  10.8 0.1 reduce
  10.9 0.1 select_reduce_fusion.1
  11.1 0.1 fusion.6
  11.2 0.1 fusion.17
  11.4 0.4 fusion.13
  11.8 0.1 concatenate.92
  11.9 0.2 select_reduce_fusion
  12.1 0.5 broadcast_select_fusion.2.take_ref
  12.7 0.6 gather_fusion.2
  13.4 0.6 gather_fusion.3
  14.1 0.6 gather_fusion
  14.7 0.1 fusion.1
  14.9 0.6 and_select_fusion.6.refs_0_
  15.5 11.9 %collective-permute-done.1 = bf16[2,256,256]{2,1,0:T(8,128)(2,1)} collective-permute-done((bf16[2,256,256]{2,1,0:T(8,128)(2,1)S(1)}, bf16[2,256,256]{2,1,0:T(8,128)(2,1)}, u32[]{:S(2)}, u32[]{:S(2)}) %collective-permute-start.1) | collective-permute-done | bytes 262176 | tf_op jit(solution)/shard_map/ppermute | solution.py:87
  27.4 0.3 collective-permute-start.5
  27.7 1.7 %constant_dynamic-update-slice_fusion.2 = bf16[6,256,256]{2,1,0:T(8,128)(2,1)} fusion(bf16[2,256,256]{2,1,0:T(8,128)(2,1)} %collective-permute-done.1), kind=kLoop, calls=%fused_computation.15 | loop fusion | bytes 524288
  29.3 0.6 collective-permute-done.2
  30.0 2.2 %collective-permute-start = (bf16[2,256,256]{2,1,0:T(8,128)(2,1)}, bf16[2,256,256]{2,1,0:T(8,128)(2,1)}, u32[]{:S(2)}, u32[]{:S(2)}) collective-permute-start(bf16[2,256,256]{2,1,0:T(8,128)(2,1)} %get-tuple-element.30), channel_id=1, source_target_pairs={{0,1},{1,0},{2,3},{3,2},{4,5},{5,4},{6,7},{7,6},{8,9},{9,8},{10,11... | collective-permute-start | bytes 786440 | tf_op jit(solution)/shard_map/ppermute | solution.py:84
  32.1 1.7 %constant_dynamic-update-slice_fusion.1 = bf16[6,256,256]{2,1,0:T(8,128)(2,1)} fusion(bf16[6,256,256]{2,1,0:T(8,128)(2,1)} %constant_dynamic-update-slice_fusion.2, bf16[2,256,256]{2,1,0:T(8,128)(2,1)} %collective-permute-done.2), kind=kLoop, calls=%fused_computation.14 | loop fusion | bytes 524288
  33.8 0.7 %constant_dynamic-update-slice_fusion.recv_ref = bf16[6,256,256]{2,1,0:T(8,128)(2,1)} fusion(bf16[6,256,256]{2,1,0:T(8,128)(2,1)} %constant_dynamic-update-slice_fusion.1, bf16[2,256,256]{2,1,0:T(8,128)(2,1)S(1)} %collective-permute-done.3), kind=kLoop, calls=%fused_computation.13 | loop fusion | bytes 524288 | tf_op jit(solution)/shard_map/concatenate | solution.py:88
  34.5 0.7 gather_fusion.4
  35.2 0.6 and_select_fusion.refs_0_
  35.8 1.3 %negate_multiply_fusion.scale_ref = f32[4,256,256]{2,1,0:T(8,128)} fusion(f32[4,256]{1,0:T(4,128)S(1)} %get-tuple-element.36, f32[4,256]{1,0:T(4,128)S(1)} %get-tuple-element.38, f32[4,256]{1,0:T(4,128)S(1)} %get-tuple-element.37, f32[4,256]{1,0:T(4,128)S(1)} %get-tuple-element.35), kind=kLoop, calls=%fused_computation.7 | loop fusion | flops 1310720 | bytes 1064960 | tf_op jit(solution)/shard_map/div | solution.py:57
  37.1 1.1 %pad_maximum_fusion.1.refs_3_ = bf16[8,256,256]{2,1,0:T(8,128)(2,1)} fusion(bf16[4,256,256]{2,1,0:T(8,128)(2,1)S(1)} %copy-done.2, bf16[4,256,256]{2,1,0:T(8,128)(2,1)S(1)} %copy-done.3), kind=kLoop, calls=%fused_computation.6 | loop fusion | flops 524288 | bytes 2097152 | tf_op jit(solution)/shard_map/concatenate | solution.py:265
  38.2 0.5 collective-permute-done.5.refs_4_
  38.7 0.2 pad_maximum_fusion
  38.9 3.1 %collective-permute-start.8 = (bf16[12,256,256]{2,1,0:T(8,128)(2,1)S(1)}, bf16[12,256,256]{2,1,0:T(8,128)(2,1)}, u32[]{:S(2)}, u32[]{:S(2)}) collective-permute-start(bf16[12,256,256]{2,1,0:T(8,128)(2,1)S(1)} %pad_maximum_fusion), channel_id=1, source_target_pairs={{0,1},{1,0},{2,3},{3,2},{4,5},{5,4},{6,7},{7,6},{8,9},{9,8},{10,11... | collective-permute-start | bytes 4718600 | tf_op jit(solution)/shard_map/ppermute | solution.py:282
  42.0 4.2 %shard_map.129 = (bf16[4,256,256]{2,1,0:T(8,128)(2,1)}, bf16[4,256,256]{2,1,0:T(8,128)(2,1)}) custom-call(s32[4]{0:T(128)} %broadcast_select_fusion.2.take_ref, bf16[2,256,256]{2,1,0:T(8,128)(2,1)} %own_ref.1, bf16[2,256,256]{2,1,0:T(8,128)(2,1)} %collective-permute-done.direct_ref, bf16[6,256,256]{2,1,0:T(8,128)(2,1)} %constant_dynamic-update-slice_fusion.recv_ref, ...), custom_call_target="tpu_custom_call" | custom-call | flops 1207959552 | bytes 2621440 | tf_op jit(solution)/shard_map/pallas_call | solution.py:144
  46.2 13.1 %shard_map.130 = (f32[4,256,256]{2,1,0:T(8,128)}, f32[4,256,256]{2,1,0:T(8,128)}, f32[4,256,256]{2,1,0:T(8,128)}, f32[4,8,128]{2,1,0:T(8,128)}) custom-call(s32[10]{0:T(128)} %and_select_fusion.refs_0_, bf16[4,256,256]{2,1,0:T(8,128)(2,1)} %get-tuple-element.12.refs_1_, bf16[4,256,256]{2,1,0:T(8,128)(2,1)} %get-tuple-element.13.refs_2_, ...), custom_call_target="tpu_custom_call" | custom-call | flops 24159191040 | bytes 15728640 | tf_op jit(solution)/shard_map/pallas_call | solution.py:240
  59.3 9.7 %shard_map.131 = (f32[4,256,256]{2,1,0:T(8,128)}, f32[4,256,256]{2,1,0:T(8,128)}, f32[4,256,256]{2,1,0:T(8,128)}, f32[4,16]{1,0:T(4,128)}) custom-call(s32[6]{0:T(128)} %and_select_fusion.6.refs_0_, bf16[4,256,256]{2,1,0:T(8,128)(2,1)} %get-tuple-element.12.refs_1_, ...), custom_call_target="tpu_custom_call", output_to_operand_aliasing={{0}: (6, {}), {1}: (7, {}), {2}: (8, {})} | custom-call | flops 14495514624 | bytes 13631488 | tf_op jit(solution)/shard_map/pallas_call | solution.py:240
  (64 shorter events, 0.7 us)
Async XLA Ops:
  0.6 13.5 %copy-start = (s32[16]{0:T(128)S(1)}, s32[16]{0:T(128)}, u32[]{:S(2)}) copy-start(s32[16]{0:T(128)} %param.16) | copy-start | bytes 196
  0.6 3.7 %copy-start.8 = (s32[16]{0:T(128)S(1)}, s32[16]{0:T(128)}, u32[]{:S(2)}) copy-start(s32[16]{0:T(128)} %param.11) | copy-start | bytes 196
  0.7 4.7 %copy-start.7 = (bf16[2,256,256]{2,1,0:T(8,128)(2,1)S(1)}, bf16[2,256,256]{2,1,0:T(8,128)(2,1)}, u32[]{:S(2)}) copy-start(bf16[2,256,256]{2,1,0:T(8,128)(2,1)} %own_ref.1) | copy-start | bytes 786436
  1.9 36.3 %collective-permute-start.7 = (bf16[4,256,256]{2,1,0:T(8,128)(2,1)S(1)}, bf16[4,256,256]{2,1,0:T(8,128)(2,1)S(1)}, u32[]{:S(2)}, u32[]{:S(2)}) collective-permute-start(bf16[4,256,256]{2,1,0:T(8,128)(2,1)S(1)} %pad_maximum_fusion.2), channel_id=1, source_target_pairs={{0,24},{8,16},{16,8},{24,0},{1,25},{9,17},{17,9},{25,1},{2,26},{10... | collective-permute-start | bytes 1572872 | tf_op jit(solution)/shard_map/ppermute | solution.py:275
  4.1 34.1 %collective-permute-start.6 = (bf16[4,256,256]{2,1,0:T(8,128)(2,1)S(1)}, bf16[4,256,256]{2,1,0:T(8,128)(2,1)S(1)}, u32[]{:S(2)}, u32[]{:S(2)}) collective-permute-start(bf16[4,256,256]{2,1,0:T(8,128)(2,1)S(1)} %pad_maximum_fusion.2), channel_id=1, source_target_pairs={{0,16},{8,24},{16,0},{24,8},{1,17},{9,25},{17,1},{25,9},{2,18},{10... | collective-permute-start | bytes 1572872 | tf_op jit(solution)/shard_map/ppermute | solution.py:275
  6.2 6.4 %copy-start.9 = (s32[16]{0:T(128)S(1)}, s32[16]{0:T(128)}, u32[]{:S(2)}) copy-start(s32[16]{0:T(128)} %param.12) | copy-start | bytes 196
  6.2 7.2 %copy-start.1 = (f32[32]{0:T(128)S(1)}, f32[32]{0:T(128)}, u32[]{:S(2)}) copy-start(f32[32]{0:T(128)} %param.13) | copy-start | bytes 388
  7.1 26.7 %collective-permute-start.3 = (bf16[2,256,256]{2,1,0:T(8,128)(2,1)}, bf16[2,256,256]{2,1,0:T(8,128)(2,1)S(1)}, u32[]{:S(2)}, u32[]{:S(2)}) collective-permute-start(bf16[2,256,256]{2,1,0:T(8,128)(2,1)} %get-tuple-element.27), channel_id=1, source_target_pairs={{0,6},{1,7},{2,4},{3,5},{4,2},{5,3},{6,0},{7,1},{8,14},{9,15},{10,... | collective-permute-start | bytes 786440 | tf_op jit(solution)/shard_map/ppermute | solution.py:87
  8.4 21.5 %collective-permute-start.2 = (bf16[2,256,256]{2,1,0:T(8,128)(2,1)}, bf16[2,256,256]{2,1,0:T(8,128)(2,1)}, u32[]{:S(2)}, u32[]{:S(2)}) collective-permute-start(bf16[2,256,256]{2,1,0:T(8,128)(2,1)} %get-tuple-element.28), channel_id=1, source_target_pairs={{0,4},{1,5},{2,6},{3,7},{4,0},{5,1},{6,2},{7,3},{8,12},{9,13},{10,... | collective-permute-start | bytes 786440 | tf_op jit(solution)/shard_map/ppermute | solution.py:87
  9.4 18.0 %collective-permute-start.1 = (bf16[2,256,256]{2,1,0:T(8,128)(2,1)S(1)}, bf16[2,256,256]{2,1,0:T(8,128)(2,1)}, u32[]{:S(2)}, u32[]{:S(2)}) collective-permute-start(bf16[2,256,256]{2,1,0:T(8,128)(2,1)S(1)} %get-tuple-element.29), channel_id=1, source_target_pairs={{0,2},{1,3},{2,0},{3,1},{4,6},{5,7},{6,4},{7,5},{8,10},{9,11},{10,... | collective-permute-start | bytes 786440 | tf_op jit(solution)/shard_map/ppermute | solution.py:87
  15.5 21.6 %copy-start.2 = (bf16[4,256,256]{2,1,0:T(8,128)(2,1)S(1)}, bf16[4,256,256]{2,1,0:T(8,128)(2,1)}, u32[]{:S(2)}) copy-start(bf16[4,256,256]{2,1,0:T(8,128)(2,1)} %param.15) | copy-start | bytes 1572868
  15.5 21.6 %copy-start.3 = (bf16[4,256,256]{2,1,0:T(8,128)(2,1)S(1)}, bf16[4,256,256]{2,1,0:T(8,128)(2,1)}, u32[]{:S(2)}) copy-start(bf16[4,256,256]{2,1,0:T(8,128)(2,1)} %param.14) | copy-start | bytes 1572868
  27.4 11.3 %collective-permute-start.5 = (bf16[4,256,256]{2,1,0:T(8,128)(2,1)S(1)}, bf16[4,256,256]{2,1,0:T(8,128)(2,1)S(1)}, u32[]{:S(2)}, u32[]{:S(2)}) collective-permute-start(bf16[4,256,256]{2,1,0:T(8,128)(2,1)S(1)} %pad_maximum_fusion.2), channel_id=1, source_target_pairs={{0,8},{8,0},{16,24},{24,16},{1,9},{9,1},{17,25},{25,17},{2,10},{10... | collective-permute-start | bytes 1572872 | tf_op jit(solution)/shard_map/ppermute | solution.py:275
  30.0 12.0 %collective-permute-start = (bf16[2,256,256]{2,1,0:T(8,128)(2,1)}, bf16[2,256,256]{2,1,0:T(8,128)(2,1)}, u32[]{:S(2)}, u32[]{:S(2)}) collective-permute-start(bf16[2,256,256]{2,1,0:T(8,128)(2,1)} %get-tuple-element.30), channel_id=1, source_target_pairs={{0,1},{1,0},{2,3},{3,2},{4,5},{5,4},{6,7},{7,6},{8,9},{9,8},{10,11... | collective-permute-start | bytes 786440 | tf_op jit(solution)/shard_map/ppermute | solution.py:84
  34.5 7.5 %collective-permute-start.4 = (bf16[6,256,256]{2,1,0:T(8,128)(2,1)}, bf16[6,256,256]{2,1,0:T(8,128)(2,1)}, u32[]{:S(2)}, u32[]{:S(2)}) collective-permute-start(bf16[6,256,256]{2,1,0:T(8,128)(2,1)} %constant_dynamic-update-slice_fusion.recv_ref), channel_id=1, source_target_pairs={{0,1},{1,0},{2,3},{3,2},{4,5},{5,4},{6,7},{7,6},{8,9},{9,8},{10,11... | collective-permute-start | bytes 2359304 | tf_op jit(solution)/shard_map/ppermute | solution.py:89
  38.2 8.0 %copy-start.4 = (bf16[4,256,256]{2,1,0:T(8,128)(2,1)}, bf16[4,256,256]{2,1,0:T(8,128)(2,1)S(1)}, u32[]{:S(2)}) copy-start(bf16[4,256,256]{2,1,0:T(8,128)(2,1)S(1)} %collective-permute-done.7.refs_6_) | copy-start | bytes 1572868
  38.2 8.0 %copy-start.5 = (bf16[4,256,256]{2,1,0:T(8,128)(2,1)}, bf16[4,256,256]{2,1,0:T(8,128)(2,1)S(1)}, u32[]{:S(2)}) copy-start(bf16[4,256,256]{2,1,0:T(8,128)(2,1)S(1)} %collective-permute-done.6.refs_5_) | copy-start | bytes 1572868
  38.7 7.5 %copy-start.6 = (bf16[4,256,256]{2,1,0:T(8,128)(2,1)}, bf16[4,256,256]{2,1,0:T(8,128)(2,1)S(1)}, u32[]{:S(2)}) copy-start(bf16[4,256,256]{2,1,0:T(8,128)(2,1)S(1)} %collective-permute-done.5.refs_4_) | copy-start | bytes 1572868
  38.9 20.4 %collective-permute-start.8 = (bf16[12,256,256]{2,1,0:T(8,128)(2,1)S(1)}, bf16[12,256,256]{2,1,0:T(8,128)(2,1)}, u32[]{:S(2)}, u32[]{:S(2)}) collective-permute-start(bf16[12,256,256]{2,1,0:T(8,128)(2,1)S(1)} %pad_maximum_fusion), channel_id=1, source_target_pairs={{0,1},{1,0},{2,3},{3,2},{4,5},{5,4},{6,7},{7,6},{8,9},{9,8},{10,11... | collective-permute-start | bytes 4718600 | tf_op jit(solution)/shard_map/ppermute | solution.py:282

commit v17 on v16

--- a/solution.py
+++ b/solution.py
@@ -86,14 +86,28 @@
     for m in range(1, chips):
         received.append(lax.ppermute(outgoing[m], "patch", xor_pairs(sources, 2 * m)))
     received = jnp.concatenate(received, axis=0)
-    forwarded = lax.ppermute(received, "patch", xor_pairs(sources, 1))
-    cand_pid = [my_index * number + jnp.arange(number, dtype=jnp.int32)]
-    cand_pid.append(lax.dynamic_index_in_dim(send_pid, partner, 0, keepdims=False)[0])
-    for core in (my_index % 2, partner % 2):
-        for m in range(1, chips):
-            source = (my_chip ^ m) * 2 + core
-            cand_pid.append(lax.dynamic_index_in_dim(send_pid, source, 0, keepdims=False)[m])
-    cand_pid = jnp.concatenate(cand_pid)
+    recv_pid = jnp.concatenate(
+        [jnp.take(send_pid[:, m], (chip_of ^ m) * 2 + devs % 2, axis=0) for m in range(1, chips)],
+        axis=1)
+    rows = recv_pid.shape[1]
+    flat_owner = row_owner.reshape(-1)
+    recv_owner = jnp.where(recv_pid >= 0, jnp.take(flat_owner, jnp.maximum(recv_pid, 0)), -1)
+    for_partner = (recv_owner == (devs ^ 1)[:, None]).astype(jnp.int32)
+    order = jnp.cumsum(for_partner, axis=1) - for_partner
+    picks = jnp.arange(CAP, dtype=jnp.int32)
+    chosen = (for_partner[:, None, :] == 1) & (order[:, None, :] == picks[None, :, None])
+    fwd_sel = jnp.where(jnp.any(chosen, axis=2),
+                        jnp.sum(jnp.where(chosen, jnp.arange(rows, dtype=jnp.int32), 0), axis=2), rows)
+    fwd_pid = jnp.where(fwd_sel < rows,
+                        jnp.take_along_axis(recv_pid, jnp.minimum(fwd_sel, rows - 1), axis=1), -1)
+    recv_padded = jnp.concatenate([received, jnp.zeros((1, extent, extent), patches.dtype)], axis=0)
+    my_fwd = lax.dynamic_index_in_dim(fwd_sel, my_index, 0, keepdims=False)
+    forwarded = lax.ppermute(jnp.take(recv_padded, my_fwd, axis=0), "patch", xor_pairs(sources, 1))
+    cand_pid = jnp.concatenate([
+        my_index * number + jnp.arange(number, dtype=jnp.int32),
+        lax.dynamic_index_in_dim(send_pid, partner, 0, keepdims=False)[0],
+        lax.dynamic_index_in_dim(recv_pid, my_index, 0, keepdims=False),
+        lax.dynamic_index_in_dim(fwd_pid, partner, 0, keepdims=False)])
     flat_owner = row_owner.reshape(-1)
     hits = (flat_owner == my_index).astype(jnp.int32)
     rank_in = jnp.cumsum(hits) - hits
@@ -121,13 +135,14 @@
         pick_own = own_ref[jnp.clip(idx, 0, number - 1)]
         pick_direct = direct_ref[jnp.clip(idx - number, 0, number - 1)]
         pick_recv = recv_ref[jnp.clip(idx - 2 * number, 0, rows - 1)]
-        pick_fwd = fwd_ref[jnp.clip(idx - 2 * number - rows, 0, rows - 1)]
+        pick_fwd = fwd_ref[jnp.clip(idx - 2 * number - rows, 0, fwd_ref.shape[0] - 1)]
         zero = jnp.zeros_like(pick_own)
         image = jnp.where(
             idx < number, pick_own,
             jnp.where(idx < 2 * number, pick_direct,
                       jnp.where(idx < 2 * number + rows, pick_recv,
-                                jnp.where(idx < 2 * number + 2 * rows, pick_fwd, zero))))
+                                jnp.where(idx < 2 * number + rows + fwd_ref.shape[0], pick_fwd,
+                                          zero))))
         half = jnp.dot(image, half_table, preferred_element_type=jnp.float32).astype(jnp.bfloat16)
         half_stack = jnp.concatenate([half[:, :extent], half[:, extent:]], axis=0)
         spec = jnp.dot(full_table, half_stack, preferred_element_type=jnp.float32)

time: 69.3 us -> 70.2 us (1.013)
  the two profiles are of different devices: /device:TPU:9 before, /device:TPU:0 now
where the time goes in v17:
time: 70.2 us; the launch traced here: 70 us
  Pallas kernels  26.9 us (38%)
  other arithmetic  12.6 us (18%)
  local copies, waits for them, and re-layouts  11.9 us (17%)
  starting transfers between devices  9.8 us (14%)
  waiting for transfers between devices  7.72 us (11%)
  between operations  1.07 us (2%)
    pallas_call x2, Pallas kernels, correlate_chunk(): pl.pallas_call(functools.partial(corr_kernel, first, last, counts, orient...  22.8 us
    ppermute x3, waiting for transfers between devices, route_patches(): lax.ppermute(outgoing[m], 'patch', xor_pairs(sources, 2 * m))  7.7 us
    ppermute x3, starting transfers between devices, correlate_all(): got = lax.ppermute(mine, 'blk', [(b, b ^ k) for b in range(blocks)])  5 us
    ppermute x3, starting transfers between devices, route_patches(): lax.ppermute(outgoing[m], 'patch', xor_pairs(sources, 2 * m))  4.17 us
    pallas_call x1, Pallas kernels, make_spectra(): pl.pallas_call(functools.partial(spectra_kernel, rows), in_specs=[pl.Bloc...  4.05 us
    div x1, other arithmetic, ctf_scale(): return ctf / extent  1.99 us
    gather x3, local copies, waits for them, and re-layouts, route_patches(): jnp.take(send_pid[:, m], (chip_of ^ m) * 2 + devs % 2, axis=0)  1.66 us
    concatenate x1, other arithmetic, correlate_all(): jnp.concatenate(late_got, axis=0)  1.56 us
  transfers between devices with their start and end apart: 9, of which 1 were waited for; matrix products, arithmetic and copies ran while one was open for 33% of the time, Pallas kernels for 25%

profile of v17, /device:TPU:0, one launch (start us, length us, event | category | flops | bytes accessed | tf_op | source)
XLA Modules:
  0.0 70.0 jit_solution(11911418102478149241)
XLA Ops:
  0.7 1.1 %constant_dynamic-slice_fusion = (bf16[2,256,256]{2,1,0:T(8,128)(2,1)S(1)}, bf16[2,256,256]{2,1,0:T(8,128)(2,1)S(1)}) fusion(bf16[4,256,256]{2,1,0:T(8,128)(2,1)} %param.17, s32[]{:T(128)S(6)} %select_n.412, bf16[4,256,256]{2,1,0:T(8,128)(2,1)} %param.16), kind=kLoop, calls=%fused_computation.92 | loop fusion | bytes 1048580 | tf_op jit(solution)/shard_map/dynamic_slice | solution.py:283
  1.9 4.0 %collective-permute-start.7 = (bf16[4,256,256]{2,1,0:T(8,128)(2,1)S(1)}, bf16[4,256,256]{2,1,0:T(8,128)(2,1)S(1)}, u32[]{:S(2)}, u32[]{:S(2)}) collective-permute-start(bf16[4,256,256]{2,1,0:T(8,128)(2,1)S(1)} %pad_maximum_fusion.3), channel_id=1, source_target_pairs={{0,24},{8,16},{16,8},{24,0},{1,25},{9,17},{17,9},{25,1},{2,26},{10... | collective-permute-start | bytes 1572872 | tf_op jit(solution)/shard_map/ppermute | solution.py:290
  5.8 0.5 collective-permute-start.6
  6.3 0.5 compare_select_fusion.5
  7.0 0.1 copy.100
  7.6 0.1 copy.115
  7.9 0.6 gather_fusion.2
  8.6 0.2 broadcast_select_fusion
  8.7 0.9 %fusion.35 = (bf16[2,256,256]{2,1,0:T(8,128)(2,1)}, bf16[2,256,256]{2,1,0:T(8,128)(2,1)}, bf16[2,256,256]{2,1,0:T(8,128)(2,1)S(1)}, bf16[2,256,256]{2,1,0:T(8,128)(2,1)S(1)}) fusion(bf16[8,256,256]{2,1,0:T(8,128)(2,1)S(1)} %broadcast_select_fusion), kind=kLoop, calls=%fused_computation.155 | loop fusion | bytes 2097152 | tf_op jit(solution)/shard_map/slice | solution.py:87
  9.6 1.6 %collective-permute-start.1 = (bf16[2,256,256]{2,1,0:T(8,128)(2,1)}, bf16[2,256,256]{2,1,0:T(8,128)(2,1)S(1)}, u32[]{:S(2)}, u32[]{:S(2)}) collective-permute-start(bf16[2,256,256]{2,1,0:T(8,128)(2,1)} %get-tuple-element.26), channel_id=1, source_target_pairs={{0,2},{1,3},{2,0},{3,1},{4,6},{5,7},{6,4},{7,5},{8,10},{9,11},{10,... | collective-permute-start | bytes 786440 | tf_op jit(solution)/shard_map/ppermute | solution.py:87
  11.2 2.5 %collective-permute-start.3 = (bf16[2,256,256]{2,1,0:T(8,128)(2,1)}, bf16[2,256,256]{2,1,0:T(8,128)(2,1)S(1)}, u32[]{:S(2)}, u32[]{:S(2)}) collective-permute-start(bf16[2,256,256]{2,1,0:T(8,128)(2,1)} %get-tuple-element.27), channel_id=1, source_target_pairs={{0,6},{1,7},{2,4},{3,5},{4,2},{5,3},{6,0},{7,1},{8,14},{9,15},{10,... | collective-permute-start | bytes 786440 | tf_op jit(solution)/shard_map/ppermute | solution.py:87
  13.7 0.1 collective-permute-start.2
  14.1 0.6 gather_fusion.10
  14.9 0.6 gather_fusion.8
  15.7 0.6 gather_fusion.9
  16.6 0.8 %gather_fusion.1 = s32[48]{0:T(128)S(1)} fusion(s32[16]{0:T(128)S(1)} %copy-done.1, s32[1024]{0:T(1024)S(1)} %pad_clamp_fusion.5), kind=kCustom, calls=%fused_computation.4 | custom fusion | bytes 576 | tf_op jit(solution)/shard_map/jit(_take)/gather | solution.py:94
  17.6 0.2 reduce_window_sum.18
  18.0 0.2 dynamic-slice_reduce_fusion
  18.2 0.5 compare_and_fusion.3
  18.8 0.1 reduce
  18.9 0.1 select_reduce_fusion.2
  19.0 0.1 fusion.12
  19.2 1.0 %pad_maximum_fusion.1.refs_3_ = bf16[8,256,256]{2,1,0:T(8,128)(2,1)} fusion(bf16[4,256,256]{2,1,0:T(8,128)(2,1)S(1)} %copy-done.3, bf16[4,256,256]{2,1,0:T(8,128)(2,1)S(1)} %copy-done.4), kind=kLoop, calls=%fused_computation.12 | loop fusion | flops 524288 | bytes 2097152 | tf_op jit(solution)/shard_map/concatenate | solution.py:280
  20.4 0.6 gather_fusion
  21.1 0.7 gather_fusion.6
  21.7 0.2 fusion.13
  22.1 0.7 gather_fusion.7
  23.0 0.2 dynamic-slice_reduce_fusion.1
  23.1 0.6 pad_clamp_fusion.3
  23.8 0.2 select_reduce_fusion.1
  24.0 0.5 broadcast_select_fusion.7.take_ref
  24.6 0.6 gather_fusion.4
  25.3 0.6 gather_fusion.5
  25.9 0.6 and_select_fusion.7.refs_0_
  26.6 0.7 and_select_fusion.refs_0_
  27.3 0.7 %fusion.3 = (f32[4,256]{1,0:T(4,128)S(1)}, f32[4,256]{1,0:T(4,128)S(1)}, f32[4,256]{1,0:T(4,128)S(1)}, f32[4,256]{1,0:T(4,128)}) fusion(f32[256]{0:T(256)S(1)} %fusion.16, f32[4]{0:T(128)S(1)} %fusion.23), kind=kLoop, calls=%fused_computation.33 | loop fusion | flops 2048 | bytes 17424 | tf_op jit(solution)/shard_map/sin | solution.py:54
  28.1 0.5 collective-permute-start.5
  28.6 7.7 %collective-permute-done.2 = bf16[2,256,256]{2,1,0:T(8,128)(2,1)S(1)} collective-permute-done((bf16[2,256,256]{2,1,0:T(8,128)(2,1)S(1)}, bf16[2,256,256]{2,1,0:T(8,128)(2,1)S(1)}, u32[]{:S(2)}, u32[]{:S(2)}) %collective-permute-start.2) | collective-permute-done | bytes 262176 | tf_op jit(solution)/shard_map/ppermute | solution.py:87
  36.3 0.1 maximum_maximum_fusion
  36.4 0.7 %gather_fusion.3 = bf16[4,256,256]{2,1,0:T(8,128)(2,1)S(1)} fusion(bf16[7,256,256]{2,1,0:T(8,128)(2,1)S(1)} %maximum_maximum_fusion, s32[1024]{0:T(1024)} %pad_clamp_fusion.3), kind=kCustom, calls=%fused_computation.6 | custom fusion | bytes 1048592 | tf_op jit(solution)/shard_map/jit(_take)/gather | solution.py:105
  37.2 0.7 %broadcast_select_fusion.1 = bf16[4,256,256]{2,1,0:T(8,128)(2,1)S(1)} fusion(bf16[4,256,256]{2,1,0:T(8,128)(2,1)S(1)} %gather_fusion.3, pred[4]{0:T(512)(128)(4,1)} %compare_and_fusion.3), kind=kLoop, calls=%fused_computation.18 | loop fusion | flops 262144 | bytes 1048580 | tf_op jit(solution)/shard_map/jit(_take)/select_n | solution.py:105
  37.9 2.0 %negate_multiply_fusion.scale_ref = f32[4,256,256]{2,1,0:T(8,128)} fusion(f32[4,256]{1,0:T(4,128)S(1)} %get-tuple-element.38, f32[4,256]{1,0:T(4,128)} %get-tuple-element.40, f32[4,256]{1,0:T(4,128)S(1)} %get-tuple-element.39, f32[4,256]{1,0:T(4,128)S(1)} %get-tuple-element.37), kind=kLoop, calls=%fused_computation.13 | loop fusion | flops 1310720 | bytes 1064960 | tf_op jit(solution)/shard_map/div | solution.py:57
  39.9 1.0 %pad_maximum_fusion.2.recv_ref = bf16[6,256,256]{2,1,0:T(8,128)(2,1)} fusion(bf16[2,256,256]{2,1,0:T(8,128)(2,1)S(1)} %collective-permute-done.3, bf16[2,256,256]{2,1,0:T(8,128)(2,1)S(1)} %collective-permute-done.2, bf16[2,256,256]{2,1,0:T(8,128)(2,1)S(1)} %collective-permute-done.1), kind=kLoop, calls=%fused_computation.16 | loop fusion | flops 786432 | bytes 1572864 | tf_op jit(solution)/shard_map/concatenate | solution.py:88
  40.9 1.6 %pad_maximum_fusion = bf16[12,256,256]{2,1,0:T(8,128)(2,1)S(1)} fusion(bf16[4,256,256]{2,1,0:T(8,128)(2,1)S(1)} %collective-permute-done.7.refs_6_, bf16[4,256,256]{2,1,0:T(8,128)(2,1)} %collective-permute-done.6.refs_5_, bf16[4,256,256]{2,1,0:T(8,128)(2,1)} %collective-permute-done.5.refs_4_), kind=kLoop, calls=%fused_computation.11 | loop fusion | flops 1572864 | bytes 3145728 | tf_op jit(solution)/shard_map/concatenate | solution.py:297
  42.5 0.6 collective-permute-start.8
  43.1 4.1 %shard_map.129 = (bf16[4,256,256]{2,1,0:T(8,128)(2,1)}, bf16[4,256,256]{2,1,0:T(8,128)(2,1)}) custom-call(s32[4]{0:T(128)} %broadcast_select_fusion.7.take_ref, bf16[2,256,256]{2,1,0:T(8,128)(2,1)} %own_ref.1, bf16[2,256,256]{2,1,0:T(8,128)(2,1)} %collective-permute-done.direct_ref, bf16[6,256,256]{2,1,0:T(8,128)(2,1)} %pad_maximum_fusion.2.recv_ref, ...), custom_call_target="tpu_custom_call" | custom-call | flops 1207959552 | bytes 2621440 | tf_op jit(solution)/shard_map/pallas_call | solution.py:159
  47.1 13.1 %shard_map.130 = (f32[4,256,256]{2,1,0:T(8,128)}, f32[4,256,256]{2,1,0:T(8,128)}, f32[4,256,256]{2,1,0:T(8,128)}, f32[4,8,128]{2,1,0:T(8,128)}) custom-call(s32[10]{0:T(128)} %and_select_fusion.refs_0_, bf16[4,256,256]{2,1,0:T(8,128)(2,1)} %get-tuple-element.13.refs_1_, bf16[4,256,256]{2,1,0:T(8,128)(2,1)} %get-tuple-element.14.refs_2_, ...), custom_call_target="tpu_custom_call" | custom-call | flops 24159191040 | bytes 15728640 | tf_op jit(solution)/shard_map/pallas_call | solution.py:255
  60.3 9.7 %shard_map.131 = (f32[4,256,256]{2,1,0:T(8,128)}, f32[4,256,256]{2,1,0:T(8,128)}, f32[4,256,256]{2,1,0:T(8,128)}, f32[4,16]{1,0:T(4,128)}) custom-call(s32[6]{0:T(128)} %and_select_fusion.7.refs_0_, bf16[4,256,256]{2,1,0:T(8,128)(2,1)} %get-tuple-element.13.refs_1_, ...), custom_call_target="tpu_custom_call", output_to_operand_aliasing={{0}: (6, {}), {1}: (7, {}), {2}: (8, {})} | custom-call | flops 14495514624 | bytes 13631488 | tf_op jit(solution)/shard_map/pallas_call | solution.py:255
  (110 shorter events, 3.4 us)
Async XLA Ops:
  0.6 19.8 %copy-start = (s32[16]{0:T(128)S(1)}, s32[16]{0:T(128)}, u32[]{:S(2)}) copy-start(s32[16]{0:T(128)} %param.18) | copy-start | bytes 196
  0.6 6.2 %copy-start.1 = (s32[16]{0:T(128)S(1)}, s32[16]{0:T(128)}, u32[]{:S(2)}) copy-start(s32[16]{0:T(128)} %param.13) | copy-start | bytes 196
  0.7 7.2 %copy-start.6 = (bf16[2,256,256]{2,1,0:T(8,128)(2,1)S(1)}, bf16[2,256,256]{2,1,0:T(8,128)(2,1)}, u32[]{:S(2)}) copy-start(bf16[2,256,256]{2,1,0:T(8,128)(2,1)} %own_ref.1) | copy-start | bytes 786436
  1.9 39.1 %collective-permute-start.7 = (bf16[4,256,256]{2,1,0:T(8,128)(2,1)S(1)}, bf16[4,256,256]{2,1,0:T(8,128)(2,1)S(1)}, u32[]{:S(2)}, u32[]{:S(2)}) collective-permute-start(bf16[4,256,256]{2,1,0:T(8,128)(2,1)S(1)} %pad_maximum_fusion.3), channel_id=1, source_target_pairs={{0,24},{8,16},{16,8},{24,0},{1,25},{9,17},{17,9},{25,1},{2,26},{10... | collective-permute-start | bytes 1572872 | tf_op jit(solution)/shard_map/ppermute | solution.py:290
  5.8 35.1 %collective-permute-start.6 = (bf16[4,256,256]{2,1,0:T(8,128)(2,1)S(1)}, bf16[4,256,256]{2,1,0:T(8,128)(2,1)}, u32[]{:S(2)}, u32[]{:S(2)}) collective-permute-start(bf16[4,256,256]{2,1,0:T(8,128)(2,1)S(1)} %pad_maximum_fusion.3), channel_id=1, source_target_pairs={{0,16},{8,24},{16,0},{24,8},{1,17},{9,25},{17,1},{25,9},{2,18},{10... | collective-permute-start | bytes 1572872 | tf_op jit(solution)/shard_map/ppermute | solution.py:290
  8.7 5.2 %copy-start.7 = (s32[8]{0:T(128)S(1)}, s32[8]{0:T(128)}, u32[]{:S(2)}) copy-start(s32[8]{0:T(128)} %get-tuple-element.47) | copy-start | bytes 100
  9.6 18.5 %collective-permute-start.1 = (bf16[2,256,256]{2,1,0:T(8,128)(2,1)}, bf16[2,256,256]{2,1,0:T(8,128)(2,1)S(1)}, u32[]{:S(2)}, u32[]{:S(2)}) collective-permute-start(bf16[2,256,256]{2,1,0:T(8,128)(2,1)} %get-tuple-element.26), channel_id=1, source_target_pairs={{0,2},{1,3},{2,0},{3,1},{4,6},{5,7},{6,4},{7,5},{8,10},{9,11},{10,... | collective-permute-start | bytes 786440 | tf_op jit(solution)/shard_map/ppermute | solution.py:87
  11.2 17.4 %collective-permute-start.3 = (bf16[2,256,256]{2,1,0:T(8,128)(2,1)}, bf16[2,256,256]{2,1,0:T(8,128)(2,1)S(1)}, u32[]{:S(2)}, u32[]{:S(2)}) collective-permute-start(bf16[2,256,256]{2,1,0:T(8,128)(2,1)} %get-tuple-element.27), channel_id=1, source_target_pairs={{0,6},{1,7},{2,4},{3,5},{4,2},{5,3},{6,0},{7,1},{8,14},{9,15},{10,... | collective-permute-start | bytes 786440 | tf_op jit(solution)/shard_map/ppermute | solution.py:87
  13.7 22.6 %collective-permute-start.2 = (bf16[2,256,256]{2,1,0:T(8,128)(2,1)S(1)}, bf16[2,256,256]{2,1,0:T(8,128)(2,1)S(1)}, u32[]{:S(2)}, u32[]{:S(2)}) collective-permute-start(bf16[2,256,256]{2,1,0:T(8,128)(2,1)S(1)} %get-tuple-element.28), channel_id=1, source_target_pairs={{0,4},{1,5},{2,6},{3,7},{4,0},{5,1},{6,2},{7,3},{8,12},{9,13},{10,... | collective-permute-start | bytes 786440 | tf_op jit(solution)/shard_map/ppermute | solution.py:87
  16.6 2.6 %copy-start.3 = (bf16[4,256,256]{2,1,0:T(8,128)(2,1)S(1)}, bf16[4,256,256]{2,1,0:T(8,128)(2,1)}, u32[]{:S(2)}) copy-start(bf16[4,256,256]{2,1,0:T(8,128)(2,1)} %param.17) | copy-start | bytes 1572868
  16.6 2.6 %copy-start.4 = (bf16[4,256,256]{2,1,0:T(8,128)(2,1)S(1)}, bf16[4,256,256]{2,1,0:T(8,128)(2,1)}, u32[]{:S(2)}) copy-start(bf16[4,256,256]{2,1,0:T(8,128)(2,1)} %param.16) | copy-start | bytes 1572868
  22.1 2.4 %copy-start.8 = (s32[16]{0:T(128)S(1)}, s32[16]{0:T(128)}, u32[]{:S(2)}) copy-start(s32[16]{0:T(128)} %param.14) | copy-start | bytes 196
  22.1 3.2 %copy-start.2 = (f32[32]{0:T(128)S(1)}, f32[32]{0:T(128)}, u32[]{:S(2)}) copy-start(f32[32]{0:T(128)} %param.15) | copy-start | bytes 388
  28.1 12.9 %collective-permute-start.5 = (bf16[4,256,256]{2,1,0:T(8,128)(2,1)S(1)}, bf16[4,256,256]{2,1,0:T(8,128)(2,1)}, u32[]{:S(2)}, u32[]{:S(2)}) collective-permute-start(bf16[4,256,256]{2,1,0:T(8,128)(2,1)S(1)} %pad_maximum_fusion.3), channel_id=1, source_target_pairs={{0,8},{8,0},{16,24},{24,16},{1,9},{9,1},{17,25},{25,17},{2,10},{10... | collective-permute-start | bytes 1572872 | tf_op jit(solution)/shard_map/ppermute | solution.py:290
  28.6 14.5 %collective-permute-start = (bf16[2,256,256]{2,1,0:T(8,128)(2,1)S(1)}, bf16[2,256,256]{2,1,0:T(8,128)(2,1)}, u32[]{:S(2)}, u32[]{:S(2)}) collective-permute-start(bf16[2,256,256]{2,1,0:T(8,128)(2,1)S(1)} %get-tuple-element.29), channel_id=1, source_target_pairs={{0,1},{1,0},{2,3},{3,2},{4,5},{5,4},{6,7},{7,6},{8,9},{9,8},{10,11... | collective-permute-start | bytes 786440 | tf_op jit(solution)/shard_map/ppermute | solution.py:84
  37.9 5.2 %collective-permute-start.4 = (bf16[4,256,256]{2,1,0:T(8,128)(2,1)S(1)}, bf16[4,256,256]{2,1,0:T(8,128)(2,1)}, u32[]{:S(2)}, u32[]{:S(2)}) collective-permute-start(bf16[4,256,256]{2,1,0:T(8,128)(2,1)S(1)} %broadcast_select_fusion.1), channel_id=1, source_target_pairs={{0,1},{1,0},{2,3},{3,2},{4,5},{5,4},{6,7},{7,6},{8,9},{9,8},{10,11... | collective-permute-start | bytes 1572872 | tf_op jit(solution)/shard_map/ppermute | solution.py:105
  40.9 1.6 %copy-start.5 = (bf16[4,256,256]{2,1,0:T(8,128)(2,1)}, bf16[4,256,256]{2,1,0:T(8,128)(2,1)S(1)}, u32[]{:S(2)}) copy-start(bf16[4,256,256]{2,1,0:T(8,128)(2,1)S(1)} %collective-permute-done.7.refs_6_) | copy-start | bytes 1572868
  42.5 17.8 %collective-permute-start.8 = (bf16[12,256,256]{2,1,0:T(8,128)(2,1)S(1)}, bf16[12,256,256]{2,1,0:T(8,128)(2,1)}, u32[]{:S(2)}, u32[]{:S(2)}) collective-permute-start(bf16[12,256,256]{2,1,0:T(8,128)(2,1)S(1)} %pad_maximum_fusion), channel_id=1, source_target_pairs={{0,1},{1,0},{2,3},{3,2},{4,5},{5,4},{6,7},{7,6},{8,9},{9,8},{10,11... | collective-permute-start | bytes 4718600 | tf_op jit(solution)/shard_map/ppermute | solution.py:297

commit v18 on v16

--- a/solution.py
+++ b/solution.py
@@ -81,15 +81,16 @@
     outgoing = jnp.take(padded, my_sel.reshape(-1), axis=0).reshape(chips, 2, extent, extent)
     partner = my_index ^ 1
     my_chip = my_index // 2
-    direct = lax.ppermute(outgoing[0], "patch", xor_pairs(sources, 1))
     received = []
     for m in range(1, chips):
         received.append(lax.ppermute(outgoing[m], "patch", xor_pairs(sources, 2 * m)))
     received = jnp.concatenate(received, axis=0)
-    forwarded = lax.ppermute(received, "patch", xor_pairs(sources, 1))
+    forwarded = lax.ppermute(jnp.concatenate([outgoing[0], received], axis=0), "patch",
+                             xor_pairs(sources, 1))
     cand_pid = [my_index * number + jnp.arange(number, dtype=jnp.int32)]
-    cand_pid.append(lax.dynamic_index_in_dim(send_pid, partner, 0, keepdims=False)[0])
-    for core in (my_index % 2, partner % 2):
+    for which, core in enumerate((my_index % 2, partner % 2)):
+        if which == 1:
+            cand_pid.append(lax.dynamic_index_in_dim(send_pid, partner, 0, keepdims=False)[0])
         for m in range(1, chips):
             source = (my_chip ^ m) * 2 + core
             cand_pid.append(lax.dynamic_index_in_dim(send_pid, source, 0, keepdims=False)[m])
@@ -106,28 +107,27 @@
     found = cand_pid[None, :] == slot_pid[:, None]
     take_idx = jnp.sum(jnp.where(found, cand_ids[None, :], 0), axis=1)
     take_idx = jnp.where(present, take_idx, cand_pid.shape[0])
-    pieces = (patches, direct, received, forwarded)
+    pieces = (patches, received, forwarded)
     return take_idx, pieces, jnp.where(present, slot_pid, sources * number), outgoing
 
 
-def spectra_kernel(rows, take_ref, own_ref, direct_ref, recv_ref, fwd_ref, scale_ref, half_ref,
-                   full_ref, re_ref, im_ref):
-    number = own_ref.shape[0]
-    extent = own_ref.shape[-1]
+def spectra_kernel(count_pieces, take_ref, *refs):
+    piece_refs = refs[:count_pieces]
+    scale_ref, half_ref, full_ref, re_ref, im_ref = refs[count_pieces:]
+    extent = piece_refs[0].shape[-1]
     half_table = half_ref[...]
     full_table = full_ref[...]
     for s in range(re_ref.shape[0]):
         idx = take_ref[s]
-        pick_own = own_ref[jnp.clip(idx, 0, number - 1)]
-        pick_direct = direct_ref[jnp.clip(idx - number, 0, number - 1)]
-        pick_recv = recv_ref[jnp.clip(idx - 2 * number, 0, rows - 1)]
-        pick_fwd = fwd_ref[jnp.clip(idx - 2 * number - rows, 0, rows - 1)]
-        zero = jnp.zeros_like(pick_own)
-        image = jnp.where(
-            idx < number, pick_own,
-            jnp.where(idx < 2 * number, pick_direct,
-                      jnp.where(idx < 2 * number + rows, pick_recv,
-                                jnp.where(idx < 2 * number + 2 * rows, pick_fwd, zero))))
+        image = jnp.zeros((extent, extent), piece_refs[0].dtype)
+        base = 0
+        bounds = []
+        for piece in piece_refs:
+            bounds.append((piece, base, piece.shape[0]))
+            base += piece.shape[0]
+        for piece, start, size in reversed(bounds):
+            picked = piece[jnp.clip(idx - start, 0, size - 1)]
+            image = jnp.where((idx >= start) & (idx < start + size), picked, image)
         half = jnp.dot(image, half_table, preferred_element_type=jnp.float32).astype(jnp.bfloat16)
         half_stack = jnp.concatenate([half[:, :extent], half[:, extent:]], axis=0)
         spec = jnp.dot(full_table, half_stack, preferred_element_type=jnp.float32)
@@ -136,20 +136,19 @@
         im_ref[s] = (spec[extent:] * scale).astype(jnp.bfloat16)
 
 
-def make_spectra(take_idx, own, direct, received, forwarded, scale, half_table, full_table):
+def make_spectra(take_idx, pieces, scale, half_table, full_table):
     count, extent = (scale.shape[0], scale.shape[-1])
-    rows = received.shape[0]
     whole = pl.BlockSpec(memory_space=pltpu.VMEM)
     spec_shape = jax.ShapeDtypeStruct((count, extent, extent), jnp.bfloat16)
     return pl.pallas_call(
-        functools.partial(spectra_kernel, rows),
-        in_specs=[pl.BlockSpec(memory_space=pltpu.SMEM)] + [whole] * 7,
+        functools.partial(spectra_kernel, len(pieces)),
+        in_specs=[pl.BlockSpec(memory_space=pltpu.SMEM)] + [whole] * (len(pieces) + 3),
         out_specs=[whole, whole],
         out_shape=[spec_shape, spec_shape],
         cost_estimate=pl.CostEstimate(
             flops=3 * count * 6 * extent * extent * extent, transcendentals=0,
             bytes_accessed=count * 10 * extent * extent),
-    )(take_idx, own, direct, received, forwarded, scale, half_table, full_table)
+    )(take_idx, *pieces, scale, half_table, full_table)
 
 
 def corr_kernel(first, last, counts, orient_total, *refs):
@@ -303,7 +302,7 @@
     groups = jnp.take(jnp.concatenate([group_of_patch, jnp.zeros((1,), jnp.int32)]), slot_row)
     focus_values = jnp.take(defocus, groups)
     scale = ctf_scale(focus_values, extent)
-    spec_re, spec_im = make_spectra(take_idx, *pieces, scale, half_table, forward)
+    spec_re, spec_im = make_spectra(take_idx, pieces, scale, half_table, forward)
     return correlate_all(spec_re, spec_im, templ_re, templ_im, orientation, forward, inverse)
 
 

time: 69.3 us -> 69.2 us (level)
  local copies, waits for them, and re-layouts: 10.7 us -> 5.85 us
  other arithmetic: 5.78 us -> 9.03 us
  waiting for transfers between devices: 13.1 us -> 14.4 us
    unnamed x22 -> x14, local copies, waits for them, and re-layouts: 3.39 us -> 0.05 us
    concatenate x1, other arithmetic: 0.17 us -> 1.53 us  [correlate_all(): jnp.concatenate(late_got, axis=0)]
    ppermute x3, waiting for transfers between devices: 12.5 us -> 13.9 us  [route_patches(): lax.ppermute(outgoing[m], 'patch', xor_pairs(sources, 2 * m))]
    concatenate x0 -> x2, other arithmetic: none -> 1.1 us  [the longest x1 0.97 us: route_patches(): received = jnp.concatenate(received, axis=0)]
    slice x1, local copies, waits for them, and re-layouts: 0.9 us -> 0.07 us  [route_patches(): outgoing[0]]
    concatenate x1, other arithmetic: 0.05 us -> 0.84 us  [correlate_all(): jnp.concatenate([lax.dynamic_slice_in_dim(templ_re, core * half, half, 0)...]
    concatenate x1 -> x0, local copies, waits for them, and re-layouts: 0.72 us -> none  [route_patches(): received = jnp.concatenate(received, axis=0)]
    ppermute x2 -> x1, starting transfers between devices: 2.16 us -> 2.23 us  [route_patches(): lax.ppermute(jnp.concatenate([outgoing[0], received], axis=0), 'patch', x...]
  transfers between devices with their start and end apart: 9 -> 8, of which waited for: 3 -> 3; matrix products, arithmetic and copies ran while one was open for 22% -> 19% of each run, Pallas kernels for 25% -> 25%
where the time goes in v18:
time: 69.2 us; the launch traced here: 69 us
  Pallas kernels  27 us (39%)
  waiting for transfers between devices  14.4 us (21%)
  starting transfers between devices  11.7 us (17%)
  other arithmetic  9.03 us (13%)
  local copies, waits for them, and re-layouts  5.85 us (8%)
  between operations  0.96 us (1%)
    pallas_call x2, Pallas kernels, correlate_chunk(): pl.pallas_call(functools.partial(corr_kernel, first, last, counts, orient...  22.9 us
    ppermute x3, waiting for transfers between devices, route_patches(): lax.ppermute(outgoing[m], 'patch', xor_pairs(sources, 2 * m))  13.9 us
    pallas_call x1, Pallas kernels, make_spectra(): pl.pallas_call(functools.partial(spectra_kernel, len(pieces)), in_specs=[...  4.16 us
    ppermute x3, starting transfers between devices, route_patches(): lax.ppermute(outgoing[m], 'patch', xor_pairs(sources, 2 * m))  3.56 us
    ppermute x1, starting transfers between devices, correlate_all(): lax.ppermute(jnp.concatenate(late_got, axis=0), 'patch', xor_pairs(source...  3.3 us
    ppermute x3, starting transfers between devices, correlate_all(): got = lax.ppermute(mine, 'blk', [(b, b ^ k) for b in range(blocks)])  2.65 us
    ppermute x1, starting transfers between devices, route_patches(): lax.ppermute(jnp.concatenate([outgoing[0], received], axis=0), 'patch', x...  2.23 us
    concatenate x1, other arithmetic, correlate_all(): jnp.concatenate(late_got, axis=0)  1.53 us
  transfers between devices with their start and end apart: 8, of which 3 were waited for; matrix products, arithmetic and copies ran while one was open for 19% of the time, Pallas kernels for 25%

profile of v18, /device:TPU:9, one launch (start us, length us, event | category | flops | bytes accessed | tf_op | source)
XLA Modules:
  0.0 69.0 jit_solution(5357703710514351479)
XLA Ops:
  0.7 1.1 %constant_dynamic-slice_fusion = (bf16[2,256,256]{2,1,0:T(8,128)(2,1)S(1)}, bf16[2,256,256]{2,1,0:T(8,128)(2,1)S(1)}) fusion(bf16[4,256,256]{2,1,0:T(8,128)(2,1)} %param.15, s32[]{:T(128)S(6)} %select_n.312, bf16[4,256,256]{2,1,0:T(8,128)(2,1)} %param.14), kind=kLoop, calls=%fused_computation.46 | loop fusion | bytes 1048580 | tf_op jit(solution)/shard_map/dynamic_slice | solution.py:267
  1.8 0.8 %pad_maximum_fusion.4 = bf16[4,256,256]{2,1,0:T(8,128)(2,1)} fusion(bf16[2,256,256]{2,1,0:T(8,128)(2,1)S(1)} %get-tuple-element.51, bf16[2,256,256]{2,1,0:T(8,128)(2,1)S(1)} %get-tuple-element.52), kind=kLoop, calls=%fused_computation.11 | loop fusion | flops 262144 | bytes 1048576 | tf_op jit(solution)/shard_map/concatenate | solution.py:265
  2.6 2.2 %collective-permute-start.6 = (bf16[4,256,256]{2,1,0:T(8,128)(2,1)}, bf16[4,256,256]{2,1,0:T(8,128)(2,1)}, u32[]{:S(2)}, u32[]{:S(2)}) collective-permute-start(bf16[4,256,256]{2,1,0:T(8,128)(2,1)} %pad_maximum_fusion.4), channel_id=1, source_target_pairs={{0,24},{8,16},{16,8},{24,0},{1,25},{9,17},{17,9},{25,1},{2,26},{10... | collective-permute-start | bytes 1572872 | tf_op jit(solution)/shard_map/ppermute | solution.py:274
  4.8 0.2 collective-permute-start.5
  5.2 0.1 copy.34
  5.3 0.1 copy.36
  5.4 0.1 copy.37
  5.5 0.1 copy.35
  5.7 0.1 fusion.2
  5.8 0.1 copy.38
  5.9 0.1 reshape.722
  6.0 0.1 reshape.721
  6.1 0.6 gather_fusion.1
  6.8 0.2 broadcast_select_fusion
  7.0 1.4 %collective-permute-start.2 = (bf16[2,256,256]{2,1,0:T(8,128)(2,1)S(1)}, bf16[2,256,256]{2,1,0:T(8,128)(2,1)S(1)}, u32[]{:S(2)}, u32[]{:S(2)}) collective-permute-start(bf16[2,256,256]{2,1,0:T(8,128)(2,1)S(1)} %get-tuple-element.28), channel_id=1, source_target_pairs={{0,6},{1,7},{2,4},{3,5},{4,2},{5,3},{6,0},{7,1},{8,14},{9,15},{10,... | collective-permute-start | bytes 786440 | tf_op jit(solution)/shard_map/ppermute | solution.py:86
  8.4 1.1 %collective-permute-start.1 = (bf16[2,256,256]{2,1,0:T(8,128)(2,1)S(1)}, bf16[2,256,256]{2,1,0:T(8,128)(2,1)S(1)}, u32[]{:S(2)}, u32[]{:S(2)}) collective-permute-start(bf16[2,256,256]{2,1,0:T(8,128)(2,1)S(1)} %get-tuple-element.29), channel_id=1, source_target_pairs={{0,4},{1,5},{2,6},{3,7},{4,0},{5,1},{6,2},{7,3},{8,12},{9,13},{10,... | collective-permute-start | bytes 786440 | tf_op jit(solution)/shard_map/ppermute | solution.py:86
  9.5 1.1 %collective-permute-start = (bf16[2,256,256]{2,1,0:T(8,128)(2,1)S(1)}, bf16[2,256,256]{2,1,0:T(8,128)(2,1)S(1)}, u32[]{:S(2)}, u32[]{:S(2)}) collective-permute-start(bf16[2,256,256]{2,1,0:T(8,128)(2,1)S(1)} %get-tuple-element.30), channel_id=1, source_target_pairs={{0,2},{1,3},{2,0},{3,1},{4,6},{5,7},{6,4},{7,5},{8,10},{9,11},{10,... | collective-permute-start | bytes 786440 | tf_op jit(solution)/shard_map/ppermute | solution.py:86
  10.7 0.1 copy.33
  10.8 0.1 reduce
  10.9 0.1 select_reduce_fusion.1
  11.0 0.1 fusion.6
  11.2 0.1 fusion.17
  11.3 0.1 fusion.20
  11.4 0.4 fusion.13
  11.8 0.1 concatenate.96
  11.9 0.2 select_reduce_fusion
  12.1 0.5 broadcast_select_fusion.2.take_ref
  12.7 0.6 gather_fusion.2
  13.4 0.6 gather_fusion.3
  14.1 0.6 gather_fusion
  14.7 0.6 and_select_fusion.6.refs_0_
  15.3 0.1 fusion.1
  15.5 10.3 %collective-permute-done.2 = bf16[2,256,256]{2,1,0:T(8,128)(2,1)S(1)} collective-permute-done((bf16[2,256,256]{2,1,0:T(8,128)(2,1)S(1)}, bf16[2,256,256]{2,1,0:T(8,128)(2,1)S(1)}, u32[]{:S(2)}, u32[]{:S(2)}) %collective-permute-start.2) | collective-permute-done | bytes 262176 | tf_op jit(solution)/shard_map/ppermute | solution.py:86
  25.7 0.3 collective-permute-start.4
  26.0 3.6 %collective-permute-done.1 = bf16[2,256,256]{2,1,0:T(8,128)(2,1)S(1)} collective-permute-done((bf16[2,256,256]{2,1,0:T(8,128)(2,1)S(1)}, bf16[2,256,256]{2,1,0:T(8,128)(2,1)S(1)}, u32[]{:S(2)}, u32[]{:S(2)}) %collective-permute-start.1) | collective-permute-done | bytes 262176 | tf_op jit(solution)/shard_map/ppermute | solution.py:86
  29.6 0.1 pad_maximum_fusion.1
  29.7 2.2 %collective-permute-start.3 = (bf16[8,256,256]{2,1,0:T(8,128)(2,1)S(1)}, bf16[8,256,256]{2,1,0:T(8,128)(2,1)}, u32[]{:S(2)}, u32[]{:S(2)}) collective-permute-start(bf16[8,256,256]{2,1,0:T(8,128)(2,1)S(1)} %pad_maximum_fusion.1), channel_id=1, source_target_pairs={{0,1},{1,0},{2,3},{3,2},{4,5},{5,4},{6,7},{7,6},{8,9},{9,8},{10,11... | collective-permute-start | bytes 3145736 | tf_op jit(solution)/shard_map/ppermute | solution.py:88
  32.0 0.7 gather_fusion.4
  32.6 0.6 and_select_fusion.refs_0_
  33.3 1.1 %pad_maximum_fusion.2.refs_3_ = bf16[8,256,256]{2,1,0:T(8,128)(2,1)} fusion(bf16[4,256,256]{2,1,0:T(8,128)(2,1)S(1)} %copy-done.2, bf16[4,256,256]{2,1,0:T(8,128)(2,1)S(1)} %copy-done.3), kind=kLoop, calls=%fused_computation.7 | loop fusion | flops 524288 | bytes 2097152 | tf_op jit(solution)/shard_map/concatenate | solution.py:264
  34.3 1.3 %negate_multiply_fusion.refs_3_ = f32[4,256,256]{2,1,0:T(8,128)} fusion(f32[4,256]{1,0:T(4,128)S(1)} %get-tuple-element.36, f32[4,256]{1,0:T(4,128)S(1)} %get-tuple-element.38, f32[4,256]{1,0:T(4,128)S(1)} %get-tuple-element.37, f32[4,256]{1,0:T(4,128)S(1)} %get-tuple-element.35), kind=kLoop, calls=%fused_computation.8 | loop fusion | flops 1310720 | bytes 1064960 | tf_op jit(solution)/shard_map/div | solution.py:57
  35.6 1.0 %pad_maximum_fusion.3.refs_1_ = bf16[6,256,256]{2,1,0:T(8,128)(2,1)} fusion(bf16[2,256,256]{2,1,0:T(8,128)(2,1)S(1)} %collective-permute-done.2, bf16[2,256,256]{2,1,0:T(8,128)(2,1)S(1)} %collective-permute-done.1, bf16[2,256,256]{2,1,0:T(8,128)(2,1)S(1)} %collective-permute-done), kind=kLoop, calls=%fused_computation.10 | loop fusion | flops 786432 | bytes 1572864 | tf_op jit(solution)/shard_map/concatenate | solution.py:87
  36.6 0.6 collective-permute-done.4.refs_4_
  37.2 1.5 %pad_maximum_fusion = bf16[12,256,256]{2,1,0:T(8,128)(2,1)S(1)} fusion(bf16[4,256,256]{2,1,0:T(8,128)(2,1)} %collective-permute-done.6.refs_6_, bf16[4,256,256]{2,1,0:T(8,128)(2,1)} %collective-permute-done.5.refs_5_, bf16[4,256,256]{2,1,0:T(8,128)(2,1)} %collective-permute-done.4.refs_4_), kind=kLoop, calls=%fused_computation.5 | loop fusion | flops 1572864 | bytes 3145728 | tf_op jit(solution)/shard_map/concatenate | solution.py:281
  38.7 3.3 %collective-permute-start.7 = (bf16[12,256,256]{2,1,0:T(8,128)(2,1)S(1)}, bf16[12,256,256]{2,1,0:T(8,128)(2,1)}, u32[]{:S(2)}, u32[]{:S(2)}) collective-permute-start(bf16[12,256,256]{2,1,0:T(8,128)(2,1)S(1)} %pad_maximum_fusion), channel_id=1, source_target_pairs={{0,1},{1,0},{2,3},{3,2},{4,5},{5,4},{6,7},{7,6},{8,9},{9,8},{10,11... | collective-permute-start | bytes 4718600 | tf_op jit(solution)/shard_map/ppermute | solution.py:281
  42.0 4.2 %shard_map.129 = (bf16[4,256,256]{2,1,0:T(8,128)(2,1)}, bf16[4,256,256]{2,1,0:T(8,128)(2,1)}) custom-call(s32[4]{0:T(128)} %broadcast_select_fusion.2.take_ref, bf16[2,256,256]{2,1,0:T(8,128)(2,1)} %refs_0_.1, bf16[6,256,256]{2,1,0:T(8,128)(2,1)} %pad_maximum_fusion.3.refs_1_, bf16[8,256,256]{2,1,0:T(8,128)(2,1)} %collective-permute-done.3.refs_2_, ...), custom_call_target="tpu_custom_call" | custom-call | flops 1207959552 | bytes 2621440 | tf_op jit(solution)/shard_map/pallas_call | solution.py:143
  46.2 13.2 %shard_map.130 = (f32[4,256,256]{2,1,0:T(8,128)}, f32[4,256,256]{2,1,0:T(8,128)}, f32[4,256,256]{2,1,0:T(8,128)}, f32[4,8,128]{2,1,0:T(8,128)}) custom-call(s32[10]{0:T(128)} %and_select_fusion.refs_0_, bf16[4,256,256]{2,1,0:T(8,128)(2,1)} %get-tuple-element.12.refs_1_, bf16[4,256,256]{2,1,0:T(8,128)(2,1)} %get-tuple-element.13.refs_2_, ...), custom_call_target="tpu_custom_call" | custom-call | flops 24159191040 | bytes 15728640 | tf_op jit(solution)/shard_map/pallas_call | solution.py:239
  59.3 9.7 %shard_map.131 = (f32[4,256,256]{2,1,0:T(8,128)}, f32[4,256,256]{2,1,0:T(8,128)}, f32[4,256,256]{2,1,0:T(8,128)}, f32[4,16]{1,0:T(4,128)}) custom-call(s32[6]{0:T(128)} %and_select_fusion.6.refs_0_, bf16[4,256,256]{2,1,0:T(8,128)(2,1)} %get-tuple-element.12.refs_1_, ...), custom_call_target="tpu_custom_call", output_to_operand_aliasing={{0}: (6, {}), {1}: (7, {}), {2}: (8, {})} | custom-call | flops 14495514624 | bytes 13631488 | tf_op jit(solution)/shard_map/pallas_call | solution.py:239
  (55 shorter events, 0.6 us)
Async XLA Ops:
  0.6 13.4 %copy-start = (s32[16]{0:T(128)S(1)}, s32[16]{0:T(128)}, u32[]{:S(2)}) copy-start(s32[16]{0:T(128)} %param.16) | copy-start | bytes 196
  0.6 4.4 %copy-start.5 = (s32[16]{0:T(128)S(1)}, s32[16]{0:T(128)}, u32[]{:S(2)}) copy-start(s32[16]{0:T(128)} %param.11) | copy-start | bytes 196
  0.7 5.4 %copy-start.4 = (bf16[2,256,256]{2,1,0:T(8,128)(2,1)S(1)}, bf16[2,256,256]{2,1,0:T(8,128)(2,1)}, u32[]{:S(2)}) copy-start(bf16[2,256,256]{2,1,0:T(8,128)(2,1)} %refs_0_.1) | copy-start | bytes 786436
  2.6 34.0 %collective-permute-start.6 = (bf16[4,256,256]{2,1,0:T(8,128)(2,1)}, bf16[4,256,256]{2,1,0:T(8,128)(2,1)}, u32[]{:S(2)}, u32[]{:S(2)}) collective-permute-start(bf16[4,256,256]{2,1,0:T(8,128)(2,1)} %pad_maximum_fusion.4), channel_id=1, source_target_pairs={{0,24},{8,16},{16,8},{24,0},{1,25},{9,17},{17,9},{25,1},{2,26},{10... | collective-permute-start | bytes 1572872 | tf_op jit(solution)/shard_map/ppermute | solution.py:274
  4.8 31.8 %collective-permute-start.5 = (bf16[4,256,256]{2,1,0:T(8,128)(2,1)}, bf16[4,256,256]{2,1,0:T(8,128)(2,1)}, u32[]{:S(2)}, u32[]{:S(2)}) collective-permute-start(bf16[4,256,256]{2,1,0:T(8,128)(2,1)} %pad_maximum_fusion.4), channel_id=1, source_target_pairs={{0,16},{8,24},{16,0},{24,8},{1,17},{9,25},{17,1},{25,9},{2,18},{10... | collective-permute-start | bytes 1572872 | tf_op jit(solution)/shard_map/ppermute | solution.py:274
  6.9 5.7 %copy-start.6 = (s32[16]{0:T(128)S(1)}, s32[16]{0:T(128)}, u32[]{:S(2)}) copy-start(s32[16]{0:T(128)} %param.12) | copy-start | bytes 196
  6.9 6.4 %copy-start.1 = (f32[32]{0:T(128)S(1)}, f32[32]{0:T(128)}, u32[]{:S(2)}) copy-start(f32[32]{0:T(128)} %param.13) | copy-start | bytes 388
  7.0 18.7 %collective-permute-start.2 = (bf16[2,256,256]{2,1,0:T(8,128)(2,1)S(1)}, bf16[2,256,256]{2,1,0:T(8,128)(2,1)S(1)}, u32[]{:S(2)}, u32[]{:S(2)}) collective-permute-start(bf16[2,256,256]{2,1,0:T(8,128)(2,1)S(1)} %get-tuple-element.28), channel_id=1, source_target_pairs={{0,6},{1,7},{2,4},{3,5},{4,2},{5,3},{6,0},{7,1},{8,14},{9,15},{10,... | collective-permute-start | bytes 786440 | tf_op jit(solution)/shard_map/ppermute | solution.py:86
  8.4 21.2 %collective-permute-start.1 = (bf16[2,256,256]{2,1,0:T(8,128)(2,1)S(1)}, bf16[2,256,256]{2,1,0:T(8,128)(2,1)S(1)}, u32[]{:S(2)}, u32[]{:S(2)}) collective-permute-start(bf16[2,256,256]{2,1,0:T(8,128)(2,1)S(1)} %get-tuple-element.29), channel_id=1, source_target_pairs={{0,4},{1,5},{2,6},{3,7},{4,0},{5,1},{6,2},{7,3},{8,12},{9,13},{10,... | collective-permute-start | bytes 786440 | tf_op jit(solution)/shard_map/ppermute | solution.py:86
  9.5 20.1 %collective-permute-start = (bf16[2,256,256]{2,1,0:T(8,128)(2,1)S(1)}, bf16[2,256,256]{2,1,0:T(8,128)(2,1)S(1)}, u32[]{:S(2)}, u32[]{:S(2)}) collective-permute-start(bf16[2,256,256]{2,1,0:T(8,128)(2,1)S(1)} %get-tuple-element.30), channel_id=1, source_target_pairs={{0,2},{1,3},{2,0},{3,1},{4,6},{5,7},{6,4},{7,5},{8,10},{9,11},{10,... | collective-permute-start | bytes 786440 | tf_op jit(solution)/shard_map/ppermute | solution.py:86
  14.1 19.2 %copy-start.2 = (bf16[4,256,256]{2,1,0:T(8,128)(2,1)S(1)}, bf16[4,256,256]{2,1,0:T(8,128)(2,1)}, u32[]{:S(2)}) copy-start(bf16[4,256,256]{2,1,0:T(8,128)(2,1)} %param.15) | copy-start | bytes 1572868
  14.1 19.2 %copy-start.3 = (bf16[4,256,256]{2,1,0:T(8,128)(2,1)S(1)}, bf16[4,256,256]{2,1,0:T(8,128)(2,1)}, u32[]{:S(2)}) copy-start(bf16[4,256,256]{2,1,0:T(8,128)(2,1)} %param.14) | copy-start | bytes 1572868
  25.7 11.4 %collective-permute-start.4 = (bf16[4,256,256]{2,1,0:T(8,128)(2,1)}, bf16[4,256,256]{2,1,0:T(8,128)(2,1)}, u32[]{:S(2)}, u32[]{:S(2)}) collective-permute-start(bf16[4,256,256]{2,1,0:T(8,128)(2,1)} %pad_maximum_fusion.4), channel_id=1, source_target_pairs={{0,8},{8,0},{16,24},{24,16},{1,9},{9,1},{17,25},{25,17},{2,10},{10... | collective-permute-start | bytes 1572872 | tf_op jit(solution)/shard_map/ppermute | solution.py:274
  29.7 12.3 %collective-permute-start.3 = (bf16[8,256,256]{2,1,0:T(8,128)(2,1)S(1)}, bf16[8,256,256]{2,1,0:T(8,128)(2,1)}, u32[]{:S(2)}, u32[]{:S(2)}) collective-permute-start(bf16[8,256,256]{2,1,0:T(8,128)(2,1)S(1)} %pad_maximum_fusion.1), channel_id=1, source_target_pairs={{0,1},{1,0},{2,3},{3,2},{4,5},{5,4},{6,7},{7,6},{8,9},{9,8},{10,11... | collective-permute-start | bytes 3145736 | tf_op jit(solution)/shard_map/ppermute | solution.py:88
  38.7 20.6 %collective-permute-start.7 = (bf16[12,256,256]{2,1,0:T(8,128)(2,1)S(1)}, bf16[12,256,256]{2,1,0:T(8,128)(2,1)}, u32[]{:S(2)}, u32[]{:S(2)}) collective-permute-start(bf16[12,256,256]{2,1,0:T(8,128)(2,1)S(1)} %pad_maximum_fusion), channel_id=1, source_target_pairs={{0,1},{1,0},{2,3},{3,2},{4,5},{5,4},{6,7},{7,6},{8,9},{9,8},{10,11... | collective-permute-start | bytes 4718600 | tf_op jit(solution)/shard_map/ppermute | solution.py:281

commit v19 on v18

--- a/solution.py
+++ b/solution.py
@@ -61,7 +61,7 @@
     return [(d, d ^ shift) for d in range(count)]
 
 
-def route_patches(patches, row_owner, my_index):
+def route_patches(patches, row_owner, my_index, tied):
     sources, number = row_owner.shape
     extent = patches.shape[-1]
     chips = sources // 2
@@ -79,6 +79,7 @@
     padded = jnp.concatenate([patches, jnp.zeros((1, extent, extent), patches.dtype)], axis=0)
     my_sel = lax.dynamic_index_in_dim(send_sel, my_index, 0, keepdims=False)
     outgoing = jnp.take(padded, my_sel.reshape(-1), axis=0).reshape(chips, 2, extent, extent)
+    outgoing, tied = lax.optimization_barrier((outgoing, tied))
     partner = my_index ^ 1
     my_chip = my_index // 2
     received = []
@@ -108,7 +109,7 @@
     take_idx = jnp.sum(jnp.where(found, cand_ids[None, :], 0), axis=1)
     take_idx = jnp.where(present, take_idx, cand_pid.shape[0])
     pieces = (patches, received, forwarded)
-    return take_idx, pieces, jnp.where(present, slot_pid, sources * number), outgoing
+    return take_idx, pieces, jnp.where(present, slot_pid, sources * number), tied
 
 
 def spectra_kernel(count_pieces, take_ref, *refs):
@@ -297,8 +298,8 @@
     number, extent = (patches.shape[0], patches.shape[1])
     forward, half_table, inverse = (jnp.asarray(table) for table in dft_tables(extent))
     row_owner = owner_of_patch.reshape(sources, number)
-    take_idx, pieces, slot_row, outgoing = route_patches(patches, row_owner, my_index)
-    templ_re, templ_im, unused = lax.optimization_barrier((templ_re, templ_im, outgoing))
+    take_idx, pieces, slot_row, (templ_re, templ_im) = route_patches(
+        patches, row_owner, my_index, (templ_re, templ_im))
     groups = jnp.take(jnp.concatenate([group_of_patch, jnp.zeros((1,), jnp.int32)]), slot_row)
     focus_values = jnp.take(defocus, groups)
     scale = ctf_scale(focus_values, extent)

time: 69.2 us -> 72.2 us (1.043)
  local copies, waits for them, and re-layouts: 5.85 us -> 8.17 us
  other arithmetic: 9.03 us -> 10.2 us
    dynamic_slice x1, local copies, waits for them, and re-layouts: 1.11 us -> 0.02 us  [correlate_all(): lax.dynamic_slice_in_dim(templ_im, core * half, half, 0)]
    unnamed x14, local copies, waits for them, and re-layouts: 0.05 us -> 1.02 us
    concatenate x1, other arithmetic: 0.13 us -> 1.1 us  [route_patches(): jnp.concatenate([outgoing[0], received], axis=0)]
    concatenate x1, local copies, waits for them, and re-layouts: 0.03 us -> 0.98 us  [route_patches(): jnp.concatenate([patches, jnp.zeros((1, extent, extent), patches.dtype)],...]
    squeeze x0 -> x1, local copies, waits for them, and re-layouts: none -> 0.86 us  [route_patches(): outgoing[0]]
  transfers between devices with their start and end apart: 8 -> 8, of which waited for: 3 -> 2; matrix products, arithmetic and copies ran while one was open for 19% -> 18% of each run, Pallas kernels for 25% -> 24%
where the time goes in v19:
time: 72.2 us; the launch traced here: 71.6 us
  Pallas kernels  27 us (37%)
  waiting for transfers between devices  14.2 us (20%)
  starting transfers between devices  11 us (15%)
  other arithmetic  10.2 us (14%)
  local copies, waits for them, and re-layouts  8.17 us (11%)
  between operations  0.97 us (1%)
    pallas_call x2, Pallas kernels, correlate_chunk(): pl.pallas_call(functools.partial(corr_kernel, first, last, counts, orient...  22.8 us
    ppermute x3, waiting for transfers between devices, route_patches(): lax.ppermute(outgoing[m], 'patch', xor_pairs(sources, 2 * m))  14.2 us
    pallas_call x1, Pallas kernels, make_spectra(): pl.pallas_call(functools.partial(spectra_kernel, len(pieces)), in_specs=[...  4.16 us
    ppermute x3, starting transfers between devices, route_patches(): lax.ppermute(outgoing[m], 'patch', xor_pairs(sources, 2 * m))  3.49 us
    ppermute x1, starting transfers between devices, correlate_all(): lax.ppermute(jnp.concatenate(late_got, axis=0), 'patch', xor_pairs(source...  2.74 us
    ppermute x3, starting transfers between devices, correlate_all(): got = lax.ppermute(mine, 'blk', [(b, b ^ k) for b in range(blocks)])  2.65 us
    ppermute x1, starting transfers between devices, route_patches(): lax.ppermute(jnp.concatenate([outgoing[0], received], axis=0), 'patch', x...  2.16 us
    concatenate x1, other arithmetic, correlate_all(): jnp.concatenate(late_got, axis=0)  1.56 us
  transfers between devices with their start and end apart: 8, of which 2 were waited for; matrix products, arithmetic and copies ran while one was open for 18% of the time, Pallas kernels for 24%

profile of v19, /device:TPU:9, one launch (start us, length us, event | category | flops | bytes accessed | tf_op | source)
XLA Modules:
  0.0 71.6 jit_solution(3435990242987171915)
XLA Ops:
  0.7 0.7 %reshape.715 = s32[8,1,2]{2,0,1:T(8,128)S(1)} reshape(s32[16]{0:T(128)} %param.11) | data formatting | bytes 128 | tf_op jit(solution)/shard_map/reshape | solution.py:300
  1.5 0.1 copy.38
  1.6 0.1 copy.40
  1.7 0.1 copy.41
  1.8 0.1 copy.39
  2.0 0.2 fusion.32
  2.2 0.1 copy.42
  2.3 0.1 copy.43
  2.4 0.1 reshape.717
  2.6 1.0 %concatenate.97 = bf16[3,256,256]{2,1,0:T(8,128)(2,1)S(1)} pad(bf16[2,256,256]{2,1,0:T(8,128)(2,1)} %refs_0_.1, bf16[]{:T(256)} %constant.183.clone.1), padding=0_1x0_0x0_0 | pad | bytes 655362 | tf_op jit(solution)/shard_map/concatenate | solution.py:79
  3.5 0.6 gather_fusion.1
  4.2 0.2 broadcast_select_fusion
  4.4 0.8 %copy-done.3 = bf16[4,256,256]{2,1,0:T(8,128)(2,1)S(1)} copy-done((bf16[4,256,256]{2,1,0:T(8,128)(2,1)S(1)}, bf16[4,256,256]{2,1,0:T(8,128)(2,1)}, u32[]{:S(2)}) %copy-start.3) | copy-done | bytes 524312
  5.2 0.1 copy-done.2
  5.4 0.8 %pad_maximum_fusion.4 = bf16[4,256,256]{2,1,0:T(8,128)(2,1)} fusion(bf16[2,256,256]{2,1,0:T(8,128)(2,1)S(1)} %constant_dynamic-slice_fusion, bf16[2,256,256]{2,1,0:T(8,128)(2,1)S(1)} %constant_dynamic-slice_fusion.1), kind=kLoop, calls=%fused_computation.11 | loop fusion | flops 262144 | bytes 1048576 | tf_op jit(solution)/shard_map/concatenate | solution.py:266
  6.2 2.2 %collective-permute-start.6 = (bf16[4,256,256]{2,1,0:T(8,128)(2,1)}, bf16[4,256,256]{2,1,0:T(8,128)(2,1)}, u32[]{:S(2)}, u32[]{:S(2)}) collective-permute-start(bf16[4,256,256]{2,1,0:T(8,128)(2,1)} %pad_maximum_fusion.4), channel_id=1, source_target_pairs={{0,24},{8,16},{16,8},{24,0},{1,25},{9,17},{17,9},{25,1},{2,26},{10... | collective-permute-start | bytes 1572872 | tf_op jit(solution)/shard_map/ppermute | solution.py:275
  8.4 0.2 collective-permute-start.5
  8.6 0.9 %slice_bitcast_fusion = (bf16[2,256,256]{2,1,0:T(8,128)(2,1)S(1)}, bf16[2,256,256]{2,1,0:T(8,128)(2,1)}, bf16[2,256,256]{2,1,0:T(8,128)(2,1)}, bf16[2,256,256]{2,1,0:T(8,128)(2,1)S(1)}) fusion(bf16[4,2,256,256]{3,2,1,0:T(8,128)(2,1)S(1)} %broadcast_select_fusion), kind=kLoop, calls=%fused_computation.12 | loop fusion | bytes 2097152 | tf_op jit(solution)/shard_map/squeeze | solution.py:89
  9.5 1.3 %collective-permute-start.2 = (bf16[2,256,256]{2,1,0:T(8,128)(2,1)}, bf16[2,256,256]{2,1,0:T(8,128)(2,1)S(1)}, u32[]{:S(2)}, u32[]{:S(2)}) collective-permute-start(bf16[2,256,256]{2,1,0:T(8,128)(2,1)} %get-tuple-element.32), channel_id=1, source_target_pairs={{0,6},{1,7},{2,4},{3,5},{4,2},{5,3},{6,0},{7,1},{8,14},{9,15},{10,... | collective-permute-start | bytes 786440 | tf_op jit(solution)/shard_map/ppermute | solution.py:87
  10.8 1.0 %collective-permute-start.1 = (bf16[2,256,256]{2,1,0:T(8,128)(2,1)}, bf16[2,256,256]{2,1,0:T(8,128)(2,1)S(1)}, u32[]{:S(2)}, u32[]{:S(2)}) collective-permute-start(bf16[2,256,256]{2,1,0:T(8,128)(2,1)} %get-tuple-element.33), channel_id=1, source_target_pairs={{0,4},{1,5},{2,6},{3,7},{4,0},{5,1},{6,2},{7,3},{8,12},{9,13},{10,... | collective-permute-start | bytes 786440 | tf_op jit(solution)/shard_map/ppermute | solution.py:87
  11.8 1.2 %collective-permute-start = (bf16[2,256,256]{2,1,0:T(8,128)(2,1)S(1)}, bf16[2,256,256]{2,1,0:T(8,128)(2,1)S(1)}, u32[]{:S(2)}, u32[]{:S(2)}) collective-permute-start(bf16[2,256,256]{2,1,0:T(8,128)(2,1)S(1)} %get-tuple-element.34), channel_id=1, source_target_pairs={{0,2},{1,3},{2,0},{3,1},{4,6},{5,7},{6,4},{7,5},{8,10},{9,11},{10,... | collective-permute-start | bytes 786440 | tf_op jit(solution)/shard_map/ppermute | solution.py:87
  13.1 0.1 copy.37
  13.2 0.1 reduce
  13.3 0.1 select_reduce_fusion.1
  13.4 0.1 fusion.6
  13.8 0.4 fusion.13
  14.3 0.2 select_reduce_fusion
  14.5 0.5 broadcast_select_fusion.2.take_ref
  15.1 0.6 gather_fusion.2
  15.8 0.6 gather_fusion.3
  16.5 0.6 gather_fusion
  17.1 0.6 and_select_fusion.6.refs_0_
  17.7 0.1 fusion.1
  17.9 10.5 %collective-permute-done.2 = bf16[2,256,256]{2,1,0:T(8,128)(2,1)S(1)} collective-permute-done((bf16[2,256,256]{2,1,0:T(8,128)(2,1)}, bf16[2,256,256]{2,1,0:T(8,128)(2,1)S(1)}, u32[]{:S(2)}, u32[]{:S(2)}) %collective-permute-start.2) | collective-permute-done | bytes 262176 | tf_op jit(solution)/shard_map/ppermute | solution.py:87
  28.4 0.3 collective-permute-start.4
  28.6 3.7 %collective-permute-done.1 = bf16[2,256,256]{2,1,0:T(8,128)(2,1)S(1)} collective-permute-done((bf16[2,256,256]{2,1,0:T(8,128)(2,1)}, bf16[2,256,256]{2,1,0:T(8,128)(2,1)S(1)}, u32[]{:S(2)}, u32[]{:S(2)}) %collective-permute-start.1) | collective-permute-done | bytes 262176 | tf_op jit(solution)/shard_map/ppermute | solution.py:87
  32.3 1.1 %pad_maximum_fusion.1 = bf16[8,256,256]{2,1,0:T(8,128)(2,1)} fusion(bf16[2,256,256]{2,1,0:T(8,128)(2,1)S(1)} %collective-permute-done.2, bf16[2,256,256]{2,1,0:T(8,128)(2,1)S(1)} %collective-permute-done.1, bf16[2,256,256]{2,1,0:T(8,128)(2,1)S(1)} %collective-permute-done, bf16[2,256,256]{2,1,0:T(8,128)(2,1)S(1)} %get-tuple-element.31), kind=kLoop, calls=%fused_computation.6 | loop fusion | flops 1572864 | bytes 2097152 | tf_op jit(solution)/shard_map/concatenate | solution.py:89
  33.4 2.2 %collective-permute-start.3 = (bf16[8,256,256]{2,1,0:T(8,128)(2,1)}, bf16[8,256,256]{2,1,0:T(8,128)(2,1)}, u32[]{:S(2)}, u32[]{:S(2)}) collective-permute-start(bf16[8,256,256]{2,1,0:T(8,128)(2,1)} %pad_maximum_fusion.1), channel_id=1, source_target_pairs={{0,1},{1,0},{2,3},{3,2},{4,5},{5,4},{6,7},{7,6},{8,9},{9,8},{10,11... | collective-permute-start | bytes 3145736 | tf_op jit(solution)/shard_map/ppermute | solution.py:89
  35.6 0.7 gather_fusion.4
  36.3 0.6 and_select_fusion.refs_0_
  36.9 1.1 %pad_maximum_fusion.2.refs_3_ = bf16[8,256,256]{2,1,0:T(8,128)(2,1)} fusion(bf16[4,256,256]{2,1,0:T(8,128)(2,1)S(1)} %copy-done.2, bf16[4,256,256]{2,1,0:T(8,128)(2,1)S(1)} %copy-done.3), kind=kLoop, calls=%fused_computation.7 | loop fusion | flops 524288 | bytes 2097152 | tf_op jit(solution)/shard_map/concatenate | solution.py:265
  37.9 1.3 %negate_multiply_fusion.refs_3_ = f32[4,256,256]{2,1,0:T(8,128)} fusion(f32[4,256]{1,0:T(4,128)S(1)} %get-tuple-element.40, f32[4,256]{1,0:T(4,128)S(1)} %get-tuple-element.42, f32[4,256]{1,0:T(4,128)S(1)} %get-tuple-element.41, f32[4,256]{1,0:T(4,128)S(1)} %get-tuple-element.39), kind=kLoop, calls=%fused_computation.8 | loop fusion | flops 1310720 | bytes 1064960 | tf_op jit(solution)/shard_map/div | solution.py:57
  39.3 1.0 %pad_maximum_fusion.3.refs_1_ = bf16[6,256,256]{2,1,0:T(8,128)(2,1)} fusion(bf16[2,256,256]{2,1,0:T(8,128)(2,1)S(1)} %collective-permute-done.2, bf16[2,256,256]{2,1,0:T(8,128)(2,1)S(1)} %collective-permute-done.1, bf16[2,256,256]{2,1,0:T(8,128)(2,1)S(1)} %collective-permute-done), kind=kLoop, calls=%fused_computation.10 | loop fusion | flops 786432 | bytes 1572864 | tf_op jit(solution)/shard_map/concatenate | solution.py:88
  40.2 1.6 %pad_maximum_fusion = bf16[12,256,256]{2,1,0:T(8,128)(2,1)S(1)} fusion(bf16[4,256,256]{2,1,0:T(8,128)(2,1)} %collective-permute-done.6.refs_6_, bf16[4,256,256]{2,1,0:T(8,128)(2,1)} %collective-permute-done.5.refs_5_, bf16[4,256,256]{2,1,0:T(8,128)(2,1)S(1)} %collective-permute-done.4.refs_4_), kind=kLoop, calls=%fused_computation.5 | loop fusion | flops 1572864 | bytes 3145728 | tf_op jit(solution)/shard_map/concatenate | solution.py:282
  41.8 2.7 %collective-permute-start.7 = (bf16[12,256,256]{2,1,0:T(8,128)(2,1)S(1)}, bf16[12,256,256]{2,1,0:T(8,128)(2,1)}, u32[]{:S(2)}, u32[]{:S(2)}) collective-permute-start(bf16[12,256,256]{2,1,0:T(8,128)(2,1)S(1)} %pad_maximum_fusion), channel_id=1, source_target_pairs={{0,1},{1,0},{2,3},{3,2},{4,5},{5,4},{6,7},{7,6},{8,9},{9,8},{10,11... | collective-permute-start | bytes 4718600 | tf_op jit(solution)/shard_map/ppermute | solution.py:282
  44.6 4.2 %shard_map.129 = (bf16[4,256,256]{2,1,0:T(8,128)(2,1)}, bf16[4,256,256]{2,1,0:T(8,128)(2,1)}) custom-call(s32[4]{0:T(128)} %broadcast_select_fusion.2.take_ref, bf16[2,256,256]{2,1,0:T(8,128)(2,1)} %refs_0_.1, bf16[6,256,256]{2,1,0:T(8,128)(2,1)} %pad_maximum_fusion.3.refs_1_, bf16[8,256,256]{2,1,0:T(8,128)(2,1)} %collective-permute-done.3.refs_2_, ...), custom_call_target="tpu_custom_call" | custom-call | flops 1207959552 | bytes 2621440 | tf_op jit(solution)/shard_map/pallas_call | solution.py:144
  48.7 13.1 %shard_map.130 = (f32[4,256,256]{2,1,0:T(8,128)}, f32[4,256,256]{2,1,0:T(8,128)}, f32[4,256,256]{2,1,0:T(8,128)}, f32[4,8,128]{2,1,0:T(8,128)}) custom-call(s32[10]{0:T(128)} %and_select_fusion.refs_0_, bf16[4,256,256]{2,1,0:T(8,128)(2,1)} %get-tuple-element.14.refs_1_, bf16[4,256,256]{2,1,0:T(8,128)(2,1)} %get-tuple-element.15.refs_2_, ...), custom_call_target="tpu_custom_call" | custom-call | flops 24159191040 | bytes 15728640 | tf_op jit(solution)/shard_map/pallas_call | solution.py:240
  61.9 9.7 %shard_map.131 = (f32[4,256,256]{2,1,0:T(8,128)}, f32[4,256,256]{2,1,0:T(8,128)}, f32[4,256,256]{2,1,0:T(8,128)}, f32[4,16]{1,0:T(4,128)}) custom-call(s32[6]{0:T(128)} %and_select_fusion.6.refs_0_, bf16[4,256,256]{2,1,0:T(8,128)(2,1)} %get-tuple-element.14.refs_1_, ...), custom_call_target="tpu_custom_call", output_to_operand_aliasing={{0}: (6, {}), {1}: (7, {}), {2}: (8, {})} | custom-call | flops 14495514624 | bytes 13631488 | tf_op jit(solution)/shard_map/pallas_call | solution.py:240
  (56 shorter events, 0.7 us)
Async XLA Ops:
  0.6 15.8 %copy-start = (s32[16]{0:T(128)S(1)}, s32[16]{0:T(128)}, u32[]{:S(2)}) copy-start(s32[16]{0:T(128)} %param.16) | copy-start | bytes 196
  4.2 1.0 %copy-start.3 = (bf16[4,256,256]{2,1,0:T(8,128)(2,1)S(1)}, bf16[4,256,256]{2,1,0:T(8,128)(2,1)}, u32[]{:S(2)}) copy-start(bf16[4,256,256]{2,1,0:T(8,128)(2,1)} %param.14) | copy-start | bytes 1572868
  4.2 1.2 %copy-start.2 = (bf16[4,256,256]{2,1,0:T(8,128)(2,1)S(1)}, bf16[4,256,256]{2,1,0:T(8,128)(2,1)}, u32[]{:S(2)}) copy-start(bf16[4,256,256]{2,1,0:T(8,128)(2,1)} %param.15) | copy-start | bytes 1572868
  5.4 7.7 %copy-start.5 = (s32[16]{0:T(128)S(1)}, s32[16]{0:T(128)}, u32[]{:S(2)}) copy-start(s32[16]{0:T(128)} %param.11) | copy-start | bytes 196
  5.4 9.7 %copy-start.6 = (s32[16]{0:T(128)S(1)}, s32[16]{0:T(128)}, u32[]{:S(2)}) copy-start(s32[16]{0:T(128)} %param.12) | copy-start | bytes 196
  6.2 9.6 %copy-start.1 = (f32[32]{0:T(128)S(1)}, f32[32]{0:T(128)}, u32[]{:S(2)}) copy-start(f32[32]{0:T(128)} %param.13) | copy-start | bytes 388
  6.2 34.0 %collective-permute-start.6 = (bf16[4,256,256]{2,1,0:T(8,128)(2,1)}, bf16[4,256,256]{2,1,0:T(8,128)(2,1)}, u32[]{:S(2)}, u32[]{:S(2)}) collective-permute-start(bf16[4,256,256]{2,1,0:T(8,128)(2,1)} %pad_maximum_fusion.4), channel_id=1, source_target_pairs={{0,24},{8,16},{16,8},{24,0},{1,25},{9,17},{17,9},{25,1},{2,26},{10... | collective-permute-start | bytes 1572872 | tf_op jit(solution)/shard_map/ppermute | solution.py:275
  8.4 31.8 %collective-permute-start.5 = (bf16[4,256,256]{2,1,0:T(8,128)(2,1)}, bf16[4,256,256]{2,1,0:T(8,128)(2,1)}, u32[]{:S(2)}, u32[]{:S(2)}) collective-permute-start(bf16[4,256,256]{2,1,0:T(8,128)(2,1)} %pad_maximum_fusion.4), channel_id=1, source_target_pairs={{0,16},{8,24},{16,0},{24,8},{1,17},{9,25},{17,1},{25,9},{2,18},{10... | collective-permute-start | bytes 1572872 | tf_op jit(solution)/shard_map/ppermute | solution.py:275
  9.5 18.9 %collective-permute-start.2 = (bf16[2,256,256]{2,1,0:T(8,128)(2,1)}, bf16[2,256,256]{2,1,0:T(8,128)(2,1)S(1)}, u32[]{:S(2)}, u32[]{:S(2)}) collective-permute-start(bf16[2,256,256]{2,1,0:T(8,128)(2,1)} %get-tuple-element.32), channel_id=1, source_target_pairs={{0,6},{1,7},{2,4},{3,5},{4,2},{5,3},{6,0},{7,1},{8,14},{9,15},{10,... | collective-permute-start | bytes 786440 | tf_op jit(solution)/shard_map/ppermute | solution.py:87
  10.8 21.5 %collective-permute-start.1 = (bf16[2,256,256]{2,1,0:T(8,128)(2,1)}, bf16[2,256,256]{2,1,0:T(8,128)(2,1)S(1)}, u32[]{:S(2)}, u32[]{:S(2)}) collective-permute-start(bf16[2,256,256]{2,1,0:T(8,128)(2,1)} %get-tuple-element.33), channel_id=1, source_target_pairs={{0,4},{1,5},{2,6},{3,7},{4,0},{5,1},{6,2},{7,3},{8,12},{9,13},{10,... | collective-permute-start | bytes 786440 | tf_op jit(solution)/shard_map/ppermute | solution.py:87
  11.8 20.5 %collective-permute-start = (bf16[2,256,256]{2,1,0:T(8,128)(2,1)S(1)}, bf16[2,256,256]{2,1,0:T(8,128)(2,1)S(1)}, u32[]{:S(2)}, u32[]{:S(2)}) collective-permute-start(bf16[2,256,256]{2,1,0:T(8,128)(2,1)S(1)} %get-tuple-element.34), channel_id=1, source_target_pairs={{0,2},{1,3},{2,0},{3,1},{4,6},{5,7},{6,4},{7,5},{8,10},{9,11},{10,... | collective-permute-start | bytes 786440 | tf_op jit(solution)/shard_map/ppermute | solution.py:87
  28.4 11.9 %collective-permute-start.4 = (bf16[4,256,256]{2,1,0:T(8,128)(2,1)}, bf16[4,256,256]{2,1,0:T(8,128)(2,1)S(1)}, u32[]{:S(2)}, u32[]{:S(2)}) collective-permute-start(bf16[4,256,256]{2,1,0:T(8,128)(2,1)} %pad_maximum_fusion.4), channel_id=1, source_target_pairs={{0,8},{8,0},{16,24},{24,16},{1,9},{9,1},{17,25},{25,17},{2,10},{10... | collective-permute-start | bytes 1572872 | tf_op jit(solution)/shard_map/ppermute | solution.py:275
  33.4 11.1 %collective-permute-start.3 = (bf16[8,256,256]{2,1,0:T(8,128)(2,1)}, bf16[8,256,256]{2,1,0:T(8,128)(2,1)}, u32[]{:S(2)}, u32[]{:S(2)}) collective-permute-start(bf16[8,256,256]{2,1,0:T(8,128)(2,1)} %pad_maximum_fusion.1), channel_id=1, source_target_pairs={{0,1},{1,0},{2,3},{3,2},{4,5},{5,4},{6,7},{7,6},{8,9},{9,8},{10,11... | collective-permute-start | bytes 3145736 | tf_op jit(solution)/shard_map/ppermute | solution.py:89
  40.2 1.6 %copy-start.4 = (bf16[4,256,256]{2,1,0:T(8,128)(2,1)}, bf16[4,256,256]{2,1,0:T(8,128)(2,1)S(1)}, u32[]{:S(2)}) copy-start(bf16[4,256,256]{2,1,0:T(8,128)(2,1)S(1)} %collective-permute-done.4.refs_4_) | copy-start | bytes 1572868
  41.8 20.0 %collective-permute-start.7 = (bf16[12,256,256]{2,1,0:T(8,128)(2,1)S(1)}, bf16[12,256,256]{2,1,0:T(8,128)(2,1)}, u32[]{:S(2)}, u32[]{:S(2)}) collective-permute-start(bf16[12,256,256]{2,1,0:T(8,128)(2,1)S(1)} %pad_maximum_fusion), channel_id=1, source_target_pairs={{0,1},{1,0},{2,3},{3,2},{4,5},{5,4},{6,7},{7,6},{8,9},{9,8},{10,11... | collective-permute-start | bytes 4718600 | tf_op jit(solution)/shard_map/ppermute | solution.py:282

commit v20 on v16

--- a/solution.py
+++ b/solution.py
@@ -116,8 +116,9 @@
     extent = own_ref.shape[-1]
     half_table = half_ref[...]
     full_table = full_ref[...]
-    for s in range(re_ref.shape[0]):
-        idx = take_ref[s]
+    step = re_ref.shape[0]
+    for s in range(step):
+        idx = take_ref[pl.program_id(0) * step + s]
         pick_own = own_ref[jnp.clip(idx, 0, number - 1)]
         pick_direct = direct_ref[jnp.clip(idx - number, 0, number - 1)]
         pick_recv = recv_ref[jnp.clip(idx - 2 * number, 0, rows - 1)]
@@ -140,11 +141,14 @@
     count, extent = (scale.shape[0], scale.shape[-1])
     rows = received.shape[0]
     whole = pl.BlockSpec(memory_space=pltpu.VMEM)
+    step = 2 if count % 2 == 0 else 1
+    plane = pl.BlockSpec((step, extent, extent), lambda s: (s, 0, 0))
     spec_shape = jax.ShapeDtypeStruct((count, extent, extent), jnp.bfloat16)
     return pl.pallas_call(
         functools.partial(spectra_kernel, rows),
-        in_specs=[pl.BlockSpec(memory_space=pltpu.SMEM)] + [whole] * 7,
-        out_specs=[whole, whole],
+        grid=(count // step,),
+        in_specs=[pl.BlockSpec(memory_space=pltpu.SMEM)] + [whole] * 4 + [plane] + [whole] * 2,
+        out_specs=[plane, plane],
         out_shape=[spec_shape, spec_shape],
         cost_estimate=pl.CostEstimate(
             flops=3 * count * 6 * extent * extent * extent, transcendentals=0,

time: 69.3 us -> 69.1 us (level)
  no operation moved by 1% of the time
where the time goes in v20:
time: 69.1 us; the launch traced here: 68.9 us
  Pallas kernels  26.9 us (39%)
  waiting for transfers between devices  13.1 us (19%)
  starting transfers between devices  11.5 us (17%)
  local copies, waits for them, and re-layouts  10.7 us (15%)
  other arithmetic  5.78 us (8%)
  between operations  0.98 us (1%)
    pallas_call x2, Pallas kernels, correlate_chunk(): pl.pallas_call(functools.partial(corr_kernel, first, last, counts, orient...  22.9 us
    ppermute x3, waiting for transfers between devices, route_patches(): lax.ppermute(outgoing[m], 'patch', xor_pairs(sources, 2 * m))  12.5 us
    pallas_call x1, Pallas kernels, make_spectra(): pl.pallas_call(functools.partial(spectra_kernel, rows), grid=(count // st...  4.02 us
    ppermute x3, starting transfers between devices, route_patches(): lax.ppermute(outgoing[m], 'patch', xor_pairs(sources, 2 * m))  3.49 us
    unnamed x22, local copies, waits for them, and re-layouts  3.39 us
    ppermute x1, starting transfers between devices, correlate_all(): lax.ppermute(jnp.concatenate(late_got, axis=0), 'patch', xor_pairs(source...  3.1 us
    ppermute x3, starting transfers between devices, correlate_all(): got = lax.ppermute(mine, 'blk', [(b, b ^ k) for b in range(blocks)])  2.71 us
    ppermute x1, starting transfers between devices, route_patches(): direct = lax.ppermute(outgoing[0], 'patch', xor_pairs(sources, 1))  2.16 us
  transfers between devices with their start and end apart: 9, of which 3 were waited for; matrix products, arithmetic and copies ran while one was open for 22% of the time, Pallas kernels for 25%

profile of v20, /device:TPU:9, one launch (start us, length us, event | category | flops | bytes accessed | tf_op | source)
XLA Modules:
  0.0 68.9 jit_solution(2577029362594536788)
XLA Ops:
  0.7 1.1 %constant_dynamic-slice_fusion = (bf16[2,256,256]{2,1,0:T(8,128)(2,1)S(1)}, bf16[2,256,256]{2,1,0:T(8,128)(2,1)S(1)}) fusion(bf16[4,256,256]{2,1,0:T(8,128)(2,1)} %param.15, s32[]{:T(128)S(6)} %select_n.312, bf16[4,256,256]{2,1,0:T(8,128)(2,1)} %param.14), kind=kLoop, calls=%fused_computation.47 | loop fusion | bytes 1048580 | tf_op jit(solution)/shard_map/dynamic_slice | solution.py:272
  1.9 2.2 %collective-permute-start.7 = (bf16[4,256,256]{2,1,0:T(8,128)(2,1)S(1)}, bf16[4,256,256]{2,1,0:T(8,128)(2,1)S(1)}, u32[]{:S(2)}, u32[]{:S(2)}) collective-permute-start(bf16[4,256,256]{2,1,0:T(8,128)(2,1)S(1)} %pad_maximum_fusion.2), channel_id=1, source_target_pairs={{0,24},{8,16},{16,8},{24,0},{1,25},{9,17},{17,9},{25,1},{2,26},{10... | collective-permute-start | bytes 1572872 | tf_op jit(solution)/shard_map/ppermute | solution.py:279
  4.1 0.2 collective-permute-start.6
  4.5 0.1 copy.34
  4.6 0.1 copy.36
  4.7 0.1 copy.37
  4.8 0.1 copy.35
  5.0 0.1 fusion.2
  5.1 0.1 copy.38
  5.2 0.1 reshape.722
  5.3 0.1 reshape.721
  5.4 0.6 gather_fusion.1
  6.0 0.2 broadcast_select_fusion
  6.2 0.9 %fusion.32 = (bf16[2,256,256]{2,1,0:T(8,128)(2,1)}, bf16[2,256,256]{2,1,0:T(8,128)(2,1)}, bf16[2,256,256]{2,1,0:T(8,128)(2,1)S(1)}, bf16[2,256,256]{2,1,0:T(8,128)(2,1)}) fusion(bf16[8,256,256]{2,1,0:T(8,128)(2,1)S(1)} %broadcast_select_fusion), kind=kLoop, calls=%fused_computation.120 | loop fusion | bytes 2097152 | tf_op jit(solution)/shard_map/slice | solution.py:87
  7.1 1.3 %collective-permute-start.3 = (bf16[2,256,256]{2,1,0:T(8,128)(2,1)}, bf16[2,256,256]{2,1,0:T(8,128)(2,1)S(1)}, u32[]{:S(2)}, u32[]{:S(2)}) collective-permute-start(bf16[2,256,256]{2,1,0:T(8,128)(2,1)} %get-tuple-element.27), channel_id=1, source_target_pairs={{0,6},{1,7},{2,4},{3,5},{4,2},{5,3},{6,0},{7,1},{8,14},{9,15},{10,... | collective-permute-start | bytes 786440 | tf_op jit(solution)/shard_map/ppermute | solution.py:87
  8.4 1.0 %collective-permute-start.2 = (bf16[2,256,256]{2,1,0:T(8,128)(2,1)}, bf16[2,256,256]{2,1,0:T(8,128)(2,1)}, u32[]{:S(2)}, u32[]{:S(2)}) collective-permute-start(bf16[2,256,256]{2,1,0:T(8,128)(2,1)} %get-tuple-element.28), channel_id=1, source_target_pairs={{0,4},{1,5},{2,6},{3,7},{4,0},{5,1},{6,2},{7,3},{8,12},{9,13},{10,... | collective-permute-start | bytes 786440 | tf_op jit(solution)/shard_map/ppermute | solution.py:87
  9.4 1.2 %collective-permute-start.1 = (bf16[2,256,256]{2,1,0:T(8,128)(2,1)S(1)}, bf16[2,256,256]{2,1,0:T(8,128)(2,1)}, u32[]{:S(2)}, u32[]{:S(2)}) collective-permute-start(bf16[2,256,256]{2,1,0:T(8,128)(2,1)S(1)} %get-tuple-element.29), channel_id=1, source_target_pairs={{0,2},{1,3},{2,0},{3,1},{4,6},{5,7},{6,4},{7,5},{8,10},{9,11},{10,... | collective-permute-start | bytes 786440 | tf_op jit(solution)/shard_map/ppermute | solution.py:87
  10.7 0.1 copy.33
  10.8 0.1 reduce
  10.9 0.1 select_reduce_fusion.1
  11.1 0.1 fusion.6
  11.2 0.1 fusion.17
  11.4 0.4 fusion.13
  11.8 0.1 concatenate.92
  11.9 0.2 select_reduce_fusion
  12.1 0.5 broadcast_select_fusion.2.take_ref
  12.7 0.6 gather_fusion.2
  13.4 0.6 gather_fusion.3
  14.1 0.6 gather_fusion
  14.7 0.1 fusion.1
  14.9 0.6 and_select_fusion.6.refs_0_
  15.5 11.9 %collective-permute-done.1 = bf16[2,256,256]{2,1,0:T(8,128)(2,1)} collective-permute-done((bf16[2,256,256]{2,1,0:T(8,128)(2,1)S(1)}, bf16[2,256,256]{2,1,0:T(8,128)(2,1)}, u32[]{:S(2)}, u32[]{:S(2)}) %collective-permute-start.1) | collective-permute-done | bytes 262176 | tf_op jit(solution)/shard_map/ppermute | solution.py:87
  27.4 0.3 collective-permute-start.5
  27.7 1.7 %constant_dynamic-update-slice_fusion.2 = bf16[6,256,256]{2,1,0:T(8,128)(2,1)} fusion(bf16[2,256,256]{2,1,0:T(8,128)(2,1)} %collective-permute-done.1), kind=kLoop, calls=%fused_computation.15 | loop fusion | bytes 524288
  29.3 0.6 collective-permute-done.2
  30.0 2.2 %collective-permute-start = (bf16[2,256,256]{2,1,0:T(8,128)(2,1)}, bf16[2,256,256]{2,1,0:T(8,128)(2,1)}, u32[]{:S(2)}, u32[]{:S(2)}) collective-permute-start(bf16[2,256,256]{2,1,0:T(8,128)(2,1)} %get-tuple-element.30), channel_id=1, source_target_pairs={{0,1},{1,0},{2,3},{3,2},{4,5},{5,4},{6,7},{7,6},{8,9},{9,8},{10,11... | collective-permute-start | bytes 786440 | tf_op jit(solution)/shard_map/ppermute | solution.py:84
  32.1 1.7 %constant_dynamic-update-slice_fusion.1 = bf16[6,256,256]{2,1,0:T(8,128)(2,1)} fusion(bf16[6,256,256]{2,1,0:T(8,128)(2,1)} %constant_dynamic-update-slice_fusion.2, bf16[2,256,256]{2,1,0:T(8,128)(2,1)} %collective-permute-done.2), kind=kLoop, calls=%fused_computation.14 | loop fusion | bytes 524288
  33.8 0.7 %constant_dynamic-update-slice_fusion.recv_ref = bf16[6,256,256]{2,1,0:T(8,128)(2,1)} fusion(bf16[6,256,256]{2,1,0:T(8,128)(2,1)} %constant_dynamic-update-slice_fusion.1, bf16[2,256,256]{2,1,0:T(8,128)(2,1)S(1)} %collective-permute-done.3), kind=kLoop, calls=%fused_computation.13 | loop fusion | bytes 524288 | tf_op jit(solution)/shard_map/concatenate | solution.py:88
  34.5 0.7 gather_fusion.4
  35.2 0.6 and_select_fusion.refs_0_
  35.8 1.3 %negate_multiply_fusion.scale_ref = f32[4,256,256]{2,1,0:T(8,128)} fusion(f32[4,256]{1,0:T(4,128)S(1)} %get-tuple-element.36, f32[4,256]{1,0:T(4,128)S(1)} %get-tuple-element.38, f32[4,256]{1,0:T(4,128)S(1)} %get-tuple-element.37, f32[4,256]{1,0:T(4,128)S(1)} %get-tuple-element.35), kind=kLoop, calls=%fused_computation.7 | loop fusion | flops 1310720 | bytes 1064960 | tf_op jit(solution)/shard_map/div | solution.py:57
  37.1 1.1 %pad_maximum_fusion.1.refs_3_ = bf16[8,256,256]{2,1,0:T(8,128)(2,1)} fusion(bf16[4,256,256]{2,1,0:T(8,128)(2,1)S(1)} %copy-done.2, bf16[4,256,256]{2,1,0:T(8,128)(2,1)S(1)} %copy-done.3), kind=kLoop, calls=%fused_computation.6 | loop fusion | flops 524288 | bytes 2097152 | tf_op jit(solution)/shard_map/concatenate | solution.py:269
  38.2 0.5 collective-permute-done.5.refs_4_
  38.7 0.2 pad_maximum_fusion
  38.9 3.1 %collective-permute-start.8 = (bf16[12,256,256]{2,1,0:T(8,128)(2,1)S(1)}, bf16[12,256,256]{2,1,0:T(8,128)(2,1)}, u32[]{:S(2)}, u32[]{:S(2)}) collective-permute-start(bf16[12,256,256]{2,1,0:T(8,128)(2,1)S(1)} %pad_maximum_fusion), channel_id=1, source_target_pairs={{0,1},{1,0},{2,3},{3,2},{4,5},{5,4},{6,7},{7,6},{8,9},{9,8},{10,11... | collective-permute-start | bytes 4718600 | tf_op jit(solution)/shard_map/ppermute | solution.py:286
  42.0 4.0 %shard_map.129 = (bf16[4,256,256]{2,1,0:T(8,128)(2,1)}, bf16[4,256,256]{2,1,0:T(8,128)(2,1)}) custom-call(s32[4]{0:T(128)} %broadcast_select_fusion.2.take_ref, bf16[2,256,256]{2,1,0:T(8,128)(2,1)} %own_ref.1, bf16[2,256,256]{2,1,0:T(8,128)(2,1)} %collective-permute-done.direct_ref, bf16[6,256,256]{2,1,0:T(8,128)(2,1)} %constant_dynamic-update-slice_fusion.recv_ref, ...), custom_call_target="tpu_custom_call" | custom-call | flops 1207959552 | bytes 2621440 | tf_op jit(solution)/shard_map/pallas_call | solution.py:147
  46.0 13.1 %shard_map.130 = (f32[4,256,256]{2,1,0:T(8,128)}, f32[4,256,256]{2,1,0:T(8,128)}, f32[4,256,256]{2,1,0:T(8,128)}, f32[4,8,128]{2,1,0:T(8,128)}) custom-call(s32[10]{0:T(128)} %and_select_fusion.refs_0_, bf16[4,256,256]{2,1,0:T(8,128)(2,1)} %get-tuple-element.12.refs_1_, bf16[4,256,256]{2,1,0:T(8,128)(2,1)} %get-tuple-element.13.refs_2_, ...), custom_call_target="tpu_custom_call" | custom-call | flops 24159191040 | bytes 15728640 | tf_op jit(solution)/shard_map/pallas_call | solution.py:244
  59.2 9.7 %shard_map.131 = (f32[4,256,256]{2,1,0:T(8,128)}, f32[4,256,256]{2,1,0:T(8,128)}, f32[4,256,256]{2,1,0:T(8,128)}, f32[4,16]{1,0:T(4,128)}) custom-call(s32[6]{0:T(128)} %and_select_fusion.6.refs_0_, bf16[4,256,256]{2,1,0:T(8,128)(2,1)} %get-tuple-element.12.refs_1_, ...), custom_call_target="tpu_custom_call", output_to_operand_aliasing={{0}: (6, {}), {1}: (7, {}), {2}: (8, {})} | custom-call | flops 14495514624 | bytes 13631488 | tf_op jit(solution)/shard_map/pallas_call | solution.py:244
  (64 shorter events, 0.7 us)
Async XLA Ops:
  0.6 13.5 %copy-start = (s32[16]{0:T(128)S(1)}, s32[16]{0:T(128)}, u32[]{:S(2)}) copy-start(s32[16]{0:T(128)} %param.16) | copy-start | bytes 196
  0.6 3.7 %copy-start.8 = (s32[16]{0:T(128)S(1)}, s32[16]{0:T(128)}, u32[]{:S(2)}) copy-start(s32[16]{0:T(128)} %param.11) | copy-start | bytes 196
  0.7 4.7 %copy-start.7 = (bf16[2,256,256]{2,1,0:T(8,128)(2,1)S(1)}, bf16[2,256,256]{2,1,0:T(8,128)(2,1)}, u32[]{:S(2)}) copy-start(bf16[2,256,256]{2,1,0:T(8,128)(2,1)} %own_ref.1) | copy-start | bytes 786436
  1.9 36.3 %collective-permute-start.7 = (bf16[4,256,256]{2,1,0:T(8,128)(2,1)S(1)}, bf16[4,256,256]{2,1,0:T(8,128)(2,1)S(1)}, u32[]{:S(2)}, u32[]{:S(2)}) collective-permute-start(bf16[4,256,256]{2,1,0:T(8,128)(2,1)S(1)} %pad_maximum_fusion.2), channel_id=1, source_target_pairs={{0,24},{8,16},{16,8},{24,0},{1,25},{9,17},{17,9},{25,1},{2,26},{10... | collective-permute-start | bytes 1572872 | tf_op jit(solution)/shard_map/ppermute | solution.py:279
  4.1 34.1 %collective-permute-start.6 = (bf16[4,256,256]{2,1,0:T(8,128)(2,1)S(1)}, bf16[4,256,256]{2,1,0:T(8,128)(2,1)S(1)}, u32[]{:S(2)}, u32[]{:S(2)}) collective-permute-start(bf16[4,256,256]{2,1,0:T(8,128)(2,1)S(1)} %pad_maximum_fusion.2), channel_id=1, source_target_pairs={{0,16},{8,24},{16,0},{24,8},{1,17},{9,25},{17,1},{25,9},{2,18},{10... | collective-permute-start | bytes 1572872 | tf_op jit(solution)/shard_map/ppermute | solution.py:279
  6.2 6.4 %copy-start.9 = (s32[16]{0:T(128)S(1)}, s32[16]{0:T(128)}, u32[]{:S(2)}) copy-start(s32[16]{0:T(128)} %param.12) | copy-start | bytes 196
  6.2 7.2 %copy-start.1 = (f32[32]{0:T(128)S(1)}, f32[32]{0:T(128)}, u32[]{:S(2)}) copy-start(f32[32]{0:T(128)} %param.13) | copy-start | bytes 388
  7.1 26.7 %collective-permute-start.3 = (bf16[2,256,256]{2,1,0:T(8,128)(2,1)}, bf16[2,256,256]{2,1,0:T(8,128)(2,1)S(1)}, u32[]{:S(2)}, u32[]{:S(2)}) collective-permute-start(bf16[2,256,256]{2,1,0:T(8,128)(2,1)} %get-tuple-element.27), channel_id=1, source_target_pairs={{0,6},{1,7},{2,4},{3,5},{4,2},{5,3},{6,0},{7,1},{8,14},{9,15},{10,... | collective-permute-start | bytes 786440 | tf_op jit(solution)/shard_map/ppermute | solution.py:87
  8.4 21.5 %collective-permute-start.2 = (bf16[2,256,256]{2,1,0:T(8,128)(2,1)}, bf16[2,256,256]{2,1,0:T(8,128)(2,1)}, u32[]{:S(2)}, u32[]{:S(2)}) collective-permute-start(bf16[2,256,256]{2,1,0:T(8,128)(2,1)} %get-tuple-element.28), channel_id=1, source_target_pairs={{0,4},{1,5},{2,6},{3,7},{4,0},{5,1},{6,2},{7,3},{8,12},{9,13},{10,... | collective-permute-start | bytes 786440 | tf_op jit(solution)/shard_map/ppermute | solution.py:87
  9.4 18.0 %collective-permute-start.1 = (bf16[2,256,256]{2,1,0:T(8,128)(2,1)S(1)}, bf16[2,256,256]{2,1,0:T(8,128)(2,1)}, u32[]{:S(2)}, u32[]{:S(2)}) collective-permute-start(bf16[2,256,256]{2,1,0:T(8,128)(2,1)S(1)} %get-tuple-element.29), channel_id=1, source_target_pairs={{0,2},{1,3},{2,0},{3,1},{4,6},{5,7},{6,4},{7,5},{8,10},{9,11},{10,... | collective-permute-start | bytes 786440 | tf_op jit(solution)/shard_map/ppermute | solution.py:87
  15.5 21.6 %copy-start.2 = (bf16[4,256,256]{2,1,0:T(8,128)(2,1)S(1)}, bf16[4,256,256]{2,1,0:T(8,128)(2,1)}, u32[]{:S(2)}) copy-start(bf16[4,256,256]{2,1,0:T(8,128)(2,1)} %param.15) | copy-start | bytes 1572868
  15.5 21.6 %copy-start.3 = (bf16[4,256,256]{2,1,0:T(8,128)(2,1)S(1)}, bf16[4,256,256]{2,1,0:T(8,128)(2,1)}, u32[]{:S(2)}) copy-start(bf16[4,256,256]{2,1,0:T(8,128)(2,1)} %param.14) | copy-start | bytes 1572868
  27.4 11.3 %collective-permute-start.5 = (bf16[4,256,256]{2,1,0:T(8,128)(2,1)S(1)}, bf16[4,256,256]{2,1,0:T(8,128)(2,1)S(1)}, u32[]{:S(2)}, u32[]{:S(2)}) collective-permute-start(bf16[4,256,256]{2,1,0:T(8,128)(2,1)S(1)} %pad_maximum_fusion.2), channel_id=1, source_target_pairs={{0,8},{8,0},{16,24},{24,16},{1,9},{9,1},{17,25},{25,17},{2,10},{10... | collective-permute-start | bytes 1572872 | tf_op jit(solution)/shard_map/ppermute | solution.py:279
  30.0 12.0 %collective-permute-start = (bf16[2,256,256]{2,1,0:T(8,128)(2,1)}, bf16[2,256,256]{2,1,0:T(8,128)(2,1)}, u32[]{:S(2)}, u32[]{:S(2)}) collective-permute-start(bf16[2,256,256]{2,1,0:T(8,128)(2,1)} %get-tuple-element.30), channel_id=1, source_target_pairs={{0,1},{1,0},{2,3},{3,2},{4,5},{5,4},{6,7},{7,6},{8,9},{9,8},{10,11... | collective-permute-start | bytes 786440 | tf_op jit(solution)/shard_map/ppermute | solution.py:84
  34.5 7.5 %collective-permute-start.4 = (bf16[6,256,256]{2,1,0:T(8,128)(2,1)}, bf16[6,256,256]{2,1,0:T(8,128)(2,1)}, u32[]{:S(2)}, u32[]{:S(2)}) collective-permute-start(bf16[6,256,256]{2,1,0:T(8,128)(2,1)} %constant_dynamic-update-slice_fusion.recv_ref), channel_id=1, source_target_pairs={{0,1},{1,0},{2,3},{3,2},{4,5},{5,4},{6,7},{7,6},{8,9},{9,8},{10,11... | collective-permute-start | bytes 2359304 | tf_op jit(solution)/shard_map/ppermute | solution.py:89
  38.2 7.9 %copy-start.4 = (bf16[4,256,256]{2,1,0:T(8,128)(2,1)}, bf16[4,256,256]{2,1,0:T(8,128)(2,1)S(1)}, u32[]{:S(2)}) copy-start(bf16[4,256,256]{2,1,0:T(8,128)(2,1)S(1)} %collective-permute-done.7.refs_6_) | copy-start | bytes 1572868
  38.2 7.8 %copy-start.5 = (bf16[4,256,256]{2,1,0:T(8,128)(2,1)}, bf16[4,256,256]{2,1,0:T(8,128)(2,1)S(1)}, u32[]{:S(2)}) copy-start(bf16[4,256,256]{2,1,0:T(8,128)(2,1)S(1)} %collective-permute-done.6.refs_5_) | copy-start | bytes 1572868
  38.7 7.3 %copy-start.6 = (bf16[4,256,256]{2,1,0:T(8,128)(2,1)}, bf16[4,256,256]{2,1,0:T(8,128)(2,1)S(1)}, u32[]{:S(2)}) copy-start(bf16[4,256,256]{2,1,0:T(8,128)(2,1)S(1)} %collective-permute-done.5.refs_4_) | copy-start | bytes 1572868
  38.9 20.3 %collective-permute-start.8 = (bf16[12,256,256]{2,1,0:T(8,128)(2,1)S(1)}, bf16[12,256,256]{2,1,0:T(8,128)(2,1)}, u32[]{:S(2)}, u32[]{:S(2)}) collective-permute-start(bf16[12,256,256]{2,1,0:T(8,128)(2,1)S(1)} %pad_maximum_fusion), channel_id=1, source_target_pairs={{0,1},{1,0},{2,3},{3,2},{4,5},{5,4},{6,7},{7,6},{8,9},{9,8},{10,11... | collective-permute-start | bytes 4718600 | tf_op jit(solution)/shard_map/ppermute | solution.py:286

commit v21 on v18

--- a/solution.py
+++ b/solution.py
@@ -117,8 +117,9 @@
     extent = piece_refs[0].shape[-1]
     half_table = half_ref[...]
     full_table = full_ref[...]
-    for s in range(re_ref.shape[0]):
-        idx = take_ref[s]
+    step = re_ref.shape[0]
+    for s in range(step):
+        idx = take_ref[pl.program_id(0) * step + s]
         image = jnp.zeros((extent, extent), piece_refs[0].dtype)
         base = 0
         bounds = []
@@ -139,11 +140,15 @@
 def make_spectra(take_idx, pieces, scale, half_table, full_table):
     count, extent = (scale.shape[0], scale.shape[-1])
     whole = pl.BlockSpec(memory_space=pltpu.VMEM)
+    step = 2 if count % 2 == 0 else 1
+    plane = pl.BlockSpec((step, extent, extent), lambda s: (s, 0, 0))
     spec_shape = jax.ShapeDtypeStruct((count, extent, extent), jnp.bfloat16)
     return pl.pallas_call(
         functools.partial(spectra_kernel, len(pieces)),
-        in_specs=[pl.BlockSpec(memory_space=pltpu.SMEM)] + [whole] * (len(pieces) + 3),
-        out_specs=[whole, whole],
+        grid=(count // step,),
+        in_specs=[pl.BlockSpec(memory_space=pltpu.SMEM)] + [whole] * len(pieces) + [plane]
+        + [whole] * 2,
+        out_specs=[plane, plane],
         out_shape=[spec_shape, spec_shape],
         cost_estimate=pl.CostEstimate(
             flops=3 * count * 6 * extent * extent * extent, transcendentals=0,

time: 69.2 us -> 69.1 us (level)
  no operation moved by 1% of the time
where the time goes in v21:
time: 69.1 us; the launch traced here: 68.9 us
  Pallas kernels  26.9 us (39%)
  waiting for transfers between devices  14.4 us (21%)
  starting transfers between devices  11.7 us (17%)
  other arithmetic  9.03 us (13%)
  local copies, waits for them, and re-layouts  5.85 us (8%)
  between operations  0.96 us (1%)
    pallas_call x2, Pallas kernels, correlate_chunk(): pl.pallas_call(functools.partial(corr_kernel, first, last, counts, orient...  22.9 us
    ppermute x3, waiting for transfers between devices, route_patches(): lax.ppermute(outgoing[m], 'patch', xor_pairs(sources, 2 * m))  13.9 us
    pallas_call x1, Pallas kernels, make_spectra(): pl.pallas_call(functools.partial(spectra_kernel, len(pieces)), grid=(coun...  4.03 us
    ppermute x3, starting transfers between devices, route_patches(): lax.ppermute(outgoing[m], 'patch', xor_pairs(sources, 2 * m))  3.56 us
    ppermute x1, starting transfers between devices, correlate_all(): lax.ppermute(jnp.concatenate(late_got, axis=0), 'patch', xor_pairs(source...  3.3 us
    ppermute x3, starting transfers between devices, correlate_all(): got = lax.ppermute(mine, 'blk', [(b, b ^ k) for b in range(blocks)])  2.65 us
    ppermute x1, starting transfers between devices, route_patches(): lax.ppermute(jnp.concatenate([outgoing[0], received], axis=0), 'patch', x...  2.23 us
    concatenate x1, other arithmetic, correlate_all(): jnp.concatenate(late_got, axis=0)  1.53 us
  transfers between devices with their start and end apart: 8, of which 3 were waited for; matrix products, arithmetic and copies ran while one was open for 19% of the time, Pallas kernels for 25%

profile of v21, /device:TPU:9, one launch (start us, length us, event | category | flops | bytes accessed | tf_op | source)
XLA Modules:
  0.0 68.9 jit_solution(1585872304834919954)
XLA Ops:
  0.7 1.1 %constant_dynamic-slice_fusion = (bf16[2,256,256]{2,1,0:T(8,128)(2,1)S(1)}, bf16[2,256,256]{2,1,0:T(8,128)(2,1)S(1)}) fusion(bf16[4,256,256]{2,1,0:T(8,128)(2,1)} %param.15, s32[]{:T(128)S(6)} %select_n.312, bf16[4,256,256]{2,1,0:T(8,128)(2,1)} %param.14), kind=kLoop, calls=%fused_computation.46 | loop fusion | bytes 1048580 | tf_op jit(solution)/shard_map/dynamic_slice | solution.py:272
  1.8 0.8 %pad_maximum_fusion.4 = bf16[4,256,256]{2,1,0:T(8,128)(2,1)} fusion(bf16[2,256,256]{2,1,0:T(8,128)(2,1)S(1)} %get-tuple-element.51, bf16[2,256,256]{2,1,0:T(8,128)(2,1)S(1)} %get-tuple-element.52), kind=kLoop, calls=%fused_computation.11 | loop fusion | flops 262144 | bytes 1048576 | tf_op jit(solution)/shard_map/concatenate | solution.py:270
  2.6 2.2 %collective-permute-start.6 = (bf16[4,256,256]{2,1,0:T(8,128)(2,1)}, bf16[4,256,256]{2,1,0:T(8,128)(2,1)}, u32[]{:S(2)}, u32[]{:S(2)}) collective-permute-start(bf16[4,256,256]{2,1,0:T(8,128)(2,1)} %pad_maximum_fusion.4), channel_id=1, source_target_pairs={{0,24},{8,16},{16,8},{24,0},{1,25},{9,17},{17,9},{25,1},{2,26},{10... | collective-permute-start | bytes 1572872 | tf_op jit(solution)/shard_map/ppermute | solution.py:279
  4.8 0.2 collective-permute-start.5
  5.2 0.1 copy.34
  5.3 0.1 copy.36
  5.4 0.1 copy.37
  5.5 0.1 copy.35
  5.7 0.1 fusion.2
  5.8 0.1 copy.38
  5.9 0.1 reshape.722
  6.0 0.1 reshape.721
  6.1 0.6 gather_fusion.1
  6.8 0.2 broadcast_select_fusion
  7.0 1.4 %collective-permute-start.2 = (bf16[2,256,256]{2,1,0:T(8,128)(2,1)S(1)}, bf16[2,256,256]{2,1,0:T(8,128)(2,1)S(1)}, u32[]{:S(2)}, u32[]{:S(2)}) collective-permute-start(bf16[2,256,256]{2,1,0:T(8,128)(2,1)S(1)} %get-tuple-element.28), channel_id=1, source_target_pairs={{0,6},{1,7},{2,4},{3,5},{4,2},{5,3},{6,0},{7,1},{8,14},{9,15},{10,... | collective-permute-start | bytes 786440 | tf_op jit(solution)/shard_map/ppermute | solution.py:86
  8.4 1.1 %collective-permute-start.1 = (bf16[2,256,256]{2,1,0:T(8,128)(2,1)S(1)}, bf16[2,256,256]{2,1,0:T(8,128)(2,1)S(1)}, u32[]{:S(2)}, u32[]{:S(2)}) collective-permute-start(bf16[2,256,256]{2,1,0:T(8,128)(2,1)S(1)} %get-tuple-element.29), channel_id=1, source_target_pairs={{0,4},{1,5},{2,6},{3,7},{4,0},{5,1},{6,2},{7,3},{8,12},{9,13},{10,... | collective-permute-start | bytes 786440 | tf_op jit(solution)/shard_map/ppermute | solution.py:86
  9.5 1.1 %collective-permute-start = (bf16[2,256,256]{2,1,0:T(8,128)(2,1)S(1)}, bf16[2,256,256]{2,1,0:T(8,128)(2,1)S(1)}, u32[]{:S(2)}, u32[]{:S(2)}) collective-permute-start(bf16[2,256,256]{2,1,0:T(8,128)(2,1)S(1)} %get-tuple-element.30), channel_id=1, source_target_pairs={{0,2},{1,3},{2,0},{3,1},{4,6},{5,7},{6,4},{7,5},{8,10},{9,11},{10,... | collective-permute-start | bytes 786440 | tf_op jit(solution)/shard_map/ppermute | solution.py:86
  10.7 0.1 copy.33
  10.8 0.1 reduce
  10.9 0.1 select_reduce_fusion.1
  11.0 0.1 fusion.6
  11.2 0.1 fusion.17
  11.3 0.1 fusion.20
  11.4 0.4 fusion.13
  11.8 0.1 concatenate.96
  11.9 0.2 select_reduce_fusion
  12.1 0.5 broadcast_select_fusion.2.take_ref
  12.7 0.6 gather_fusion.2
  13.4 0.6 gather_fusion.3
  14.1 0.6 gather_fusion
  14.7 0.6 and_select_fusion.6.refs_0_
  15.3 0.1 fusion.1
  15.5 10.3 %collective-permute-done.2 = bf16[2,256,256]{2,1,0:T(8,128)(2,1)S(1)} collective-permute-done((bf16[2,256,256]{2,1,0:T(8,128)(2,1)S(1)}, bf16[2,256,256]{2,1,0:T(8,128)(2,1)S(1)}, u32[]{:S(2)}, u32[]{:S(2)}) %collective-permute-start.2) | collective-permute-done | bytes 262176 | tf_op jit(solution)/shard_map/ppermute | solution.py:86
  25.7 0.3 collective-permute-start.4
  26.0 3.6 %collective-permute-done.1 = bf16[2,256,256]{2,1,0:T(8,128)(2,1)S(1)} collective-permute-done((bf16[2,256,256]{2,1,0:T(8,128)(2,1)S(1)}, bf16[2,256,256]{2,1,0:T(8,128)(2,1)S(1)}, u32[]{:S(2)}, u32[]{:S(2)}) %collective-permute-start.1) | collective-permute-done | bytes 262176 | tf_op jit(solution)/shard_map/ppermute | solution.py:86
  29.6 0.1 pad_maximum_fusion.1
  29.7 2.2 %collective-permute-start.3 = (bf16[8,256,256]{2,1,0:T(8,128)(2,1)S(1)}, bf16[8,256,256]{2,1,0:T(8,128)(2,1)}, u32[]{:S(2)}, u32[]{:S(2)}) collective-permute-start(bf16[8,256,256]{2,1,0:T(8,128)(2,1)S(1)} %pad_maximum_fusion.1), channel_id=1, source_target_pairs={{0,1},{1,0},{2,3},{3,2},{4,5},{5,4},{6,7},{7,6},{8,9},{9,8},{10,11... | collective-permute-start | bytes 3145736 | tf_op jit(solution)/shard_map/ppermute | solution.py:88
  32.0 0.7 gather_fusion.4
  32.6 0.6 and_select_fusion.refs_0_
  33.3 1.1 %pad_maximum_fusion.2.refs_3_ = bf16[8,256,256]{2,1,0:T(8,128)(2,1)} fusion(bf16[4,256,256]{2,1,0:T(8,128)(2,1)S(1)} %copy-done.2, bf16[4,256,256]{2,1,0:T(8,128)(2,1)S(1)} %copy-done.3), kind=kLoop, calls=%fused_computation.7 | loop fusion | flops 524288 | bytes 2097152 | tf_op jit(solution)/shard_map/concatenate | solution.py:269
  34.3 1.3 %negate_multiply_fusion.refs_3_ = f32[4,256,256]{2,1,0:T(8,128)} fusion(f32[4,256]{1,0:T(4,128)S(1)} %get-tuple-element.36, f32[4,256]{1,0:T(4,128)S(1)} %get-tuple-element.38, f32[4,256]{1,0:T(4,128)S(1)} %get-tuple-element.37, f32[4,256]{1,0:T(4,128)S(1)} %get-tuple-element.35), kind=kLoop, calls=%fused_computation.8 | loop fusion | flops 1310720 | bytes 1064960 | tf_op jit(solution)/shard_map/div | solution.py:57
  35.6 1.0 %pad_maximum_fusion.3.refs_1_ = bf16[6,256,256]{2,1,0:T(8,128)(2,1)} fusion(bf16[2,256,256]{2,1,0:T(8,128)(2,1)S(1)} %collective-permute-done.2, bf16[2,256,256]{2,1,0:T(8,128)(2,1)S(1)} %collective-permute-done.1, bf16[2,256,256]{2,1,0:T(8,128)(2,1)S(1)} %collective-permute-done), kind=kLoop, calls=%fused_computation.10 | loop fusion | flops 786432 | bytes 1572864 | tf_op jit(solution)/shard_map/concatenate | solution.py:87
  36.6 0.6 collective-permute-done.4.refs_4_
  37.2 1.5 %pad_maximum_fusion = bf16[12,256,256]{2,1,0:T(8,128)(2,1)S(1)} fusion(bf16[4,256,256]{2,1,0:T(8,128)(2,1)} %collective-permute-done.6.refs_6_, bf16[4,256,256]{2,1,0:T(8,128)(2,1)} %collective-permute-done.5.refs_5_, bf16[4,256,256]{2,1,0:T(8,128)(2,1)} %collective-permute-done.4.refs_4_), kind=kLoop, calls=%fused_computation.5 | loop fusion | flops 1572864 | bytes 3145728 | tf_op jit(solution)/shard_map/concatenate | solution.py:286
  38.7 3.3 %collective-permute-start.7 = (bf16[12,256,256]{2,1,0:T(8,128)(2,1)S(1)}, bf16[12,256,256]{2,1,0:T(8,128)(2,1)}, u32[]{:S(2)}, u32[]{:S(2)}) collective-permute-start(bf16[12,256,256]{2,1,0:T(8,128)(2,1)S(1)} %pad_maximum_fusion), channel_id=1, source_target_pairs={{0,1},{1,0},{2,3},{3,2},{4,5},{5,4},{6,7},{7,6},{8,9},{9,8},{10,11... | collective-permute-start | bytes 4718600 | tf_op jit(solution)/shard_map/ppermute | solution.py:286
  42.0 4.0 %shard_map.129 = (bf16[4,256,256]{2,1,0:T(8,128)(2,1)}, bf16[4,256,256]{2,1,0:T(8,128)(2,1)}) custom-call(s32[4]{0:T(128)} %broadcast_select_fusion.2.take_ref, bf16[2,256,256]{2,1,0:T(8,128)(2,1)} %refs_0_.1, bf16[6,256,256]{2,1,0:T(8,128)(2,1)} %pad_maximum_fusion.3.refs_1_, bf16[8,256,256]{2,1,0:T(8,128)(2,1)} %collective-permute-done.3.refs_2_, ...), custom_call_target="tpu_custom_call" | custom-call | flops 1207959552 | bytes 2621440 | tf_op jit(solution)/shard_map/pallas_call | solution.py:146
  46.0 13.1 %shard_map.130 = (f32[4,256,256]{2,1,0:T(8,128)}, f32[4,256,256]{2,1,0:T(8,128)}, f32[4,256,256]{2,1,0:T(8,128)}, f32[4,8,128]{2,1,0:T(8,128)}) custom-call(s32[10]{0:T(128)} %and_select_fusion.refs_0_, bf16[4,256,256]{2,1,0:T(8,128)(2,1)} %get-tuple-element.12.refs_1_, bf16[4,256,256]{2,1,0:T(8,128)(2,1)} %get-tuple-element.13.refs_2_, ...), custom_call_target="tpu_custom_call" | custom-call | flops 24159191040 | bytes 15728640 | tf_op jit(solution)/shard_map/pallas_call | solution.py:244
  59.2 9.7 %shard_map.131 = (f32[4,256,256]{2,1,0:T(8,128)}, f32[4,256,256]{2,1,0:T(8,128)}, f32[4,256,256]{2,1,0:T(8,128)}, f32[4,16]{1,0:T(4,128)}) custom-call(s32[6]{0:T(128)} %and_select_fusion.6.refs_0_, bf16[4,256,256]{2,1,0:T(8,128)(2,1)} %get-tuple-element.12.refs_1_, ...), custom_call_target="tpu_custom_call", output_to_operand_aliasing={{0}: (6, {}), {1}: (7, {}), {2}: (8, {})} | custom-call | flops 14495514624 | bytes 13631488 | tf_op jit(solution)/shard_map/pallas_call | solution.py:244
  (55 shorter events, 0.6 us)
Async XLA Ops:
  0.6 13.4 %copy-start = (s32[16]{0:T(128)S(1)}, s32[16]{0:T(128)}, u32[]{:S(2)}) copy-start(s32[16]{0:T(128)} %param.16) | copy-start | bytes 196
  0.6 4.4 %copy-start.5 = (s32[16]{0:T(128)S(1)}, s32[16]{0:T(128)}, u32[]{:S(2)}) copy-start(s32[16]{0:T(128)} %param.11) | copy-start | bytes 196
  0.7 5.4 %copy-start.4 = (bf16[2,256,256]{2,1,0:T(8,128)(2,1)S(1)}, bf16[2,256,256]{2,1,0:T(8,128)(2,1)}, u32[]{:S(2)}) copy-start(bf16[2,256,256]{2,1,0:T(8,128)(2,1)} %refs_0_.1) | copy-start | bytes 786436
  2.6 34.0 %collective-permute-start.6 = (bf16[4,256,256]{2,1,0:T(8,128)(2,1)}, bf16[4,256,256]{2,1,0:T(8,128)(2,1)}, u32[]{:S(2)}, u32[]{:S(2)}) collective-permute-start(bf16[4,256,256]{2,1,0:T(8,128)(2,1)} %pad_maximum_fusion.4), channel_id=1, source_target_pairs={{0,24},{8,16},{16,8},{24,0},{1,25},{9,17},{17,9},{25,1},{2,26},{10... | collective-permute-start | bytes 1572872 | tf_op jit(solution)/shard_map/ppermute | solution.py:279
  4.8 31.8 %collective-permute-start.5 = (bf16[4,256,256]{2,1,0:T(8,128)(2,1)}, bf16[4,256,256]{2,1,0:T(8,128)(2,1)}, u32[]{:S(2)}, u32[]{:S(2)}) collective-permute-start(bf16[4,256,256]{2,1,0:T(8,128)(2,1)} %pad_maximum_fusion.4), channel_id=1, source_target_pairs={{0,16},{8,24},{16,0},{24,8},{1,17},{9,25},{17,1},{25,9},{2,18},{10... | collective-permute-start | bytes 1572872 | tf_op jit(solution)/shard_map/ppermute | solution.py:279
  6.9 5.7 %copy-start.6 = (s32[16]{0:T(128)S(1)}, s32[16]{0:T(128)}, u32[]{:S(2)}) copy-start(s32[16]{0:T(128)} %param.12) | copy-start | bytes 196
  6.9 6.4 %copy-start.1 = (f32[32]{0:T(128)S(1)}, f32[32]{0:T(128)}, u32[]{:S(2)}) copy-start(f32[32]{0:T(128)} %param.13) | copy-start | bytes 388
  7.0 18.7 %collective-permute-start.2 = (bf16[2,256,256]{2,1,0:T(8,128)(2,1)S(1)}, bf16[2,256,256]{2,1,0:T(8,128)(2,1)S(1)}, u32[]{:S(2)}, u32[]{:S(2)}) collective-permute-start(bf16[2,256,256]{2,1,0:T(8,128)(2,1)S(1)} %get-tuple-element.28), channel_id=1, source_target_pairs={{0,6},{1,7},{2,4},{3,5},{4,2},{5,3},{6,0},{7,1},{8,14},{9,15},{10,... | collective-permute-start | bytes 786440 | tf_op jit(solution)/shard_map/ppermute | solution.py:86
  8.4 21.2 %collective-permute-start.1 = (bf16[2,256,256]{2,1,0:T(8,128)(2,1)S(1)}, bf16[2,256,256]{2,1,0:T(8,128)(2,1)S(1)}, u32[]{:S(2)}, u32[]{:S(2)}) collective-permute-start(bf16[2,256,256]{2,1,0:T(8,128)(2,1)S(1)} %get-tuple-element.29), channel_id=1, source_target_pairs={{0,4},{1,5},{2,6},{3,7},{4,0},{5,1},{6,2},{7,3},{8,12},{9,13},{10,... | collective-permute-start | bytes 786440 | tf_op jit(solution)/shard_map/ppermute | solution.py:86
  9.5 20.1 %collective-permute-start = (bf16[2,256,256]{2,1,0:T(8,128)(2,1)S(1)}, bf16[2,256,256]{2,1,0:T(8,128)(2,1)S(1)}, u32[]{:S(2)}, u32[]{:S(2)}) collective-permute-start(bf16[2,256,256]{2,1,0:T(8,128)(2,1)S(1)} %get-tuple-element.30), channel_id=1, source_target_pairs={{0,2},{1,3},{2,0},{3,1},{4,6},{5,7},{6,4},{7,5},{8,10},{9,11},{10,... | collective-permute-start | bytes 786440 | tf_op jit(solution)/shard_map/ppermute | solution.py:86
  14.1 19.2 %copy-start.2 = (bf16[4,256,256]{2,1,0:T(8,128)(2,1)S(1)}, bf16[4,256,256]{2,1,0:T(8,128)(2,1)}, u32[]{:S(2)}) copy-start(bf16[4,256,256]{2,1,0:T(8,128)(2,1)} %param.15) | copy-start | bytes 1572868
  14.1 19.2 %copy-start.3 = (bf16[4,256,256]{2,1,0:T(8,128)(2,1)S(1)}, bf16[4,256,256]{2,1,0:T(8,128)(2,1)}, u32[]{:S(2)}) copy-start(bf16[4,256,256]{2,1,0:T(8,128)(2,1)} %param.14) | copy-start | bytes 1572868
  25.7 11.4 %collective-permute-start.4 = (bf16[4,256,256]{2,1,0:T(8,128)(2,1)}, bf16[4,256,256]{2,1,0:T(8,128)(2,1)}, u32[]{:S(2)}, u32[]{:S(2)}) collective-permute-start(bf16[4,256,256]{2,1,0:T(8,128)(2,1)} %pad_maximum_fusion.4), channel_id=1, source_target_pairs={{0,8},{8,0},{16,24},{24,16},{1,9},{9,1},{17,25},{25,17},{2,10},{10... | collective-permute-start | bytes 1572872 | tf_op jit(solution)/shard_map/ppermute | solution.py:279
  29.7 12.3 %collective-permute-start.3 = (bf16[8,256,256]{2,1,0:T(8,128)(2,1)S(1)}, bf16[8,256,256]{2,1,0:T(8,128)(2,1)}, u32[]{:S(2)}, u32[]{:S(2)}) collective-permute-start(bf16[8,256,256]{2,1,0:T(8,128)(2,1)S(1)} %pad_maximum_fusion.1), channel_id=1, source_target_pairs={{0,1},{1,0},{2,3},{3,2},{4,5},{5,4},{6,7},{7,6},{8,9},{9,8},{10,11... | collective-permute-start | bytes 3145736 | tf_op jit(solution)/shard_map/ppermute | solution.py:88
  38.7 20.5 %collective-permute-start.7 = (bf16[12,256,256]{2,1,0:T(8,128)(2,1)S(1)}, bf16[12,256,256]{2,1,0:T(8,128)(2,1)}, u32[]{:S(2)}, u32[]{:S(2)}) collective-permute-start(bf16[12,256,256]{2,1,0:T(8,128)(2,1)S(1)} %pad_maximum_fusion), channel_id=1, source_target_pairs={{0,1},{1,0},{2,3},{3,2},{4,5},{5,4},{6,7},{7,6},{8,9},{9,8},{10,11... | collective-permute-start | bytes 4718600 | tf_op jit(solution)/shard_map/ppermute | solution.py:286
